TPU v7x, 32 devices: a whole 2x2x4 slice. The times are simulated.
32 devices in a mesh: groups: 2 (over x), height: 16 (over z, y, core).
Axes of the slice: x: 2, y: 2, z: 4, core: 2. Of those that a mesh axis runs over, the one named last changes fastest.
Arguments:
- latent: bfloat16 [3, 64, 80, 512], P(None, ('groups', 'height')), parts along dimension 1, may hold values from -120 to 120
- gain_first: float32 [512], replicated, may hold values from 0.1 to 1.9
- shift_first: float32 [512], replicated, may hold values from -3 to 3
- kernel_first: bfloat16 [27, 512, 512], P(None, 'height'), may hold values from -0.0546875 to 0.0546875
- bias_first: float32 [512], replicated, may hold values from -2 to 2
- gain_second: float32 [512], replicated, may hold values from 0.1 to 1.9
- shift_second: float32 [512], replicated, may hold values from -3 to 3
- kernel_second: bfloat16 [27, 512, 512], P(None, 'height'), may hold values from -0.0546875 to 0.0546875
- bias_second: float32 [512], replicated, may hold values from -2 to 2
Outputs:
- upsampled: bfloat16 [3, 128, 160, 512], P(None, ('groups', 'height')), parts along dimension 1
There are 2 independent parts, one for each index of `groups`. A program takes and returns all parts, laid end to end along the dimension named above; an argument that names none is the same for every part. Nothing has to cross between parts.
All inputs are finite; a program needn't handle non-finite values.
Results may differ from a plain program's by a relative error of at most 0.0045.
Values may be sent and summed in bfloat16 or wider, within the bound.
No kernel may reach another device: no remote copies, remote signals or barrier semaphores. Data moves between devices by JAX's collectives and lax.ppermute only.
A program may use at most 128 MiB of HBM per device.

v0:
```python
import jax
import jax.numpy as jnp
from jax import lax
from jax.experimental import pallas as pl
from jax.experimental.pallas import tpu as pltpu
from jax.sharding import Mesh
from jax.sharding import PartitionSpec as P

GROUPS = 32
CHAN_BLOCKS = 4
EPS = 1e-06


def shift_pairs(count, step):
    return [(i, (i + step) % count) for i in range(count)]


def butterfly_stats(sums, squares, count, axes):
    for axis in axes:
        size = lax.axis_size(axis)
        bit = 1
        while bit < size:
            pairs = [(i, i ^ bit) for i in range(size)]
            other_sums, other_squares = lax.ppermute((sums, squares), axis, pairs)
            gap = sums - other_sums
            squares = (squares + other_squares) + gap * gap / (2.0 * count)
            sums = sums + other_sums
            count = count * 2
            bit *= 2
    return sums, squares, count


def local_stats(values, groups):
    frames, rows, cols, chans = values.shape
    grouped = values.reshape(frames * rows * cols, groups, chans // groups)
    count = float(frames * rows * cols * (chans // groups))
    sums = jnp.sum(grouped, axis=(0, 2))
    centred = grouped - (sums / count)[None, :, None]
    squares = jnp.sum(centred * centred, axis=(0, 2))
    return sums, squares, count


def group_scale(sums, squares, count, group_size):
    mean = sums / count
    scale = lax.rsqrt(squares / count + EPS)
    return jnp.repeat(mean, group_size), jnp.repeat(scale, group_size)


def activate(values, mean_chan, scale_chan, gain, shift):
    normed = (values - mean_chan) * scale_chan * gain + shift
    return jax.nn.silu(normed).astype(jnp.bfloat16)


def gather_blocks(block, axis_name, dim, total):
    size = lax.axis_size(axis_name)
    me = lax.axis_index(axis_name)
    width = block.shape[dim]
    shape = list(block.shape)
    shape[dim] = total
    out = jnp.zeros(shape, block.dtype)
    for step in range(size):
        piece = block if step == 0 else lax.ppermute(block, axis_name, shift_pairs(size, step))
        source = (me - step) % size
        start = [0] * len(shape)
        start[dim] = source * width
        out = lax.dynamic_update_slice(out, piece, start)
    return out


def with_row_halo(cells, axis_name):
    size = lax.axis_size(axis_name)
    down = [(i, i + 1) for i in range(size - 1)]
    up = [(i + 1, i) for i in range(size - 1)]
    top = lax.ppermute(cells[:, -1:], axis_name, down)
    bottom = lax.ppermute(cells[:, :1], axis_name, up)
    return jnp.concatenate([top, cells, bottom], axis=1)


def conv_body(x_ref, w_ref, b_ref, o_ref, acc_ref):
    step = pl.program_id(0)
    rows, cols, outs = o_ref.shape[1:]
    chans = x_ref.shape[-1]
    acc_ref[...] = jnp.broadcast_to(b_ref[...], acc_ref.shape)
    for i in range(3):
        for j in range(3):
            for k in range(3):
                patch = x_ref[step + i, pl.ds(j, rows), pl.ds(k, cols), :]
                acc_ref[...] += jnp.dot(
                    patch.reshape(rows * cols, chans),
                    w_ref[9 * i + 3 * j + k],
                    preferred_element_type=jnp.float32,
                )
    o_ref[0] = acc_ref[...].reshape(rows, cols, outs).astype(o_ref.dtype)


def causal_conv(extended, kernel, bias, out_dtype):
    leading = jnp.concatenate([extended[:1], extended[:1], extended], axis=0)
    padded = jnp.pad(leading, ((0, 0), (0, 0), (1, 1), (0, 0)))
    frames = extended.shape[0]
    rows = extended.shape[1] - 2
    cols = extended.shape[2]
    taps, chans, outs = kernel.shape
    flops = 2 * frames * rows * cols * chans * outs * taps
    moved = padded.size * 2 + kernel.size * 2 + frames * rows * cols * outs * 4
    return pl.pallas_call(
        conv_body,
        grid=(frames,),
        in_specs=[
            pl.BlockSpec(padded.shape, lambda t: (0, 0, 0, 0)),
            pl.BlockSpec(kernel.shape, lambda t: (0, 0, 0)),
            pl.BlockSpec((1, outs), lambda t: (0, 0)),
        ],
        out_specs=pl.BlockSpec((1, rows, cols, outs), lambda t: (t, 0, 0, 0)),
        out_shape=jax.ShapeDtypeStruct((frames, rows, cols, outs), out_dtype),
        scratch_shapes=[pltpu.VMEM((rows * cols, outs), jnp.float32)],
        cost_estimate=pl.CostEstimate(flops=flops, bytes_accessed=moved, transcendentals=0),
    )(padded, kernel, bias.reshape(1, outs))


def kernel_block(shard, chans):
    size = lax.axis_size("hq")
    me = lax.axis_index("hq")
    taps, in_block, outs = shard.shape
    width = outs // size
    out = jnp.zeros((taps, in_block * size, width), shard.dtype)
    for step in range(size):
        target = (me + step) % size
        piece = lax.dynamic_slice_in_dim(shard, target * width, width, axis=2)
        if step:
            piece = lax.ppermute(piece, "hq", shift_pairs(size, step))
        source = (me - step) % size
        out = lax.dynamic_update_slice(out, piece, (0, source * in_block, 0))
    return lax.all_gather(out, "hz", axis=1, tiled=True)


def scatter_rows(branch, slab_rows, chans):
    size = lax.axis_size("hq")
    me = lax.axis_index("hq")
    frames, rows, cols, width = branch.shape
    out = jnp.zeros((frames, slab_rows, cols, chans), branch.dtype)
    for step in range(size):
        target = (me + step) % size
        piece = lax.dynamic_slice_in_dim(branch, target * slab_rows, slab_rows, axis=1)
        if step:
            piece = lax.ppermute(piece, "hq", shift_pairs(size, step))
        source = (me - step) % size
        out = lax.dynamic_update_slice(out, piece, (0, 0, 0, source * width))
    return out


def per_device(
    latent,
    gain_first,
    shift_first,
    kernel_first,
    bias_first,
    gain_second,
    shift_second,
    kernel_second,
    bias_second,
):
    frames, slab_rows, cols, chans = latent.shape
    blocks = lax.axis_size("hq")
    width = chans // blocks
    me = lax.axis_index("hq")
    group_size = chans // GROUPS

    weights_first = kernel_block(kernel_first, chans)
    weights_second = kernel_block(kernel_second, chans)

    values = latent.astype(jnp.float32)
    sums, squares, count = local_stats(values, GROUPS)
    sums, squares, count = butterfly_stats(sums, squares, count, ("hq", "hz"))
    mean_chan, scale_chan = group_scale(sums, squares, count, group_size)
    act_first = activate(values, mean_chan, scale_chan, gain_first, shift_first)

    group_rows = gather_blocks(act_first, "hq", 1, slab_rows * blocks)
    extended = with_row_halo(group_rows, "hz")
    own_bias = lax.dynamic_slice_in_dim(bias_first, me * width, width)
    hidden = causal_conv(extended, weights_first, own_bias, jnp.bfloat16)

    hidden_values = hidden.astype(jnp.float32)
    sums, squares, count = local_stats(hidden_values, width // group_size)
    sums, squares, count = butterfly_stats(sums, squares, count, ("hz",))
    mean_own, scale_own = group_scale(sums, squares, count, group_size)
    own_gain = lax.dynamic_slice_in_dim(gain_second, me * width, width)
    own_shift = lax.dynamic_slice_in_dim(shift_second, me * width, width)
    act_second = activate(hidden_values, mean_own, scale_own, own_gain, own_shift)

    extended_next = with_row_halo(act_second, "hz")
    extended_next = gather_blocks(extended_next, "hq", 3, chans)
    own_bias_next = lax.dynamic_slice_in_dim(bias_second, me * width, width)
    branch = causal_conv(extended_next, weights_second, own_bias_next, jnp.float32)

    branch_rows = scatter_rows(branch, slab_rows, chans)
    summed = (values + branch_rows).astype(jnp.bfloat16)
    return jnp.repeat(jnp.repeat(summed, 2, axis=1), 2, axis=2)


def solution(mesh):
    groups = mesh.shape["groups"]
    height = mesh.shape["height"]
    blocks = CHAN_BLOCKS
    split = Mesh(mesh.devices.reshape(groups, height // blocks, blocks), ("groups", "hz", "hq"))
    rows = ("groups", "hz", "hq")
    placed = (
        P(None, rows, None, None),
        P(),
        P(),
        P(None, ("hz", "hq"), None),
        P(),
        P(),
        P(),
        P(None, ("hz", "hq"), None),
        P(),
    )
    return jax.shard_map(
        per_device,
        mesh=split,
        in_specs=placed,
        out_specs=P(None, rows, None, None),
        check_vma=False,
    )
```

profile of v0, /device:TPU:1, one launch (start us, length us, event | category | flops | bytes accessed | tf_op | source)
XLA Modules:
  0.0 222.8 jit_solution(13904089369344183937)
XLA Ops:
  8.2 2.7 %collective-permute-start.13 = (bf16[27,32,128]{2,1,0:T(8,128)(2,1)S(1)}, bf16[27,32,128]{2,1,0:T(8,128)(2,1)S(1)}, u32[]{:S(2)}, u32[]{:S(2)}) collective-permute-start(bf16[27,32,128]{2,1,0:T(8,128)(2,1)S(1)} %get-tuple-element.18), channel_id=1, source_target_pairs={{0,1},{1,2},{2,3},{3,0},{4,5},{5,6},{6,7},{7,4},{8,9},{9,10},{10,1... | collective-permute-start | bytes 663560 | tf_op jit(solution)/shard_map/ppermute | solution.py:130
  11.3 4.2 %collective-permute-done.13 = bf16[27,32,128]{2,1,0:T(8,128)(2,1)S(1)} collective-permute-done((bf16[27,32,128]{2,1,0:T(8,128)(2,1)S(1)}, bf16[27,32,128]{2,1,0:T(8,128)(2,1)S(1)}, u32[]{:S(2)}, u32[]{:S(2)}) %collective-permute-start.13) | collective-permute-done | bytes 221216 | tf_op jit(solution)/shard_map/ppermute | solution.py:130
  15.5 4.7 %collective-permute-done.14 = bf16[27,32,128]{2,1,0:T(8,128)(2,1)S(1)} collective-permute-done((bf16[27,32,128]{2,1,0:T(8,128)(2,1)S(1)}, bf16[27,32,128]{2,1,0:T(8,128)(2,1)S(1)}, u32[]{:S(2)}, u32[]{:S(2)}) %collective-permute-start.14) | collective-permute-done | bytes 221216 | tf_op jit(solution)/shard_map/ppermute | solution.py:130
  32.2 2.3 %collective-permute-start.3 = (f32[32]{0:T(128)S(1)}, f32[32]{0:T(128)S(1)}, u32[]{:S(2)}, u32[]{:S(2)}) collective-permute-start(f32[32]{0:T(128)S(1)} %get-tuple-element.32), channel_id=1, source_target_pairs={{0,8},{4,12},{8,0},{12,4},{1,9},{5,13},{9,1},{13,5},{2,10},{6,14},... | collective-permute-start | bytes 392 | tf_op jit(solution)/shard_map/ppermute | solution.py:24
  35.5 3.2 %collective-permute-done.7 = f32[32]{0:T(128)S(1)} collective-permute-done((f32[32]{0:T(128)S(1)}, f32[32]{0:T(128)S(1)}, u32[]{:S(2)}, u32[]{:S(2)}) %collective-permute-start.7) | collective-permute-done | bytes 160 | tf_op jit(solution)/shard_map/ppermute | solution.py:24
  40.4 3.9 %collective-permute-start.8 = (bf16[3,2,80,512]{3,2,1,0:T(8,128)(2,1)}, bf16[3,2,80,512]{3,2,1,0:T(8,128)(2,1)}, u32[]{:S(2)}, u32[]{:S(2)}) collective-permute-start(bf16[3,2,80,512]{3,2,1,0:T(8,128)(2,1)} %get-tuple-element.6), channel_id=1, source_target_pairs={{0,1},{1,2},{2,3},{3,0},{4,5},{5,6},{6,7},{7,4},{8,9},{9,10},{10,1... | collective-permute-start | bytes 1474568 | tf_op jit(solution)/shard_map/ppermute | solution.py:62
  44.3 2.5 %collective-permute-start.9 = (bf16[3,2,80,512]{3,2,1,0:T(8,128)(2,1)}, bf16[3,2,80,512]{3,2,1,0:T(8,128)(2,1)}, u32[]{:S(2)}, u32[]{:S(2)}) collective-permute-start(bf16[3,2,80,512]{3,2,1,0:T(8,128)(2,1)} %get-tuple-element.6), channel_id=1, source_target_pairs={{0,2},{1,3},{2,0},{3,1},{4,6},{5,7},{6,4},{7,5},{8,10},{9,11},{10,... | collective-permute-start | bytes 1474568 | tf_op jit(solution)/shard_map/ppermute | solution.py:62
  47.1 2.2 constant_dynamic-slice_fusion.2
  54.2 4.6 %collective-permute-start.27 = (bf16[27,32,128]{2,1,0:T(8,128)(2,1)}, bf16[27,32,128]{2,1,0:T(8,128)(2,1)S(1)}, u32[]{:S(2)}, u32[]{:S(2)}) collective-permute-start(bf16[27,32,128]{2,1,0:T(8,128)(2,1)} %get-tuple-element.13), channel_id=1, source_target_pairs={{0,3},{1,0},{2,1},{3,2},{4,7},{5,4},{6,5},{7,6},{8,11},{9,8},{10,9... | collective-permute-start | bytes 663560 | tf_op jit(solution)/shard_map/ppermute | solution.py:130
  59.9 9.1 %collective-permute-done.9 = bf16[3,2,80,512]{3,2,1,0:T(8,128)(2,1)} collective-permute-done((bf16[3,2,80,512]{3,2,1,0:T(8,128)(2,1)}, bf16[3,2,80,512]{3,2,1,0:T(8,128)(2,1)}, u32[]{:S(2)}, u32[]{:S(2)}) %collective-permute-start.9) | collective-permute-done | bytes 491552 | tf_op jit(solution)/shard_map/ppermute | solution.py:62
  73.2 4.7 %collective-permute-start.11 = (bf16[3,1,80,512]{3,2,1,0:T(8,128)(2,1)}, bf16[3,1,80,512]{3,2,1,0:T(8,128)(2,1)}, u32[]{:S(2)}, u32[]{:S(2)}) collective-permute-start(bf16[3,1,80,512]{3,2,1,0:T(8,128)(2,1)} %get-tuple-element.7), channel_id=1, source_target_pairs={{0,4},{4,8},{8,12},{1,5},{5,9},{9,13},{2,6},{6,10},{10,14},{3,7},{... | collective-permute-start | bytes 737288 | tf_op jit(solution)/shard_map/ppermute | solution.py:74
  80.9 10.6 %collective-permute-done.12 = bf16[3,1,80,512]{3,2,1,0:T(8,128)(2,1)} collective-permute-done((bf16[3,1,80,512]{3,2,1,0:T(8,128)(2,1)}, bf16[3,1,80,512]{3,2,1,0:T(8,128)(2,1)}, u32[]{:S(2)}, u32[]{:S(2)}) %collective-permute-start.12) | collective-permute-done | bytes 245792 | tf_op jit(solution)/shard_map/ppermute | solution.py:75
  92.5 4.7 %fusion.7.x_ref = bf16[5,10,82,512]{3,2,1,0:T(8,128)(2,1)} fusion(bf16[3,1,80,512]{3,2,1,0:T(8,128)(2,1)} %collective-permute-done.12, bf16[1,10,80,512]{3,2,1,0:T(8,128)(2,1)S(1)} %pad_maximum_fusion, bf16[3,8,80,512]{3,2,1,0:T(8,128)(2,1)S(1)} %constant_dynamic-update-slice_fusion.13, bf16[3,1,80,512]{3,2,1,0:T(8,128)(2,1)} %collective-permute-done.11), kind=kLoop, calls=%fused_computation.11 | loop fusion | flops 37785600 | bytes 7475200 | tf_op jit(solution)/shard_map/concatenate | solution.py:97
  98.5 18.5 %shard_map.91 = bf16[3,8,80,128]{3,2,1,0:T(8,128)(2,1)} custom-call(bf16[5,10,82,512]{3,2,1,0:T(8,128)(2,1)} %fusion.7.x_ref, bf16[27,512,128]{2,1,0:T(8,128)(2,1)} %all-gather.3.cloned.1.call-done.w_ref, f32[1,128]{1,0:T(1,128)} %dynamic-slice_bitcast_fusion.1.b_ref), custom_call_target="tpu_custom_call" | custom-call | flops 6794772480 | bytes 8720384 | tf_op jit(solution)/shard_map/pallas_call | solution.py:105
  123.0 3.3 %collective-permute-start.17 = (f32[8]{0:T(128)S(1)}, f32[8]{0:T(128)S(1)}, u32[]{:S(2)}, u32[]{:S(2)}) collective-permute-start(f32[8]{0:T(128)S(1)} %get-tuple-element.28), channel_id=1, source_target_pairs={{0,8},{4,12},{8,0},{12,4},{1,9},{5,13},{9,1},{13,5},{2,10},{6,14},... | collective-permute-start | bytes 104 | tf_op jit(solution)/shard_map/ppermute | solution.py:24
  126.4 2.0 collective-permute-done.17
  133.0 4.0 %collective-permute-start.20 = (bf16[3,1,80,128]{3,2,1,0:T(8,128)(2,1)S(1)}, bf16[3,1,80,128]{3,2,1,0:T(8,128)(2,1)S(1)}, u32[]{:S(2)}, u32[]{:S(2)}) collective-permute-start(bf16[3,1,80,128]{3,2,1,0:T(8,128)(2,1)S(1)} %get-tuple-element.23), channel_id=1, source_target_pairs={{0,4},{4,8},{8,12},{1,5},{5,9},{9,13},{2,6},{6,10},{10,14},{3,7},{... | collective-permute-start | bytes 184328 | tf_op jit(solution)/shard_map/ppermute | solution.py:74
  140.7 5.6 %collective-permute-start.22 = (bf16[3,10,80,128]{3,2,1,0:T(8,128)(2,1)}, bf16[3,10,80,128]{3,2,1,0:T(8,128)(2,1)}, u32[]{:S(2)}, u32[]{:S(2)}) collective-permute-start(bf16[3,10,80,128]{3,2,1,0:T(8,128)(2,1)} %get-tuple-element.21), channel_id=1, source_target_pairs={{0,1},{1,2},{2,3},{3,0},{4,5},{5,6},{6,7},{7,4},{8,9},{9,10},{10,1... | collective-permute-start | bytes 1843208 | tf_op jit(solution)/shard_map/ppermute | solution.py:62
  148.1 11.7 %collective-permute-done.22 = bf16[3,10,80,128]{3,2,1,0:T(8,128)(2,1)} collective-permute-done((bf16[3,10,80,128]{3,2,1,0:T(8,128)(2,1)}, bf16[3,10,80,128]{3,2,1,0:T(8,128)(2,1)}, u32[]{:S(2)}, u32[]{:S(2)}) %collective-permute-start.22) | collective-permute-done | bytes 614432 | tf_op jit(solution)/shard_map/ppermute | solution.py:62
  161.0 12.8 %collective-permute-done.23 = bf16[3,10,80,128]{3,2,1,0:T(8,128)(2,1)} collective-permute-done((bf16[3,10,80,128]{3,2,1,0:T(8,128)(2,1)}, bf16[3,10,80,128]{3,2,1,0:T(8,128)(2,1)}, u32[]{:S(2)}, u32[]{:S(2)}) %collective-permute-start.23) | collective-permute-done | bytes 614432 | tf_op jit(solution)/shard_map/ppermute | solution.py:62
  176.3 3.1 %select_maximum_fusion.x_ref = bf16[5,10,82,512]{3,2,1,0:T(8,128)(2,1)} fusion(bf16[3,10,80,512]{3,2,1,0:T(8,128)(2,1)S(1)} %constant_dynamic-update-slice_fusion.6, bf16[1,10,80,512]{3,2,1,0:T(8,128)(2,1)S(1)} %slice.30), kind=kLoop, calls=%fused_computation.3 | loop fusion | flops 25190400 | bytes 7475200 | tf_op jit(solution)/shard_map/concatenate | solution.py:97
  179.4 18.5 %shard_map.92 = f32[3,8,80,128]{3,2,1,0:T(8,128)} custom-call(bf16[5,10,82,512]{3,2,1,0:T(8,128)(2,1)} %select_maximum_fusion.x_ref, bf16[27,512,128]{2,1,0:T(8,128)(2,1)} %all-gather.5.cloned.1.call-done.w_ref, f32[1,128]{1,0:T(1,128)} %dynamic-slice_bitcast_fusion.b_ref), custom_call_target="tpu_custom_call" | custom-call | flops 6794772480 | bytes 8720384 | tf_op jit(solution)/shard_map/pallas_call | solution.py:105
  203.3 7.4 %collective-permute-done.29 = f32[3,2,80,128]{3,2,1,0:T(8,128)S(1)} collective-permute-done((f32[3,2,80,128]{3,2,1,0:T(8,128)S(1)}, f32[3,2,80,128]{3,2,1,0:T(8,128)S(1)}, u32[]{:S(2)}, u32[]{:S(2)}) %collective-permute-start.29) | collective-permute-done | bytes 245792 | tf_op jit(solution)/shard_map/ppermute | solution.py:145
  213.8 2.2 reshape.37
  (130 shorter events, 60.7 us)
Async XLA Ops:
  6.5 91.9 %all-gather.3.cloned.1.call-start = ((), (), s32[]{:S(2)}) async-start(), calls=%async_computation | async-start | bytes 4423680 | tf_op jit(solution)/shard_map/all_gather | solution.py:133
  8.2 7.3 %collective-permute-start.13 = (bf16[27,32,128]{2,1,0:T(8,128)(2,1)S(1)}, bf16[27,32,128]{2,1,0:T(8,128)(2,1)S(1)}, u32[]{:S(2)}, u32[]{:S(2)}) collective-permute-start(bf16[27,32,128]{2,1,0:T(8,128)(2,1)S(1)} %get-tuple-element.18), channel_id=1, source_target_pairs={{0,1},{1,2},{2,3},{3,0},{4,5},{5,6},{6,7},{7,4},{8,9},{9,10},{10,1... | collective-permute-start | bytes 663560 | tf_op jit(solution)/shard_map/ppermute | solution.py:130
  10.8 9.4 %collective-permute-start.14 = (bf16[27,32,128]{2,1,0:T(8,128)(2,1)S(1)}, bf16[27,32,128]{2,1,0:T(8,128)(2,1)S(1)}, u32[]{:S(2)}, u32[]{:S(2)}) collective-permute-start(bf16[27,32,128]{2,1,0:T(8,128)(2,1)S(1)} %get-tuple-element.20), channel_id=1, source_target_pairs={{0,2},{1,3},{2,0},{3,1},{4,6},{5,7},{6,4},{7,5},{8,10},{9,11},{10,... | collective-permute-start | bytes 663560 | tf_op jit(solution)/shard_map/ppermute | solution.py:130
  10.8 9.9 %collective-permute-start.15 = (bf16[27,32,128]{2,1,0:T(8,128)(2,1)S(1)}, bf16[27,32,128]{2,1,0:T(8,128)(2,1)S(1)}, u32[]{:S(2)}, u32[]{:S(2)}) collective-permute-start(bf16[27,32,128]{2,1,0:T(8,128)(2,1)S(1)} %get-tuple-element.17), channel_id=1, source_target_pairs={{0,3},{1,0},{2,1},{3,2},{4,7},{5,4},{6,5},{7,6},{8,11},{9,8},{10,9... | collective-permute-start | bytes 663560 | tf_op jit(solution)/shard_map/ppermute | solution.py:130
  21.7 157.8 %all-gather.5.cloned.1.call-start = ((), (), s32[]{:S(2)}) async-start(), calls=%async_computation.1 | async-start | bytes 4423680 | tf_op jit(solution)/shard_map/all_gather | solution.py:133
  34.5 4.2 %collective-permute-start.7 = (f32[32]{0:T(128)S(1)}, f32[32]{0:T(128)S(1)}, u32[]{:S(2)}, u32[]{:S(2)}) collective-permute-start(f32[32]{0:T(128)S(1)} %get-tuple-element.31), channel_id=1, source_target_pairs={{0,8},{4,12},{8,0},{12,4},{1,9},{5,13},{9,1},{13,5},{2,10},{6,14},... | collective-permute-start | bytes 392 | tf_op jit(solution)/shard_map/ppermute | solution.py:24
  40.4 13.8 %collective-permute-start.8 = (bf16[3,2,80,512]{3,2,1,0:T(8,128)(2,1)}, bf16[3,2,80,512]{3,2,1,0:T(8,128)(2,1)}, u32[]{:S(2)}, u32[]{:S(2)}) collective-permute-start(bf16[3,2,80,512]{3,2,1,0:T(8,128)(2,1)} %get-tuple-element.6), channel_id=1, source_target_pairs={{0,1},{1,2},{2,3},{3,0},{4,5},{5,6},{6,7},{7,4},{8,9},{9,10},{10,1... | collective-permute-start | bytes 1474568 | tf_op jit(solution)/shard_map/ppermute | solution.py:62
  44.3 24.6 %collective-permute-start.9 = (bf16[3,2,80,512]{3,2,1,0:T(8,128)(2,1)}, bf16[3,2,80,512]{3,2,1,0:T(8,128)(2,1)}, u32[]{:S(2)}, u32[]{:S(2)}) collective-permute-start(bf16[3,2,80,512]{3,2,1,0:T(8,128)(2,1)} %get-tuple-element.6), channel_id=1, source_target_pairs={{0,2},{1,3},{2,0},{3,1},{4,6},{5,7},{6,4},{7,5},{8,10},{9,11},{10,... | collective-permute-start | bytes 1474568 | tf_op jit(solution)/shard_map/ppermute | solution.py:62
  46.9 23.2 %collective-permute-start.10 = (bf16[3,2,80,512]{3,2,1,0:T(8,128)(2,1)}, bf16[3,2,80,512]{3,2,1,0:T(8,128)(2,1)}, u32[]{:S(2)}, u32[]{:S(2)}) collective-permute-start(bf16[3,2,80,512]{3,2,1,0:T(8,128)(2,1)} %get-tuple-element.6), channel_id=1, source_target_pairs={{0,3},{1,0},{2,1},{3,2},{4,7},{5,4},{6,5},{7,6},{8,11},{9,8},{10,9... | collective-permute-start | bytes 1474568 | tf_op jit(solution)/shard_map/ppermute | solution.py:62
  49.2 28.7 %collective-permute-start.25 = (bf16[27,32,128]{2,1,0:T(8,128)(2,1)}, bf16[27,32,128]{2,1,0:T(8,128)(2,1)}, u32[]{:S(2)}, u32[]{:S(2)}) collective-permute-start(bf16[27,32,128]{2,1,0:T(8,128)(2,1)} %get-tuple-element.14), channel_id=1, source_target_pairs={{0,1},{1,2},{2,3},{3,0},{4,5},{5,6},{6,7},{7,4},{8,9},{9,10},{10,1... | collective-permute-start | bytes 663560 | tf_op jit(solution)/shard_map/ppermute | solution.py:130
  51.0 27.9 %collective-permute-start.26 = (bf16[27,32,128]{2,1,0:T(8,128)(2,1)}, bf16[27,32,128]{2,1,0:T(8,128)(2,1)}, u32[]{:S(2)}, u32[]{:S(2)}) collective-permute-start(bf16[27,32,128]{2,1,0:T(8,128)(2,1)} %get-tuple-element.16), channel_id=1, source_target_pairs={{0,2},{1,3},{2,0},{3,1},{4,6},{5,7},{6,4},{7,5},{8,10},{9,11},{10,... | collective-permute-start | bytes 663560 | tf_op jit(solution)/shard_map/ppermute | solution.py:130
  54.2 25.7 %collective-permute-start.27 = (bf16[27,32,128]{2,1,0:T(8,128)(2,1)}, bf16[27,32,128]{2,1,0:T(8,128)(2,1)S(1)}, u32[]{:S(2)}, u32[]{:S(2)}) collective-permute-start(bf16[27,32,128]{2,1,0:T(8,128)(2,1)} %get-tuple-element.13), channel_id=1, source_target_pairs={{0,3},{1,0},{2,1},{3,2},{4,7},{5,4},{6,5},{7,6},{8,11},{9,8},{10,9... | collective-permute-start | bytes 663560 | tf_op jit(solution)/shard_map/ppermute | solution.py:130
  72.0 19.5 %collective-permute-start.12 = (bf16[3,1,80,512]{3,2,1,0:T(8,128)(2,1)}, bf16[3,1,80,512]{3,2,1,0:T(8,128)(2,1)}, u32[]{:S(2)}, u32[]{:S(2)}) collective-permute-start(bf16[3,1,80,512]{3,2,1,0:T(8,128)(2,1)} %get-tuple-element.8), channel_id=1, source_target_pairs={{4,0},{8,4},{12,8},{5,1},{9,5},{13,9},{6,2},{10,6},{14,10},{7,3},{... | collective-permute-start | bytes 737288 | tf_op jit(solution)/shard_map/ppermute | solution.py:75
  73.2 18.3 %collective-permute-start.11 = (bf16[3,1,80,512]{3,2,1,0:T(8,128)(2,1)}, bf16[3,1,80,512]{3,2,1,0:T(8,128)(2,1)}, u32[]{:S(2)}, u32[]{:S(2)}) collective-permute-start(bf16[3,1,80,512]{3,2,1,0:T(8,128)(2,1)} %get-tuple-element.7), channel_id=1, source_target_pairs={{0,4},{4,8},{8,12},{1,5},{5,9},{9,13},{2,6},{6,10},{10,14},{3,7},{... | collective-permute-start | bytes 737288 | tf_op jit(solution)/shard_map/ppermute | solution.py:74
  123.0 5.4 %collective-permute-start.17 = (f32[8]{0:T(128)S(1)}, f32[8]{0:T(128)S(1)}, u32[]{:S(2)}, u32[]{:S(2)}) collective-permute-start(f32[8]{0:T(128)S(1)} %get-tuple-element.28), channel_id=1, source_target_pairs={{0,8},{4,12},{8,0},{12,4},{1,9},{5,13},{9,1},{13,5},{2,10},{6,14},... | collective-permute-start | bytes 104 | tf_op jit(solution)/shard_map/ppermute | solution.py:24
  126.3 3.7 %collective-permute-start.19 = (f32[8]{0:T(128)S(1)}, f32[8]{0:T(128)S(1)}, u32[]{:S(2)}, u32[]{:S(2)}) collective-permute-start(f32[8]{0:T(128)S(1)} %get-tuple-element.27), channel_id=1, source_target_pairs={{0,8},{4,12},{8,0},{12,4},{1,9},{5,13},{9,1},{13,5},{2,10},{6,14},... | collective-permute-start | bytes 104 | tf_op jit(solution)/shard_map/ppermute | solution.py:24
  131.7 7.0 %collective-permute-start.21 = (bf16[3,1,80,128]{3,2,1,0:T(8,128)(2,1)S(1)}, bf16[3,1,80,128]{3,2,1,0:T(8,128)(2,1)S(1)}, u32[]{:S(2)}, u32[]{:S(2)}) collective-permute-start(bf16[3,1,80,128]{3,2,1,0:T(8,128)(2,1)S(1)} %get-tuple-element.24), channel_id=1, source_target_pairs={{4,0},{8,4},{12,8},{5,1},{9,5},{13,9},{6,2},{10,6},{14,10},{7,3},{... | collective-permute-start | bytes 184328 | tf_op jit(solution)/shard_map/ppermute | solution.py:75
  133.0 6.4 %collective-permute-start.20 = (bf16[3,1,80,128]{3,2,1,0:T(8,128)(2,1)S(1)}, bf16[3,1,80,128]{3,2,1,0:T(8,128)(2,1)S(1)}, u32[]{:S(2)}, u32[]{:S(2)}) collective-permute-start(bf16[3,1,80,128]{3,2,1,0:T(8,128)(2,1)S(1)} %get-tuple-element.23), channel_id=1, source_target_pairs={{0,4},{4,8},{8,12},{1,5},{5,9},{9,13},{2,6},{6,10},{10,14},{3,7},{... | collective-permute-start | bytes 184328 | tf_op jit(solution)/shard_map/ppermute | solution.py:74
  140.7 19.0 %collective-permute-start.22 = (bf16[3,10,80,128]{3,2,1,0:T(8,128)(2,1)}, bf16[3,10,80,128]{3,2,1,0:T(8,128)(2,1)}, u32[]{:S(2)}, u32[]{:S(2)}) collective-permute-start(bf16[3,10,80,128]{3,2,1,0:T(8,128)(2,1)} %get-tuple-element.21), channel_id=1, source_target_pairs={{0,1},{1,2},{2,3},{3,0},{4,5},{5,6},{6,7},{7,4},{8,9},{9,10},{10,1... | collective-permute-start | bytes 1843208 | tf_op jit(solution)/shard_map/ppermute | solution.py:62
  146.3 27.5 %collective-permute-start.23 = (bf16[3,10,80,128]{3,2,1,0:T(8,128)(2,1)}, bf16[3,10,80,128]{3,2,1,0:T(8,128)(2,1)}, u32[]{:S(2)}, u32[]{:S(2)}) collective-permute-start(bf16[3,10,80,128]{3,2,1,0:T(8,128)(2,1)} %get-tuple-element.21), channel_id=1, source_target_pairs={{0,2},{1,3},{2,0},{3,1},{4,6},{5,7},{6,4},{7,5},{8,10},{9,11},{10,... | collective-permute-start | bytes 1843208 | tf_op jit(solution)/shard_map/ppermute | solution.py:62
  146.7 28.3 %collective-permute-start.24 = (bf16[3,10,80,128]{3,2,1,0:T(8,128)(2,1)}, bf16[3,10,80,128]{3,2,1,0:T(8,128)(2,1)}, u32[]{:S(2)}, u32[]{:S(2)}) collective-permute-start(bf16[3,10,80,128]{3,2,1,0:T(8,128)(2,1)} %get-tuple-element.21), channel_id=1, source_target_pairs={{0,3},{1,0},{2,1},{3,2},{4,7},{5,4},{6,5},{7,6},{8,11},{9,8},{10,9... | collective-permute-start | bytes 1843208 | tf_op jit(solution)/shard_map/ppermute | solution.py:62
  199.5 3.8 %collective-permute-start.28 = (f32[3,2,80,128]{3,2,1,0:T(8,128)S(1)}, f32[3,2,80,128]{3,2,1,0:T(8,128)S(1)}, u32[]{:S(2)}, u32[]{:S(2)}) collective-permute-start(f32[3,2,80,128]{3,2,1,0:T(8,128)S(1)} %get-tuple-element.11), channel_id=1, source_target_pairs={{0,1},{1,2},{2,3},{3,0},{4,5},{5,6},{6,7},{7,4},{8,9},{9,10},{10,1... | collective-permute-start | bytes 737288 | tf_op jit(solution)/shard_map/ppermute | solution.py:145
  199.6 11.1 %collective-permute-start.29 = (f32[3,2,80,128]{3,2,1,0:T(8,128)S(1)}, f32[3,2,80,128]{3,2,1,0:T(8,128)S(1)}, u32[]{:S(2)}, u32[]{:S(2)}) collective-permute-start(f32[3,2,80,128]{3,2,1,0:T(8,128)S(1)} %get-tuple-element.10), channel_id=1, source_target_pairs={{0,2},{1,3},{2,0},{3,1},{4,6},{5,7},{6,4},{7,5},{8,10},{9,11},{10,... | collective-permute-start | bytes 737288 | tf_op jit(solution)/shard_map/ppermute | solution.py:145
  200.7 11.4 %collective-permute-start.30 = (f32[3,2,80,128]{3,2,1,0:T(8,128)S(1)}, f32[3,2,80,128]{3,2,1,0:T(8,128)S(1)}, u32[]{:S(2)}, u32[]{:S(2)}) collective-permute-start(f32[3,2,80,128]{3,2,1,0:T(8,128)S(1)} %get-tuple-element.9), channel_id=1, source_target_pairs={{0,3},{1,0},{2,1},{3,2},{4,7},{5,4},{6,5},{7,6},{8,11},{9,8},{10,9... | collective-permute-start | bytes 737288 | tf_op jit(solution)/shard_map/ppermute | solution.py:145
  (15 other events, 149.9 us)
Sparse Core Ops, SparseCore 0:
  21.8 76.6 all-gather.2
  100.0 69.8 all-gather.4
where the time goes:
time: 226 us; the launch traced here: 223 us
  waiting for transfers between devices  83.5 us (37%)
  starting transfers between devices  46.3 us (20%)
  Pallas kernels  37 us (16%)
  local copies, waits for them, and re-layouts  26.1 us (12%)
  other arithmetic  16.1 us (7%)
  between operations  13.8 us (6%)
    pallas_call x2, Pallas kernels, causal_conv(): pl.pallas_call(conv_body, grid=(frames,), in_specs=[pl.BlockSpec(padded.s...  37 us
    ppermute x6, waiting for transfers between devices, gather_blocks(): lax.ppermute(block, axis_name, shift_pairs(size, step))  34.6 us
    ppermute x12, waiting for transfers between devices, butterfly_stats(): other_sums, other_squares = lax.ppermute((sums, squares), axis, pairs)  14.7 us
    ppermute x6, starting transfers between devices, gather_blocks(): lax.ppermute(block, axis_name, shift_pairs(size, step))  12.4 us
    ppermute x2, waiting for transfers between devices, with_row_halo(): bottom = lax.ppermute(cells[:, :1], axis_name, up)  12.3 us
    ppermute x12, starting transfers between devices, butterfly_stats(): other_sums, other_squares = lax.ppermute((sums, squares), axis, pairs)  11.2 us
    ppermute x3, waiting for transfers between devices, scatter_rows(): piece = lax.ppermute(piece, 'hq', shift_pairs(size, step))  10.6 us
    ppermute x6, starting transfers between devices, kernel_block(): piece = lax.ppermute(piece, 'hq', shift_pairs(size, step))  9.51 us
  transfers between devices with their start and end apart: 33, of which 25 were waited for; matrix products, arithmetic and copies ran while one was open for 15% of the time, Pallas kernels for 8%

commit v1 on v0

--- a/solution.py
+++ b/solution.py
@@ -9,6 +9,7 @@
 GROUPS = 32
 CHAN_BLOCKS = 4
 EPS = 1e-06
+HQ = ("ha", "hb")
 
 
 def shift_pairs(count, step):
@@ -51,20 +52,38 @@
     return jax.nn.silu(normed).astype(jnp.bfloat16)
 
 
-def gather_blocks(block, axis_name, dim, total):
-    size = lax.axis_size(axis_name)
-    me = lax.axis_index(axis_name)
+def chip_gather(block, dim):
+    count_a = lax.axis_size("ha")
+    count_b = lax.axis_size("hb")
+    me_a = lax.axis_index("ha")
+    me_b = lax.axis_index("hb")
     width = block.shape[dim]
     shape = list(block.shape)
-    shape[dim] = total
+    shape[dim] = width * count_a * count_b
+    firsts = [block]
+    sources = [me_a]
+    for step in range(1, count_a):
+        firsts.append(lax.ppermute(block, "ha", shift_pairs(count_a, step)))
+        sources.append((me_a - step) % count_a)
+    firsts = tuple(firsts)
     out = jnp.zeros(shape, block.dtype)
-    for step in range(size):
-        piece = block if step == 0 else lax.ppermute(block, axis_name, shift_pairs(size, step))
-        source = (me - step) % size
-        start = [0] * len(shape)
-        start[dim] = source * width
-        out = lax.dynamic_update_slice(out, piece, start)
+    for step in range(count_b):
+        bundle = firsts if step == 0 else lax.ppermute(firsts, "hb", shift_pairs(count_b, step))
+        source_b = (me_b - step) % count_b
+        for piece, source_a in zip(bundle, sources):
+            start = [0] * len(shape)
+            start[dim] = (source_a * count_b + source_b) * width
+            out = lax.dynamic_update_slice(out, piece, start)
     return out
+
+
+def edge_mask(cells):
+    size = lax.axis_size("hz")
+    me = lax.axis_index("hz")
+    rows = cells.shape[1]
+    row = lax.broadcasted_iota(jnp.int32, (1, rows, 1, 1), 1)
+    keep = ((row > 0) | (me > 0)) & ((row < rows - 1) | (me < size - 1))
+    return jnp.where(keep, cells, jnp.zeros_like(cells))
 
 
 def with_row_halo(cells, axis_name):
@@ -118,8 +137,8 @@
 
 
 def kernel_block(shard, chans):
-    size = lax.axis_size("hq")
-    me = lax.axis_index("hq")
+    size = lax.axis_size("ha") * lax.axis_size("hb")
+    me = lax.axis_index(HQ)
     taps, in_block, outs = shard.shape
     width = outs // size
     out = jnp.zeros((taps, in_block * size, width), shard.dtype)
@@ -127,22 +146,22 @@
         target = (me + step) % size
         piece = lax.dynamic_slice_in_dim(shard, target * width, width, axis=2)
         if step:
-            piece = lax.ppermute(piece, "hq", shift_pairs(size, step))
+            piece = lax.ppermute(piece, HQ, shift_pairs(size, step))
         source = (me - step) % size
         out = lax.dynamic_update_slice(out, piece, (0, source * in_block, 0))
     return lax.all_gather(out, "hz", axis=1, tiled=True)
 
 
 def scatter_rows(branch, slab_rows, chans):
-    size = lax.axis_size("hq")
-    me = lax.axis_index("hq")
+    size = lax.axis_size("ha") * lax.axis_size("hb")
+    me = lax.axis_index(HQ)
     frames, rows, cols, width = branch.shape
     out = jnp.zeros((frames, slab_rows, cols, chans), branch.dtype)
     for step in range(size):
         target = (me + step) % size
         piece = lax.dynamic_slice_in_dim(branch, target * slab_rows, slab_rows, axis=1)
         if step:
-            piece = lax.ppermute(piece, "hq", shift_pairs(size, step))
+            piece = lax.ppermute(piece, HQ, shift_pairs(size, step))
         source = (me - step) % size
         out = lax.dynamic_update_slice(out, piece, (0, 0, 0, source * width))
     return out
@@ -160,9 +179,9 @@
     bias_second,
 ):
     frames, slab_rows, cols, chans = latent.shape
-    blocks = lax.axis_size("hq")
+    blocks = lax.axis_size("ha") * lax.axis_size("hb")
     width = chans // blocks
-    me = lax.axis_index("hq")
+    me = lax.axis_index(HQ)
     group_size = chans // GROUPS
 
     weights_first = kernel_block(kernel_first, chans)
@@ -170,27 +189,21 @@
 
     values = latent.astype(jnp.float32)
     sums, squares, count = local_stats(values, GROUPS)
-    sums, squares, count = butterfly_stats(sums, squares, count, ("hq", "hz"))
+    raw_rows = with_row_halo(chip_gather(latent, 1), "hz")
+    sums, squares, count = butterfly_stats(sums, squares, count, ("ha", "hb", "hz"))
     mean_chan, scale_chan = group_scale(sums, squares, count, group_size)
-    act_first = activate(values, mean_chan, scale_chan, gain_first, shift_first)
-
-    group_rows = gather_blocks(act_first, "hq", 1, slab_rows * blocks)
-    extended = with_row_halo(group_rows, "hz")
+    act_first = activate(raw_rows.astype(jnp.float32), mean_chan, scale_chan, gain_first, shift_first)
     own_bias = lax.dynamic_slice_in_dim(bias_first, me * width, width)
-    hidden = causal_conv(extended, weights_first, own_bias, jnp.bfloat16)
-
-    hidden_values = hidden.astype(jnp.float32)
-    sums, squares, count = local_stats(hidden_values, width // group_size)
+    hidden = causal_conv(edge_mask(act_first), weights_first, own_bias, jnp.bfloat16)
+
+    sums, squares, count = local_stats(hidden.astype(jnp.float32), width // group_size)
+    raw_next = chip_gather(with_row_halo(hidden, "hz"), 3)
     sums, squares, count = butterfly_stats(sums, squares, count, ("hz",))
-    mean_own, scale_own = group_scale(sums, squares, count, group_size)
-    own_gain = lax.dynamic_slice_in_dim(gain_second, me * width, width)
-    own_shift = lax.dynamic_slice_in_dim(shift_second, me * width, width)
-    act_second = activate(hidden_values, mean_own, scale_own, own_gain, own_shift)
-
-    extended_next = with_row_halo(act_second, "hz")
-    extended_next = gather_blocks(extended_next, "hq", 3, chans)
+    packed = chip_gather(jnp.stack([sums, squares]), 1)
+    mean_chan, scale_chan = group_scale(packed[0], packed[1], count, group_size)
+    act_second = activate(raw_next.astype(jnp.float32), mean_chan, scale_chan, gain_second, shift_second)
     own_bias_next = lax.dynamic_slice_in_dim(bias_second, me * width, width)
-    branch = causal_conv(extended_next, weights_second, own_bias_next, jnp.float32)
+    branch = causal_conv(edge_mask(act_second), weights_second, own_bias_next, jnp.float32)
 
     branch_rows = scatter_rows(branch, slab_rows, chans)
     summed = (values + branch_rows).astype(jnp.bfloat16)
@@ -201,17 +214,21 @@
     groups = mesh.shape["groups"]
     height = mesh.shape["height"]
     blocks = CHAN_BLOCKS
-    split = Mesh(mesh.devices.reshape(groups, height // blocks, blocks), ("groups", "hz", "hq"))
-    rows = ("groups", "hz", "hq")
+    split = Mesh(
+        mesh.devices.reshape(groups, height // blocks, 2, blocks // 2),
+        ("groups", "hz", "ha", "hb"),
+    )
+    rows = ("groups", "hz", "ha", "hb")
+    slabs = ("hz", "ha", "hb")
     placed = (
         P(None, rows, None, None),
         P(),
         P(),
-        P(None, ("hz", "hq"), None),
-        P(),
-        P(),
-        P(),
-        P(None, ("hz", "hq"), None),
+        P(None, slabs, None),
+        P(),
+        P(),
+        P(),
+        P(None, slabs, None),
         P(),
     )
     return jax.shard_map(

time: 226 us -> 215 us (0.951); the launches traced: 223 us -> 215 us
  waiting for transfers between devices: 83.5 us -> 76.3 us
    ppermute x15 -> x18, waiting for transfers between devices: 54.6 us -> 20.3 us  [the longest x3 11.2 us: scatter_rows(): piece = lax.ppermute(piece, HQ, shift_pairs(size, step))]
    all_gather x2, waiting for transfers between devices: 1.2 us -> 26.8 us  [kernel_block(): return lax.all_gather(out, 'hz', axis=1, tiled=True)]
    select_n x0 -> x2, other arithmetic: none -> 4.82 us  [edge_mask(): return jnp.where(keep, cells, jnp.zeros_like(cells))]
    ppermute x15 -> x18, starting transfers between devices: 23.8 us -> 22.4 us  [the longest x6 9.29 us: chip_gather(): lax.ppermute(firsts, 'hb', shift_pairs(count_b, step))]
    dynamic_update_slice x6 -> x11, local copies, waits for them, and re-layouts: 6.86 us -> 7.69 us  [chip_gather(): out = lax.dynamic_update_slice(out, piece, start)]
  transfers between devices with their start and end apart: 33 -> 36, of which waited for: 25 -> 21; matrix products, arithmetic and copies ran while one was open for 15% -> 15% of each run, Pallas kernels for 8% -> 9%
where the time goes in v1:
time: 215 us
  waiting for transfers between devices  76.3 us (35%)
  starting transfers between devices  45.7 us (21%)
  Pallas kernels  37 us (17%)
  local copies, waits for them, and re-layouts  27.1 us (13%)
  other arithmetic  14.7 us (7%)
  between operations  13.9 us (6%)
    pallas_call x2, Pallas kernels, causal_conv(): pl.pallas_call(conv_body, grid=(frames,), in_specs=[pl.BlockSpec(padded.s...  37 us
    all_gather x2, waiting for transfers between devices, kernel_block(): return lax.all_gather(out, 'hz', axis=1, tiled=True)  26.8 us
    ppermute x12, waiting for transfers between devices, butterfly_stats(): other_sums, other_squares = lax.ppermute((sums, squares), axis, pairs)  16.5 us
    ppermute x2, waiting for transfers between devices, with_row_halo(): bottom = lax.ppermute(cells[:, :1], axis_name, up)  12.7 us
    ppermute x12, starting transfers between devices, butterfly_stats(): other_sums, other_squares = lax.ppermute((sums, squares), axis, pairs)  11.7 us
    ppermute x3, waiting for transfers between devices, scatter_rows(): piece = lax.ppermute(piece, HQ, shift_pairs(size, step))  11.2 us
    ppermute x6, starting transfers between devices, chip_gather(): lax.ppermute(firsts, 'hb', shift_pairs(count_b, step))  9.29 us
    ppermute x2, starting transfers between devices, with_row_halo(): top = lax.ppermute(cells[:, -1:], axis_name, down)  8.88 us
  transfers between devices with their start and end apart: 36, of which 21 were waited for; matrix products, arithmetic and copies ran while one was open for 15% of the time, Pallas kernels for 9%

profile of v1, /device:TPU:1, one launch (start us, length us, event | category | flops | bytes accessed | tf_op | source)
XLA Modules:
  0.0 214.5 jit_solution(8293078731895722347)
XLA Ops:
  8.3 2.7 %collective-permute-start.13 = (bf16[27,32,128]{2,1,0:T(8,128)(2,1)S(1)}, bf16[27,32,128]{2,1,0:T(8,128)(2,1)}, u32[]{:S(2)}, u32[]{:S(2)}) collective-permute-start(bf16[27,32,128]{2,1,0:T(8,128)(2,1)S(1)} %get-tuple-element.16), channel_id=1, source_target_pairs={{0,1},{1,2},{2,3},{3,0},{4,5},{5,6},{6,7},{7,4},{8,9},{9,10},{10,1... | collective-permute-start | bytes 663560 | tf_op jit(solution)/shard_map/ppermute | solution.py:149
  11.5 4.2 %collective-permute-done.13 = bf16[27,32,128]{2,1,0:T(8,128)(2,1)} collective-permute-done((bf16[27,32,128]{2,1,0:T(8,128)(2,1)S(1)}, bf16[27,32,128]{2,1,0:T(8,128)(2,1)}, u32[]{:S(2)}, u32[]{:S(2)}) %collective-permute-start.13) | collective-permute-done | bytes 221216 | tf_op jit(solution)/shard_map/ppermute | solution.py:149
  16.6 3.8 %collective-permute-done.14 = bf16[27,32,128]{2,1,0:T(8,128)(2,1)S(1)} collective-permute-done((bf16[27,32,128]{2,1,0:T(8,128)(2,1)S(1)}, bf16[27,32,128]{2,1,0:T(8,128)(2,1)S(1)}, u32[]{:S(2)}, u32[]{:S(2)}) %collective-permute-start.14) | collective-permute-done | bytes 221216 | tf_op jit(solution)/shard_map/ppermute | solution.py:149
  21.9 2.1 collective-permute-start
  29.5 6.1 %collective-permute-done.5 = f32[32]{0:T(128)S(1)} collective-permute-done((f32[32]{0:T(128)S(1)}, f32[32]{0:T(128)S(1)}, u32[]{:S(2)}, u32[]{:S(2)}) %collective-permute-start.5) | collective-permute-done | bytes 160 | tf_op jit(solution)/shard_map/ppermute | solution.py:25
  46.1 2.3 %collective-permute-done.12 = f32[32]{0:T(128)S(1)} collective-permute-done((f32[32]{0:T(128)S(1)}, f32[32]{0:T(128)S(1)}, u32[]{:S(2)}, u32[]{:S(2)}) %collective-permute-start.12) | collective-permute-done | bytes 160 | tf_op jit(solution)/shard_map/ppermute | solution.py:25
  56.0 4.7 %collective-permute-start.3 = (bf16[3,1,80,512]{3,2,1,0:T(8,128)(2,1)}, bf16[3,1,80,512]{3,2,1,0:T(8,128)(2,1)}, u32[]{:S(2)}, u32[]{:S(2)}) collective-permute-start(bf16[3,1,80,512]{3,2,1,0:T(8,128)(2,1)} %get-tuple-element.5), channel_id=1, source_target_pairs={{0,4},{4,8},{8,12},{1,5},{5,9},{9,13},{2,6},{6,10},{10,14},{3,7},{... | collective-permute-start | bytes 737288 | tf_op jit(solution)/shard_map/ppermute | solution.py:93
  64.7 11.5 %collective-permute-done.4 = bf16[3,1,80,512]{3,2,1,0:T(8,128)(2,1)} collective-permute-done((bf16[3,1,80,512]{3,2,1,0:T(8,128)(2,1)}, bf16[3,1,80,512]{3,2,1,0:T(8,128)(2,1)}, u32[]{:S(2)}, u32[]{:S(2)}) %collective-permute-start.4) | collective-permute-done | bytes 245792 | tf_op jit(solution)/shard_map/ppermute | solution.py:94
  76.2 2.9 %fusion.6 = bf16[3,10,80,512]{3,2,1,0:T(8,128)(2,1)S(1)} fusion(bf16[3,1,80,512]{3,2,1,0:T(8,128)(2,1)} %collective-permute-done.4, bf16[3,8,80,512]{3,2,1,0:T(8,128)(2,1)S(1)} %constant_dynamic-update-slice_fusion.13, bf16[3,1,80,512]{3,2,1,0:T(8,128)(2,1)} %collective-permute-done.3, f32[512]{0:T(512)S(1)} %copy-done.6, f32[512]{0:T(512)S(1)} %copy-done.7, ...), kind=kLoop, calls=%fused_computation.12 | loop fusion | flops 15974400 | bytes 4923402 | tf_op jit(solution)/shard_map/jit(_where)/select_n | solution.py:86
  79.2 3.2 %fusion.5.x_ref = bf16[5,10,82,512]{3,2,1,0:T(8,128)(2,1)} fusion(bf16[3,10,80,512]{3,2,1,0:T(8,128)(2,1)S(1)} %fusion.6, bf16[1,10,80,512]{3,2,1,0:T(8,128)(2,1)S(1)} %slice.36), kind=kLoop, calls=%fused_computation.11 | loop fusion | flops 25190400 | bytes 7475200 | tf_op jit(solution)/shard_map/concatenate | solution.py:116
  82.3 16.3 %all-gather.3.cloned.1.call-done.w_ref = bf16[27,512,128]{2,1,0:T(8,128)(2,1)} async-done(((bf16[27,128,128]{2,1,0:T(8,128)(2,1)}), bf16[27,512,128]{2,1,0:T(8,128)(2,1)}) %all-gather.3.cloned.1.call-update) | async-done | bytes 3538960 | tf_op jit(solution)/shard_map/all_gather | solution.py:152
  98.7 18.5 %shard_map.91 = bf16[3,8,80,128]{3,2,1,0:T(8,128)(2,1)} custom-call(bf16[5,10,82,512]{3,2,1,0:T(8,128)(2,1)} %fusion.5.x_ref, bf16[27,512,128]{2,1,0:T(8,128)(2,1)} %all-gather.3.cloned.1.call-done.w_ref, f32[1,128]{1,0:T(1,128)} %dynamic-slice_bitcast_fusion.1.b_ref), custom_call_target="tpu_custom_call" | custom-call | flops 6794772480 | bytes 8720384 | tf_op jit(solution)/shard_map/pallas_call | solution.py:124
  119.4 4.2 %collective-permute-start.16 = (bf16[3,1,80,128]{3,2,1,0:T(8,128)(2,1)S(1)}, bf16[3,1,80,128]{3,2,1,0:T(8,128)(2,1)S(1)}, u32[]{:S(2)}, u32[]{:S(2)}) collective-permute-start(bf16[3,1,80,128]{3,2,1,0:T(8,128)(2,1)S(1)} %get-tuple-element.21), channel_id=1, source_target_pairs={{0,4},{4,8},{8,12},{1,5},{5,9},{9,13},{2,6},{6,10},{10,14},{3,7},{... | collective-permute-start | bytes 184328 | tf_op jit(solution)/shard_map/ppermute | solution.py:93
  126.3 2.0 pad_maximum_fusion
  129.9 2.7 %collective-permute-start.21 = (f32[8]{0:T(128)S(1)}, f32[8]{0:T(128)S(1)}, u32[]{:S(2)}, u32[]{:S(2)}) collective-permute-start(f32[8]{0:T(128)S(1)} %reduce_sum.72), channel_id=1, source_target_pairs={{0,4},{4,0},{8,12},{12,8},{1,5},{5,1},{9,13},{13,9},{2,6},{6,2},{1... | collective-permute-start | bytes 104 | tf_op jit(solution)/shard_map/ppermute | solution.py:25
  133.9 3.2 %collective-permute-done.23 = f32[8]{0:T(128)S(1)} collective-permute-done((f32[8]{0:T(128)S(1)}, f32[8]{0:T(128)S(1)}, u32[]{:S(2)}, u32[]{:S(2)}) %collective-permute-start.23) | collective-permute-done | bytes 64 | tf_op jit(solution)/shard_map/ppermute | solution.py:25
  139.4 2.3 %collective-permute-start.19 = (bf16[3,10,80,128]{3,2,1,0:T(8,128)(2,1)}, bf16[3,10,80,128]{3,2,1,0:T(8,128)(2,1)}, u32[]{:S(2)}, u32[]{:S(2)}) collective-permute-start(bf16[3,10,80,128]{3,2,1,0:T(8,128)(2,1)} %get-tuple-element.19), channel_id=1, source_target_pairs={{0,1},{1,0},{2,3},{3,2},{4,5},{5,4},{6,7},{7,6},{8,9},{9,8},{10,11... | collective-permute-start | bytes 1843208 | tf_op jit(solution)/shard_map/ppermute | solution.py:71
  141.7 3.2 %collective-permute-start.20 = (bf16[3,10,80,128]{3,2,1,0:T(8,128)(2,1)}, bf16[3,10,80,128]{3,2,1,0:T(8,128)(2,1)}, u32[]{:S(2)}, u32[]{:S(2)}) collective-permute-start(bf16[3,10,80,128]{3,2,1,0:T(8,128)(2,1)} %collective-permute-done.18), channel_id=1, source_target_pairs={{0,1},{1,0},{2,3},{3,2},{4,5},{5,4},{6,7},{7,6},{8,9},{9,8},{10,11... | collective-permute-start | bytes 1843208 | tf_op jit(solution)/shard_map/ppermute | solution.py:71
  156.6 3.2 %select_maximum_fusion.x_ref = bf16[5,10,82,512]{3,2,1,0:T(8,128)(2,1)} fusion(bf16[3,10,80,512]{3,2,1,0:T(8,128)(2,1)S(1)} %fusion.7, bf16[1,10,80,512]{3,2,1,0:T(8,128)(2,1)S(1)} %slice.39), kind=kLoop, calls=%fused_computation.5 | loop fusion | flops 25190400 | bytes 7475200 | tf_op jit(solution)/shard_map/concatenate | solution.py:116
  159.8 10.4 %all-gather.5.cloned.1.call-done.w_ref = bf16[27,512,128]{2,1,0:T(8,128)(2,1)} async-done(((bf16[27,128,128]{2,1,0:T(8,128)(2,1)}), bf16[27,512,128]{2,1,0:T(8,128)(2,1)}) %all-gather.5.cloned.1.call-update) | async-done | bytes 3538960 | tf_op jit(solution)/shard_map/all_gather | solution.py:152
  170.2 18.5 %shard_map.92 = f32[3,8,80,128]{3,2,1,0:T(8,128)} custom-call(bf16[5,10,82,512]{3,2,1,0:T(8,128)(2,1)} %select_maximum_fusion.x_ref, bf16[27,512,128]{2,1,0:T(8,128)(2,1)} %all-gather.5.cloned.1.call-done.w_ref, f32[1,128]{1,0:T(1,128)} %dynamic-slice_bitcast_fusion.b_ref), custom_call_target="tpu_custom_call" | custom-call | flops 6794772480 | bytes 8720384 | tf_op jit(solution)/shard_map/pallas_call | solution.py:124
  192.5 4.7 %collective-permute-done.31 = f32[3,2,80,128]{3,2,1,0:T(8,128)S(1)} collective-permute-done((f32[3,2,80,128]{3,2,1,0:T(8,128)S(1)}, f32[3,2,80,128]{3,2,1,0:T(8,128)S(1)}, u32[]{:S(2)}, u32[]{:S(2)}) %collective-permute-start.31) | collective-permute-done | bytes 245792 | tf_op jit(solution)/shard_map/ppermute | solution.py:164
  197.2 5.9 %collective-permute-done.32 = f32[3,2,80,128]{3,2,1,0:T(8,128)S(1)} collective-permute-done((f32[3,2,80,128]{3,2,1,0:T(8,128)S(1)}, f32[3,2,80,128]{3,2,1,0:T(8,128)S(1)}, u32[]{:S(2)}, u32[]{:S(2)}) %collective-permute-start.32) | collective-permute-done | bytes 245792 | tf_op jit(solution)/shard_map/ppermute | solution.py:164
  205.5 2.2 %reshape.59 = bf16[3,4,160,512]{3,2,1,0:T(8,128)(2,1)} reshape(bf16[3,4,80,2,512]{4,3,2,1,0:T(2,128)(2,1)S(1)} %broadcast_in_dim.53) | data formatting | bytes 3932160 | tf_op jit(solution)/shard_map/reshape | solution.py:210
  (151 shorter events, 60.0 us)
Async XLA Ops:
  6.5 92.1 %all-gather.3.cloned.1.call-start = ((), (), s32[]{:S(2)}) async-start(), calls=%async_computation | async-start | bytes 4423680 | tf_op jit(solution)/shard_map/all_gather | solution.py:152
  8.3 7.3 %collective-permute-start.13 = (bf16[27,32,128]{2,1,0:T(8,128)(2,1)S(1)}, bf16[27,32,128]{2,1,0:T(8,128)(2,1)}, u32[]{:S(2)}, u32[]{:S(2)}) collective-permute-start(bf16[27,32,128]{2,1,0:T(8,128)(2,1)S(1)} %get-tuple-element.16), channel_id=1, source_target_pairs={{0,1},{1,2},{2,3},{3,0},{4,5},{5,6},{6,7},{7,4},{8,9},{9,10},{10,1... | collective-permute-start | bytes 663560 | tf_op jit(solution)/shard_map/ppermute | solution.py:149
  11.0 9.4 %collective-permute-start.14 = (bf16[27,32,128]{2,1,0:T(8,128)(2,1)S(1)}, bf16[27,32,128]{2,1,0:T(8,128)(2,1)S(1)}, u32[]{:S(2)}, u32[]{:S(2)}) collective-permute-start(bf16[27,32,128]{2,1,0:T(8,128)(2,1)S(1)} %get-tuple-element.18), channel_id=1, source_target_pairs={{0,2},{1,3},{2,0},{3,1},{4,6},{5,7},{6,4},{7,5},{8,10},{9,11},{10,... | collective-permute-start | bytes 663560 | tf_op jit(solution)/shard_map/ppermute | solution.py:149
  11.0 9.9 %collective-permute-start.15 = (bf16[27,32,128]{2,1,0:T(8,128)(2,1)S(1)}, bf16[27,32,128]{2,1,0:T(8,128)(2,1)S(1)}, u32[]{:S(2)}, u32[]{:S(2)}) collective-permute-start(bf16[27,32,128]{2,1,0:T(8,128)(2,1)S(1)} %get-tuple-element.15), channel_id=1, source_target_pairs={{0,3},{1,0},{2,1},{3,2},{4,7},{5,4},{6,5},{7,6},{8,11},{9,8},{10,9... | collective-permute-start | bytes 663560 | tf_op jit(solution)/shard_map/ppermute | solution.py:149
  21.9 148.3 %all-gather.5.cloned.1.call-start = ((), (), s32[]{:S(2)}) async-start(), calls=%async_computation.1 | async-start | bytes 4423680 | tf_op jit(solution)/shard_map/all_gather | solution.py:152
  21.9 17.4 %collective-permute-start = (bf16[3,2,80,512]{3,2,1,0:T(8,128)(2,1)S(1)}, bf16[3,2,80,512]{3,2,1,0:T(8,128)(2,1)}, u32[]{:S(2)}, u32[]{:S(2)}) collective-permute-start(bf16[3,2,80,512]{3,2,1,0:T(8,128)(2,1)S(1)} %copy-done.1), channel_id=1, source_target_pairs={{0,2},{2,0},{1,3},{3,1},{4,6},{6,4},{5,7},{7,5},{8,10},{10,8},{9,1... | collective-permute-start | bytes 1474568 | tf_op jit(solution)/shard_map/ppermute | solution.py:66
  24.0 27.7 %collective-permute-start.1 = (bf16[3,2,80,512]{3,2,1,0:T(8,128)(2,1)S(1)}, bf16[3,2,80,512]{3,2,1,0:T(8,128)(2,1)}, u32[]{:S(2)}, u32[]{:S(2)}) collective-permute-start(bf16[3,2,80,512]{3,2,1,0:T(8,128)(2,1)S(1)} %copy-done.1), channel_id=1, source_target_pairs={{0,1},{1,0},{2,3},{3,2},{4,5},{5,4},{6,7},{7,6},{8,9},{9,8},{10,11... | collective-permute-start | bytes 1474568 | tf_op jit(solution)/shard_map/ppermute | solution.py:71
  24.3 11.3 %collective-permute-start.5 = (f32[32]{0:T(128)S(1)}, f32[32]{0:T(128)S(1)}, u32[]{:S(2)}, u32[]{:S(2)}) collective-permute-start(f32[32]{0:T(128)S(1)} %reduce_sum.51), channel_id=1, source_target_pairs={{0,2},{2,0},{1,3},{3,1},{4,6},{6,4},{5,7},{7,5},{8,10},{10,8},{9,1... | collective-permute-start | bytes 392 | tf_op jit(solution)/shard_map/ppermute | solution.py:25
  25.1 10.4 %collective-permute-start.9 = (f32[32]{0:T(128)S(1)}, f32[32]{0:T(128)S(1)}, u32[]{:S(2)}, u32[]{:S(2)}) collective-permute-start(f32[32]{0:T(128)S(1)} %reduce_sum.54), channel_id=1, source_target_pairs={{0,2},{2,0},{1,3},{3,1},{4,6},{6,4},{5,7},{7,5},{8,10},{10,8},{9,1... | collective-permute-start | bytes 392 | tf_op jit(solution)/shard_map/ppermute | solution.py:25
  27.6 33.2 %collective-permute-start.28 = (bf16[27,32,128]{2,1,0:T(8,128)(2,1)}, bf16[27,32,128]{2,1,0:T(8,128)(2,1)}, u32[]{:S(2)}, u32[]{:S(2)}) collective-permute-start(bf16[27,32,128]{2,1,0:T(8,128)(2,1)} %get-tuple-element.12), channel_id=1, source_target_pairs={{0,1},{1,2},{2,3},{3,0},{4,5},{5,6},{6,7},{7,4},{8,9},{9,10},{10,1... | collective-permute-start | bytes 663560 | tf_op jit(solution)/shard_map/ppermute | solution.py:149
  39.3 13.5 %collective-permute-start.2 = (bf16[3,2,80,512]{3,2,1,0:T(8,128)(2,1)}, bf16[3,2,80,512]{3,2,1,0:T(8,128)(2,1)}, u32[]{:S(2)}, u32[]{:S(2)}) collective-permute-start(bf16[3,2,80,512]{3,2,1,0:T(8,128)(2,1)} %collective-permute-done), channel_id=1, source_target_pairs={{0,1},{1,0},{2,3},{3,2},{4,5},{5,4},{6,7},{7,6},{8,9},{9,8},{10,11... | collective-permute-start | bytes 1474568 | tf_op jit(solution)/shard_map/ppermute | solution.py:71
  45.7 16.0 %collective-permute-start.29 = (bf16[27,32,128]{2,1,0:T(8,128)(2,1)}, bf16[27,32,128]{2,1,0:T(8,128)(2,1)}, u32[]{:S(2)}, u32[]{:S(2)}) collective-permute-start(bf16[27,32,128]{2,1,0:T(8,128)(2,1)} %get-tuple-element.14), channel_id=1, source_target_pairs={{0,2},{1,3},{2,0},{3,1},{4,6},{5,7},{6,4},{7,5},{8,10},{9,11},{10,... | collective-permute-start | bytes 663560 | tf_op jit(solution)/shard_map/ppermute | solution.py:149
  48.5 14.3 %collective-permute-start.30 = (bf16[27,32,128]{2,1,0:T(8,128)(2,1)}, bf16[27,32,128]{2,1,0:T(8,128)(2,1)}, u32[]{:S(2)}, u32[]{:S(2)}) collective-permute-start(bf16[27,32,128]{2,1,0:T(8,128)(2,1)} %get-tuple-element.11), channel_id=1, source_target_pairs={{0,3},{1,0},{2,1},{3,2},{4,7},{5,4},{6,5},{7,6},{8,11},{9,8},{10,9... | collective-permute-start | bytes 663560 | tf_op jit(solution)/shard_map/ppermute | solution.py:149
  54.8 21.5 %collective-permute-start.4 = (bf16[3,1,80,512]{3,2,1,0:T(8,128)(2,1)}, bf16[3,1,80,512]{3,2,1,0:T(8,128)(2,1)}, u32[]{:S(2)}, u32[]{:S(2)}) collective-permute-start(bf16[3,1,80,512]{3,2,1,0:T(8,128)(2,1)} %get-tuple-element.6), channel_id=1, source_target_pairs={{4,0},{8,4},{12,8},{5,1},{9,5},{13,9},{6,2},{10,6},{14,10},{7,3},{... | collective-permute-start | bytes 737288 | tf_op jit(solution)/shard_map/ppermute | solution.py:94
  56.0 20.2 %collective-permute-start.3 = (bf16[3,1,80,512]{3,2,1,0:T(8,128)(2,1)}, bf16[3,1,80,512]{3,2,1,0:T(8,128)(2,1)}, u32[]{:S(2)}, u32[]{:S(2)}) collective-permute-start(bf16[3,1,80,512]{3,2,1,0:T(8,128)(2,1)} %get-tuple-element.5), channel_id=1, source_target_pairs={{0,4},{4,8},{8,12},{1,5},{5,9},{9,13},{2,6},{6,10},{10,14},{3,7},{... | collective-permute-start | bytes 737288 | tf_op jit(solution)/shard_map/ppermute | solution.py:93
  118.1 8.0 %collective-permute-start.17 = (bf16[3,1,80,128]{3,2,1,0:T(8,128)(2,1)S(1)}, bf16[3,1,80,128]{3,2,1,0:T(8,128)(2,1)S(1)}, u32[]{:S(2)}, u32[]{:S(2)}) collective-permute-start(bf16[3,1,80,128]{3,2,1,0:T(8,128)(2,1)S(1)} %get-tuple-element.22), channel_id=1, source_target_pairs={{4,0},{8,4},{12,8},{5,1},{9,5},{13,9},{6,2},{10,6},{14,10},{7,3},{... | collective-permute-start | bytes 184328 | tf_op jit(solution)/shard_map/ppermute | solution.py:94
  128.3 13.4 %collective-permute-start.18 = (bf16[3,10,80,128]{3,2,1,0:T(8,128)(2,1)}, bf16[3,10,80,128]{3,2,1,0:T(8,128)(2,1)}, u32[]{:S(2)}, u32[]{:S(2)}) collective-permute-start(bf16[3,10,80,128]{3,2,1,0:T(8,128)(2,1)} %get-tuple-element.19), channel_id=1, source_target_pairs={{0,2},{2,0},{1,3},{3,1},{4,6},{6,4},{5,7},{7,5},{8,10},{10,8},{9,1... | collective-permute-start | bytes 1843208 | tf_op jit(solution)/shard_map/ppermute | solution.py:66
  137.1 7.8 %collective-permute-start.22 = (f32[8]{0:T(128)S(1)}, f32[8]{0:T(128)S(1)}, u32[]{:S(2)}, u32[]{:S(2)}) collective-permute-start(f32[8]{0:T(128)S(1)} %get-tuple-element.28), channel_id=1, source_target_pairs={{0,8},{4,12},{8,0},{12,4},{1,9},{5,13},{9,1},{13,5},{2,10},{6,14},... | collective-permute-start | bytes 104 | tf_op jit(solution)/shard_map/ppermute | solution.py:25
  138.0 6.9 %collective-permute-start.24 = (f32[8]{0:T(128)S(1)}, f32[8]{0:T(128)S(1)}, u32[]{:S(2)}, u32[]{:S(2)}) collective-permute-start(f32[8]{0:T(128)S(1)} %get-tuple-element.27), channel_id=1, source_target_pairs={{0,8},{4,12},{8,0},{12,4},{1,9},{5,13},{9,1},{13,5},{2,10},{6,14},... | collective-permute-start | bytes 104 | tf_op jit(solution)/shard_map/ppermute | solution.py:25
  139.4 12.6 %collective-permute-start.19 = (bf16[3,10,80,128]{3,2,1,0:T(8,128)(2,1)}, bf16[3,10,80,128]{3,2,1,0:T(8,128)(2,1)}, u32[]{:S(2)}, u32[]{:S(2)}) collective-permute-start(bf16[3,10,80,128]{3,2,1,0:T(8,128)(2,1)} %get-tuple-element.19), channel_id=1, source_target_pairs={{0,1},{1,0},{2,3},{3,2},{4,5},{5,4},{6,7},{7,6},{8,9},{9,8},{10,11... | collective-permute-start | bytes 1843208 | tf_op jit(solution)/shard_map/ppermute | solution.py:71
  141.7 11.6 %collective-permute-start.20 = (bf16[3,10,80,128]{3,2,1,0:T(8,128)(2,1)}, bf16[3,10,80,128]{3,2,1,0:T(8,128)(2,1)}, u32[]{:S(2)}, u32[]{:S(2)}) collective-permute-start(bf16[3,10,80,128]{3,2,1,0:T(8,128)(2,1)} %collective-permute-done.18), channel_id=1, source_target_pairs={{0,1},{1,0},{2,3},{3,2},{4,5},{5,4},{6,7},{7,6},{8,9},{9,8},{10,11... | collective-permute-start | bytes 1843208 | tf_op jit(solution)/shard_map/ppermute | solution.py:71
  190.2 7.0 %collective-permute-start.31 = (f32[3,2,80,128]{3,2,1,0:T(8,128)S(1)}, f32[3,2,80,128]{3,2,1,0:T(8,128)S(1)}, u32[]{:S(2)}, u32[]{:S(2)}) collective-permute-start(f32[3,2,80,128]{3,2,1,0:T(8,128)S(1)} %get-tuple-element.9), channel_id=1, source_target_pairs={{0,1},{1,2},{2,3},{3,0},{4,5},{5,6},{6,7},{7,4},{8,9},{9,10},{10,1... | collective-permute-start | bytes 737288 | tf_op jit(solution)/shard_map/ppermute | solution.py:164
  192.0 11.1 %collective-permute-start.32 = (f32[3,2,80,128]{3,2,1,0:T(8,128)S(1)}, f32[3,2,80,128]{3,2,1,0:T(8,128)S(1)}, u32[]{:S(2)}, u32[]{:S(2)}) collective-permute-start(f32[3,2,80,128]{3,2,1,0:T(8,128)S(1)} %get-tuple-element.8), channel_id=1, source_target_pairs={{0,2},{1,3},{2,0},{3,1},{4,6},{5,7},{6,4},{7,5},{8,10},{9,11},{10,... | collective-permute-start | bytes 737288 | tf_op jit(solution)/shard_map/ppermute | solution.py:164
  192.3 11.5 %collective-permute-start.33 = (f32[3,2,80,128]{3,2,1,0:T(8,128)S(1)}, f32[3,2,80,128]{3,2,1,0:T(8,128)S(1)}, u32[]{:S(2)}, u32[]{:S(2)}) collective-permute-start(f32[3,2,80,128]{3,2,1,0:T(8,128)S(1)} %get-tuple-element.7), channel_id=1, source_target_pairs={{0,3},{1,0},{2,1},{3,2},{4,7},{5,4},{6,5},{7,6},{8,11},{9,8},{10,9... | collective-permute-start | bytes 737288 | tf_op jit(solution)/shard_map/ppermute | solution.py:164
  (22 other events, 267.6 us)
Sparse Core Ops, SparseCore 0:
  22.0 76.6 all-gather.2
  100.2 69.9 all-gather.4

commit v2 on v1

--- a/solution.py
+++ b/solution.py
@@ -149,7 +149,18 @@
             piece = lax.ppermute(piece, HQ, shift_pairs(size, step))
         source = (me - step) % size
         out = lax.dynamic_update_slice(out, piece, (0, source * in_block, 0))
-    return lax.all_gather(out, "hz", axis=1, tiled=True)
+    parts = lax.axis_size("groups")
+    part = lax.axis_index("groups")
+    share = width // parts
+    mine = lax.dynamic_slice_in_dim(out, part * share, share, axis=2)
+    gathered = lax.all_gather(mine, "hz", axis=1, tiled=True)
+    result = jnp.zeros((taps, chans, width), shard.dtype)
+    result = lax.dynamic_update_slice(result, gathered, (0, 0, part * share))
+    for step in range(1, parts):
+        other = lax.ppermute(gathered, "groups", shift_pairs(parts, step))
+        source = (part - step) % parts
+        result = lax.dynamic_update_slice(result, other, (0, 0, source * share))
+    return result
 
 
 def scatter_rows(branch, slab_rows, chans):

time: 215 us -> 426 us (1.98)
  local copies, waits for them, and re-layouts: 27.1 us -> 175 us
  waiting for transfers between devices: 76.3 us -> 135 us
    dynamic_update_slice x0 -> x4, local copies, waits for them, and re-layouts: none -> 129 us  [the longest x2 70 us: kernel_block(): result = lax.dynamic_update_slice(result, other, (0, 0, source * share))]
    all_gather x2, waiting for transfers between devices: 26.8 us -> 99.2 us  [kernel_block(): gathered = lax.all_gather(mine, 'hz', axis=1, tiled=True)]
    ppermute x12, waiting for transfers between devices: 16.5 us -> 1.75 us  [butterfly_stats(): other_sums, other_squares = lax.ppermute((sums, squares), axis, pairs)]
    ppermute x6, waiting for transfers between devices: 8.4 us -> 22.4 us  [kernel_block(): piece = lax.ppermute(piece, HQ, shift_pairs(size, step))]
    ppermute x2, waiting for transfers between devices: 12.7 us -> 0.01 us  [with_row_halo(): bottom = lax.ppermute(cells[:, :1], axis_name, up)]
    all_gather x0 -> x2, local copies, waits for them, and re-layouts: none -> 9.12 us  [kernel_block(): gathered = lax.all_gather(mine, 'hz', axis=1, tiled=True)]
    ppermute x0 -> x2, local copies, waits for them, and re-layouts: none -> 6.73 us  [kernel_block(): other = lax.ppermute(gathered, 'groups', shift_pairs(parts, step))]
    another operation x3 -> x5, local copies, waits for them, and re-layouts: 0.64 us -> 7.22 us
  transfers between devices with their start and end apart: 36 -> 38, of which waited for: 21 -> 13; matrix products, arithmetic and copies ran while one was open for 15% -> 42% of each run, Pallas kernels for 9% -> 4%
where the time goes in v2:
time: 426 us; the launch traced here: 422 us
  local copies, waits for them, and re-layouts  175 us (41%)
  waiting for transfers between devices  135 us (32%)
  starting transfers between devices  43.2 us (10%)
  Pallas kernels  37 us (9%)
  other arithmetic  17.2 us (4%)
  between operations  13.9 us (3%)
    all_gather x2, waiting for transfers between devices, kernel_block(): gathered = lax.all_gather(mine, 'hz', axis=1, tiled=True)  99.2 us
    dynamic_update_slice x2, local copies, waits for them, and re-layouts, kernel_block(): result = lax.dynamic_update_slice(result, other, (0, 0, source * share))  70 us
    dynamic_update_slice x2, local copies, waits for them, and re-layouts, kernel_block(): result = lax.dynamic_update_slice(result, gathered, (0, 0, part * share))  58.6 us
    pallas_call x2, Pallas kernels, causal_conv(): pl.pallas_call(conv_body, grid=(frames,), in_specs=[pl.BlockSpec(padded.s...  37 us
    ppermute x6, waiting for transfers between devices, kernel_block(): piece = lax.ppermute(piece, HQ, shift_pairs(size, step))  22.4 us
    ppermute x3, waiting for transfers between devices, scatter_rows(): piece = lax.ppermute(piece, HQ, shift_pairs(size, step))  11.4 us
    ppermute x12, starting transfers between devices, butterfly_stats(): other_sums, other_squares = lax.ppermute((sums, squares), axis, pairs)  10.5 us
    ppermute x6, starting transfers between devices, chip_gather(): lax.ppermute(firsts, 'hb', shift_pairs(count_b, step))  9.51 us
  transfers between devices with their start and end apart: 38, of which 13 were waited for; matrix products, arithmetic and copies ran while one was open for 42% of the time, Pallas kernels for 4%

profile of v2, /device:TPU:1, one launch (start us, length us, event | category | flops | bytes accessed | tf_op | source)
XLA Modules:
  0.0 422.1 jit_solution(13563807439900308249)
XLA Ops:
  11.4 4.2 collective-permute-done.13
  16.5 3.8 collective-permute-done.14
  28.7 10.1 %collective-permute-done.29 = bf16[27,32,128]{2,1,0:T(8,128)(2,1)S(1)} collective-permute-done((bf16[27,32,128]{2,1,0:T(8,128)(2,1)}, bf16[27,32,128]{2,1,0:T(8,128)(2,1)S(1)}, u32[]{:S(2)}, u32[]{:S(2)}) %collective-permute-start.29) | collective-permute-done | bytes 221216 | tf_op jit(solution)/shard_map/ppermute | solution.py:149
  53.0 2.8 collective-permute-start.3
  57.3 3.6 collective-permute-start.12
  60.9 38.4 %all-gather.3.cloned.1.call-done = bf16[27,512,64]{2,1,0:T(8,128)(2,1)} async-done(((bf16[27,128,64]{2,1,0:T(8,128)(2,1)}), bf16[27,512,64]{2,1,0:T(8,128)(2,1)}) %all-gather.3.cloned.1.call-update) | async-done | bytes 1769488 | tf_op jit(solution)/shard_map/all_gather | solution.py:156
  99.4 4.6 %copy.10 = bf16[27,512,64]{1,2,0:T(8,128)(2,1)} copy(bf16[27,512,64]{2,1,0:T(8,128)(2,1)} %all-gather.3.cloned.1.call-done) | data formatting | bytes 3538944 | tf_op jit(solution)/shard_map/all_gather | solution.py:156
  105.6 3.2 fusion.6
  108.8 60.8 %all-gather.5.cloned.1.call-done = bf16[27,512,64]{2,1,0:T(8,128)(2,1)} async-done(((bf16[27,128,64]{2,1,0:T(8,128)(2,1)}), bf16[27,512,64]{2,1,0:T(8,128)(2,1)}) %all-gather.5.cloned.1.call-update) | async-done | bytes 1769488 | tf_op jit(solution)/shard_map/all_gather | solution.py:156
  169.6 4.5 %copy.12 = bf16[27,512,64]{1,2,0:T(8,128)(2,1)} copy(bf16[27,512,64]{2,1,0:T(8,128)(2,1)} %all-gather.5.cloned.1.call-done) | data formatting | bytes 3538944 | tf_op jit(solution)/shard_map/all_gather | solution.py:156
  175.3 3.2 fusion.5.x_ref
  181.2 29.3 %dynamic_update_slice.92 = bf16[27,512,128]{2,1,0:T(8,128)(2,1)} dynamic-update-slice(bf16[27,512,128]{2,1,0:T(8,128)(2,1)} %broadcast.110.clone, bf16[27,512,64]{2,1,0:T(8,128)(2,1)S(1)} %copy-done.2, s32[]{:T(128)} %constant.162.clone.1, s32[]{:T(128)} %constant.162.clone.1, s32[]{:T(128)S(6)} %select_n.229) | dynamic-update-slice | bytes 3538948 | tf_op jit(solution)/shard_map/dynamic_update_slice | solution.py:158
  210.5 3.4 copy.11
  213.8 35.0 %dynamic_update_slice.93.w_ref = bf16[27,512,128]{2,1,0:T(8,128)(2,1)} dynamic-update-slice(bf16[27,512,128]{2,1,0:T(8,128)(2,1)} %dynamic_update_slice.92, bf16[27,512,64]{2,1,0:T(8,128)(2,1)S(1)} %copy.11, s32[]{:T(128)} %constant.162.clone.1, s32[]{:T(128)} %constant.162.clone.1, s32[]{:T(128)S(6)} %select_n.231) | dynamic-update-slice | bytes 3538948 | tf_op jit(solution)/shard_map/dynamic_update_slice | solution.py:162
  248.8 18.5 %shard_map.91 = bf16[3,8,80,128]{3,2,1,0:T(8,128)(2,1)} custom-call(bf16[5,10,82,512]{3,2,1,0:T(8,128)(2,1)} %fusion.5.x_ref, bf16[27,512,128]{2,1,0:T(8,128)(2,1)} %dynamic_update_slice.93.w_ref, f32[1,128]{1,0:T(1,128)} %dynamic-slice_bitcast_fusion.1.b_ref), custom_call_target="tpu_custom_call" | custom-call | flops 6794772480 | bytes 8720384 | tf_op jit(solution)/shard_map/pallas_call | solution.py:124
  276.2 29.3 %dynamic_update_slice.106 = bf16[27,512,128]{2,1,0:T(8,128)(2,1)} dynamic-update-slice(bf16[27,512,128]{2,1,0:T(8,128)(2,1)} %broadcast.110.clone.1, bf16[27,512,64]{2,1,0:T(8,128)(2,1)S(1)} %copy-done.3, s32[]{:T(128)} %constant.162.clone.1, s32[]{:T(128)} %constant.162.clone.1, s32[]{:T(128)S(6)} %select_n.229) | dynamic-update-slice | bytes 3538948 | tf_op jit(solution)/shard_map/dynamic_update_slice | solution.py:158
  314.1 3.4 copy.13
  317.5 35.0 %dynamic_update_slice.107.w_ref = bf16[27,512,128]{2,1,0:T(8,128)(2,1)} dynamic-update-slice(bf16[27,512,128]{2,1,0:T(8,128)(2,1)} %dynamic_update_slice.106, bf16[27,512,64]{2,1,0:T(8,128)(2,1)S(1)} %copy.13, s32[]{:T(128)} %constant.162.clone.1, s32[]{:T(128)} %constant.162.clone.1, s32[]{:T(128)S(6)} %select_n.231) | dynamic-update-slice | bytes 3538948 | tf_op jit(solution)/shard_map/dynamic_update_slice | solution.py:162
  359.4 4.1 collective-permute-start.27
  371.7 3.2 fusion.7
  374.9 3.2 select_maximum_fusion.x_ref
  378.1 18.5 %shard_map.92 = f32[3,8,80,128]{3,2,1,0:T(8,128)} custom-call(bf16[5,10,82,512]{3,2,1,0:T(8,128)(2,1)} %select_maximum_fusion.x_ref, bf16[27,512,128]{2,1,0:T(8,128)(2,1)} %dynamic_update_slice.107.w_ref, f32[1,128]{1,0:T(1,128)} %dynamic-slice_bitcast_fusion.b_ref), custom_call_target="tpu_custom_call" | custom-call | flops 6794772480 | bytes 8720384 | tf_op jit(solution)/shard_map/pallas_call | solution.py:124
  399.9 4.0 collective-permute-done.33
  403.9 6.7 %collective-permute-done.34 = f32[3,2,80,128]{3,2,1,0:T(8,128)S(1)} collective-permute-done((f32[3,2,80,128]{3,2,1,0:T(8,128)S(1)}, f32[3,2,80,128]{3,2,1,0:T(8,128)S(1)}, u32[]{:S(2)}, u32[]{:S(2)}) %collective-permute-start.34) | collective-permute-done | bytes 245792 | tf_op jit(solution)/shard_map/ppermute | solution.py:175
  (175 shorter events, 75.6 us)
Async XLA Ops:
  6.5 92.8 %all-gather.3.cloned.1.call-start = ((), (), s32[]{:S(2)}) async-start(), calls=%async_computation | async-start | bytes 4423680 | tf_op jit(solution)/shard_map/all_gather | solution.py:156
  10.9 9.4 %collective-permute-start.14 = (bf16[27,32,128]{2,1,0:T(8,128)(2,1)S(1)}, bf16[27,32,128]{2,1,0:T(8,128)(2,1)}, u32[]{:S(2)}, u32[]{:S(2)}) collective-permute-start(bf16[27,32,128]{2,1,0:T(8,128)(2,1)S(1)} %get-tuple-element.18), channel_id=1, source_target_pairs={{0,2},{1,3},{2,0},{3,1},{4,6},{5,7},{6,4},{7,5},{8,10},{9,11},{10,... | collective-permute-start | bytes 663560 | tf_op jit(solution)/shard_map/ppermute | solution.py:149
  10.9 10.3 %collective-permute-start.15 = (bf16[27,32,128]{2,1,0:T(8,128)(2,1)S(1)}, bf16[27,32,128]{2,1,0:T(8,128)(2,1)S(1)}, u32[]{:S(2)}, u32[]{:S(2)}) collective-permute-start(bf16[27,32,128]{2,1,0:T(8,128)(2,1)S(1)} %get-tuple-element.15), channel_id=1, source_target_pairs={{0,3},{1,0},{2,1},{3,2},{4,7},{5,4},{6,5},{7,6},{8,11},{9,8},{10,9... | collective-permute-start | bytes 663560 | tf_op jit(solution)/shard_map/ppermute | solution.py:149
  22.6 147.1 %all-gather.5.cloned.1.call-start = ((), (), s32[]{:S(2)}) async-start(), calls=%async_computation.1 | async-start | bytes 4423680 | tf_op jit(solution)/shard_map/all_gather | solution.py:156
  22.6 25.6 %collective-permute-start = (bf16[3,2,80,512]{3,2,1,0:T(8,128)(2,1)S(1)}, bf16[3,2,80,512]{3,2,1,0:T(8,128)(2,1)S(1)}, u32[]{:S(2)}, u32[]{:S(2)}) collective-permute-start(bf16[3,2,80,512]{3,2,1,0:T(8,128)(2,1)S(1)} %copy-done.5), channel_id=1, source_target_pairs={{0,2},{2,0},{1,3},{3,1},{4,6},{6,4},{5,7},{7,5},{8,10},{10,8},{9,1... | collective-permute-start | bytes 1474568 | tf_op jit(solution)/shard_map/ppermute | solution.py:66
  24.7 27.0 %collective-permute-start.1 = (bf16[3,2,80,512]{3,2,1,0:T(8,128)(2,1)S(1)}, bf16[3,2,80,512]{3,2,1,0:T(8,128)(2,1)S(1)}, u32[]{:S(2)}, u32[]{:S(2)}) collective-permute-start(bf16[3,2,80,512]{3,2,1,0:T(8,128)(2,1)S(1)} %copy-done.5), channel_id=1, source_target_pairs={{0,1},{1,0},{2,3},{3,2},{4,5},{5,4},{6,7},{7,6},{8,9},{9,8},{10,11... | collective-permute-start | bytes 1474568 | tf_op jit(solution)/shard_map/ppermute | solution.py:71
  25.9 12.9 %collective-permute-start.29 = (bf16[27,32,128]{2,1,0:T(8,128)(2,1)}, bf16[27,32,128]{2,1,0:T(8,128)(2,1)S(1)}, u32[]{:S(2)}, u32[]{:S(2)}) collective-permute-start(bf16[27,32,128]{2,1,0:T(8,128)(2,1)} %get-tuple-element.12), channel_id=1, source_target_pairs={{0,1},{1,2},{2,3},{3,0},{4,5},{5,6},{6,7},{7,4},{8,9},{9,10},{10,1... | collective-permute-start | bytes 663560 | tf_op jit(solution)/shard_map/ppermute | solution.py:149
  26.4 17.8 %collective-permute-start.30 = (bf16[27,32,128]{2,1,0:T(8,128)(2,1)}, bf16[27,32,128]{2,1,0:T(8,128)(2,1)S(1)}, u32[]{:S(2)}, u32[]{:S(2)}) collective-permute-start(bf16[27,32,128]{2,1,0:T(8,128)(2,1)} %get-tuple-element.14), channel_id=1, source_target_pairs={{0,2},{1,3},{2,0},{3,1},{4,6},{5,7},{6,4},{7,5},{8,10},{9,11},{10,... | collective-permute-start | bytes 663560 | tf_op jit(solution)/shard_map/ppermute | solution.py:149
  28.1 20.3 %collective-permute-start.5 = (f32[32]{0:T(128)S(1)}, f32[32]{0:T(128)S(1)}, u32[]{:S(2)}, u32[]{:S(2)}) collective-permute-start(f32[32]{0:T(128)S(1)} %reduce_sum.51), channel_id=1, source_target_pairs={{0,2},{2,0},{1,3},{3,1},{4,6},{6,4},{5,7},{7,5},{8,10},{10,8},{9,1... | collective-permute-start | bytes 392 | tf_op jit(solution)/shard_map/ppermute | solution.py:25
  53.0 52.5 %collective-permute-start.3 = (bf16[3,1,80,512]{3,2,1,0:T(8,128)(2,1)S(1)}, bf16[3,1,80,512]{3,2,1,0:T(8,128)(2,1)S(1)}, u32[]{:S(2)}, u32[]{:S(2)}) collective-permute-start(bf16[3,1,80,512]{3,2,1,0:T(8,128)(2,1)S(1)} %get-tuple-element.5), channel_id=1, source_target_pairs={{0,4},{4,8},{8,12},{1,5},{5,9},{9,13},{2,6},{6,10},{10,14},{3,7},{... | collective-permute-start | bytes 737288 | tf_op jit(solution)/shard_map/ppermute | solution.py:93
  55.8 49.7 %collective-permute-start.4 = (bf16[3,1,80,512]{3,2,1,0:T(8,128)(2,1)S(1)}, bf16[3,1,80,512]{3,2,1,0:T(8,128)(2,1)S(1)}, u32[]{:S(2)}, u32[]{:S(2)}) collective-permute-start(bf16[3,1,80,512]{3,2,1,0:T(8,128)(2,1)S(1)} %get-tuple-element.6), channel_id=1, source_target_pairs={{4,0},{8,4},{12,8},{5,1},{9,5},{13,9},{6,2},{10,6},{14,10},{7,3},{... | collective-permute-start | bytes 737288 | tf_op jit(solution)/shard_map/ppermute | solution.py:94
  57.3 47.9 %collective-permute-start.12 = (f32[32]{0:T(128)S(1)}, f32[32]{0:T(128)S(1)}, u32[]{:S(2)}, u32[]{:S(2)}) collective-permute-start(f32[32]{0:T(128)S(1)} %get-tuple-element.31), channel_id=1, source_target_pairs={{0,8},{4,12},{8,0},{12,4},{1,9},{5,13},{9,1},{13,5},{2,10},{6,14},... | collective-permute-start | bytes 392 | tf_op jit(solution)/shard_map/ppermute | solution.py:25
  60.9 44.3 %collective-permute-start.8 = (f32[32]{0:T(128)S(1)}, f32[32]{0:T(128)S(1)}, u32[]{:S(2)}, u32[]{:S(2)}) collective-permute-start(f32[32]{0:T(128)S(1)} %get-tuple-element.32), channel_id=1, source_target_pairs={{0,8},{4,12},{8,0},{12,4},{1,9},{5,13},{9,1},{13,5},{2,10},{6,14},... | collective-permute-start | bytes 392 | tf_op jit(solution)/shard_map/ppermute | solution.py:25
  104.0 106.5 %collective-permute-start.16 = (bf16[27,512,64]{1,2,0:T(8,128)(2,1)}, bf16[27,512,64]{1,2,0:T(8,128)(2,1)}, u32[]{:S(2)}, u32[]{:S(2)}) collective-permute-start(bf16[27,512,64]{1,2,0:T(8,128)(2,1)} %copy.10), channel_id=1, source_target_pairs={{0,16},{16,0},{1,17},{17,1},{2,18},{18,2},{3,19},{19,3},{4,20},{20... | collective-permute-start | bytes 5308424 | tf_op jit(solution)/shard_map/ppermute | solution.py:160
  174.2 139.9 %collective-permute-start.32 = (bf16[27,512,64]{1,2,0:T(8,128)(2,1)}, bf16[27,512,64]{1,2,0:T(8,128)(2,1)}, u32[]{:S(2)}, u32[]{:S(2)}) collective-permute-start(bf16[27,512,64]{1,2,0:T(8,128)(2,1)} %copy.12), channel_id=1, source_target_pairs={{0,16},{16,0},{1,17},{17,1},{2,18},{18,2},{3,19},{19,3},{4,20},{20... | collective-permute-start | bytes 5308424 | tf_op jit(solution)/shard_map/ppermute | solution.py:160
  269.0 36.5 %collective-permute-start.17 = (bf16[3,1,80,128]{3,2,1,0:T(8,128)(2,1)}, bf16[3,1,80,128]{3,2,1,0:T(8,128)(2,1)}, u32[]{:S(2)}, u32[]{:S(2)}) collective-permute-start(bf16[3,1,80,128]{3,2,1,0:T(8,128)(2,1)} %get-tuple-element.21), channel_id=1, source_target_pairs={{0,4},{4,8},{8,12},{1,5},{5,9},{9,13},{2,6},{6,10},{10,14},{3,7},{... | collective-permute-start | bytes 184328 | tf_op jit(solution)/shard_map/ppermute | solution.py:93
  270.9 34.6 %collective-permute-start.18 = (bf16[3,1,80,128]{3,2,1,0:T(8,128)(2,1)}, bf16[3,1,80,128]{3,2,1,0:T(8,128)(2,1)}, u32[]{:S(2)}, u32[]{:S(2)}) collective-permute-start(bf16[3,1,80,128]{3,2,1,0:T(8,128)(2,1)} %get-tuple-element.22), channel_id=1, source_target_pairs={{4,0},{8,4},{12,8},{5,1},{9,5},{13,9},{6,2},{10,6},{14,10},{7,3},{... | collective-permute-start | bytes 184328 | tf_op jit(solution)/shard_map/ppermute | solution.py:94
  309.5 49.0 %collective-permute-start.19 = (bf16[3,10,80,128]{3,2,1,0:T(8,128)(2,1)}, bf16[3,10,80,128]{3,2,1,0:T(8,128)(2,1)}, u32[]{:S(2)}, u32[]{:S(2)}) collective-permute-start(bf16[3,10,80,128]{3,2,1,0:T(8,128)(2,1)} %get-tuple-element.19), channel_id=1, source_target_pairs={{0,2},{2,0},{1,3},{3,1},{4,6},{6,4},{5,7},{7,5},{8,10},{10,8},{9,1... | collective-permute-start | bytes 1843208 | tf_op jit(solution)/shard_map/ppermute | solution.py:66
  311.2 41.8 %collective-permute-start.22 = (f32[8]{0:T(128)S(1)}, f32[8]{0:T(128)}, u32[]{:S(2)}, u32[]{:S(2)}) collective-permute-start(f32[8]{0:T(128)S(1)} %reduce_sum.72), channel_id=1, source_target_pairs={{0,4},{4,0},{8,12},{12,8},{1,5},{5,1},{9,13},{13,9},{2,6},{6,2},{1... | collective-permute-start | bytes 104 | tf_op jit(solution)/shard_map/ppermute | solution.py:25
  314.0 38.5 %collective-permute-start.24 = (f32[8]{0:T(128)S(1)}, f32[8]{0:T(128)S(1)}, u32[]{:S(2)}, u32[]{:S(2)}) collective-permute-start(f32[8]{0:T(128)S(1)} %reduce_sum.75), channel_id=1, source_target_pairs={{0,4},{4,0},{8,12},{12,8},{1,5},{5,1},{9,13},{13,9},{2,6},{6,2},{1... | collective-permute-start | bytes 104 | tf_op jit(solution)/shard_map/ppermute | solution.py:25
  356.0 13.9 %collective-permute-start.20 = (bf16[3,10,80,128]{3,2,1,0:T(8,128)(2,1)}, bf16[3,10,80,128]{3,2,1,0:T(8,128)(2,1)S(1)}, u32[]{:S(2)}, u32[]{:S(2)}) collective-permute-start(bf16[3,10,80,128]{3,2,1,0:T(8,128)(2,1)} %get-tuple-element.19), channel_id=1, source_target_pairs={{0,1},{1,0},{2,3},{3,2},{4,5},{5,4},{6,7},{7,6},{8,9},{9,8},{10,11... | collective-permute-start | bytes 1843208 | tf_op jit(solution)/shard_map/ppermute | solution.py:71
  358.5 12.3 %collective-permute-start.21 = (bf16[3,10,80,128]{3,2,1,0:T(8,128)(2,1)}, bf16[3,10,80,128]{3,2,1,0:T(8,128)(2,1)S(1)}, u32[]{:S(2)}, u32[]{:S(2)}) collective-permute-start(bf16[3,10,80,128]{3,2,1,0:T(8,128)(2,1)} %collective-permute-done.19), channel_id=1, source_target_pairs={{0,1},{1,0},{2,3},{3,2},{4,5},{5,4},{6,7},{7,6},{8,9},{9,8},{10,11... | collective-permute-start | bytes 1843208 | tf_op jit(solution)/shard_map/ppermute | solution.py:71
  398.7 11.9 %collective-permute-start.34 = (f32[3,2,80,128]{3,2,1,0:T(8,128)S(1)}, f32[3,2,80,128]{3,2,1,0:T(8,128)S(1)}, u32[]{:S(2)}, u32[]{:S(2)}) collective-permute-start(f32[3,2,80,128]{3,2,1,0:T(8,128)S(1)} %get-tuple-element.8), channel_id=1, source_target_pairs={{0,2},{1,3},{2,0},{3,1},{4,6},{5,7},{6,4},{7,5},{8,10},{9,11},{10,... | collective-permute-start | bytes 737288 | tf_op jit(solution)/shard_map/ppermute | solution.py:175
  399.9 11.5 %collective-permute-start.35 = (f32[3,2,80,128]{3,2,1,0:T(8,128)S(1)}, f32[3,2,80,128]{3,2,1,0:T(8,128)S(1)}, u32[]{:S(2)}, u32[]{:S(2)}) collective-permute-start(f32[3,2,80,128]{3,2,1,0:T(8,128)S(1)} %get-tuple-element.7), channel_id=1, source_target_pairs={{0,3},{1,0},{2,1},{3,2},{4,7},{5,4},{6,5},{7,6},{8,11},{9,8},{10,9... | collective-permute-start | bytes 737288 | tf_op jit(solution)/shard_map/ppermute | solution.py:175
  (28 other events, 377.4 us)
Sparse Core Ops, SparseCore 0:
  22.7 76.6 all-gather.2
  100.9 68.6 all-gather.4

commit v3 on v1

--- a/solution.py
+++ b/solution.py
@@ -141,15 +141,28 @@
     me = lax.axis_index(HQ)
     taps, in_block, outs = shard.shape
     width = outs // size
-    out = jnp.zeros((taps, in_block * size, width), shard.dtype)
+    flipped = jnp.transpose(shard, (1, 0, 2))
+    out = jnp.zeros((in_block * size, taps, width), shard.dtype)
     for step in range(size):
         target = (me + step) % size
-        piece = lax.dynamic_slice_in_dim(shard, target * width, width, axis=2)
+        piece = lax.dynamic_slice_in_dim(flipped, target * width, width, axis=2)
         if step:
             piece = lax.ppermute(piece, HQ, shift_pairs(size, step))
         source = (me - step) % size
-        out = lax.dynamic_update_slice(out, piece, (0, source * in_block, 0))
-    return lax.all_gather(out, "hz", axis=1, tiled=True)
+        out = lax.dynamic_update_slice(out, piece, (source * in_block, 0, 0))
+    parts = lax.axis_size("groups")
+    part = lax.axis_index("groups")
+    rows = lax.axis_size("hz")
+    share = (in_block * size) // parts
+    mine = lax.dynamic_slice_in_dim(out, part * share, share, axis=0)
+    gathered = lax.all_gather(mine, "hz", axis=0)
+    result = jnp.zeros((rows, parts, share, taps, width), shard.dtype)
+    result = lax.dynamic_update_slice(result, gathered[:, None], (0, part, 0, 0, 0))
+    for step in range(1, parts):
+        other = lax.ppermute(gathered, "groups", shift_pairs(parts, step))
+        source = (part - step) % parts
+        result = lax.dynamic_update_slice(result, other[:, None], (0, source, 0, 0, 0))
+    return jnp.transpose(result.reshape(chans, taps, width), (1, 0, 2))
 
 
 def scatter_rows(branch, slab_rows, chans):

time: 215 us -> 226 us (1.051)
  local copies, waits for them, and re-layouts: 27.1 us -> 39.3 us
    ppermute x2, waiting for transfers between devices: 12.7 us -> 1.24 us  [with_row_halo(): bottom = lax.ppermute(cells[:, :1], axis_name, up)]
    dynamic_update_slice x6 -> x12, local copies, waits for them, and re-layouts: 3.94 us -> 12.1 us  [the longest x2 6.64 us: kernel_block(): lax.dynamic_update_slice(result, other[:, None], (0, source, 0, 0, 0))]
    all_gather x2, waiting for transfers between devices: 26.8 us -> 33.1 us  [kernel_block(): gathered = lax.all_gather(mine, 'hz', axis=0)]
    another operation x3 -> x5, local copies, waits for them, and re-layouts: 0.64 us -> 5.98 us
    ppermute x6, waiting for transfers between devices: 8.4 us -> 12.5 us  [kernel_block(): piece = lax.ppermute(piece, HQ, shift_pairs(size, step))]
    ppermute x2, starting transfers between devices: 8.88 us -> 5.11 us  [with_row_halo(): top = lax.ppermute(cells[:, -1:], axis_name, down)]
    ppermute x12, starting transfers between devices: 11.7 us -> 15.1 us  [butterfly_stats(): other_sums, other_squares = lax.ppermute((sums, squares), axis, pairs)]
    ppermute x0 -> x2, starting transfers between devices: none -> 2.43 us  [kernel_block(): other = lax.ppermute(gathered, 'groups', shift_pairs(parts, step))]
  transfers between devices with their start and end apart: 36 -> 38, of which waited for: 21 -> 18; matrix products, arithmetic and copies ran while one was open for 15% -> 18% of each run, Pallas kernels for 9% -> 8%
where the time goes in v3:
time: 226 us
  waiting for transfers between devices  74.5 us (33%)
  starting transfers between devices  46.3 us (20%)
  local copies, waits for them, and re-layouts  39.3 us (17%)
  Pallas kernels  37 us (16%)
  other arithmetic  14.5 us (6%)
  between operations  13.9 us (6%)
    pallas_call x2, Pallas kernels, causal_conv(): pl.pallas_call(conv_body, grid=(frames,), in_specs=[pl.BlockSpec(padded.s...  37 us
    all_gather x2, waiting for transfers between devices, kernel_block(): gathered = lax.all_gather(mine, 'hz', axis=0)  33.1 us
    ppermute x12, starting transfers between devices, butterfly_stats(): other_sums, other_squares = lax.ppermute((sums, squares), axis, pairs)  15.1 us
    ppermute x12, waiting for transfers between devices, butterfly_stats(): other_sums, other_squares = lax.ppermute((sums, squares), axis, pairs)  14.6 us
    ppermute x6, waiting for transfers between devices, kernel_block(): piece = lax.ppermute(piece, HQ, shift_pairs(size, step))  12.5 us
    ppermute x3, waiting for transfers between devices, scatter_rows(): piece = lax.ppermute(piece, HQ, shift_pairs(size, step))  11.2 us
    ppermute x6, starting transfers between devices, chip_gather(): lax.ppermute(firsts, 'hb', shift_pairs(count_b, step))  9.79 us
    dynamic_update_slice x11, local copies, waits for them, and re-layouts, chip_gather(): out = lax.dynamic_update_slice(out, piece, start)  7.67 us
  transfers between devices with their start and end apart: 38, of which 18 were waited for; matrix products, arithmetic and copies ran while one was open for 18% of the time, Pallas kernels for 8%

profile of v3, /device:TPU:1, one launch (start us, length us, event | category | flops | bytes accessed | tf_op | source)
XLA Modules:
  0.0 225.6 jit_solution(15181153483533949349)
XLA Ops:
  7.9 2.7 %collective-permute-start.13 = (bf16[32,27,128]{2,0,1:T(8,128)(2,1)S(1)}, bf16[32,27,128]{2,0,1:T(8,128)(2,1)S(1)}, u32[]{:S(2)}, u32[]{:S(2)}) collective-permute-start(bf16[32,27,128]{2,0,1:T(8,128)(2,1)S(1)} %get-tuple-element.15), channel_id=1, source_target_pairs={{0,1},{1,2},{2,3},{3,0},{4,5},{5,6},{6,7},{7,4},{8,9},{9,10},{10,1... | collective-permute-start | bytes 663560 | tf_op jit(solution)/shard_map/ppermute | solution.py:150
  12.3 3.0 %collective-permute-done.13 = bf16[32,27,128]{2,0,1:T(8,128)(2,1)S(1)} collective-permute-done((bf16[32,27,128]{2,0,1:T(8,128)(2,1)S(1)}, bf16[32,27,128]{2,0,1:T(8,128)(2,1)S(1)}, u32[]{:S(2)}, u32[]{:S(2)}) %collective-permute-start.13) | collective-permute-done | bytes 221216 | tf_op jit(solution)/shard_map/ppermute | solution.py:150
  15.3 4.7 %collective-permute-done.14 = bf16[32,27,128]{2,0,1:T(8,128)(2,1)S(1)} collective-permute-done((bf16[32,27,128]{2,0,1:T(8,128)(2,1)S(1)}, bf16[32,27,128]{2,0,1:T(8,128)(2,1)S(1)}, u32[]{:S(2)}, u32[]{:S(2)}) %collective-permute-start.14) | collective-permute-done | bytes 221216 | tf_op jit(solution)/shard_map/ppermute | solution.py:150
  30.4 4.7 %collective-permute-done.9 = f32[32]{0:T(128)S(1)} collective-permute-done((f32[32]{0:T(128)S(1)}, f32[32]{0:T(128)S(1)}, u32[]{:S(2)}, u32[]{:S(2)}) %collective-permute-start.9) | collective-permute-done | bytes 160 | tf_op jit(solution)/shard_map/ppermute | solution.py:25
  40.1 4.0 %collective-permute-done.30 = bf16[32,27,128]{2,0,1:T(8,128)(2,1)S(1)} collective-permute-done((bf16[32,27,128]{2,0,1:T(8,128)(2,1)}, bf16[32,27,128]{2,0,1:T(8,128)(2,1)S(1)}, u32[]{:S(2)}, u32[]{:S(2)}) %collective-permute-start.30) | collective-permute-done | bytes 221216 | tf_op jit(solution)/shard_map/ppermute | solution.py:150
  51.3 3.3 %collective-permute-start.3 = (bf16[3,1,80,512]{3,2,1,0:T(8,128)(2,1)S(1)}, bf16[3,1,80,512]{3,2,1,0:T(8,128)(2,1)S(1)}, u32[]{:S(2)}, u32[]{:S(2)}) collective-permute-start(bf16[3,1,80,512]{3,2,1,0:T(8,128)(2,1)S(1)} %get-tuple-element.5), channel_id=1, source_target_pairs={{0,4},{4,8},{8,12},{1,5},{5,9},{9,13},{2,6},{6,10},{10,14},{3,7},{... | collective-permute-start | bytes 737288 | tf_op jit(solution)/shard_map/ppermute | solution.py:93
  56.2 3.2 %collective-permute-start.12 = (f32[32]{0:T(128)S(1)}, f32[32]{0:T(128)S(1)}, u32[]{:S(2)}, u32[]{:S(2)}) collective-permute-start(f32[32]{0:T(128)S(1)} %get-tuple-element.29), channel_id=1, source_target_pairs={{0,8},{4,12},{8,0},{12,4},{1,9},{5,13},{9,1},{13,5},{2,10},{6,14},... | collective-permute-start | bytes 392 | tf_op jit(solution)/shard_map/ppermute | solution.py:25
  59.4 8.8 %collective-permute-done.12 = f32[32]{0:T(128)S(1)} collective-permute-done((f32[32]{0:T(128)S(1)}, f32[32]{0:T(128)S(1)}, u32[]{:S(2)}, u32[]{:S(2)}) %collective-permute-start.12) | collective-permute-done | bytes 160 | tf_op jit(solution)/shard_map/ppermute | solution.py:25
  71.8 3.1 %fusion.5.x_ref = bf16[5,10,82,512]{3,2,1,0:T(8,128)(2,1)} fusion(bf16[3,10,80,512]{3,2,1,0:T(8,128)(2,1)S(1)} %fusion.6, bf16[1,10,80,512]{3,2,1,0:T(8,128)(2,1)S(1)} %slice.36), kind=kLoop, calls=%fused_computation.11 | loop fusion | flops 25190400 | bytes 7475200 | tf_op jit(solution)/shard_map/concatenate | solution.py:116
  75.0 33.1 %all-gather.7.cloned.1.call-done = bf16[256,27,128]{2,0,1:T(8,128)(2,1)} async-done(((bf16[64,27,128]{2,0,1:T(8,128)(2,1)}), bf16[256,27,128]{2,0,1:T(8,128)(2,1)}) %all-gather.7.cloned.1.call-update) | async-done | bytes 1769488 | tf_op jit(solution)/shard_map/all_gather | solution.py:158
  109.2 2.7 %broadcast.110.clone = bf16[4,2,64,27,128]{4,2,1,0,3:T(8,128)(2,1)} broadcast(bf16[]{:T(256)} %constant.167.clone.1), dimensions={} | broadcast | bytes 3538946 | tf_op jit(solution)/shard_map/broadcast.20
  113.6 2.7 %broadcast.110.clone.1 = bf16[4,2,64,27,128]{4,2,1,0,3:T(8,128)(2,1)} broadcast(bf16[]{:T(256)} %constant.167.clone.1), dimensions={} | broadcast | bytes 3538946 | tf_op jit(solution)/shard_map/broadcast.20
  117.9 3.3 %bitcast_dynamic-update-slice_fusion.1 = bf16[4,2,64,27,128]{4,2,1,0,3:T(8,128)(2,1)} fusion(bf16[4,2,64,27,128]{4,2,1,0,3:T(8,128)(2,1)} %constant_dynamic-update-slice_fusion.11, s32[]{:T(128)S(6)} %select_n.234, bf16[4,64,27,128]{3,1,0,2:T(8,128)(2,1)} %collective-permute-done.16), kind=kLoop, calls=%fused_computation.15 | loop fusion | bytes 3538948 | tf_op jit(solution)/shard_map/dynamic_update_slice | solution.py:164
  121.2 18.5 %shard_map.91 = bf16[3,8,80,128]{3,2,1,0:T(8,128)(2,1)} custom-call(bf16[5,10,82,512]{3,2,1,0:T(8,128)(2,1)} %fusion.5.x_ref, bf16[27,512,128]{2,1,0:T(8,128)(2,1)} %bitcast.8.w_ref, f32[1,128]{1,0:T(1,128)} %dynamic-slice_bitcast_fusion.7.b_ref), custom_call_target="tpu_custom_call" | custom-call | flops 6794772480 | bytes 8720384 | tf_op jit(solution)/shard_map/pallas_call | solution.py:124
  145.5 2.2 collective-permute-start.22
  154.3 3.3 %bitcast_dynamic-update-slice_fusion = bf16[4,2,64,27,128]{4,2,1,0,3:T(8,128)(2,1)} fusion(bf16[4,2,64,27,128]{4,2,1,0,3:T(8,128)(2,1)} %constant_dynamic-update-slice_fusion.3, s32[]{:T(128)S(6)} %select_n.234, bf16[4,64,27,128]{3,1,0,2:T(8,128)(2,1)} %collective-permute-done.32), kind=kLoop, calls=%fused_computation.14 | loop fusion | bytes 3538948 | tf_op jit(solution)/shard_map/dynamic_update_slice | solution.py:164
  157.8 2.2 collective-permute-start.25
  160.1 3.5 %collective-permute-start.20 = (bf16[3,10,80,128]{3,2,1,0:T(8,128)(2,1)}, bf16[3,10,80,128]{3,2,1,0:T(8,128)(2,1)}, u32[]{:S(2)}, u32[]{:S(2)}) collective-permute-start(bf16[3,10,80,128]{3,2,1,0:T(8,128)(2,1)} %get-tuple-element.17), channel_id=1, source_target_pairs={{0,1},{1,0},{2,3},{3,2},{4,5},{5,4},{6,7},{7,6},{8,9},{9,8},{10,11... | collective-permute-start | bytes 1843208 | tf_op jit(solution)/shard_map/ppermute | solution.py:71
  164.2 3.5 %collective-permute-start.21 = (bf16[3,10,80,128]{3,2,1,0:T(8,128)(2,1)}, bf16[3,10,80,128]{3,2,1,0:T(8,128)(2,1)}, u32[]{:S(2)}, u32[]{:S(2)}) collective-permute-start(bf16[3,10,80,128]{3,2,1,0:T(8,128)(2,1)} %collective-permute-done.19), channel_id=1, source_target_pairs={{0,1},{1,0},{2,3},{3,2},{4,5},{5,4},{6,7},{7,6},{8,9},{9,8},{10,11... | collective-permute-start | bytes 1843208 | tf_op jit(solution)/shard_map/ppermute | solution.py:71
  178.4 3.1 %select_maximum_fusion.x_ref = bf16[5,10,82,512]{3,2,1,0:T(8,128)(2,1)} fusion(bf16[3,10,80,512]{3,2,1,0:T(8,128)(2,1)S(1)} %fusion.7, bf16[1,10,80,512]{3,2,1,0:T(8,128)(2,1)S(1)} %slice.39), kind=kLoop, calls=%fused_computation.5 | loop fusion | flops 25190400 | bytes 7475200 | tf_op jit(solution)/shard_map/concatenate | solution.py:116
  181.6 18.5 %shard_map.92 = f32[3,8,80,128]{3,2,1,0:T(8,128)} custom-call(bf16[5,10,82,512]{3,2,1,0:T(8,128)(2,1)} %select_maximum_fusion.x_ref, bf16[27,512,128]{2,1,0:T(8,128)(2,1)} %bitcast.22.w_ref, f32[1,128]{1,0:T(1,128)} %dynamic-slice_bitcast_fusion.6.b_ref), custom_call_target="tpu_custom_call" | custom-call | flops 6794772480 | bytes 8720384 | tf_op jit(solution)/shard_map/pallas_call | solution.py:124
  203.5 4.7 %collective-permute-done.33 = f32[3,2,80,128]{3,2,1,0:T(8,128)S(1)} collective-permute-done((f32[3,2,80,128]{3,2,1,0:T(8,128)S(1)}, f32[3,2,80,128]{3,2,1,0:T(8,128)S(1)}, u32[]{:S(2)}, u32[]{:S(2)}) %collective-permute-start.33) | collective-permute-done | bytes 245792 | tf_op jit(solution)/shard_map/ppermute | solution.py:177
  208.3 5.8 %collective-permute-done.34 = f32[3,2,80,128]{3,2,1,0:T(8,128)S(1)} collective-permute-done((f32[3,2,80,128]{3,2,1,0:T(8,128)S(1)}, f32[3,2,80,128]{3,2,1,0:T(8,128)S(1)}, u32[]{:S(2)}, u32[]{:S(2)}) %collective-permute-start.34) | collective-permute-done | bytes 245792 | tf_op jit(solution)/shard_map/ppermute | solution.py:177
  216.5 2.2 reshape.67
  (165 shorter events, 64.9 us)
Async XLA Ops:
  6.5 62.0 %all-gather.5.cloned.1.call-start = ((), (), s32[]{:S(2)}) async-start(), calls=%async_computation | async-start | bytes 2211840 | tf_op jit(solution)/shard_map/all_gather | solution.py:158
  10.6 9.9 %collective-permute-start.15 = (bf16[32,27,128]{2,0,1:T(8,128)(2,1)S(1)}, bf16[32,27,128]{2,0,1:T(8,128)(2,1)S(1)}, u32[]{:S(2)}, u32[]{:S(2)}) collective-permute-start(bf16[32,27,128]{2,0,1:T(8,128)(2,1)S(1)} %get-tuple-element.14), channel_id=1, source_target_pairs={{0,3},{1,0},{2,1},{3,2},{4,7},{5,4},{6,5},{7,6},{8,11},{9,8},{10,9... | collective-permute-start | bytes 663560 | tf_op jit(solution)/shard_map/ppermute | solution.py:150
  21.4 86.7 %all-gather.7.cloned.1.call-start = ((), (), s32[]{:S(2)}) async-start(), calls=%async_computation.1 | async-start | bytes 2211840 | tf_op jit(solution)/shard_map/all_gather | solution.py:158
  21.4 24.0 %collective-permute-start = (bf16[3,2,80,512]{3,2,1,0:T(8,128)(2,1)S(1)}, bf16[3,2,80,512]{3,2,1,0:T(8,128)(2,1)}, u32[]{:S(2)}, u32[]{:S(2)}) collective-permute-start(bf16[3,2,80,512]{3,2,1,0:T(8,128)(2,1)S(1)} %copy-done.1), channel_id=1, source_target_pairs={{0,2},{2,0},{1,3},{3,1},{4,6},{6,4},{5,7},{7,5},{8,10},{10,8},{9,1... | collective-permute-start | bytes 1474568 | tf_op jit(solution)/shard_map/ppermute | solution.py:66
  23.5 25.6 %collective-permute-start.1 = (bf16[3,2,80,512]{3,2,1,0:T(8,128)(2,1)S(1)}, bf16[3,2,80,512]{3,2,1,0:T(8,128)(2,1)}, u32[]{:S(2)}, u32[]{:S(2)}) collective-permute-start(bf16[3,2,80,512]{3,2,1,0:T(8,128)(2,1)S(1)} %copy-done.1), channel_id=1, source_target_pairs={{0,1},{1,0},{2,3},{3,2},{4,5},{5,4},{6,7},{7,6},{8,9},{9,8},{10,11... | collective-permute-start | bytes 1474568 | tf_op jit(solution)/shard_map/ppermute | solution.py:71
  23.8 11.3 %collective-permute-start.5 = (f32[32]{0:T(128)S(1)}, f32[32]{0:T(128)S(1)}, u32[]{:S(2)}, u32[]{:S(2)}) collective-permute-start(f32[32]{0:T(128)S(1)} %reduce_sum.51), channel_id=1, source_target_pairs={{0,2},{2,0},{1,3},{3,1},{4,6},{6,4},{5,7},{7,5},{8,10},{10,8},{9,1... | collective-permute-start | bytes 392 | tf_op jit(solution)/shard_map/ppermute | solution.py:25
  24.6 10.4 %collective-permute-start.9 = (f32[32]{0:T(128)S(1)}, f32[32]{0:T(128)S(1)}, u32[]{:S(2)}, u32[]{:S(2)}) collective-permute-start(f32[32]{0:T(128)S(1)} %reduce_sum.54), channel_id=1, source_target_pairs={{0,2},{2,0},{1,3},{3,1},{4,6},{6,4},{5,7},{7,5},{8,10},{10,8},{9,1... | collective-permute-start | bytes 392 | tf_op jit(solution)/shard_map/ppermute | solution.py:25
  26.9 10.7 %collective-permute-start.29 = (bf16[32,27,128]{2,0,1:T(8,128)(2,1)}, bf16[32,27,128]{2,0,1:T(8,128)(2,1)}, u32[]{:S(2)}, u32[]{:S(2)}) collective-permute-start(bf16[32,27,128]{2,0,1:T(8,128)(2,1)} %get-tuple-element.12), channel_id=1, source_target_pairs={{0,1},{1,2},{2,3},{3,0},{4,5},{5,6},{6,7},{7,4},{8,9},{9,10},{10,1... | collective-permute-start | bytes 663560 | tf_op jit(solution)/shard_map/ppermute | solution.py:150
  37.3 9.8 %collective-permute-start.31 = (bf16[32,27,128]{2,0,1:T(8,128)(2,1)}, bf16[32,27,128]{2,0,1:T(8,128)(2,1)S(1)}, u32[]{:S(2)}, u32[]{:S(2)}) collective-permute-start(bf16[32,27,128]{2,0,1:T(8,128)(2,1)} %get-tuple-element.11), channel_id=1, source_target_pairs={{0,3},{1,0},{2,1},{3,2},{4,7},{5,4},{6,5},{7,6},{8,11},{9,8},{10,9... | collective-permute-start | bytes 663560 | tf_op jit(solution)/shard_map/ppermute | solution.py:150
  37.5 18.6 %collective-permute-start.11 = (f32[32]{0:T(128)S(1)}, f32[32]{0:T(128)S(1)}, u32[]{:S(2)}, u32[]{:S(2)}) collective-permute-start(f32[32]{0:T(128)S(1)} %get-tuple-element.31), channel_id=1, source_target_pairs={{0,4},{4,0},{8,12},{12,8},{1,5},{5,1},{9,13},{13,9},{2,6},{6,2},{1... | collective-permute-start | bytes 392 | tf_op jit(solution)/shard_map/ppermute | solution.py:25
  44.0 12.1 %collective-permute-start.7 = (f32[32]{0:T(128)S(1)}, f32[32]{0:T(128)S(1)}, u32[]{:S(2)}, u32[]{:S(2)}) collective-permute-start(f32[32]{0:T(128)S(1)} %get-tuple-element.32), channel_id=1, source_target_pairs={{0,4},{4,0},{8,12},{12,8},{1,5},{5,1},{9,13},{13,9},{2,6},{6,2},{1... | collective-permute-start | bytes 392 | tf_op jit(solution)/shard_map/ppermute | solution.py:25
  51.3 18.5 %collective-permute-start.3 = (bf16[3,1,80,512]{3,2,1,0:T(8,128)(2,1)S(1)}, bf16[3,1,80,512]{3,2,1,0:T(8,128)(2,1)S(1)}, u32[]{:S(2)}, u32[]{:S(2)}) collective-permute-start(bf16[3,1,80,512]{3,2,1,0:T(8,128)(2,1)S(1)} %get-tuple-element.5), channel_id=1, source_target_pairs={{0,4},{4,8},{8,12},{1,5},{5,9},{9,13},{2,6},{6,10},{10,14},{3,7},{... | collective-permute-start | bytes 737288 | tf_op jit(solution)/shard_map/ppermute | solution.py:93
  54.6 15.2 %collective-permute-start.4 = (bf16[3,1,80,512]{3,2,1,0:T(8,128)(2,1)S(1)}, bf16[3,1,80,512]{3,2,1,0:T(8,128)(2,1)S(1)}, u32[]{:S(2)}, u32[]{:S(2)}) collective-permute-start(bf16[3,1,80,512]{3,2,1,0:T(8,128)(2,1)S(1)} %get-tuple-element.6), channel_id=1, source_target_pairs={{4,0},{8,4},{12,8},{5,1},{9,5},{13,9},{6,2},{10,6},{14,10},{7,3},{... | collective-permute-start | bytes 737288 | tf_op jit(solution)/shard_map/ppermute | solution.py:94
  56.2 12.0 %collective-permute-start.12 = (f32[32]{0:T(128)S(1)}, f32[32]{0:T(128)S(1)}, u32[]{:S(2)}, u32[]{:S(2)}) collective-permute-start(f32[32]{0:T(128)S(1)} %get-tuple-element.29), channel_id=1, source_target_pairs={{0,8},{4,12},{8,0},{12,4},{1,9},{5,13},{9,1},{13,5},{2,10},{6,14},... | collective-permute-start | bytes 392 | tf_op jit(solution)/shard_map/ppermute | solution.py:25
  68.6 49.3 %collective-permute-start.16 = (bf16[4,64,27,128]{3,1,0,2:T(8,128)(2,1)}, bf16[4,64,27,128]{3,1,0,2:T(8,128)(2,1)}, u32[]{:S(2)}, u32[]{:S(2)}) collective-permute-start(bf16[4,64,27,128]{3,1,0,2:T(8,128)(2,1)} %bitcast.44), channel_id=1, source_target_pairs={{0,16},{16,0},{1,17},{17,1},{2,18},{18,2},{3,19},{19,3},{4,20},{20... | collective-permute-start | bytes 5308424 | tf_op jit(solution)/shard_map/ppermute | solution.py:162
  108.1 46.3 %collective-permute-start.32 = (bf16[4,64,27,128]{3,1,0,2:T(8,128)(2,1)}, bf16[4,64,27,128]{3,1,0,2:T(8,128)(2,1)}, u32[]{:S(2)}, u32[]{:S(2)}) collective-permute-start(bf16[4,64,27,128]{3,1,0,2:T(8,128)(2,1)} %bitcast.46), channel_id=1, source_target_pairs={{0,16},{16,0},{1,17},{17,1},{2,18},{18,2},{3,19},{19,3},{4,20},{20... | collective-permute-start | bytes 5308424 | tf_op jit(solution)/shard_map/ppermute | solution.py:162
  145.5 12.2 %collective-permute-start.22 = (f32[8]{0:T(128)S(1)}, f32[8]{0:T(128)S(1)}, u32[]{:S(2)}, u32[]{:S(2)}) collective-permute-start(f32[8]{0:T(128)S(1)} %reduce_sum.72), channel_id=1, source_target_pairs={{0,4},{4,0},{8,12},{12,8},{1,5},{5,1},{9,13},{13,9},{2,6},{6,2},{1... | collective-permute-start | bytes 104 | tf_op jit(solution)/shard_map/ppermute | solution.py:25
  151.1 13.1 %collective-permute-start.19 = (bf16[3,10,80,128]{3,2,1,0:T(8,128)(2,1)}, bf16[3,10,80,128]{3,2,1,0:T(8,128)(2,1)}, u32[]{:S(2)}, u32[]{:S(2)}) collective-permute-start(bf16[3,10,80,128]{3,2,1,0:T(8,128)(2,1)} %get-tuple-element.17), channel_id=1, source_target_pairs={{0,2},{2,0},{1,3},{3,1},{4,6},{6,4},{5,7},{7,5},{8,10},{10,8},{9,1... | collective-permute-start | bytes 1843208 | tf_op jit(solution)/shard_map/ppermute | solution.py:66
  157.6 10.1 %collective-permute-start.23 = (f32[8]{0:T(128)S(1)}, f32[8]{0:T(128)S(1)}, u32[]{:S(2)}, u32[]{:S(2)}) collective-permute-start(f32[8]{0:T(128)S(1)} %get-tuple-element.26), channel_id=1, source_target_pairs={{0,8},{4,12},{8,0},{12,4},{1,9},{5,13},{9,1},{13,5},{2,10},{6,14},... | collective-permute-start | bytes 104 | tf_op jit(solution)/shard_map/ppermute | solution.py:25
  157.8 9.9 %collective-permute-start.25 = (f32[8]{0:T(128)S(1)}, f32[8]{0:T(128)S(1)}, u32[]{:S(2)}, u32[]{:S(2)}) collective-permute-start(f32[8]{0:T(128)S(1)} %get-tuple-element.25), channel_id=1, source_target_pairs={{0,8},{4,12},{8,0},{12,4},{1,9},{5,13},{9,1},{13,5},{2,10},{6,14},... | collective-permute-start | bytes 104 | tf_op jit(solution)/shard_map/ppermute | solution.py:25
  160.1 13.9 %collective-permute-start.20 = (bf16[3,10,80,128]{3,2,1,0:T(8,128)(2,1)}, bf16[3,10,80,128]{3,2,1,0:T(8,128)(2,1)}, u32[]{:S(2)}, u32[]{:S(2)}) collective-permute-start(bf16[3,10,80,128]{3,2,1,0:T(8,128)(2,1)} %get-tuple-element.17), channel_id=1, source_target_pairs={{0,1},{1,0},{2,3},{3,2},{4,5},{5,4},{6,7},{7,6},{8,9},{9,8},{10,11... | collective-permute-start | bytes 1843208 | tf_op jit(solution)/shard_map/ppermute | solution.py:71
  164.2 11.0 %collective-permute-start.21 = (bf16[3,10,80,128]{3,2,1,0:T(8,128)(2,1)}, bf16[3,10,80,128]{3,2,1,0:T(8,128)(2,1)}, u32[]{:S(2)}, u32[]{:S(2)}) collective-permute-start(bf16[3,10,80,128]{3,2,1,0:T(8,128)(2,1)} %collective-permute-done.19), channel_id=1, source_target_pairs={{0,1},{1,0},{2,3},{3,2},{4,5},{5,4},{6,7},{7,6},{8,9},{9,8},{10,11... | collective-permute-start | bytes 1843208 | tf_op jit(solution)/shard_map/ppermute | solution.py:71
  203.1 11.0 %collective-permute-start.34 = (f32[3,2,80,128]{3,2,1,0:T(8,128)S(1)}, f32[3,2,80,128]{3,2,1,0:T(8,128)S(1)}, u32[]{:S(2)}, u32[]{:S(2)}) collective-permute-start(f32[3,2,80,128]{3,2,1,0:T(8,128)S(1)} %get-tuple-element.8), channel_id=1, source_target_pairs={{0,2},{1,3},{2,0},{3,1},{4,6},{5,7},{6,4},{7,5},{8,10},{9,11},{10,... | collective-permute-start | bytes 737288 | tf_op jit(solution)/shard_map/ppermute | solution.py:177
  203.3 11.5 %collective-permute-start.35 = (f32[3,2,80,128]{3,2,1,0:T(8,128)S(1)}, f32[3,2,80,128]{3,2,1,0:T(8,128)S(1)}, u32[]{:S(2)}, u32[]{:S(2)}) collective-permute-start(f32[3,2,80,128]{3,2,1,0:T(8,128)S(1)} %get-tuple-element.7), channel_id=1, source_target_pairs={{0,3},{1,0},{2,1},{3,2},{4,7},{5,4},{6,5},{7,6},{8,11},{9,8},{10,9... | collective-permute-start | bytes 737288 | tf_op jit(solution)/shard_map/ppermute | solution.py:177
  (24 other events, 302.5 us)
Sparse Core Ops, SparseCore 0:
  21.5 44.0 all-gather.4
  67.2 40.8 all-gather.6

commit v4 on v3

--- a/solution.py
+++ b/solution.py
@@ -151,18 +151,27 @@
         source = (me - step) % size
         out = lax.dynamic_update_slice(out, piece, (source * in_block, 0, 0))
     parts = lax.axis_size("groups")
+    share = (in_block * size) // parts
     part = lax.axis_index("groups")
-    rows = lax.axis_size("hz")
-    share = (in_block * size) // parts
     mine = lax.dynamic_slice_in_dim(out, part * share, share, axis=0)
-    gathered = lax.all_gather(mine, "hz", axis=0)
-    result = jnp.zeros((rows, parts, share, taps, width), shard.dtype)
-    result = lax.dynamic_update_slice(result, gathered[:, None], (0, part, 0, 0, 0))
+    return lax.all_gather(mine, "hz", axis=0)
+
+
+def swap_shares(gathered):
+    parts = lax.axis_size("groups")
+    part = lax.axis_index("groups")
+    received = [gathered]
     for step in range(1, parts):
-        other = lax.ppermute(gathered, "groups", shift_pairs(parts, step))
-        source = (part - step) % parts
-        result = lax.dynamic_update_slice(result, other[:, None], (0, source, 0, 0, 0))
-    return jnp.transpose(result.reshape(chans, taps, width), (1, 0, 2))
+        received.append(lax.ppermute(gathered, "groups", shift_pairs(parts, step)))
+    slots = []
+    for slot in range(parts):
+        piece = received[0]
+        for step in range(1, parts):
+            piece = jnp.where((part - step) % parts == slot, received[step], piece)
+        slots.append(piece)
+    rows, share, taps, width = gathered.shape
+    stacked = jnp.stack(slots, axis=1).reshape(rows * parts * share, taps, width)
+    return jnp.transpose(stacked, (1, 0, 2))
 
 
 def scatter_rows(branch, slab_rows, chans):
@@ -197,8 +206,8 @@
     me = lax.axis_index(HQ)
     group_size = chans // GROUPS
 
-    weights_first = kernel_block(kernel_first, chans)
-    weights_second = kernel_block(kernel_second, chans)
+    weights_first = swap_shares(kernel_block(kernel_first, chans))
+    gathered_second = kernel_block(kernel_second, chans)
 
     values = latent.astype(jnp.float32)
     sums, squares, count = local_stats(values, GROUPS)
@@ -209,6 +218,8 @@
     own_bias = lax.dynamic_slice_in_dim(bias_first, me * width, width)
     hidden = causal_conv(edge_mask(act_first), weights_first, own_bias, jnp.bfloat16)
 
+    hidden, gathered_second = lax.optimization_barrier((hidden, gathered_second))
+    weights_second = swap_shares(gathered_second)
     sums, squares, count = local_stats(hidden.astype(jnp.float32), width // group_size)
     raw_next = chip_gather(with_row_halo(hidden, "hz"), 3)
     sums, squares, count = butterfly_stats(sums, squares, count, ("hz",))

time: 226 us -> 240 us (1.062)
  waiting for transfers between devices: 74.5 us -> 92.3 us
  local copies, waits for them, and re-layouts: 39.3 us -> 29.2 us
  other arithmetic: 14.5 us -> 20.3 us
    ppermute x2, waiting for transfers between devices: 0.01 us -> 39.4 us  [swap_shares(): received.append(lax.ppermute(gathered, 'groups', shift_pairs(parts, step)))]
    all_gather x2, waiting for transfers between devices: 33.1 us -> 13.5 us  [kernel_block(): return lax.all_gather(mine, 'hz', axis=0)]
    dynamic_update_slice x4 -> x0, local copies, waits for them, and re-layouts: 9.94 us -> none  [the longest x2 6.64 us: kernel_block(): lax.dynamic_update_slice(result, other[:, None], (0, source, 0, 0, 0))]
    ppermute x12, waiting for transfers between devices: 14.6 us -> 9.7 us  [butterfly_stats(): other_sums, other_squares = lax.ppermute((sums, squares), axis, pairs)]
    another operation x0 -> x4, other arithmetic: none -> 4.59 us  [swap_shares(): jnp.stack(slots, axis=1).reshape(rows * parts * share, taps, width)]
    ppermute x12, starting transfers between devices: 15.1 us -> 10.6 us  [butterfly_stats(): other_sums, other_squares = lax.ppermute((sums, squares), axis, pairs)]
    ppermute x3, starting transfers between devices: 1.93 us -> 5.87 us  [scatter_rows(): piece = lax.ppermute(piece, HQ, shift_pairs(size, step))]
    another operation x5 -> x4, local copies, waits for them, and re-layouts: 5.98 us -> 3.23 us  [the longest x1 2.58 us: swap_shares(): jnp.stack(slots, axis=1).reshape(rows * parts * share, taps, width)]
  transfers between devices with their start and end apart: 38 -> 38, of which waited for: 18 -> 19; matrix products, arithmetic and copies ran while one was open for 18% -> 17% of each run, Pallas kernels for 8% -> 8%
where the time goes in v4:
time: 240 us
  waiting for transfers between devices  92.3 us (38%)
  starting transfers between devices  46.9 us (20%)
  Pallas kernels  37 us (15%)
  local copies, waits for them, and re-layouts  29.2 us (12%)
  other arithmetic  20.3 us (8%)
  between operations  14 us (6%)
    ppermute x2, waiting for transfers between devices, swap_shares(): received.append(lax.ppermute(gathered, 'groups', shift_pairs(parts, step)))  39.4 us
    pallas_call x2, Pallas kernels, causal_conv(): pl.pallas_call(conv_body, grid=(frames,), in_specs=[pl.BlockSpec(padded.s...  37 us
    all_gather x2, waiting for transfers between devices, kernel_block(): return lax.all_gather(mine, 'hz', axis=0)  13.5 us
    ppermute x6, waiting for transfers between devices, kernel_block(): piece = lax.ppermute(piece, HQ, shift_pairs(size, step))  13.2 us
    ppermute x3, waiting for transfers between devices, scatter_rows(): piece = lax.ppermute(piece, HQ, shift_pairs(size, step))  11.4 us
    ppermute x12, starting transfers between devices, butterfly_stats(): other_sums, other_squares = lax.ppermute((sums, squares), axis, pairs)  10.6 us
    ppermute x12, waiting for transfers between devices, butterfly_stats(): other_sums, other_squares = lax.ppermute((sums, squares), axis, pairs)  9.7 us
    ppermute x6, starting transfers between devices, chip_gather(): lax.ppermute(firsts, 'hb', shift_pairs(count_b, step))  9.18 us
  transfers between devices with their start and end apart: 38, of which 19 were waited for; matrix products, arithmetic and copies ran while one was open for 17% of the time, Pallas kernels for 8%

profile of v4, /device:TPU:1, one launch (start us, length us, event | category | flops | bytes accessed | tf_op | source)
XLA Modules:
  0.0 239.6 jit_solution(16517786746391709371)
XLA Ops:
  6.5 2.1 collective-permute-start
  15.2 8.3 %collective-permute-done.13 = bf16[32,27,128]{2,0,1:T(8,128)(2,1)S(1)} collective-permute-done((bf16[32,27,128]{2,0,1:T(8,128)(2,1)S(1)}, bf16[32,27,128]{2,0,1:T(8,128)(2,1)S(1)}, u32[]{:S(2)}, u32[]{:S(2)}) %collective-permute-start.13) | collective-permute-done | bytes 221216 | tf_op jit(solution)/shard_map/ppermute | solution.py:150
  25.0 3.2 %collective-permute-done.14 = bf16[32,27,128]{2,0,1:T(8,128)(2,1)S(1)} collective-permute-done((bf16[32,27,128]{2,0,1:T(8,128)(2,1)S(1)}, bf16[32,27,128]{2,0,1:T(8,128)(2,1)S(1)}, u32[]{:S(2)}, u32[]{:S(2)}) %collective-permute-start.14) | collective-permute-done | bytes 221216 | tf_op jit(solution)/shard_map/ppermute | solution.py:150
  41.4 2.7 %collective-permute-start.12 = (f32[32]{0:T(128)S(1)}, f32[32]{0:T(128)S(1)}, u32[]{:S(2)}, u32[]{:S(2)}) collective-permute-start(f32[32]{0:T(128)S(1)} %get-tuple-element.35), channel_id=1, source_target_pairs={{0,8},{4,12},{8,0},{12,4},{1,9},{5,13},{9,1},{13,5},{2,10},{6,14},... | collective-permute-start | bytes 392 | tf_op jit(solution)/shard_map/ppermute | solution.py:25
  45.5 2.5 %collective-permute-done.8 = f32[32]{0:T(128)S(1)} collective-permute-done((f32[32]{0:T(128)S(1)}, f32[32]{0:T(128)S(1)}, u32[]{:S(2)}, u32[]{:S(2)}) %collective-permute-start.8) | collective-permute-done | bytes 160 | tf_op jit(solution)/shard_map/ppermute | solution.py:25
  48.0 2.7 %collective-permute-start.19 = (bf16[32,27,128]{2,0,1:T(8,128)(2,1)}, bf16[32,27,128]{2,0,1:T(8,128)(2,1)}, u32[]{:S(2)}, u32[]{:S(2)}) collective-permute-start(bf16[32,27,128]{2,0,1:T(8,128)(2,1)} %get-tuple-element.19), channel_id=1, source_target_pairs={{0,3},{1,0},{2,1},{3,2},{4,7},{5,4},{6,5},{7,6},{8,11},{9,8},{10,9... | collective-permute-start | bytes 663560 | tf_op jit(solution)/shard_map/ppermute | solution.py:150
  56.1 2.3 collective-permute-start.3
  61.8 13.5 %all-gather.5.cloned.1.call-done = bf16[256,27,128]{2,0,1:T(8,128)(2,1)} async-done(((bf16[64,27,128]{2,0,1:T(8,128)(2,1)}), bf16[256,27,128]{2,0,1:T(8,128)(2,1)}) %all-gather.5.cloned.1.call-update) | async-done | bytes 1769488 | tf_op jit(solution)/shard_map/all_gather | solution.py:157
  77.4 2.9 %fusion.6 = bf16[3,10,80,512]{3,2,1,0:T(8,128)(2,1)S(1)} fusion(bf16[3,1,80,512]{3,2,1,0:T(8,128)(2,1)} %collective-permute-done.4, bf16[3,8,80,512]{3,2,1,0:T(8,128)(2,1)S(1)} %constant_dynamic-update-slice_fusion.13, bf16[3,1,80,512]{3,2,1,0:T(8,128)(2,1)} %collective-permute-done.3, f32[512]{0:T(512)S(1)} %copy-done.5, f32[512]{0:T(512)S(1)} %copy-done.6, ...), kind=kLoop, calls=%fused_computation.14 | loop fusion | flops 15974400 | bytes 4923402 | tf_op jit(solution)/shard_map/jit(_where)/select_n | solution.py:86
  80.3 3.1 %fusion.5.x_ref = bf16[5,10,82,512]{3,2,1,0:T(8,128)(2,1)} fusion(bf16[3,10,80,512]{3,2,1,0:T(8,128)(2,1)S(1)} %fusion.6, bf16[1,10,80,512]{3,2,1,0:T(8,128)(2,1)S(1)} %slice.36), kind=kLoop, calls=%fused_computation.11 | loop fusion | flops 25190400 | bytes 7475200 | tf_op jit(solution)/shard_map/concatenate | solution.py:116
  83.5 30.9 %collective-permute-done.16 = bf16[4,64,27,128]{3,1,0,2:T(8,128)(2,1)} collective-permute-done((bf16[4,64,27,128]{3,1,0,2:T(8,128)(2,1)}, bf16[4,64,27,128]{3,1,0,2:T(8,128)(2,1)}, u32[]{:S(2)}, u32[]{:S(2)}) %collective-permute-start.16) | collective-permute-done | bytes 1769504 | tf_op jit(solution)/shard_map/ppermute | solution.py:165
  116.7 2.6 %copy.12 = bf16[4,2,64,27,128]{4,2,1,0,3:T(8,128)(2,1)} copy(bf16[4,2,64,27,128]{4,2,0,3,1:T(8,128)(2,1)S(1)} %pad_maximum_fusion) | data formatting | bytes 7077888 | tf_op jit(solution)/shard_map/stack | solution.py:173
  119.3 18.5 %shard_map.91 = bf16[3,8,80,128]{3,2,1,0:T(8,128)(2,1)} custom-call(bf16[5,10,82,512]{3,2,1,0:T(8,128)(2,1)} %fusion.5.x_ref, bf16[27,512,128]{2,1,0:T(8,128)(2,1)} %bitcast.49, f32[1,128]{1,0:T(1,128)} %dynamic-slice_bitcast_fusion.7.b_ref), custom_call_target="tpu_custom_call" | custom-call | flops 6794772480 | bytes 8720384 | tf_op jit(solution)/shard_map/pallas_call | solution.py:124
  138.6 4.3 %collective-permute-start.20 = (bf16[3,1,80,128]{3,2,1,0:T(8,128)(2,1)S(1)}, bf16[3,1,80,128]{3,2,1,0:T(8,128)(2,1)S(1)}, u32[]{:S(2)}, u32[]{:S(2)}) collective-permute-start(bf16[3,1,80,128]{3,2,1,0:T(8,128)(2,1)S(1)} %get-tuple-element.26), channel_id=1, source_target_pairs={{0,4},{4,8},{8,12},{1,5},{5,9},{9,13},{2,6},{6,10},{10,14},{3,7},{... | collective-permute-start | bytes 184328 | tf_op jit(solution)/shard_map/ppermute | solution.py:93
  147.1 2.6 %collective-permute-done.21 = bf16[3,1,80,128]{3,2,1,0:T(8,128)(2,1)S(1)} collective-permute-done((bf16[3,1,80,128]{3,2,1,0:T(8,128)(2,1)S(1)}, bf16[3,1,80,128]{3,2,1,0:T(8,128)(2,1)S(1)}, u32[]{:S(2)}, u32[]{:S(2)}) %collective-permute-start.21) | collective-permute-done | bytes 61472 | tf_op jit(solution)/shard_map/ppermute | solution.py:94
  155.3 2.7 %collective-permute-done.27 = f32[8]{0:T(128)S(1)} collective-permute-done((f32[8]{0:T(128)S(1)}, f32[8]{0:T(128)S(1)}, u32[]{:S(2)}, u32[]{:S(2)}) %collective-permute-start.27) | collective-permute-done | bytes 64 | tf_op jit(solution)/shard_map/ppermute | solution.py:25
  160.4 5.2 %collective-permute-start.23 = (bf16[3,10,80,128]{3,2,1,0:T(8,128)(2,1)S(1)}, bf16[3,10,80,128]{3,2,1,0:T(8,128)(2,1)}, u32[]{:S(2)}, u32[]{:S(2)}) collective-permute-start(bf16[3,10,80,128]{3,2,1,0:T(8,128)(2,1)S(1)} %constant_dynamic-update-slice_fusion.17), channel_id=1, source_target_pairs={{0,1},{1,0},{2,3},{3,2},{4,5},{5,4},{6,7},{7,6},{8,9},{9,8},{10,11... | collective-permute-start | bytes 1843208 | tf_op jit(solution)/shard_map/ppermute | solution.py:71
  177.5 3.1 %select_maximum_fusion.x_ref = bf16[5,10,82,512]{3,2,1,0:T(8,128)(2,1)} fusion(bf16[3,10,80,512]{3,2,1,0:T(8,128)(2,1)S(1)} %fusion.7, bf16[1,10,80,512]{3,2,1,0:T(8,128)(2,1)S(1)} %slice.37), kind=kLoop, calls=%fused_computation.5 | loop fusion | flops 25190400 | bytes 7475200 | tf_op jit(solution)/shard_map/concatenate | solution.py:116
  180.6 8.5 %collective-permute-done.32 = bf16[4,64,27,128]{3,1,0,2:T(8,128)(2,1)S(1)} collective-permute-done((bf16[4,64,27,128]{3,1,0,2:T(8,128)(2,1)}, bf16[4,64,27,128]{3,1,0,2:T(8,128)(2,1)S(1)}, u32[]{:S(2)}, u32[]{:S(2)}) %collective-permute-start.32) | collective-permute-done | bytes 1769504 | tf_op jit(solution)/shard_map/ppermute | solution.py:165
  191.5 18.5 %shard_map.92 = f32[3,8,80,128]{3,2,1,0:T(8,128)} custom-call(bf16[5,10,82,512]{3,2,1,0:T(8,128)(2,1)} %select_maximum_fusion.x_ref, bf16[27,512,128]{2,1,0:T(8,128)(2,1)} %bitcast.48, f32[1,128]{1,0:T(1,128)} %dynamic-slice_bitcast_fusion.6.b_ref), custom_call_target="tpu_custom_call" | custom-call | flops 6794772480 | bytes 8720384 | tf_op jit(solution)/shard_map/pallas_call | solution.py:124
  211.5 4.7 %collective-permute-start.33 = (f32[3,2,80,128]{3,2,1,0:T(8,128)S(1)}, f32[3,2,80,128]{3,2,1,0:T(8,128)S(1)}, u32[]{:S(2)}, u32[]{:S(2)}) collective-permute-start(f32[3,2,80,128]{3,2,1,0:T(8,128)S(1)} %get-tuple-element.17), channel_id=1, source_target_pairs={{0,1},{1,2},{2,3},{3,0},{4,5},{5,6},{6,7},{7,4},{8,9},{9,10},{10,1... | collective-permute-start | bytes 737288 | tf_op jit(solution)/shard_map/ppermute | solution.py:186
  217.4 4.0 %collective-permute-done.33 = f32[3,2,80,128]{3,2,1,0:T(8,128)S(1)} collective-permute-done((f32[3,2,80,128]{3,2,1,0:T(8,128)S(1)}, f32[3,2,80,128]{3,2,1,0:T(8,128)S(1)}, u32[]{:S(2)}, u32[]{:S(2)}) %collective-permute-start.33) | collective-permute-done | bytes 245792 | tf_op jit(solution)/shard_map/ppermute | solution.py:186
  221.4 6.8 %collective-permute-done.34 = f32[3,2,80,128]{3,2,1,0:T(8,128)S(1)} collective-permute-done((f32[3,2,80,128]{3,2,1,0:T(8,128)S(1)}, f32[3,2,80,128]{3,2,1,0:T(8,128)S(1)}, u32[]{:S(2)}, u32[]{:S(2)}) %collective-permute-start.34) | collective-permute-done | bytes 245792 | tf_op jit(solution)/shard_map/ppermute | solution.py:186
  230.6 2.2 reshape.67
  (165 shorter events, 67.6 us)
Async XLA Ops:
  6.5 68.8 %all-gather.5.cloned.1.call-start = ((), (), s32[]{:S(2)}) async-start(), calls=%async_computation | async-start | bytes 2211840 | tf_op jit(solution)/shard_map/all_gather | solution.py:157
  6.5 44.1 %collective-permute-start = (bf16[3,2,80,512]{3,2,1,0:T(8,128)(2,1)}, bf16[3,2,80,512]{3,2,1,0:T(8,128)(2,1)}, u32[]{:S(2)}, u32[]{:S(2)}) collective-permute-start(bf16[3,2,80,512]{3,2,1,0:T(8,128)(2,1)} %param.9), channel_id=1, source_target_pairs={{0,2},{2,0},{1,3},{3,1},{4,6},{6,4},{5,7},{7,5},{8,10},{10,8},{9,1... | collective-permute-start | bytes 1474568 | tf_op jit(solution)/shard_map/ppermute | solution.py:66
  8.7 44.4 %collective-permute-start.1 = (bf16[3,2,80,512]{3,2,1,0:T(8,128)(2,1)}, bf16[3,2,80,512]{3,2,1,0:T(8,128)(2,1)}, u32[]{:S(2)}, u32[]{:S(2)}) collective-permute-start(bf16[3,2,80,512]{3,2,1,0:T(8,128)(2,1)} %param.9), channel_id=1, source_target_pairs={{0,1},{1,0},{2,3},{3,2},{4,5},{5,4},{6,7},{7,6},{8,9},{9,8},{10,11... | collective-permute-start | bytes 1474568 | tf_op jit(solution)/shard_map/ppermute | solution.py:71
  10.9 12.7 %collective-permute-start.13 = (bf16[32,27,128]{2,0,1:T(8,128)(2,1)S(1)}, bf16[32,27,128]{2,0,1:T(8,128)(2,1)S(1)}, u32[]{:S(2)}, u32[]{:S(2)}) collective-permute-start(bf16[32,27,128]{2,0,1:T(8,128)(2,1)S(1)} %get-tuple-element.23), channel_id=1, source_target_pairs={{0,1},{1,2},{2,3},{3,0},{4,5},{5,6},{6,7},{7,4},{8,9},{9,10},{10,1... | collective-permute-start | bytes 663560 | tf_op jit(solution)/shard_map/ppermute | solution.py:150
  10.9 17.3 %collective-permute-start.14 = (bf16[32,27,128]{2,0,1:T(8,128)(2,1)S(1)}, bf16[32,27,128]{2,0,1:T(8,128)(2,1)S(1)}, u32[]{:S(2)}, u32[]{:S(2)}) collective-permute-start(bf16[32,27,128]{2,0,1:T(8,128)(2,1)S(1)} %get-tuple-element.24), channel_id=1, source_target_pairs={{0,2},{1,3},{2,0},{3,1},{4,6},{5,7},{6,4},{7,5},{8,10},{9,11},{10,... | collective-permute-start | bytes 663560 | tf_op jit(solution)/shard_map/ppermute | solution.py:150
  13.6 22.5 %collective-permute-start.5 = (f32[32]{0:T(128)S(1)}, f32[32]{0:T(128)S(1)}, u32[]{:S(2)}, u32[]{:S(2)}) collective-permute-start(f32[32]{0:T(128)S(1)} %reduce_sum.51), channel_id=1, source_target_pairs={{0,2},{2,0},{1,3},{3,1},{4,6},{6,4},{5,7},{7,5},{8,10},{10,8},{9,1... | collective-permute-start | bytes 392 | tf_op jit(solution)/shard_map/ppermute | solution.py:25
  30.7 107.0 %all-gather.7.cloned.1.call-start = ((), (), s32[]{:S(2)}) async-start(), calls=%async_computation.1 | async-start | bytes 2211840 | tf_op jit(solution)/shard_map/all_gather | solution.py:157
  33.6 17.4 %collective-permute-start.17 = (bf16[32,27,128]{2,0,1:T(8,128)(2,1)}, bf16[32,27,128]{2,0,1:T(8,128)(2,1)}, u32[]{:S(2)}, u32[]{:S(2)}) collective-permute-start(bf16[32,27,128]{2,0,1:T(8,128)(2,1)} %get-tuple-element.20), channel_id=1, source_target_pairs={{0,1},{1,2},{2,3},{3,0},{4,5},{5,6},{6,7},{7,4},{8,9},{9,10},{10,1... | collective-permute-start | bytes 663560 | tf_op jit(solution)/shard_map/ppermute | solution.py:150
  45.5 14.3 %collective-permute-start.18 = (bf16[32,27,128]{2,0,1:T(8,128)(2,1)}, bf16[32,27,128]{2,0,1:T(8,128)(2,1)}, u32[]{:S(2)}, u32[]{:S(2)}) collective-permute-start(bf16[32,27,128]{2,0,1:T(8,128)(2,1)} %get-tuple-element.21), channel_id=1, source_target_pairs={{0,2},{1,3},{2,0},{3,1},{4,6},{5,7},{6,4},{7,5},{8,10},{9,11},{10,... | collective-permute-start | bytes 663560 | tf_op jit(solution)/shard_map/ppermute | solution.py:150
  48.0 12.8 %collective-permute-start.19 = (bf16[32,27,128]{2,0,1:T(8,128)(2,1)}, bf16[32,27,128]{2,0,1:T(8,128)(2,1)}, u32[]{:S(2)}, u32[]{:S(2)}) collective-permute-start(bf16[32,27,128]{2,0,1:T(8,128)(2,1)} %get-tuple-element.19), channel_id=1, source_target_pairs={{0,3},{1,0},{2,1},{3,2},{4,7},{5,4},{6,5},{7,6},{8,11},{9,8},{10,9... | collective-permute-start | bytes 663560 | tf_op jit(solution)/shard_map/ppermute | solution.py:150
  56.1 21.3 %collective-permute-start.3 = (bf16[3,1,80,512]{3,2,1,0:T(8,128)(2,1)}, bf16[3,1,80,512]{3,2,1,0:T(8,128)(2,1)}, u32[]{:S(2)}, u32[]{:S(2)}) collective-permute-start(bf16[3,1,80,512]{3,2,1,0:T(8,128)(2,1)} %get-tuple-element.13), channel_id=1, source_target_pairs={{0,4},{4,8},{8,12},{1,5},{5,9},{9,13},{2,6},{6,10},{10,14},{3,7},{... | collective-permute-start | bytes 737288 | tf_op jit(solution)/shard_map/ppermute | solution.py:93
  58.4 19.0 %collective-permute-start.4 = (bf16[3,1,80,512]{3,2,1,0:T(8,128)(2,1)}, bf16[3,1,80,512]{3,2,1,0:T(8,128)(2,1)}, u32[]{:S(2)}, u32[]{:S(2)}) collective-permute-start(bf16[3,1,80,512]{3,2,1,0:T(8,128)(2,1)} %get-tuple-element.14), channel_id=1, source_target_pairs={{4,0},{8,4},{12,8},{5,1},{9,5},{13,9},{6,2},{10,6},{14,10},{7,3},{... | collective-permute-start | bytes 737288 | tf_op jit(solution)/shard_map/ppermute | solution.py:94
  75.3 39.1 %collective-permute-start.16 = (bf16[4,64,27,128]{3,1,0,2:T(8,128)(2,1)}, bf16[4,64,27,128]{3,1,0,2:T(8,128)(2,1)}, u32[]{:S(2)}, u32[]{:S(2)}) collective-permute-start(bf16[4,64,27,128]{3,1,0,2:T(8,128)(2,1)} %bitcast.50), channel_id=1, source_target_pairs={{0,16},{16,0},{1,17},{17,1},{2,18},{18,2},{3,19},{19,3},{4,20},{20... | collective-permute-start | bytes 5308424 | tf_op jit(solution)/shard_map/ppermute | solution.py:165
  138.6 7.4 %collective-permute-start.20 = (bf16[3,1,80,128]{3,2,1,0:T(8,128)(2,1)S(1)}, bf16[3,1,80,128]{3,2,1,0:T(8,128)(2,1)S(1)}, u32[]{:S(2)}, u32[]{:S(2)}) collective-permute-start(bf16[3,1,80,128]{3,2,1,0:T(8,128)(2,1)S(1)} %get-tuple-element.26), channel_id=1, source_target_pairs={{0,4},{4,8},{8,12},{1,5},{5,9},{9,13},{2,6},{6,10},{10,14},{3,7},{... | collective-permute-start | bytes 184328 | tf_op jit(solution)/shard_map/ppermute | solution.py:93
  149.7 16.0 %collective-permute-start.22 = (bf16[3,10,80,128]{3,2,1,0:T(8,128)(2,1)S(1)}, bf16[3,10,80,128]{3,2,1,0:T(8,128)(2,1)S(1)}, u32[]{:S(2)}, u32[]{:S(2)}) collective-permute-start(bf16[3,10,80,128]{3,2,1,0:T(8,128)(2,1)S(1)} %constant_dynamic-update-slice_fusion.17), channel_id=1, source_target_pairs={{0,2},{2,0},{1,3},{3,1},{4,6},{6,4},{5,7},{7,5},{8,10},{10,8},{9,1... | collective-permute-start | bytes 1843208 | tf_op jit(solution)/shard_map/ppermute | solution.py:66
  150.9 7.1 %collective-permute-start.25 = (f32[8]{0:T(128)S(1)}, f32[8]{0:T(128)S(1)}, u32[]{:S(2)}, u32[]{:S(2)}) collective-permute-start(f32[8]{0:T(128)S(1)} %reduce_sum.72), channel_id=1, source_target_pairs={{0,4},{4,0},{8,12},{12,8},{1,5},{5,1},{9,13},{13,9},{2,6},{6,2},{1... | collective-permute-start | bytes 104 | tf_op jit(solution)/shard_map/ppermute | solution.py:25
  152.4 36.8 %collective-permute-start.32 = (bf16[4,64,27,128]{3,1,0,2:T(8,128)(2,1)}, bf16[4,64,27,128]{3,1,0,2:T(8,128)(2,1)S(1)}, u32[]{:S(2)}, u32[]{:S(2)}) collective-permute-start(bf16[4,64,27,128]{3,1,0,2:T(8,128)(2,1)} %bitcast.52), channel_id=1, source_target_pairs={{0,16},{16,0},{1,17},{17,1},{2,18},{18,2},{3,19},{19,3},{4,20},{20... | collective-permute-start | bytes 5308424 | tf_op jit(solution)/shard_map/ppermute | solution.py:165
  158.0 7.7 %collective-permute-start.26 = (f32[8]{0:T(128)S(1)}, f32[8]{0:T(128)S(1)}, u32[]{:S(2)}, u32[]{:S(2)}) collective-permute-start(f32[8]{0:T(128)S(1)} %get-tuple-element.32), channel_id=1, source_target_pairs={{0,8},{4,12},{8,0},{12,4},{1,9},{5,13},{9,1},{13,5},{2,10},{6,14},... | collective-permute-start | bytes 104 | tf_op jit(solution)/shard_map/ppermute | solution.py:25
  158.4 7.2 %collective-permute-start.28 = (f32[8]{0:T(128)S(1)}, f32[8]{0:T(128)S(1)}, u32[]{:S(2)}, u32[]{:S(2)}) collective-permute-start(f32[8]{0:T(128)S(1)} %get-tuple-element.31), channel_id=1, source_target_pairs={{0,8},{4,12},{8,0},{12,4},{1,9},{5,13},{9,1},{13,5},{2,10},{6,14},... | collective-permute-start | bytes 104 | tf_op jit(solution)/shard_map/ppermute | solution.py:25
  160.4 12.6 %collective-permute-start.23 = (bf16[3,10,80,128]{3,2,1,0:T(8,128)(2,1)S(1)}, bf16[3,10,80,128]{3,2,1,0:T(8,128)(2,1)}, u32[]{:S(2)}, u32[]{:S(2)}) collective-permute-start(bf16[3,10,80,128]{3,2,1,0:T(8,128)(2,1)S(1)} %constant_dynamic-update-slice_fusion.17), channel_id=1, source_target_pairs={{0,1},{1,0},{2,3},{3,2},{4,5},{5,4},{6,7},{7,6},{8,9},{9,8},{10,11... | collective-permute-start | bytes 1843208 | tf_op jit(solution)/shard_map/ppermute | solution.py:71
  165.7 8.6 %collective-permute-start.24 = (bf16[3,10,80,128]{3,2,1,0:T(8,128)(2,1)S(1)}, bf16[3,10,80,128]{3,2,1,0:T(8,128)(2,1)}, u32[]{:S(2)}, u32[]{:S(2)}) collective-permute-start(bf16[3,10,80,128]{3,2,1,0:T(8,128)(2,1)S(1)} %collective-permute-done.22), channel_id=1, source_target_pairs={{0,1},{1,0},{2,3},{3,2},{4,5},{5,4},{6,7},{7,6},{8,9},{9,8},{10,11... | collective-permute-start | bytes 1843208 | tf_op jit(solution)/shard_map/ppermute | solution.py:71
  211.5 9.9 %collective-permute-start.33 = (f32[3,2,80,128]{3,2,1,0:T(8,128)S(1)}, f32[3,2,80,128]{3,2,1,0:T(8,128)S(1)}, u32[]{:S(2)}, u32[]{:S(2)}) collective-permute-start(f32[3,2,80,128]{3,2,1,0:T(8,128)S(1)} %get-tuple-element.17), channel_id=1, source_target_pairs={{0,1},{1,2},{2,3},{3,0},{4,5},{5,6},{6,7},{7,4},{8,9},{9,10},{10,1... | collective-permute-start | bytes 737288 | tf_op jit(solution)/shard_map/ppermute | solution.py:186
  216.2 12.0 %collective-permute-start.34 = (f32[3,2,80,128]{3,2,1,0:T(8,128)S(1)}, f32[3,2,80,128]{3,2,1,0:T(8,128)S(1)}, u32[]{:S(2)}, u32[]{:S(2)}) collective-permute-start(f32[3,2,80,128]{3,2,1,0:T(8,128)S(1)} %get-tuple-element.16), channel_id=1, source_target_pairs={{0,2},{1,3},{2,0},{3,1},{4,6},{5,7},{6,4},{7,5},{8,10},{9,11},{10,... | collective-permute-start | bytes 737288 | tf_op jit(solution)/shard_map/ppermute | solution.py:186
  217.4 11.5 %collective-permute-start.35 = (f32[3,2,80,128]{3,2,1,0:T(8,128)S(1)}, f32[3,2,80,128]{3,2,1,0:T(8,128)S(1)}, u32[]{:S(2)}, u32[]{:S(2)}) collective-permute-start(f32[3,2,80,128]{3,2,1,0:T(8,128)S(1)} %get-tuple-element.15), channel_id=1, source_target_pairs={{0,3},{1,0},{2,1},{3,2},{4,7},{5,4},{6,5},{7,6},{8,11},{9,8},{10,9... | collective-permute-start | bytes 737288 | tf_op jit(solution)/shard_map/ppermute | solution.py:186
  (23 other events, 258.1 us)
Sparse Core Ops, SparseCore 0:
  30.9 44.3 all-gather.4
  77.4 40.7 all-gather.6

commit v5 on v1

--- a/solution.py
+++ b/solution.py
@@ -149,7 +149,14 @@
             piece = lax.ppermute(piece, HQ, shift_pairs(size, step))
         source = (me - step) % size
         out = lax.dynamic_update_slice(out, piece, (0, source * in_block, 0))
-    return lax.all_gather(out, "hz", axis=1, tiled=True)
+    parts = lax.axis_size("groups")
+    part = lax.axis_index("groups")
+    rows = lax.axis_size("hz")
+    share = (in_block * size) // parts
+    mine = lax.dynamic_slice_in_dim(out, part * share, share, axis=1)
+    gathered = lax.all_gather(mine, ("groups", "hz"), axis=1, tiled=True)
+    ordered = gathered.reshape(taps, parts, rows, share, width)
+    return jnp.transpose(ordered, (0, 2, 1, 3, 4)).reshape(taps, chans, width)
 
 
 def scatter_rows(branch, slab_rows, chans):
@@ -205,9 +212,10 @@
     own_bias_next = lax.dynamic_slice_in_dim(bias_second, me * width, width)
     branch = causal_conv(edge_mask(act_second), weights_second, own_bias_next, jnp.float32)
 
-    branch_rows = scatter_rows(branch, slab_rows, chans)
-    summed = (values + branch_rows).astype(jnp.bfloat16)
-    return jnp.repeat(jnp.repeat(summed, 2, axis=1), 2, axis=2)
+    own_latent = lax.dynamic_slice_in_dim(raw_rows[:, 1:-1], me * width, width, axis=3)
+    summed = (own_latent.astype(jnp.float32) + branch).astype(jnp.bfloat16)
+    summed_rows = scatter_rows(summed, slab_rows, chans)
+    return jnp.repeat(jnp.repeat(summed_rows, 2, axis=1), 2, axis=2)
 
 
 def solution(mesh):

time: 215 us -> 226 us (1.051)
  waiting for transfers between devices: 76.3 us -> 88.2 us
  starting transfers between devices: 45.7 us -> 37.9 us
  local copies, waits for them, and re-layouts: 27.1 us -> 32.7 us
    ppermute x2, waiting for transfers between devices: 12.7 us -> 2.22 us  [with_row_halo(): bottom = lax.ppermute(cells[:, :1], axis_name, up)]
    ppermute x6, waiting for transfers between devices: 8.4 us -> 18.4 us  [kernel_block(): piece = lax.ppermute(piece, HQ, shift_pairs(size, step))]
    transpose x0 -> x2, local copies, waits for them, and re-layouts: none -> 9.95 us  [kernel_block(): return jnp.transpose(ordered, (0, 2, 1, 3, 4)).reshape(taps, chans, width)]
    ppermute x3, waiting for transfers between devices: 0.15 us -> 8.1 us  [chip_gather(): firsts.append(lax.ppermute(block, 'ha', shift_pairs(count_a, step)))]
    all_gather x2, waiting for transfers between devices: 26.8 us -> 34.2 us  [kernel_block(): gathered = lax.all_gather(mine, ('groups', 'hz'), axis=1, tiled=True)]
    ppermute x3, waiting for transfers between devices: 11.2 us -> 5.99 us  [scatter_rows(): piece = lax.ppermute(piece, HQ, shift_pairs(size, step))]
    dynamic_update_slice x6, local copies, waits for them, and re-layouts: 3.94 us -> 1.11 us  [kernel_block(): out = lax.dynamic_update_slice(out, piece, (0, source * in_block, 0))]
    ppermute x2, starting transfers between devices: 8.88 us -> 6.21 us  [with_row_halo(): top = lax.ppermute(cells[:, -1:], axis_name, down)]
  transfers between devices with their start and end apart: 36 -> 36, of which waited for: 21 -> 17; matrix products, arithmetic and copies ran while one was open for 15% -> 15% of each run, Pallas kernels for 9% -> 8%
where the time goes in v5:
time: 226 us
  waiting for transfers between devices  88.2 us (39%)
  starting transfers between devices  37.9 us (17%)
  Pallas kernels  37 us (16%)
  local copies, waits for them, and re-layouts  32.7 us (14%)
  other arithmetic  16.1 us (7%)
  between operations  13.9 us (6%)
    pallas_call x2, Pallas kernels, causal_conv(): pl.pallas_call(conv_body, grid=(frames,), in_specs=[pl.BlockSpec(padded.s...  37 us
    all_gather x2, waiting for transfers between devices, kernel_block(): gathered = lax.all_gather(mine, ('groups', 'hz'), axis=1, tiled=True)  34.2 us
    ppermute x12, waiting for transfers between devices, butterfly_stats(): other_sums, other_squares = lax.ppermute((sums, squares), axis, pairs)  18.7 us
    ppermute x6, waiting for transfers between devices, kernel_block(): piece = lax.ppermute(piece, HQ, shift_pairs(size, step))  18.4 us
    ppermute x12, starting transfers between devices, butterfly_stats(): other_sums, other_squares = lax.ppermute((sums, squares), axis, pairs)  11.2 us
    transpose x2, local copies, waits for them, and re-layouts, kernel_block(): return jnp.transpose(ordered, (0, 2, 1, 3, 4)).reshape(taps, chans, width)  9.95 us
    ppermute x3, waiting for transfers between devices, chip_gather(): firsts.append(lax.ppermute(block, 'ha', shift_pairs(count_a, step)))  8.1 us
    dynamic_update_slice x11, local copies, waits for them, and re-layouts, chip_gather(): out = lax.dynamic_update_slice(out, piece, start)  7.84 us
  transfers between devices with their start and end apart: 36, of which 17 were waited for; matrix products, arithmetic and copies ran while one was open for 15% of the time, Pallas kernels for 8%

profile of v5, /device:TPU:1, one launch (start us, length us, event | category | flops | bytes accessed | tf_op | source)
XLA Modules:
  0.0 225.8 jit_solution(673220010288857584)
XLA Ops:
  8.2 2.7 %collective-permute-start.13 = (bf16[27,32,128]{2,1,0:T(8,128)(2,1)S(1)}, bf16[27,32,128]{2,1,0:T(8,128)(2,1)}, u32[]{:S(2)}, u32[]{:S(2)}) collective-permute-start(bf16[27,32,128]{2,1,0:T(8,128)(2,1)S(1)} %get-tuple-element.12), channel_id=1, source_target_pairs={{0,1},{1,2},{2,3},{3,0},{4,5},{5,6},{6,7},{7,4},{8,9},{9,10},{10,1... | collective-permute-start | bytes 663560 | tf_op jit(solution)/shard_map/ppermute | solution.py:149
  11.4 4.2 %collective-permute-done.13 = bf16[27,32,128]{2,1,0:T(8,128)(2,1)} collective-permute-done((bf16[27,32,128]{2,1,0:T(8,128)(2,1)S(1)}, bf16[27,32,128]{2,1,0:T(8,128)(2,1)}, u32[]{:S(2)}, u32[]{:S(2)}) %collective-permute-start.13) | collective-permute-done | bytes 221216 | tf_op jit(solution)/shard_map/ppermute | solution.py:149
  16.5 3.8 %collective-permute-done.14 = bf16[27,32,128]{2,1,0:T(8,128)(2,1)S(1)} collective-permute-done((bf16[27,32,128]{2,1,0:T(8,128)(2,1)S(1)}, bf16[27,32,128]{2,1,0:T(8,128)(2,1)S(1)}, u32[]{:S(2)}, u32[]{:S(2)}) %collective-permute-start.14) | collective-permute-done | bytes 221216 | tf_op jit(solution)/shard_map/ppermute | solution.py:149
  22.2 2.1 collective-permute-start.29
  25.1 8.9 %collective-permute-done.29 = bf16[27,32,128]{2,1,0:T(8,128)(2,1)S(1)} collective-permute-done((bf16[27,32,128]{2,1,0:T(8,128)(2,1)S(1)}, bf16[27,32,128]{2,1,0:T(8,128)(2,1)S(1)}, u32[]{:S(2)}, u32[]{:S(2)}) %collective-permute-start.29) | collective-permute-done | bytes 221216 | tf_op jit(solution)/shard_map/ppermute | solution.py:149
  39.5 8.1 %collective-permute-done = bf16[3,2,80,512]{3,2,1,0:T(8,128)(2,1)S(1)} collective-permute-done((bf16[3,2,80,512]{3,2,1,0:T(8,128)(2,1)S(1)}, bf16[3,2,80,512]{3,2,1,0:T(8,128)(2,1)S(1)}, u32[]{:S(2)}, u32[]{:S(2)}) %collective-permute-start) | collective-permute-done | bytes 491552 | tf_op jit(solution)/shard_map/ppermute | solution.py:66
  52.7 3.3 %collective-permute-start.3 = (bf16[3,1,80,512]{3,2,1,0:T(8,128)(2,1)S(1)}, bf16[3,1,80,512]{3,2,1,0:T(8,128)(2,1)S(1)}, u32[]{:S(2)}, u32[]{:S(2)}) collective-permute-start(bf16[3,1,80,512]{3,2,1,0:T(8,128)(2,1)S(1)} %get-tuple-element.5), channel_id=1, source_target_pairs={{0,4},{4,8},{8,12},{1,5},{5,9},{9,13},{2,6},{6,10},{10,14},{3,7},{... | collective-permute-start | bytes 737288 | tf_op jit(solution)/shard_map/ppermute | solution.py:93
  57.3 2.9 %collective-permute-start.12 = (f32[32]{0:T(128)S(1)}, f32[32]{0:T(128)S(1)}, u32[]{:S(2)}, u32[]{:S(2)}) collective-permute-start(f32[32]{0:T(128)S(1)} %get-tuple-element.31), channel_id=1, source_target_pairs={{0,8},{4,12},{8,0},{12,4},{1,9},{5,13},{9,1},{13,5},{2,10},{6,14},... | collective-permute-start | bytes 392 | tf_op jit(solution)/shard_map/ppermute | solution.py:25
  60.3 17.0 %collective-permute-done.12 = f32[32]{0:T(128)S(1)} collective-permute-done((f32[32]{0:T(128)S(1)}, f32[32]{0:T(128)S(1)}, u32[]{:S(2)}, u32[]{:S(2)}) %collective-permute-start.12) | collective-permute-done | bytes 160 | tf_op jit(solution)/shard_map/ppermute | solution.py:25
  79.6 3.1 %fusion.5.x_ref = bf16[5,10,82,512]{3,2,1,0:T(8,128)(2,1)} fusion(bf16[3,10,80,512]{3,2,1,0:T(8,128)(2,1)S(1)} %fusion.6, bf16[1,10,80,512]{3,2,1,0:T(8,128)(2,1)S(1)} %slice.36), kind=kLoop, calls=%fused_computation.11 | loop fusion | flops 25190400 | bytes 7475200 | tf_op jit(solution)/shard_map/concatenate | solution.py:116
  82.8 7.8 %all-gather.3.cloned.1.call-done = bf16[27,512,128]{2,1,0:T(8,128)(2,1)} async-done(((bf16[27,64,128]{2,1,0:T(8,128)(2,1)}), bf16[27,512,128]{2,1,0:T(8,128)(2,1)}) %all-gather.3.cloned.1.call-update) | async-done | bytes 3538960 | tf_op jit(solution)/shard_map/all_gather | solution.py:157
  90.6 5.0 %copy.10 = bf16[27,4,2,64,128]{4,3,2,1,0:T(8,128)(2,1)} copy(bf16[27,4,2,64,128]{4,3,1,2,0:T(8,128)(2,1)} %bitcast.23) | data formatting | bytes 7077888 | tf_op jit(solution)/shard_map/transpose | solution.py:159
  95.5 18.5 %shard_map.91 = bf16[3,8,80,128]{3,2,1,0:T(8,128)(2,1)} custom-call(bf16[5,10,82,512]{3,2,1,0:T(8,128)(2,1)} %fusion.5.x_ref, bf16[27,512,128]{2,1,0:T(8,128)(2,1)} %bitcast.25, f32[1,128]{1,0:T(1,128)} %dynamic-slice_bitcast_fusion.1.b_ref), custom_call_target="tpu_custom_call" | custom-call | flops 6794772480 | bytes 8720384 | tf_op jit(solution)/shard_map/pallas_call | solution.py:124
  114.9 2.9 %collective-permute-start.16 = (bf16[3,1,80,128]{3,2,1,0:T(8,128)(2,1)S(1)}, bf16[3,1,80,128]{3,2,1,0:T(8,128)(2,1)S(1)}, u32[]{:S(2)}, u32[]{:S(2)}) collective-permute-start(bf16[3,1,80,128]{3,2,1,0:T(8,128)(2,1)S(1)} %get-tuple-element.21), channel_id=1, source_target_pairs={{0,4},{4,8},{8,12},{1,5},{5,9},{9,13},{2,6},{6,10},{10,14},{3,7},{... | collective-permute-start | bytes 184328 | tf_op jit(solution)/shard_map/ppermute | solution.py:93
  120.6 2.2 collective-permute-done.17
  130.5 26.4 %all-gather.5.cloned.1.call-done = bf16[27,512,128]{2,1,0:T(8,128)(2,1)} async-done(((bf16[27,64,128]{2,1,0:T(8,128)(2,1)}), bf16[27,512,128]{2,1,0:T(8,128)(2,1)}) %all-gather.5.cloned.1.call-update) | async-done | bytes 3538960 | tf_op jit(solution)/shard_map/all_gather | solution.py:157
  157.0 5.0 %copy.11 = bf16[27,4,2,64,128]{4,3,2,1,0:T(8,128)(2,1)} copy(bf16[27,4,2,64,128]{4,3,1,2,0:T(8,128)(2,1)} %bitcast.22) | data formatting | bytes 7077888 | tf_op jit(solution)/shard_map/transpose | solution.py:159
  164.4 2.2 collective-permute-start.19
  168.4 3.1 %collective-permute-start.26 = (f32[2,8]{1,0:T(2,128)S(1)}, f32[2,8]{1,0:T(2,128)S(1)}, u32[]{:S(2)}, u32[]{:S(2)}) collective-permute-start(f32[2,8]{1,0:T(2,128)S(1)} %pad_maximum_fusion.1), channel_id=1, source_target_pairs={{0,1},{1,0},{2,3},{3,2},{4,5},{5,4},{6,7},{7,6},{8,9},{9,8},{10,11... | collective-permute-start | bytes 200 | tf_op jit(solution)/shard_map/ppermute | solution.py:71
  180.9 3.2 %fusion.7 = bf16[3,10,80,512]{3,2,1,0:T(8,128)(2,1)S(1)} fusion(bf16[3,10,80,512]{3,2,1,0:T(8,128)(2,1)} %constant_dynamic-update-slice_fusion.6, f32[512]{0:T(512)S(1)} %copy-done.6, f32[512]{0:T(512)S(1)} %copy-done.7, f32[512]{0:T(512)S(1)} %mul.226, f32[512]{0:T(512)S(1)} %sub.111, pred[10]{0:T(512)(128)(4,1)S(1)} %or_and_fusion), kind=kLoop, calls=%fused_computation.13 | loop fusion | flops 13516800 | bytes 4923402 | tf_op jit(solution)/shard_map/jit(_where)/select_n | solution.py:86
  184.1 3.1 %select_maximum_fusion.x_ref = bf16[5,10,82,512]{3,2,1,0:T(8,128)(2,1)} fusion(bf16[3,10,80,512]{3,2,1,0:T(8,128)(2,1)S(1)} %fusion.7, bf16[1,10,80,512]{3,2,1,0:T(8,128)(2,1)S(1)} %slice.39), kind=kLoop, calls=%fused_computation.5 | loop fusion | flops 25190400 | bytes 7475200 | tf_op jit(solution)/shard_map/concatenate | solution.py:116
  187.2 18.5 %shard_map.92 = f32[3,8,80,128]{3,2,1,0:T(8,128)} custom-call(bf16[5,10,82,512]{3,2,1,0:T(8,128)(2,1)} %select_maximum_fusion.x_ref, bf16[27,512,128]{2,1,0:T(8,128)(2,1)} %bitcast.24, f32[1,128]{1,0:T(1,128)} %dynamic-slice_bitcast_fusion.b_ref), custom_call_target="tpu_custom_call" | custom-call | flops 6794772480 | bytes 8720384 | tf_op jit(solution)/shard_map/pallas_call | solution.py:124
  211.2 3.2 %collective-permute-done.32 = bf16[3,2,80,128]{3,2,1,0:T(8,128)(2,1)S(1)} collective-permute-done((bf16[3,2,80,128]{3,2,1,0:T(8,128)(2,1)S(1)}, bf16[3,2,80,128]{3,2,1,0:T(8,128)(2,1)S(1)}, u32[]{:S(2)}, u32[]{:S(2)}) %collective-permute-start.32) | collective-permute-done | bytes 122912 | tf_op jit(solution)/shard_map/ppermute | solution.py:171
  216.7 2.2 reshape.75
  (151 shorter events, 52.5 us)
Async XLA Ops:
  6.5 84.0 %all-gather.3.cloned.1.call-start = ((), (), s32[]{:S(2)}) async-start(), calls=%async_computation | async-start | bytes 3981312 | tf_op jit(solution)/shard_map/all_gather | solution.py:157
  8.2 7.3 %collective-permute-start.13 = (bf16[27,32,128]{2,1,0:T(8,128)(2,1)S(1)}, bf16[27,32,128]{2,1,0:T(8,128)(2,1)}, u32[]{:S(2)}, u32[]{:S(2)}) collective-permute-start(bf16[27,32,128]{2,1,0:T(8,128)(2,1)S(1)} %get-tuple-element.12), channel_id=1, source_target_pairs={{0,1},{1,2},{2,3},{3,0},{4,5},{5,6},{6,7},{7,4},{8,9},{9,10},{10,1... | collective-permute-start | bytes 663560 | tf_op jit(solution)/shard_map/ppermute | solution.py:149
  10.9 9.4 %collective-permute-start.14 = (bf16[27,32,128]{2,1,0:T(8,128)(2,1)S(1)}, bf16[27,32,128]{2,1,0:T(8,128)(2,1)S(1)}, u32[]{:S(2)}, u32[]{:S(2)}) collective-permute-start(bf16[27,32,128]{2,1,0:T(8,128)(2,1)S(1)} %get-tuple-element.14), channel_id=1, source_target_pairs={{0,2},{1,3},{2,0},{3,1},{4,6},{5,7},{6,4},{7,5},{8,10},{9,11},{10,... | collective-permute-start | bytes 663560 | tf_op jit(solution)/shard_map/ppermute | solution.py:149
  10.9 9.9 %collective-permute-start.15 = (bf16[27,32,128]{2,1,0:T(8,128)(2,1)S(1)}, bf16[27,32,128]{2,1,0:T(8,128)(2,1)S(1)}, u32[]{:S(2)}, u32[]{:S(2)}) collective-permute-start(bf16[27,32,128]{2,1,0:T(8,128)(2,1)S(1)} %get-tuple-element.11), channel_id=1, source_target_pairs={{0,3},{1,0},{2,1},{3,2},{4,7},{5,4},{6,5},{7,6},{8,11},{9,8},{10,9... | collective-permute-start | bytes 663560 | tf_op jit(solution)/shard_map/ppermute | solution.py:149
  21.7 135.3 %all-gather.5.cloned.1.call-start = ((), (), s32[]{:S(2)}) async-start(), calls=%async_computation.1 | async-start | bytes 3981312 | tf_op jit(solution)/shard_map/all_gather | solution.py:157
  22.2 11.8 %collective-permute-start.29 = (bf16[27,32,128]{2,1,0:T(8,128)(2,1)S(1)}, bf16[27,32,128]{2,1,0:T(8,128)(2,1)S(1)}, u32[]{:S(2)}, u32[]{:S(2)}) collective-permute-start(bf16[27,32,128]{2,1,0:T(8,128)(2,1)S(1)} %get-tuple-element.10), channel_id=1, source_target_pairs={{0,2},{1,3},{2,0},{3,1},{4,6},{5,7},{6,4},{7,5},{8,10},{9,11},{10,... | collective-permute-start | bytes 663560 | tf_op jit(solution)/shard_map/ppermute | solution.py:149
  24.3 10.8 %collective-permute-start.30 = (bf16[27,32,128]{2,1,0:T(8,128)(2,1)S(1)}, bf16[27,32,128]{2,1,0:T(8,128)(2,1)S(1)}, u32[]{:S(2)}, u32[]{:S(2)}) collective-permute-start(bf16[27,32,128]{2,1,0:T(8,128)(2,1)S(1)} %get-tuple-element.7), channel_id=1, source_target_pairs={{0,3},{1,0},{2,1},{3,2},{4,7},{5,4},{6,5},{7,6},{8,11},{9,8},{10,9... | collective-permute-start | bytes 663560 | tf_op jit(solution)/shard_map/ppermute | solution.py:149
  35.9 11.7 %collective-permute-start = (bf16[3,2,80,512]{3,2,1,0:T(8,128)(2,1)S(1)}, bf16[3,2,80,512]{3,2,1,0:T(8,128)(2,1)S(1)}, u32[]{:S(2)}, u32[]{:S(2)}) collective-permute-start(bf16[3,2,80,512]{3,2,1,0:T(8,128)(2,1)S(1)} %copy-done.2), channel_id=1, source_target_pairs={{0,2},{2,0},{1,3},{3,1},{4,6},{6,4},{5,7},{7,5},{8,10},{10,8},{9,1... | collective-permute-start | bytes 1474568 | tf_op jit(solution)/shard_map/ppermute | solution.py:66
  36.0 15.5 %collective-permute-start.1 = (bf16[3,2,80,512]{3,2,1,0:T(8,128)(2,1)S(1)}, bf16[3,2,80,512]{3,2,1,0:T(8,128)(2,1)S(1)}, u32[]{:S(2)}, u32[]{:S(2)}) collective-permute-start(bf16[3,2,80,512]{3,2,1,0:T(8,128)(2,1)S(1)} %copy-done.2), channel_id=1, source_target_pairs={{0,1},{1,0},{2,3},{3,2},{4,5},{5,4},{6,7},{7,6},{8,9},{9,8},{10,11... | collective-permute-start | bytes 1474568 | tf_op jit(solution)/shard_map/ppermute | solution.py:71
  36.4 11.2 %collective-permute-start.5 = (f32[32]{0:T(128)S(1)}, f32[32]{0:T(128)S(1)}, u32[]{:S(2)}, u32[]{:S(2)}) collective-permute-start(f32[32]{0:T(128)S(1)} %reduce_sum.51), channel_id=1, source_target_pairs={{0,2},{2,0},{1,3},{3,1},{4,6},{6,4},{5,7},{7,5},{8,10},{10,8},{9,1... | collective-permute-start | bytes 392 | tf_op jit(solution)/shard_map/ppermute | solution.py:25
  38.4 9.3 %collective-permute-start.9 = (f32[32]{0:T(128)S(1)}, f32[32]{0:T(128)S(1)}, u32[]{:S(2)}, u32[]{:S(2)}) collective-permute-start(f32[32]{0:T(128)S(1)} %reduce_sum.54), channel_id=1, source_target_pairs={{0,2},{2,0},{1,3},{3,1},{4,6},{6,4},{5,7},{7,5},{8,10},{10,8},{9,1... | collective-permute-start | bytes 392 | tf_op jit(solution)/shard_map/ppermute | solution.py:25
  49.5 7.8 %collective-permute-start.11 = (f32[32]{0:T(128)S(1)}, f32[32]{0:T(128)S(1)}, u32[]{:S(2)}, u32[]{:S(2)}) collective-permute-start(f32[32]{0:T(128)S(1)} %get-tuple-element.33), channel_id=1, source_target_pairs={{0,4},{4,0},{8,12},{12,8},{1,5},{5,1},{9,13},{13,9},{2,6},{6,2},{1... | collective-permute-start | bytes 392 | tf_op jit(solution)/shard_map/ppermute | solution.py:25
  51.3 5.9 %collective-permute-start.7 = (f32[32]{0:T(128)S(1)}, f32[32]{0:T(128)S(1)}, u32[]{:S(2)}, u32[]{:S(2)}) collective-permute-start(f32[32]{0:T(128)S(1)} %get-tuple-element.34), channel_id=1, source_target_pairs={{0,4},{4,0},{8,12},{12,8},{1,5},{5,1},{9,13},{13,9},{2,6},{6,2},{1... | collective-permute-start | bytes 392 | tf_op jit(solution)/shard_map/ppermute | solution.py:25
  52.7 25.0 %collective-permute-start.3 = (bf16[3,1,80,512]{3,2,1,0:T(8,128)(2,1)S(1)}, bf16[3,1,80,512]{3,2,1,0:T(8,128)(2,1)S(1)}, u32[]{:S(2)}, u32[]{:S(2)}) collective-permute-start(bf16[3,1,80,512]{3,2,1,0:T(8,128)(2,1)S(1)} %get-tuple-element.5), channel_id=1, source_target_pairs={{0,4},{4,8},{8,12},{1,5},{5,9},{9,13},{2,6},{6,10},{10,14},{3,7},{... | collective-permute-start | bytes 737288 | tf_op jit(solution)/shard_map/ppermute | solution.py:93
  56.0 21.7 %collective-permute-start.4 = (bf16[3,1,80,512]{3,2,1,0:T(8,128)(2,1)S(1)}, bf16[3,1,80,512]{3,2,1,0:T(8,128)(2,1)S(1)}, u32[]{:S(2)}, u32[]{:S(2)}) collective-permute-start(bf16[3,1,80,512]{3,2,1,0:T(8,128)(2,1)S(1)} %get-tuple-element.6), channel_id=1, source_target_pairs={{4,0},{8,4},{12,8},{5,1},{9,5},{13,9},{6,2},{10,6},{14,10},{7,3},{... | collective-permute-start | bytes 737288 | tf_op jit(solution)/shard_map/ppermute | solution.py:94
  57.3 20.0 %collective-permute-start.12 = (f32[32]{0:T(128)S(1)}, f32[32]{0:T(128)S(1)}, u32[]{:S(2)}, u32[]{:S(2)}) collective-permute-start(f32[32]{0:T(128)S(1)} %get-tuple-element.31), channel_id=1, source_target_pairs={{0,8},{4,12},{8,0},{12,4},{1,9},{5,13},{9,1},{13,5},{2,10},{6,14},... | collective-permute-start | bytes 392 | tf_op jit(solution)/shard_map/ppermute | solution.py:25
  60.2 17.1 %collective-permute-start.8 = (f32[32]{0:T(128)S(1)}, f32[32]{0:T(128)S(1)}, u32[]{:S(2)}, u32[]{:S(2)}) collective-permute-start(f32[32]{0:T(128)S(1)} %get-tuple-element.32), channel_id=1, source_target_pairs={{0,8},{4,12},{8,0},{12,4},{1,9},{5,13},{9,1},{13,5},{2,10},{6,14},... | collective-permute-start | bytes 392 | tf_op jit(solution)/shard_map/ppermute | solution.py:25
  126.6 40.0 %collective-permute-start.18 = (bf16[3,10,80,128]{3,2,1,0:T(8,128)(2,1)S(1)}, bf16[3,10,80,128]{3,2,1,0:T(8,128)(2,1)}, u32[]{:S(2)}, u32[]{:S(2)}) collective-permute-start(bf16[3,10,80,128]{3,2,1,0:T(8,128)(2,1)S(1)} %get-tuple-element.15), channel_id=1, source_target_pairs={{0,2},{2,0},{1,3},{3,1},{4,6},{6,4},{5,7},{7,5},{8,10},{10,8},{9,1... | collective-permute-start | bytes 1843208 | tf_op jit(solution)/shard_map/ppermute | solution.py:66
  128.3 33.7 %collective-permute-start.21 = (f32[8]{0:T(128)S(1)}, f32[8]{0:T(128)S(1)}, u32[]{:S(2)}, u32[]{:S(2)}) collective-permute-start(f32[8]{0:T(128)S(1)} %reduce_sum.72), channel_id=1, source_target_pairs={{0,4},{4,0},{8,12},{12,8},{1,5},{5,1},{9,13},{13,9},{2,6},{6,2},{1... | collective-permute-start | bytes 104 | tf_op jit(solution)/shard_map/ppermute | solution.py:25
  130.4 31.5 %collective-permute-start.23 = (f32[8]{0:T(128)S(1)}, f32[8]{0:T(128)S(1)}, u32[]{:S(2)}, u32[]{:S(2)}) collective-permute-start(f32[8]{0:T(128)S(1)} %reduce_sum.75), channel_id=1, source_target_pairs={{0,4},{4,0},{8,12},{12,8},{1,5},{5,1},{9,13},{13,9},{2,6},{6,2},{1... | collective-permute-start | bytes 104 | tf_op jit(solution)/shard_map/ppermute | solution.py:25
  164.4 12.5 %collective-permute-start.19 = (bf16[3,10,80,128]{3,2,1,0:T(8,128)(2,1)S(1)}, bf16[3,10,80,128]{3,2,1,0:T(8,128)(2,1)}, u32[]{:S(2)}, u32[]{:S(2)}) collective-permute-start(bf16[3,10,80,128]{3,2,1,0:T(8,128)(2,1)S(1)} %get-tuple-element.15), channel_id=1, source_target_pairs={{0,1},{1,0},{2,3},{3,2},{4,5},{5,4},{6,7},{7,6},{8,9},{9,8},{10,11... | collective-permute-start | bytes 1843208 | tf_op jit(solution)/shard_map/ppermute | solution.py:71
  166.6 12.3 %collective-permute-start.20 = (bf16[3,10,80,128]{3,2,1,0:T(8,128)(2,1)}, bf16[3,10,80,128]{3,2,1,0:T(8,128)(2,1)}, u32[]{:S(2)}, u32[]{:S(2)}) collective-permute-start(bf16[3,10,80,128]{3,2,1,0:T(8,128)(2,1)} %collective-permute-done.18), channel_id=1, source_target_pairs={{0,1},{1,0},{2,3},{3,2},{4,5},{5,4},{6,7},{7,6},{8,9},{9,8},{10,11... | collective-permute-start | bytes 1843208 | tf_op jit(solution)/shard_map/ppermute | solution.py:71
  208.6 5.8 %collective-permute-start.32 = (bf16[3,2,80,128]{3,2,1,0:T(8,128)(2,1)S(1)}, bf16[3,2,80,128]{3,2,1,0:T(8,128)(2,1)S(1)}, u32[]{:S(2)}, u32[]{:S(2)}) collective-permute-start(bf16[3,2,80,128]{3,2,1,0:T(8,128)(2,1)S(1)} %get-tuple-element.18), channel_id=1, source_target_pairs={{0,2},{1,3},{2,0},{3,1},{4,6},{5,7},{6,4},{7,5},{8,10},{9,11},{10,... | collective-permute-start | bytes 368648 | tf_op jit(solution)/shard_map/ppermute | solution.py:171
  208.9 6.2 %collective-permute-start.33 = (bf16[3,2,80,128]{3,2,1,0:T(8,128)(2,1)S(1)}, bf16[3,2,80,128]{3,2,1,0:T(8,128)(2,1)S(1)}, u32[]{:S(2)}, u32[]{:S(2)}) collective-permute-start(bf16[3,2,80,128]{3,2,1,0:T(8,128)(2,1)S(1)} %get-tuple-element.17), channel_id=1, source_target_pairs={{0,3},{1,0},{2,1},{3,2},{4,7},{5,4},{6,5},{7,6},{8,11},{9,8},{10,9... | collective-permute-start | bytes 368648 | tf_op jit(solution)/shard_map/ppermute | solution.py:171
  (20 other events, 266.7 us)
Sparse Core Ops, SparseCore 0:
  21.8 68.7 all-gather.2
  92.7 64.2 all-gather.4

commit v6 on v1

--- a/solution.py
+++ b/solution.py
@@ -138,17 +138,11 @@
 
 def kernel_block(shard, chans):
     size = lax.axis_size("ha") * lax.axis_size("hb")
-    me = lax.axis_index(HQ)
     taps, in_block, outs = shard.shape
     width = outs // size
-    out = jnp.zeros((taps, in_block * size, width), shard.dtype)
-    for step in range(size):
-        target = (me + step) % size
-        piece = lax.dynamic_slice_in_dim(shard, target * width, width, axis=2)
-        if step:
-            piece = lax.ppermute(piece, HQ, shift_pairs(size, step))
-        source = (me - step) % size
-        out = lax.dynamic_update_slice(out, piece, (0, source * in_block, 0))
+    pieces = jnp.transpose(shard.reshape(taps, in_block, size, width), (2, 0, 1, 3))
+    pieces = lax.all_to_all(pieces, HQ, 0, 0, tiled=True)
+    out = jnp.transpose(pieces, (1, 0, 2, 3)).reshape(taps, size * in_block, width)
     return lax.all_gather(out, "hz", axis=1, tiled=True)
 
 
@@ -205,9 +199,10 @@
     own_bias_next = lax.dynamic_slice_in_dim(bias_second, me * width, width)
     branch = causal_conv(edge_mask(act_second), weights_second, own_bias_next, jnp.float32)
 
-    branch_rows = scatter_rows(branch, slab_rows, chans)
-    summed = (values + branch_rows).astype(jnp.bfloat16)
-    return jnp.repeat(jnp.repeat(summed, 2, axis=1), 2, axis=2)
+    own_latent = lax.dynamic_slice_in_dim(raw_rows[:, 1:-1], me * width, width, axis=3)
+    summed = (own_latent.astype(jnp.float32) + branch).astype(jnp.bfloat16)
+    summed_rows = scatter_rows(summed, slab_rows, chans)
+    return jnp.repeat(jnp.repeat(summed_rows, 2, axis=1), 2, axis=2)
 
 
 def solution(mesh):

time: 215 us -> 212 us (0.986)
  blocking collectives: 0 us -> 15.9 us
  waiting for transfers between devices: 76.3 us -> 64.9 us
  starting transfers between devices: 45.7 us -> 38 us
    all_to_all x0 -> x1, blocking collectives: none -> 15.9 us  [kernel_block(): pieces = lax.all_to_all(pieces, HQ, 0, 0, tiled=True)]
    ppermute x6 -> x0, waiting for transfers between devices: 8.4 us -> none  [kernel_block(): piece = lax.ppermute(piece, HQ, shift_pairs(size, step))]
    ppermute x6 -> x0, starting transfers between devices: 6.48 us -> none  [kernel_block(): piece = lax.ppermute(piece, HQ, shift_pairs(size, step))]
    ppermute x3, waiting for transfers between devices: 0.15 us -> 6.26 us  [chip_gather(): firsts.append(lax.ppermute(block, 'ha', shift_pairs(count_a, step)))]
    ppermute x2, waiting for transfers between devices: 12.7 us -> 7.38 us  [with_row_halo(): bottom = lax.ppermute(cells[:, :1], axis_name, up)]
    ppermute x3, waiting for transfers between devices: 11.2 us -> 5.98 us  [scatter_rows(): piece = lax.ppermute(piece, HQ, shift_pairs(size, step))]
    ppermute x2, starting transfers between devices: 8.88 us -> 4.49 us  [with_row_halo(): top = lax.ppermute(cells[:, -1:], axis_name, down)]
    all_to_all x0 -> x1, starting transfers between devices: none -> 4.06 us  [kernel_block(): pieces = lax.all_to_all(pieces, HQ, 0, 0, tiled=True)]
  transfers between devices with their start and end apart: 36 -> 31, of which waited for: 21 -> 14; matrix products, arithmetic and copies ran while one was open for 15% -> 16% of each run, Pallas kernels for 9% -> 9%
where the time goes in v6:
time: 212 us
  waiting for transfers between devices  64.9 us (31%)
  starting transfers between devices  38 us (18%)
  Pallas kernels  37 us (17%)
  local copies, waits for them, and re-layouts  26.3 us (12%)
  other arithmetic  16.1 us (8%)
  blocking collectives  15.9 us (8%)
  between operations  13.7 us (6%)
    pallas_call x2, Pallas kernels, causal_conv(): pl.pallas_call(conv_body, grid=(frames,), in_specs=[pl.BlockSpec(padded.s...  37 us
    all_gather x2, waiting for transfers between devices, kernel_block(): return lax.all_gather(out, 'hz', axis=1, tiled=True)  26.4 us
    ppermute x12, waiting for transfers between devices, butterfly_stats(): other_sums, other_squares = lax.ppermute((sums, squares), axis, pairs)  18.4 us
    all_to_all x1, blocking collectives, kernel_block(): pieces = lax.all_to_all(pieces, HQ, 0, 0, tiled=True)  15.9 us
    ppermute x12, starting transfers between devices, butterfly_stats(): other_sums, other_squares = lax.ppermute((sums, squares), axis, pairs)  10.9 us
    ppermute x6, starting transfers between devices, chip_gather(): lax.ppermute(firsts, 'hb', shift_pairs(count_b, step))  10.4 us
    dynamic_update_slice x11, local copies, waits for them, and re-layouts, chip_gather(): out = lax.dynamic_update_slice(out, piece, start)  9.93 us
    ppermute x2, waiting for transfers between devices, with_row_halo(): bottom = lax.ppermute(cells[:, :1], axis_name, up)  7.38 us
  transfers between devices with their start and end apart: 31, of which 14 were waited for; matrix products, arithmetic and copies ran while one was open for 16% of the time, Pallas kernels for 9%

profile of v6, /device:TPU:1, one launch (start us, length us, event | category | flops | bytes accessed | tf_op | source)
XLA Modules:
  0.0 211.8 jit_solution(11225724475127308306)
XLA Ops:
  8.6 15.9 %all_to_all.10 = bf16[4,27,32,128]{3,2,1,0:T(8,128)(2,1)S(1)} all-to-all(bf16[4,27,32,128]{3,2,1,0:T(8,128)(2,1)S(1)} %copy.16), channel_id=1, replica_groups=mesh['groups'=2,'hz'=4,'ha'=2,'hb'=2] {'ha','hb'}, dimensions={0} | all-to-all | bytes 1769472 | tf_op jit(solution)/shard_map/all_to_all | solution.py:144
  30.7 4.1 %all-to-all-start.1 = ((bf16[4,27,32,128]{3,2,1,0:T(8,128)(2,1)}), bf16[4,27,32,128]{3,2,1,0:T(8,128)(2,1)S(1)}, u32[]{:S(2)}, u32[]{:S(2)}) async-start(bf16[4,27,32,128]{3,2,1,0:T(8,128)(2,1)} %copy.18), calls=%async_computation.1 | async-start | bytes 1769472 | tf_op jit(solution)/shard_map/all_to_all | solution.py:144
  37.5 3.1 %collective-permute-start.2 = (bf16[3,2,80,512]{3,2,1,0:T(8,128)(2,1)}, bf16[3,2,80,512]{3,2,1,0:T(8,128)(2,1)}, u32[]{:S(2)}, u32[]{:S(2)}) collective-permute-start(bf16[3,2,80,512]{3,2,1,0:T(8,128)(2,1)} %collective-permute-done), channel_id=1, source_target_pairs={{0,1},{1,0},{2,3},{3,2},{4,5},{5,4},{6,7},{7,6},{8,9},{9,8},{10,11... | collective-permute-start | bytes 1474568 | tf_op jit(solution)/shard_map/ppermute | solution.py:71
  47.8 3.2 %collective-permute-start.3 = (bf16[3,1,80,512]{3,2,1,0:T(8,128)(2,1)}, bf16[3,1,80,512]{3,2,1,0:T(8,128)(2,1)S(1)}, u32[]{:S(2)}, u32[]{:S(2)}) collective-permute-start(bf16[3,1,80,512]{3,2,1,0:T(8,128)(2,1)} %get-tuple-element.5), channel_id=1, source_target_pairs={{0,4},{4,8},{8,12},{1,5},{5,9},{9,13},{2,6},{6,10},{10,14},{3,7},{... | collective-permute-start | bytes 737288 | tf_op jit(solution)/shard_map/ppermute | solution.py:93
  52.3 3.1 %collective-permute-start.12 = (f32[32]{0:T(128)S(1)}, f32[32]{0:T(128)S(1)}, u32[]{:S(2)}, u32[]{:S(2)}) collective-permute-start(f32[32]{0:T(128)S(1)} %get-tuple-element.23), channel_id=1, source_target_pairs={{0,8},{4,12},{8,0},{12,4},{1,9},{5,13},{9,1},{13,5},{2,10},{6,14},... | collective-permute-start | bytes 392 | tf_op jit(solution)/shard_map/ppermute | solution.py:25
  55.5 16.1 %collective-permute-done.12 = f32[32]{0:T(128)S(1)} collective-permute-done((f32[32]{0:T(128)S(1)}, f32[32]{0:T(128)S(1)}, u32[]{:S(2)}, u32[]{:S(2)}) %collective-permute-start.12) | collective-permute-done | bytes 160 | tf_op jit(solution)/shard_map/ppermute | solution.py:25
  75.2 3.1 %fusion.5.x_ref = bf16[5,10,82,512]{3,2,1,0:T(8,128)(2,1)} fusion(bf16[3,10,80,512]{3,2,1,0:T(8,128)(2,1)S(1)} %fusion.6, bf16[1,10,80,512]{3,2,1,0:T(8,128)(2,1)S(1)} %slice.36), kind=kLoop, calls=%fused_computation.11 | loop fusion | flops 25190400 | bytes 7475200 | tf_op jit(solution)/shard_map/concatenate | solution.py:116
  78.3 23.1 %all-gather.3.cloned.1.call-done.w_ref = bf16[27,512,128]{2,1,0:T(8,128)(2,1)} async-done(((bf16[27,128,128]{2,1,0:T(8,128)(2,1)}), bf16[27,512,128]{2,1,0:T(8,128)(2,1)}) %all-gather.3.cloned.1.call-update) | async-done | bytes 3538960 | tf_op jit(solution)/shard_map/all_gather | solution.py:146
  101.4 18.5 %shard_map.91 = bf16[3,8,80,128]{3,2,1,0:T(8,128)(2,1)} custom-call(bf16[5,10,82,512]{3,2,1,0:T(8,128)(2,1)} %fusion.5.x_ref, bf16[27,512,128]{2,1,0:T(8,128)(2,1)} %all-gather.3.cloned.1.call-done.w_ref, f32[1,128]{1,0:T(1,128)} %dynamic-slice_bitcast_fusion.1.b_ref), custom_call_target="tpu_custom_call" | custom-call | flops 6794772480 | bytes 8720384 | tf_op jit(solution)/shard_map/pallas_call | solution.py:124
  124.9 7.2 %collective-permute-done.14 = bf16[3,1,80,128]{3,2,1,0:T(8,128)(2,1)S(1)} collective-permute-done((bf16[3,1,80,128]{3,2,1,0:T(8,128)(2,1)S(1)}, bf16[3,1,80,128]{3,2,1,0:T(8,128)(2,1)S(1)}, u32[]{:S(2)}, u32[]{:S(2)}) %collective-permute-start.14) | collective-permute-done | bytes 61472 | tf_op jit(solution)/shard_map/ppermute | solution.py:94
  133.9 2.0 pad_maximum_fusion
  141.3 2.4 %collective-permute-start.21 = (f32[8]{0:T(128)S(1)}, f32[8]{0:T(128)S(1)}, u32[]{:S(2)}, u32[]{:S(2)}) collective-permute-start(f32[8]{0:T(128)S(1)} %get-tuple-element.19), channel_id=1, source_target_pairs={{0,8},{4,12},{8,0},{12,4},{1,9},{5,13},{9,1},{13,5},{2,10},{6,14},... | collective-permute-start | bytes 104 | tf_op jit(solution)/shard_map/ppermute | solution.py:25
  143.6 4.3 %collective-permute-start.16 = (bf16[3,10,80,128]{3,2,1,0:T(8,128)(2,1)S(1)}, bf16[3,10,80,128]{3,2,1,0:T(8,128)(2,1)}, u32[]{:S(2)}, u32[]{:S(2)}) collective-permute-start(bf16[3,10,80,128]{3,2,1,0:T(8,128)(2,1)S(1)} %get-tuple-element.7), channel_id=1, source_target_pairs={{0,1},{1,0},{2,3},{3,2},{4,5},{5,4},{6,7},{7,6},{8,9},{9,8},{10,11... | collective-permute-start | bytes 1843208 | tf_op jit(solution)/shard_map/ppermute | solution.py:71
  147.9 3.3 %collective-permute-done.15 = bf16[3,10,80,128]{3,2,1,0:T(8,128)(2,1)} collective-permute-done((bf16[3,10,80,128]{3,2,1,0:T(8,128)(2,1)S(1)}, bf16[3,10,80,128]{3,2,1,0:T(8,128)(2,1)}, u32[]{:S(2)}, u32[]{:S(2)}) %collective-permute-start.15) | collective-permute-done | bytes 614432 | tf_op jit(solution)/shard_map/ppermute | solution.py:66
  157.3 2.0 constant_dynamic-update-slice_fusion.5
  159.3 2.0 constant_dynamic-update-slice_fusion.4
  161.3 2.0 constant_dynamic-update-slice_fusion.3
  163.2 3.2 %fusion.7 = bf16[3,10,80,512]{3,2,1,0:T(8,128)(2,1)S(1)} fusion(bf16[3,10,80,512]{3,2,1,0:T(8,128)(2,1)} %constant_dynamic-update-slice_fusion.3, f32[512]{0:T(512)S(1)} %copy-done.6, f32[512]{0:T(512)S(1)} %copy-done.7, f32[512]{0:T(512)S(1)} %mul.181, f32[512]{0:T(512)S(1)} %sub.102, pred[10]{0:T(512)(128)(4,1)S(1)} %or_and_fusion), kind=kLoop, calls=%fused_computation.13 | loop fusion | flops 13516800 | bytes 4923402 | tf_op jit(solution)/shard_map/jit(_where)/select_n | solution.py:86
  166.5 3.1 %select_maximum_fusion.x_ref = bf16[5,10,82,512]{3,2,1,0:T(8,128)(2,1)} fusion(bf16[3,10,80,512]{3,2,1,0:T(8,128)(2,1)S(1)} %fusion.7, bf16[1,10,80,512]{3,2,1,0:T(8,128)(2,1)S(1)} %slice.39), kind=kLoop, calls=%fused_computation.5 | loop fusion | flops 25190400 | bytes 7475200 | tf_op jit(solution)/shard_map/concatenate | solution.py:116
  169.6 3.3 %all-gather.5.cloned.1.call-done.w_ref = bf16[27,512,128]{2,1,0:T(8,128)(2,1)} async-done(((bf16[27,128,128]{2,1,0:T(8,128)(2,1)}), bf16[27,512,128]{2,1,0:T(8,128)(2,1)}) %all-gather.5.cloned.1.call-update) | async-done | bytes 3538960 | tf_op jit(solution)/shard_map/all_gather | solution.py:146
  172.9 18.5 %shard_map.92 = f32[3,8,80,128]{3,2,1,0:T(8,128)} custom-call(bf16[5,10,82,512]{3,2,1,0:T(8,128)(2,1)} %select_maximum_fusion.x_ref, bf16[27,512,128]{2,1,0:T(8,128)(2,1)} %all-gather.5.cloned.1.call-done.w_ref, f32[1,128]{1,0:T(1,128)} %dynamic-slice_bitcast_fusion.b_ref), custom_call_target="tpu_custom_call" | custom-call | flops 6794772480 | bytes 8720384 | tf_op jit(solution)/shard_map/pallas_call | solution.py:124
  195.1 2.1 collective-permute-done.25
  197.2 3.3 %collective-permute-done.26 = bf16[3,2,80,128]{3,2,1,0:T(8,128)(2,1)S(1)} collective-permute-done((bf16[3,2,80,128]{3,2,1,0:T(8,128)(2,1)S(1)}, bf16[3,2,80,128]{3,2,1,0:T(8,128)(2,1)S(1)}, u32[]{:S(2)}, u32[]{:S(2)}) %collective-permute-start.26) | collective-permute-done | bytes 122912 | tf_op jit(solution)/shard_map/ppermute | solution.py:158
  202.7 2.2 %reshape.75 = bf16[3,4,160,512]{3,2,1,0:T(8,128)(2,1)} reshape(bf16[3,4,80,2,512]{4,3,2,1,0:T(2,128)(2,1)S(1)} %broadcast_in_dim.53) | data formatting | bytes 3932160 | tf_op jit(solution)/shard_map/reshape | solution.py:205
  (134 shorter events, 47.0 us)
Async XLA Ops:
  6.5 94.9 %all-gather.3.cloned.1.call-start = ((), (), s32[]{:S(2)}) async-start(), calls=%async_computation.2 | async-start | bytes 4423680 | tf_op jit(solution)/shard_map/all_gather | solution.py:146
  25.6 11.9 %collective-permute-start = (bf16[3,2,80,512]{3,2,1,0:T(8,128)(2,1)S(1)}, bf16[3,2,80,512]{3,2,1,0:T(8,128)(2,1)}, u32[]{:S(2)}, u32[]{:S(2)}) collective-permute-start(bf16[3,2,80,512]{3,2,1,0:T(8,128)(2,1)S(1)} %copy-done.2), channel_id=1, source_target_pairs={{0,2},{2,0},{1,3},{3,1},{4,6},{6,4},{5,7},{7,5},{8,10},{10,8},{9,1... | collective-permute-start | bytes 1474568 | tf_op jit(solution)/shard_map/ppermute | solution.py:66
  26.1 18.7 %collective-permute-start.1 = (bf16[3,2,80,512]{3,2,1,0:T(8,128)(2,1)S(1)}, bf16[3,2,80,512]{3,2,1,0:T(8,128)(2,1)}, u32[]{:S(2)}, u32[]{:S(2)}) collective-permute-start(bf16[3,2,80,512]{3,2,1,0:T(8,128)(2,1)S(1)} %copy-done.2), channel_id=1, source_target_pairs={{0,1},{1,0},{2,3},{3,2},{4,5},{5,4},{6,7},{7,6},{8,9},{9,8},{10,11... | collective-permute-start | bytes 1474568 | tf_op jit(solution)/shard_map/ppermute | solution.py:71
  27.2 13.4 %collective-permute-start.5 = (f32[32]{0:T(128)S(1)}, f32[32]{0:T(128)S(1)}, u32[]{:S(2)}, u32[]{:S(2)}) collective-permute-start(f32[32]{0:T(128)S(1)} %reduce_sum.51), channel_id=1, source_target_pairs={{0,2},{2,0},{1,3},{3,1},{4,6},{6,4},{5,7},{7,5},{8,10},{10,8},{9,1... | collective-permute-start | bytes 392 | tf_op jit(solution)/shard_map/ppermute | solution.py:25
  29.2 11.4 %collective-permute-start.9 = (f32[32]{0:T(128)S(1)}, f32[32]{0:T(128)S(1)}, u32[]{:S(2)}, u32[]{:S(2)}) collective-permute-start(f32[32]{0:T(128)S(1)} %reduce_sum.54), channel_id=1, source_target_pairs={{0,2},{2,0},{1,3},{3,1},{4,6},{6,4},{5,7},{7,5},{8,10},{10,8},{9,1... | collective-permute-start | bytes 392 | tf_op jit(solution)/shard_map/ppermute | solution.py:25
  30.7 41.3 %all-to-all-start.1 = ((bf16[4,27,32,128]{3,2,1,0:T(8,128)(2,1)}), bf16[4,27,32,128]{3,2,1,0:T(8,128)(2,1)S(1)}, u32[]{:S(2)}, u32[]{:S(2)}) async-start(bf16[4,27,32,128]{3,2,1,0:T(8,128)(2,1)} %copy.18), calls=%async_computation.1 | async-start | bytes 1769472 | tf_op jit(solution)/shard_map/all_to_all | solution.py:144
  34.7 138.2 %all-gather.5.cloned.1.call-start = ((), (), s32[]{:S(2)}) async-start(), calls=%async_computation.3 | async-start | bytes 4423680 | tf_op jit(solution)/shard_map/all_gather | solution.py:146
  37.5 8.3 %collective-permute-start.2 = (bf16[3,2,80,512]{3,2,1,0:T(8,128)(2,1)}, bf16[3,2,80,512]{3,2,1,0:T(8,128)(2,1)}, u32[]{:S(2)}, u32[]{:S(2)}) collective-permute-start(bf16[3,2,80,512]{3,2,1,0:T(8,128)(2,1)} %collective-permute-done), channel_id=1, source_target_pairs={{0,1},{1,0},{2,3},{3,2},{4,5},{5,4},{6,7},{7,6},{8,9},{9,8},{10,11... | collective-permute-start | bytes 1474568 | tf_op jit(solution)/shard_map/ppermute | solution.py:71
  42.1 10.1 %collective-permute-start.11 = (f32[32]{0:T(128)S(1)}, f32[32]{0:T(128)S(1)}, u32[]{:S(2)}, u32[]{:S(2)}) collective-permute-start(f32[32]{0:T(128)S(1)} %get-tuple-element.25), channel_id=1, source_target_pairs={{0,4},{4,0},{8,12},{12,8},{1,5},{5,1},{9,13},{13,9},{2,6},{6,2},{1... | collective-permute-start | bytes 392 | tf_op jit(solution)/shard_map/ppermute | solution.py:25
  43.5 8.8 %collective-permute-start.7 = (f32[32]{0:T(128)S(1)}, f32[32]{0:T(128)S(1)}, u32[]{:S(2)}, u32[]{:S(2)}) collective-permute-start(f32[32]{0:T(128)S(1)} %get-tuple-element.26), channel_id=1, source_target_pairs={{0,4},{4,0},{8,12},{12,8},{1,5},{5,1},{9,13},{13,9},{2,6},{6,2},{1... | collective-permute-start | bytes 392 | tf_op jit(solution)/shard_map/ppermute | solution.py:25
  47.8 25.3 %collective-permute-start.3 = (bf16[3,1,80,512]{3,2,1,0:T(8,128)(2,1)}, bf16[3,1,80,512]{3,2,1,0:T(8,128)(2,1)S(1)}, u32[]{:S(2)}, u32[]{:S(2)}) collective-permute-start(bf16[3,1,80,512]{3,2,1,0:T(8,128)(2,1)} %get-tuple-element.5), channel_id=1, source_target_pairs={{0,4},{4,8},{8,12},{1,5},{5,9},{9,13},{2,6},{6,10},{10,14},{3,7},{... | collective-permute-start | bytes 737288 | tf_op jit(solution)/shard_map/ppermute | solution.py:93
  51.0 22.2 %collective-permute-start.4 = (bf16[3,1,80,512]{3,2,1,0:T(8,128)(2,1)}, bf16[3,1,80,512]{3,2,1,0:T(8,128)(2,1)S(1)}, u32[]{:S(2)}, u32[]{:S(2)}) collective-permute-start(bf16[3,1,80,512]{3,2,1,0:T(8,128)(2,1)} %get-tuple-element.6), channel_id=1, source_target_pairs={{4,0},{8,4},{12,8},{5,1},{9,5},{13,9},{6,2},{10,6},{14,10},{7,3},{... | collective-permute-start | bytes 737288 | tf_op jit(solution)/shard_map/ppermute | solution.py:94
  52.3 19.3 %collective-permute-start.12 = (f32[32]{0:T(128)S(1)}, f32[32]{0:T(128)S(1)}, u32[]{:S(2)}, u32[]{:S(2)}) collective-permute-start(f32[32]{0:T(128)S(1)} %get-tuple-element.23), channel_id=1, source_target_pairs={{0,8},{4,12},{8,0},{12,4},{1,9},{5,13},{9,1},{13,5},{2,10},{6,14},... | collective-permute-start | bytes 392 | tf_op jit(solution)/shard_map/ppermute | solution.py:25
  55.5 16.2 %collective-permute-start.8 = (f32[32]{0:T(128)S(1)}, f32[32]{0:T(128)S(1)}, u32[]{:S(2)}, u32[]{:S(2)}) collective-permute-start(f32[32]{0:T(128)S(1)} %get-tuple-element.24), channel_id=1, source_target_pairs={{0,8},{4,12},{8,0},{12,4},{1,9},{5,13},{9,1},{13,5},{2,10},{6,14},... | collective-permute-start | bytes 392 | tf_op jit(solution)/shard_map/ppermute | solution.py:25
  120.8 4.1 %collective-permute-start.13 = (bf16[3,1,80,128]{3,2,1,0:T(8,128)(2,1)S(1)}, bf16[3,1,80,128]{3,2,1,0:T(8,128)(2,1)S(1)}, u32[]{:S(2)}, u32[]{:S(2)}) collective-permute-start(bf16[3,1,80,128]{3,2,1,0:T(8,128)(2,1)S(1)} %get-tuple-element.13), channel_id=1, source_target_pairs={{0,4},{4,8},{8,12},{1,5},{5,9},{9,13},{2,6},{6,10},{10,14},{3,7},{... | collective-permute-start | bytes 184328 | tf_op jit(solution)/shard_map/ppermute | solution.py:93
  122.1 10.0 %collective-permute-start.14 = (bf16[3,1,80,128]{3,2,1,0:T(8,128)(2,1)S(1)}, bf16[3,1,80,128]{3,2,1,0:T(8,128)(2,1)S(1)}, u32[]{:S(2)}, u32[]{:S(2)}) collective-permute-start(bf16[3,1,80,128]{3,2,1,0:T(8,128)(2,1)S(1)} %get-tuple-element.14), channel_id=1, source_target_pairs={{4,0},{8,4},{12,8},{5,1},{9,5},{13,9},{6,2},{10,6},{14,10},{7,3},{... | collective-permute-start | bytes 184328 | tf_op jit(solution)/shard_map/ppermute | solution.py:94
  135.9 15.3 %collective-permute-start.15 = (bf16[3,10,80,128]{3,2,1,0:T(8,128)(2,1)S(1)}, bf16[3,10,80,128]{3,2,1,0:T(8,128)(2,1)}, u32[]{:S(2)}, u32[]{:S(2)}) collective-permute-start(bf16[3,10,80,128]{3,2,1,0:T(8,128)(2,1)S(1)} %get-tuple-element.7), channel_id=1, source_target_pairs={{0,2},{2,0},{1,3},{3,1},{4,6},{6,4},{5,7},{7,5},{8,10},{10,8},{9,1... | collective-permute-start | bytes 1843208 | tf_op jit(solution)/shard_map/ppermute | solution.py:66
  141.2 11.1 %collective-permute-start.19 = (f32[8]{0:T(128)S(1)}, f32[8]{0:T(128)S(1)}, u32[]{:S(2)}, u32[]{:S(2)}) collective-permute-start(f32[8]{0:T(128)S(1)} %get-tuple-element.20), channel_id=1, source_target_pairs={{0,8},{4,12},{8,0},{12,4},{1,9},{5,13},{9,1},{13,5},{2,10},{6,14},... | collective-permute-start | bytes 104 | tf_op jit(solution)/shard_map/ppermute | solution.py:25
  141.3 11.0 %collective-permute-start.21 = (f32[8]{0:T(128)S(1)}, f32[8]{0:T(128)S(1)}, u32[]{:S(2)}, u32[]{:S(2)}) collective-permute-start(f32[8]{0:T(128)S(1)} %get-tuple-element.19), channel_id=1, source_target_pairs={{0,8},{4,12},{8,0},{12,4},{1,9},{5,13},{9,1},{13,5},{2,10},{6,14},... | collective-permute-start | bytes 104 | tf_op jit(solution)/shard_map/ppermute | solution.py:25
  143.6 15.7 %collective-permute-start.16 = (bf16[3,10,80,128]{3,2,1,0:T(8,128)(2,1)S(1)}, bf16[3,10,80,128]{3,2,1,0:T(8,128)(2,1)}, u32[]{:S(2)}, u32[]{:S(2)}) collective-permute-start(bf16[3,10,80,128]{3,2,1,0:T(8,128)(2,1)S(1)} %get-tuple-element.7), channel_id=1, source_target_pairs={{0,1},{1,0},{2,3},{3,2},{4,5},{5,4},{6,7},{7,6},{8,9},{9,8},{10,11... | collective-permute-start | bytes 1843208 | tf_op jit(solution)/shard_map/ppermute | solution.py:71
  151.2 10.1 %collective-permute-start.17 = (bf16[3,10,80,128]{3,2,1,0:T(8,128)(2,1)}, bf16[3,10,80,128]{3,2,1,0:T(8,128)(2,1)}, u32[]{:S(2)}, u32[]{:S(2)}) collective-permute-start(bf16[3,10,80,128]{3,2,1,0:T(8,128)(2,1)} %collective-permute-done.15), channel_id=1, source_target_pairs={{0,1},{1,0},{2,3},{3,2},{4,5},{5,4},{6,7},{7,6},{8,9},{9,8},{10,11... | collective-permute-start | bytes 1843208 | tf_op jit(solution)/shard_map/ppermute | solution.py:71
  192.9 4.3 %collective-permute-start.25 = (bf16[3,2,80,128]{3,2,1,0:T(8,128)(2,1)S(1)}, bf16[3,2,80,128]{3,2,1,0:T(8,128)(2,1)S(1)}, u32[]{:S(2)}, u32[]{:S(2)}) collective-permute-start(bf16[3,2,80,128]{3,2,1,0:T(8,128)(2,1)S(1)} %get-tuple-element.11), channel_id=1, source_target_pairs={{0,1},{1,2},{2,3},{3,0},{4,5},{5,6},{6,7},{7,4},{8,9},{9,10},{10,1... | collective-permute-start | bytes 368648 | tf_op jit(solution)/shard_map/ppermute | solution.py:158
  194.7 5.9 %collective-permute-start.26 = (bf16[3,2,80,128]{3,2,1,0:T(8,128)(2,1)S(1)}, bf16[3,2,80,128]{3,2,1,0:T(8,128)(2,1)S(1)}, u32[]{:S(2)}, u32[]{:S(2)}) collective-permute-start(bf16[3,2,80,128]{3,2,1,0:T(8,128)(2,1)S(1)} %get-tuple-element.10), channel_id=1, source_target_pairs={{0,2},{1,3},{2,0},{3,1},{4,6},{5,7},{6,4},{7,5},{8,10},{9,11},{10,... | collective-permute-start | bytes 368648 | tf_op jit(solution)/shard_map/ppermute | solution.py:158
  195.0 6.2 %collective-permute-start.27 = (bf16[3,2,80,128]{3,2,1,0:T(8,128)(2,1)S(1)}, bf16[3,2,80,128]{3,2,1,0:T(8,128)(2,1)S(1)}, u32[]{:S(2)}, u32[]{:S(2)}) collective-permute-start(bf16[3,2,80,128]{3,2,1,0:T(8,128)(2,1)S(1)} %get-tuple-element.9), channel_id=1, source_target_pairs={{0,3},{1,0},{2,1},{3,2},{4,7},{5,4},{6,5},{7,6},{8,11},{9,8},{10,9... | collective-permute-start | bytes 368648 | tf_op jit(solution)/shard_map/ppermute | solution.py:158
  (15 other events, 256.0 us)
Sparse Core Ops, SparseCore 0:
  25.7 75.6 all-gather.2
  103.0 69.8 all-gather.4

commit v7 on v1

--- a/solution.py
+++ b/solution.py
@@ -205,9 +205,10 @@
     own_bias_next = lax.dynamic_slice_in_dim(bias_second, me * width, width)
     branch = causal_conv(edge_mask(act_second), weights_second, own_bias_next, jnp.float32)
 
-    branch_rows = scatter_rows(branch, slab_rows, chans)
-    summed = (values + branch_rows).astype(jnp.bfloat16)
-    return jnp.repeat(jnp.repeat(summed, 2, axis=1), 2, axis=2)
+    own_latent = lax.dynamic_slice_in_dim(raw_rows[:, 1:-1], me * width, width, axis=3)
+    summed = (own_latent.astype(jnp.float32) + branch).astype(jnp.bfloat16)
+    summed_rows = scatter_rows(summed, slab_rows, chans)
+    return jnp.repeat(jnp.repeat(summed_rows, 2, axis=1), 2, axis=2)
 
 
 def solution(mesh):

time: 215 us -> 210 us (0.977)
  waiting for transfers between devices: 76.3 us -> 64.6 us
  local copies, waits for them, and re-layouts: 27.1 us -> 29.4 us
  starting transfers between devices: 45.7 us -> 48 us
    all_gather x2, waiting for transfers between devices: 26.8 us -> 20.9 us  [kernel_block(): return lax.all_gather(out, 'hz', axis=1, tiled=True)]
    ppermute x3, waiting for transfers between devices: 11.2 us -> 5.93 us  [scatter_rows(): piece = lax.ppermute(piece, HQ, shift_pairs(size, step))]
    ppermute x6, starting transfers between devices: 9.29 us -> 12.3 us  [chip_gather(): lax.ppermute(firsts, 'hb', shift_pairs(count_b, step))]
    dynamic_update_slice x11, local copies, waits for them, and re-layouts: 7.69 us -> 9.92 us  [chip_gather(): out = lax.dynamic_update_slice(out, piece, start)]
  transfers between devices with their start and end apart: 36 -> 36, of which waited for: 21 -> 20; matrix products, arithmetic and copies ran while one was open for 15% -> 18% of each run, Pallas kernels for 9% -> 9%
where the time goes in v7:
time: 210 us; the launch traced here: 209 us
  waiting for transfers between devices  64.6 us (31%)
  starting transfers between devices  48 us (23%)
  Pallas kernels  37 us (18%)
  local copies, waits for them, and re-layouts  29.4 us (14%)
  other arithmetic  16.1 us (8%)
  between operations  13.9 us (7%)
    pallas_call x2, Pallas kernels, causal_conv(): pl.pallas_call(conv_body, grid=(frames,), in_specs=[pl.BlockSpec(padded.s...  37 us
    all_gather x2, waiting for transfers between devices, kernel_block(): return lax.all_gather(out, 'hz', axis=1, tiled=True)  20.9 us
    ppermute x12, waiting for transfers between devices, butterfly_stats(): other_sums, other_squares = lax.ppermute((sums, squares), axis, pairs)  15.5 us
    ppermute x2, waiting for transfers between devices, with_row_halo(): bottom = lax.ppermute(cells[:, :1], axis_name, up)  13.4 us
    ppermute x6, starting transfers between devices, chip_gather(): lax.ppermute(firsts, 'hb', shift_pairs(count_b, step))  12.3 us
    ppermute x12, starting transfers between devices, butterfly_stats(): other_sums, other_squares = lax.ppermute((sums, squares), axis, pairs)  11.7 us
    dynamic_update_slice x11, local copies, waits for them, and re-layouts, chip_gather(): out = lax.dynamic_update_slice(out, piece, start)  9.92 us
    ppermute x6, waiting for transfers between devices, kernel_block(): piece = lax.ppermute(piece, HQ, shift_pairs(size, step))  8.4 us
  transfers between devices with their start and end apart: 36, of which 20 were waited for; matrix products, arithmetic and copies ran while one was open for 18% of the time, Pallas kernels for 9%

profile of v7, /device:TPU:1, one launch (start us, length us, event | category | flops | bytes accessed | tf_op | source)
XLA Modules:
  0.0 209.0 jit_solution(1472923963063926924)
XLA Ops:
  8.3 2.7 %collective-permute-start.13 = (bf16[27,32,128]{2,1,0:T(8,128)(2,1)S(1)}, bf16[27,32,128]{2,1,0:T(8,128)(2,1)}, u32[]{:S(2)}, u32[]{:S(2)}) collective-permute-start(bf16[27,32,128]{2,1,0:T(8,128)(2,1)S(1)} %get-tuple-element.12), channel_id=1, source_target_pairs={{0,1},{1,2},{2,3},{3,0},{4,5},{5,6},{6,7},{7,4},{8,9},{9,10},{10,1... | collective-permute-start | bytes 663560 | tf_op jit(solution)/shard_map/ppermute | solution.py:149
  11.5 4.2 %collective-permute-done.13 = bf16[27,32,128]{2,1,0:T(8,128)(2,1)} collective-permute-done((bf16[27,32,128]{2,1,0:T(8,128)(2,1)S(1)}, bf16[27,32,128]{2,1,0:T(8,128)(2,1)}, u32[]{:S(2)}, u32[]{:S(2)}) %collective-permute-start.13) | collective-permute-done | bytes 221216 | tf_op jit(solution)/shard_map/ppermute | solution.py:149
  16.6 3.8 %collective-permute-done.14 = bf16[27,32,128]{2,1,0:T(8,128)(2,1)S(1)} collective-permute-done((bf16[27,32,128]{2,1,0:T(8,128)(2,1)S(1)}, bf16[27,32,128]{2,1,0:T(8,128)(2,1)S(1)}, u32[]{:S(2)}, u32[]{:S(2)}) %collective-permute-start.14) | collective-permute-done | bytes 221216 | tf_op jit(solution)/shard_map/ppermute | solution.py:149
  21.9 2.1 collective-permute-start
  29.5 6.1 %collective-permute-done.5 = f32[32]{0:T(128)S(1)} collective-permute-done((f32[32]{0:T(128)S(1)}, f32[32]{0:T(128)S(1)}, u32[]{:S(2)}, u32[]{:S(2)}) %collective-permute-start.5) | collective-permute-done | bytes 160 | tf_op jit(solution)/shard_map/ppermute | solution.py:25
  46.1 2.3 %collective-permute-done.12 = f32[32]{0:T(128)S(1)} collective-permute-done((f32[32]{0:T(128)S(1)}, f32[32]{0:T(128)S(1)}, u32[]{:S(2)}, u32[]{:S(2)}) %collective-permute-start.12) | collective-permute-done | bytes 160 | tf_op jit(solution)/shard_map/ppermute | solution.py:25
  56.0 4.0 %collective-permute-start.3 = (bf16[3,1,80,512]{3,2,1,0:T(8,128)(2,1)}, bf16[3,1,80,512]{3,2,1,0:T(8,128)(2,1)S(1)}, u32[]{:S(2)}, u32[]{:S(2)}) collective-permute-start(bf16[3,1,80,512]{3,2,1,0:T(8,128)(2,1)} %get-tuple-element.5), channel_id=1, source_target_pairs={{0,4},{4,8},{8,12},{1,5},{5,9},{9,13},{2,6},{6,10},{10,14},{3,7},{... | collective-permute-start | bytes 737288 | tf_op jit(solution)/shard_map/ppermute | solution.py:93
  64.0 12.2 %collective-permute-done.4 = bf16[3,1,80,512]{3,2,1,0:T(8,128)(2,1)S(1)} collective-permute-done((bf16[3,1,80,512]{3,2,1,0:T(8,128)(2,1)}, bf16[3,1,80,512]{3,2,1,0:T(8,128)(2,1)S(1)}, u32[]{:S(2)}, u32[]{:S(2)}) %collective-permute-start.4) | collective-permute-done | bytes 245792 | tf_op jit(solution)/shard_map/ppermute | solution.py:94
  78.2 3.2 %fusion.5.x_ref = bf16[5,10,82,512]{3,2,1,0:T(8,128)(2,1)} fusion(bf16[3,10,80,512]{3,2,1,0:T(8,128)(2,1)S(1)} %fusion.6, bf16[1,10,80,512]{3,2,1,0:T(8,128)(2,1)S(1)} %slice.36), kind=kLoop, calls=%fused_computation.11 | loop fusion | flops 25190400 | bytes 7475200 | tf_op jit(solution)/shard_map/concatenate | solution.py:116
  81.4 17.3 %all-gather.3.cloned.1.call-done.w_ref = bf16[27,512,128]{2,1,0:T(8,128)(2,1)} async-done(((bf16[27,128,128]{2,1,0:T(8,128)(2,1)}), bf16[27,512,128]{2,1,0:T(8,128)(2,1)}) %all-gather.3.cloned.1.call-update) | async-done | bytes 3538960 | tf_op jit(solution)/shard_map/all_gather | solution.py:152
  98.7 18.5 %shard_map.91 = bf16[3,8,80,128]{3,2,1,0:T(8,128)(2,1)} custom-call(bf16[5,10,82,512]{3,2,1,0:T(8,128)(2,1)} %fusion.5.x_ref, bf16[27,512,128]{2,1,0:T(8,128)(2,1)} %all-gather.3.cloned.1.call-done.w_ref, f32[1,128]{1,0:T(1,128)} %dynamic-slice_bitcast_fusion.1.b_ref), custom_call_target="tpu_custom_call" | custom-call | flops 6794772480 | bytes 8720384 | tf_op jit(solution)/shard_map/pallas_call | solution.py:124
  119.4 4.2 %collective-permute-start.16 = (bf16[3,1,80,128]{3,2,1,0:T(8,128)(2,1)S(1)}, bf16[3,1,80,128]{3,2,1,0:T(8,128)(2,1)S(1)}, u32[]{:S(2)}, u32[]{:S(2)}) collective-permute-start(bf16[3,1,80,128]{3,2,1,0:T(8,128)(2,1)S(1)} %get-tuple-element.21), channel_id=1, source_target_pairs={{0,4},{4,8},{8,12},{1,5},{5,9},{9,13},{2,6},{6,10},{10,14},{3,7},{... | collective-permute-start | bytes 184328 | tf_op jit(solution)/shard_map/ppermute | solution.py:93
  127.8 2.0 pad_maximum_fusion
  131.4 2.7 %collective-permute-start.21 = (f32[8]{0:T(128)S(1)}, f32[8]{0:T(128)S(1)}, u32[]{:S(2)}, u32[]{:S(2)}) collective-permute-start(f32[8]{0:T(128)S(1)} %reduce_sum.72), channel_id=1, source_target_pairs={{0,4},{4,0},{8,12},{12,8},{1,5},{5,1},{9,13},{13,9},{2,6},{6,2},{1... | collective-permute-start | bytes 104 | tf_op jit(solution)/shard_map/ppermute | solution.py:25
  134.8 2.2 %collective-permute-done.21 = f32[8]{0:T(128)S(1)} collective-permute-done((f32[8]{0:T(128)S(1)}, f32[8]{0:T(128)S(1)}, u32[]{:S(2)}, u32[]{:S(2)}) %collective-permute-start.21) | collective-permute-done | bytes 64 | tf_op jit(solution)/shard_map/ppermute | solution.py:25
  140.0 5.1 %collective-permute-start.19 = (bf16[3,10,80,128]{3,2,1,0:T(8,128)(2,1)S(1)}, bf16[3,10,80,128]{3,2,1,0:T(8,128)(2,1)}, u32[]{:S(2)}, u32[]{:S(2)}) collective-permute-start(bf16[3,10,80,128]{3,2,1,0:T(8,128)(2,1)S(1)} %get-tuple-element.15), channel_id=1, source_target_pairs={{0,1},{1,0},{2,3},{3,2},{4,5},{5,4},{6,7},{7,6},{8,9},{9,8},{10,11... | collective-permute-start | bytes 1843208 | tf_op jit(solution)/shard_map/ppermute | solution.py:71
  147.4 3.4 %collective-permute-start.26 = (f32[2,8]{1,0:T(2,128)S(1)}, f32[2,8]{1,0:T(2,128)S(1)}, u32[]{:S(2)}, u32[]{:S(2)}) collective-permute-start(f32[2,8]{1,0:T(2,128)S(1)} %pad_maximum_fusion.1), channel_id=1, source_target_pairs={{0,1},{1,0},{2,3},{3,2},{4,5},{5,4},{6,7},{7,6},{8,9},{9,8},{10,11... | collective-permute-start | bytes 200 | tf_op jit(solution)/shard_map/ppermute | solution.py:71
  160.2 3.2 %fusion.7 = bf16[3,10,80,512]{3,2,1,0:T(8,128)(2,1)S(1)} fusion(bf16[3,10,80,512]{3,2,1,0:T(8,128)(2,1)} %constant_dynamic-update-slice_fusion.6, f32[512]{0:T(512)S(1)} %copy-done.8, f32[512]{0:T(512)S(1)} %copy-done.9, f32[512]{0:T(512)S(1)} %mul.221, f32[512]{0:T(512)S(1)} %sub.111, pred[10]{0:T(512)(128)(4,1)S(1)} %or_and_fusion), kind=kLoop, calls=%fused_computation.13 | loop fusion | flops 13516800 | bytes 4923402 | tf_op jit(solution)/shard_map/jit(_where)/select_n | solution.py:86
  163.4 3.2 %select_maximum_fusion.x_ref = bf16[5,10,82,512]{3,2,1,0:T(8,128)(2,1)} fusion(bf16[3,10,80,512]{3,2,1,0:T(8,128)(2,1)S(1)} %fusion.7, bf16[1,10,80,512]{3,2,1,0:T(8,128)(2,1)S(1)} %slice.39), kind=kLoop, calls=%fused_computation.5 | loop fusion | flops 25190400 | bytes 7475200 | tf_op jit(solution)/shard_map/concatenate | solution.py:116
  166.6 3.6 %all-gather.5.cloned.1.call-done.w_ref = bf16[27,512,128]{2,1,0:T(8,128)(2,1)} async-done(((bf16[27,128,128]{2,1,0:T(8,128)(2,1)}), bf16[27,512,128]{2,1,0:T(8,128)(2,1)}) %all-gather.5.cloned.1.call-update) | async-done | bytes 3538960 | tf_op jit(solution)/shard_map/all_gather | solution.py:152
  170.2 18.5 %shard_map.92 = f32[3,8,80,128]{3,2,1,0:T(8,128)} custom-call(bf16[5,10,82,512]{3,2,1,0:T(8,128)(2,1)} %select_maximum_fusion.x_ref, bf16[27,512,128]{2,1,0:T(8,128)(2,1)} %all-gather.5.cloned.1.call-done.w_ref, f32[1,128]{1,0:T(1,128)} %dynamic-slice_bitcast_fusion.b_ref), custom_call_target="tpu_custom_call" | custom-call | flops 6794772480 | bytes 8720384 | tf_op jit(solution)/shard_map/pallas_call | solution.py:124
  192.4 2.1 collective-permute-done.31
  194.5 3.3 %collective-permute-done.32 = bf16[3,2,80,128]{3,2,1,0:T(8,128)(2,1)S(1)} collective-permute-done((bf16[3,2,80,128]{3,2,1,0:T(8,128)(2,1)S(1)}, bf16[3,2,80,128]{3,2,1,0:T(8,128)(2,1)S(1)}, u32[]{:S(2)}, u32[]{:S(2)}) %collective-permute-start.32) | collective-permute-done | bytes 122912 | tf_op jit(solution)/shard_map/ppermute | solution.py:164
  200.0 2.2 %reshape.59 = bf16[3,4,160,512]{3,2,1,0:T(8,128)(2,1)} reshape(bf16[3,4,80,2,512]{4,3,2,1,0:T(2,128)(2,1)S(1)} %broadcast_in_dim.53) | data formatting | bytes 3932160 | tf_op jit(solution)/shard_map/reshape | solution.py:211
  (151 shorter events, 63.4 us)
Async XLA Ops:
  6.5 92.1 %all-gather.3.cloned.1.call-start = ((), (), s32[]{:S(2)}) async-start(), calls=%async_computation | async-start | bytes 4423680 | tf_op jit(solution)/shard_map/all_gather | solution.py:152
  8.3 7.3 %collective-permute-start.13 = (bf16[27,32,128]{2,1,0:T(8,128)(2,1)S(1)}, bf16[27,32,128]{2,1,0:T(8,128)(2,1)}, u32[]{:S(2)}, u32[]{:S(2)}) collective-permute-start(bf16[27,32,128]{2,1,0:T(8,128)(2,1)S(1)} %get-tuple-element.12), channel_id=1, source_target_pairs={{0,1},{1,2},{2,3},{3,0},{4,5},{5,6},{6,7},{7,4},{8,9},{9,10},{10,1... | collective-permute-start | bytes 663560 | tf_op jit(solution)/shard_map/ppermute | solution.py:149
  11.0 9.4 %collective-permute-start.14 = (bf16[27,32,128]{2,1,0:T(8,128)(2,1)S(1)}, bf16[27,32,128]{2,1,0:T(8,128)(2,1)S(1)}, u32[]{:S(2)}, u32[]{:S(2)}) collective-permute-start(bf16[27,32,128]{2,1,0:T(8,128)(2,1)S(1)} %get-tuple-element.14), channel_id=1, source_target_pairs={{0,2},{1,3},{2,0},{3,1},{4,6},{5,7},{6,4},{7,5},{8,10},{9,11},{10,... | collective-permute-start | bytes 663560 | tf_op jit(solution)/shard_map/ppermute | solution.py:149
  11.0 9.9 %collective-permute-start.15 = (bf16[27,32,128]{2,1,0:T(8,128)(2,1)S(1)}, bf16[27,32,128]{2,1,0:T(8,128)(2,1)S(1)}, u32[]{:S(2)}, u32[]{:S(2)}) collective-permute-start(bf16[27,32,128]{2,1,0:T(8,128)(2,1)S(1)} %get-tuple-element.11), channel_id=1, source_target_pairs={{0,3},{1,0},{2,1},{3,2},{4,7},{5,4},{6,5},{7,6},{8,11},{9,8},{10,9... | collective-permute-start | bytes 663560 | tf_op jit(solution)/shard_map/ppermute | solution.py:149
  21.9 148.3 %all-gather.5.cloned.1.call-start = ((), (), s32[]{:S(2)}) async-start(), calls=%async_computation.1 | async-start | bytes 4423680 | tf_op jit(solution)/shard_map/all_gather | solution.py:152
  21.9 17.4 %collective-permute-start = (bf16[3,2,80,512]{3,2,1,0:T(8,128)(2,1)S(1)}, bf16[3,2,80,512]{3,2,1,0:T(8,128)(2,1)}, u32[]{:S(2)}, u32[]{:S(2)}) collective-permute-start(bf16[3,2,80,512]{3,2,1,0:T(8,128)(2,1)S(1)} %copy-done.2), channel_id=1, source_target_pairs={{0,2},{2,0},{1,3},{3,1},{4,6},{6,4},{5,7},{7,5},{8,10},{10,8},{9,1... | collective-permute-start | bytes 1474568 | tf_op jit(solution)/shard_map/ppermute | solution.py:66
  24.0 27.7 %collective-permute-start.1 = (bf16[3,2,80,512]{3,2,1,0:T(8,128)(2,1)S(1)}, bf16[3,2,80,512]{3,2,1,0:T(8,128)(2,1)}, u32[]{:S(2)}, u32[]{:S(2)}) collective-permute-start(bf16[3,2,80,512]{3,2,1,0:T(8,128)(2,1)S(1)} %copy-done.2), channel_id=1, source_target_pairs={{0,1},{1,0},{2,3},{3,2},{4,5},{5,4},{6,7},{7,6},{8,9},{9,8},{10,11... | collective-permute-start | bytes 1474568 | tf_op jit(solution)/shard_map/ppermute | solution.py:71
  24.3 11.3 %collective-permute-start.5 = (f32[32]{0:T(128)S(1)}, f32[32]{0:T(128)S(1)}, u32[]{:S(2)}, u32[]{:S(2)}) collective-permute-start(f32[32]{0:T(128)S(1)} %reduce_sum.51), channel_id=1, source_target_pairs={{0,2},{2,0},{1,3},{3,1},{4,6},{6,4},{5,7},{7,5},{8,10},{10,8},{9,1... | collective-permute-start | bytes 392 | tf_op jit(solution)/shard_map/ppermute | solution.py:25
  25.1 10.4 %collective-permute-start.9 = (f32[32]{0:T(128)S(1)}, f32[32]{0:T(128)S(1)}, u32[]{:S(2)}, u32[]{:S(2)}) collective-permute-start(f32[32]{0:T(128)S(1)} %reduce_sum.54), channel_id=1, source_target_pairs={{0,2},{2,0},{1,3},{3,1},{4,6},{6,4},{5,7},{7,5},{8,10},{10,8},{9,1... | collective-permute-start | bytes 392 | tf_op jit(solution)/shard_map/ppermute | solution.py:25
  27.6 32.4 %collective-permute-start.28 = (bf16[27,32,128]{2,1,0:T(8,128)(2,1)}, bf16[27,32,128]{2,1,0:T(8,128)(2,1)}, u32[]{:S(2)}, u32[]{:S(2)}) collective-permute-start(bf16[27,32,128]{2,1,0:T(8,128)(2,1)} %get-tuple-element.8), channel_id=1, source_target_pairs={{0,1},{1,2},{2,3},{3,0},{4,5},{5,6},{6,7},{7,4},{8,9},{9,10},{10,1... | collective-permute-start | bytes 663560 | tf_op jit(solution)/shard_map/ppermute | solution.py:149
  39.3 13.5 %collective-permute-start.2 = (bf16[3,2,80,512]{3,2,1,0:T(8,128)(2,1)}, bf16[3,2,80,512]{3,2,1,0:T(8,128)(2,1)}, u32[]{:S(2)}, u32[]{:S(2)}) collective-permute-start(bf16[3,2,80,512]{3,2,1,0:T(8,128)(2,1)} %collective-permute-done), channel_id=1, source_target_pairs={{0,1},{1,0},{2,3},{3,2},{4,5},{5,4},{6,7},{7,6},{8,9},{9,8},{10,11... | collective-permute-start | bytes 1474568 | tf_op jit(solution)/shard_map/ppermute | solution.py:71
  45.7 15.3 %collective-permute-start.29 = (bf16[27,32,128]{2,1,0:T(8,128)(2,1)}, bf16[27,32,128]{2,1,0:T(8,128)(2,1)}, u32[]{:S(2)}, u32[]{:S(2)}) collective-permute-start(bf16[27,32,128]{2,1,0:T(8,128)(2,1)} %get-tuple-element.10), channel_id=1, source_target_pairs={{0,2},{1,3},{2,0},{3,1},{4,6},{5,7},{6,4},{7,5},{8,10},{9,11},{10,... | collective-permute-start | bytes 663560 | tf_op jit(solution)/shard_map/ppermute | solution.py:149
  48.5 13.6 %collective-permute-start.30 = (bf16[27,32,128]{2,1,0:T(8,128)(2,1)}, bf16[27,32,128]{2,1,0:T(8,128)(2,1)}, u32[]{:S(2)}, u32[]{:S(2)}) collective-permute-start(bf16[27,32,128]{2,1,0:T(8,128)(2,1)} %get-tuple-element.7), channel_id=1, source_target_pairs={{0,3},{1,0},{2,1},{3,2},{4,7},{5,4},{6,5},{7,6},{8,11},{9,8},{10,9... | collective-permute-start | bytes 663560 | tf_op jit(solution)/shard_map/ppermute | solution.py:149
  54.8 21.5 %collective-permute-start.4 = (bf16[3,1,80,512]{3,2,1,0:T(8,128)(2,1)}, bf16[3,1,80,512]{3,2,1,0:T(8,128)(2,1)S(1)}, u32[]{:S(2)}, u32[]{:S(2)}) collective-permute-start(bf16[3,1,80,512]{3,2,1,0:T(8,128)(2,1)} %get-tuple-element.6), channel_id=1, source_target_pairs={{4,0},{8,4},{12,8},{5,1},{9,5},{13,9},{6,2},{10,6},{14,10},{7,3},{... | collective-permute-start | bytes 737288 | tf_op jit(solution)/shard_map/ppermute | solution.py:94
  56.0 20.2 %collective-permute-start.3 = (bf16[3,1,80,512]{3,2,1,0:T(8,128)(2,1)}, bf16[3,1,80,512]{3,2,1,0:T(8,128)(2,1)S(1)}, u32[]{:S(2)}, u32[]{:S(2)}) collective-permute-start(bf16[3,1,80,512]{3,2,1,0:T(8,128)(2,1)} %get-tuple-element.5), channel_id=1, source_target_pairs={{0,4},{4,8},{8,12},{1,5},{5,9},{9,13},{2,6},{6,10},{10,14},{3,7},{... | collective-permute-start | bytes 737288 | tf_op jit(solution)/shard_map/ppermute | solution.py:93
  118.1 8.0 %collective-permute-start.17 = (bf16[3,1,80,128]{3,2,1,0:T(8,128)(2,1)S(1)}, bf16[3,1,80,128]{3,2,1,0:T(8,128)(2,1)S(1)}, u32[]{:S(2)}, u32[]{:S(2)}) collective-permute-start(bf16[3,1,80,128]{3,2,1,0:T(8,128)(2,1)S(1)} %get-tuple-element.22), channel_id=1, source_target_pairs={{4,0},{8,4},{12,8},{5,1},{9,5},{13,9},{6,2},{10,6},{14,10},{7,3},{... | collective-permute-start | bytes 184328 | tf_op jit(solution)/shard_map/ppermute | solution.py:94
  119.4 6.7 %collective-permute-start.16 = (bf16[3,1,80,128]{3,2,1,0:T(8,128)(2,1)S(1)}, bf16[3,1,80,128]{3,2,1,0:T(8,128)(2,1)S(1)}, u32[]{:S(2)}, u32[]{:S(2)}) collective-permute-start(bf16[3,1,80,128]{3,2,1,0:T(8,128)(2,1)S(1)} %get-tuple-element.21), channel_id=1, source_target_pairs={{0,4},{4,8},{8,12},{1,5},{5,9},{9,13},{2,6},{6,10},{10,14},{3,7},{... | collective-permute-start | bytes 184328 | tf_op jit(solution)/shard_map/ppermute | solution.py:93
  129.8 15.2 %collective-permute-start.18 = (bf16[3,10,80,128]{3,2,1,0:T(8,128)(2,1)S(1)}, bf16[3,10,80,128]{3,2,1,0:T(8,128)(2,1)}, u32[]{:S(2)}, u32[]{:S(2)}) collective-permute-start(bf16[3,10,80,128]{3,2,1,0:T(8,128)(2,1)S(1)} %get-tuple-element.15), channel_id=1, source_target_pairs={{0,2},{2,0},{1,3},{3,1},{4,6},{6,4},{5,7},{7,5},{8,10},{10,8},{9,1... | collective-permute-start | bytes 1843208 | tf_op jit(solution)/shard_map/ppermute | solution.py:66
  137.6 8.6 %collective-permute-start.22 = (f32[8]{0:T(128)S(1)}, f32[8]{0:T(128)S(1)}, u32[]{:S(2)}, u32[]{:S(2)}) collective-permute-start(f32[8]{0:T(128)S(1)} %get-tuple-element.28), channel_id=1, source_target_pairs={{0,8},{4,12},{8,0},{12,4},{1,9},{5,13},{9,1},{13,5},{2,10},{6,14},... | collective-permute-start | bytes 104 | tf_op jit(solution)/shard_map/ppermute | solution.py:25
  139.5 6.7 %collective-permute-start.24 = (f32[8]{0:T(128)S(1)}, f32[8]{0:T(128)S(1)}, u32[]{:S(2)}, u32[]{:S(2)}) collective-permute-start(f32[8]{0:T(128)S(1)} %get-tuple-element.27), channel_id=1, source_target_pairs={{0,8},{4,12},{8,0},{12,4},{1,9},{5,13},{9,1},{13,5},{2,10},{6,14},... | collective-permute-start | bytes 104 | tf_op jit(solution)/shard_map/ppermute | solution.py:25
  140.0 16.3 %collective-permute-start.19 = (bf16[3,10,80,128]{3,2,1,0:T(8,128)(2,1)S(1)}, bf16[3,10,80,128]{3,2,1,0:T(8,128)(2,1)}, u32[]{:S(2)}, u32[]{:S(2)}) collective-permute-start(bf16[3,10,80,128]{3,2,1,0:T(8,128)(2,1)S(1)} %get-tuple-element.15), channel_id=1, source_target_pairs={{0,1},{1,0},{2,3},{3,2},{4,5},{5,4},{6,7},{7,6},{8,9},{9,8},{10,11... | collective-permute-start | bytes 1843208 | tf_op jit(solution)/shard_map/ppermute | solution.py:71
  145.0 13.2 %collective-permute-start.20 = (bf16[3,10,80,128]{3,2,1,0:T(8,128)(2,1)}, bf16[3,10,80,128]{3,2,1,0:T(8,128)(2,1)}, u32[]{:S(2)}, u32[]{:S(2)}) collective-permute-start(bf16[3,10,80,128]{3,2,1,0:T(8,128)(2,1)} %collective-permute-done.18), channel_id=1, source_target_pairs={{0,1},{1,0},{2,3},{3,2},{4,5},{5,4},{6,7},{7,6},{8,9},{9,8},{10,11... | collective-permute-start | bytes 1843208 | tf_op jit(solution)/shard_map/ppermute | solution.py:71
  191.9 5.9 %collective-permute-start.32 = (bf16[3,2,80,128]{3,2,1,0:T(8,128)(2,1)S(1)}, bf16[3,2,80,128]{3,2,1,0:T(8,128)(2,1)S(1)}, u32[]{:S(2)}, u32[]{:S(2)}) collective-permute-start(bf16[3,2,80,128]{3,2,1,0:T(8,128)(2,1)S(1)} %get-tuple-element.18), channel_id=1, source_target_pairs={{0,2},{1,3},{2,0},{3,1},{4,6},{5,7},{6,4},{7,5},{8,10},{9,11},{10,... | collective-permute-start | bytes 368648 | tf_op jit(solution)/shard_map/ppermute | solution.py:164
  192.2 6.2 %collective-permute-start.33 = (bf16[3,2,80,128]{3,2,1,0:T(8,128)(2,1)S(1)}, bf16[3,2,80,128]{3,2,1,0:T(8,128)(2,1)S(1)}, u32[]{:S(2)}, u32[]{:S(2)}) collective-permute-start(bf16[3,2,80,128]{3,2,1,0:T(8,128)(2,1)S(1)} %get-tuple-element.17), channel_id=1, source_target_pairs={{0,3},{1,0},{2,1},{3,2},{4,7},{5,4},{6,5},{7,6},{8,11},{9,8},{10,9... | collective-permute-start | bytes 368648 | tf_op jit(solution)/shard_map/ppermute | solution.py:164
  (22 other events, 282.8 us)
Sparse Core Ops, SparseCore 0:
  22.0 76.6 all-gather.2
  100.2 69.8 all-gather.4

commit v8 on v5

--- a/solution.py
+++ b/solution.py
@@ -57,24 +57,25 @@
     count_b = lax.axis_size("hb")
     me_a = lax.axis_index("ha")
     me_b = lax.axis_index("hb")
-    width = block.shape[dim]
-    shape = list(block.shape)
-    shape[dim] = width * count_a * count_b
     firsts = [block]
-    sources = [me_a]
     for step in range(1, count_a):
         firsts.append(lax.ppermute(block, "ha", shift_pairs(count_a, step)))
-        sources.append((me_a - step) % count_a)
     firsts = tuple(firsts)
-    out = jnp.zeros(shape, block.dtype)
-    for step in range(count_b):
-        bundle = firsts if step == 0 else lax.ppermute(firsts, "hb", shift_pairs(count_b, step))
-        source_b = (me_b - step) % count_b
-        for piece, source_a in zip(bundle, sources):
-            start = [0] * len(shape)
-            start[dim] = (source_a * count_b + source_b) * width
-            out = lax.dynamic_update_slice(out, piece, start)
-    return out
+    bundles = [firsts]
+    for step in range(1, count_b):
+        bundles.append(lax.ppermute(firsts, "hb", shift_pairs(count_b, step)))
+    slots = []
+    for slot_a in range(count_a):
+        for slot_b in range(count_b):
+            piece = bundles[0][0]
+            for sb in range(count_b):
+                for sa in range(count_a):
+                    if sa == 0 and sb == 0:
+                        continue
+                    hit = ((me_a - sa) % count_a == slot_a) & ((me_b - sb) % count_b == slot_b)
+                    piece = jnp.where(hit, bundles[sb][sa], piece)
+            slots.append(piece)
+    return jnp.concatenate(slots, axis=dim)
 
 
 def edge_mask(cells):
@@ -136,7 +137,7 @@
     )(padded, kernel, bias.reshape(1, outs))
 
 
-def kernel_block(shard, chans):
+def redistribute(shard):
     size = lax.axis_size("ha") * lax.axis_size("hb")
     me = lax.axis_index(HQ)
     taps, in_block, outs = shard.shape
@@ -149,14 +150,33 @@
             piece = lax.ppermute(piece, HQ, shift_pairs(size, step))
         source = (me - step) % size
         out = lax.dynamic_update_slice(out, piece, (0, source * in_block, 0))
+    return out
+
+
+def kernel_block(shard, chans):
+    return lax.all_gather(redistribute(shard), "hz", axis=1, tiled=True)
+
+
+def split_block(shard, chans):
+    out = redistribute(shard)
+    taps, rows_in, width = out.shape
     parts = lax.axis_size("groups")
     part = lax.axis_index("groups")
     rows = lax.axis_size("hz")
-    share = (in_block * size) // parts
+    share = rows_in // parts
     mine = lax.dynamic_slice_in_dim(out, part * share, share, axis=1)
-    gathered = lax.all_gather(mine, ("groups", "hz"), axis=1, tiled=True)
-    ordered = gathered.reshape(taps, parts, rows, share, width)
-    return jnp.transpose(ordered, (0, 2, 1, 3, 4)).reshape(taps, chans, width)
+    gathered = lax.all_gather(mine, "hz", axis=1)
+    received = [gathered]
+    for step in range(1, parts):
+        received.append(lax.ppermute(gathered, "groups", shift_pairs(parts, step)))
+    slots = []
+    for slot in range(parts):
+        piece = received[0]
+        for step in range(1, parts):
+            piece = jnp.where((part - step) % parts == slot, received[step], piece)
+        slots.append(piece)
+    stacked = jnp.stack(slots, axis=2)
+    return stacked.reshape(taps, chans, width)
 
 
 def scatter_rows(branch, slab_rows, chans):
@@ -191,7 +211,7 @@
     me = lax.axis_index(HQ)
     group_size = chans // GROUPS
 
-    weights_first = kernel_block(kernel_first, chans)
+    weights_first = split_block(kernel_first, chans)
     weights_second = kernel_block(kernel_second, chans)
 
     values = latent.astype(jnp.float32)

time: 226 us -> 220 us (0.973)
  waiting for transfers between devices: 88.2 us -> 70.4 us
  starting transfers between devices: 37.9 us -> 48.4 us
  other arithmetic: 16.1 us -> 25.1 us
  local copies, waits for them, and re-layouts: 32.7 us -> 24.8 us
    all_gather x2, waiting for transfers between devices: 34.2 us -> 0.01 us  [the longest x1 0.01 us: split_block(): gathered = lax.all_gather(mine, 'hz', axis=1)]
    ppermute x12 -> x13, waiting for transfers between devices: 18.9 us -> 36.8 us  [the longest x1 26.3 us: split_block(): received.append(lax.ppermute(gathered, 'groups', shift_pairs(parts, step)))]
    transpose x2 -> x0, local copies, waits for them, and re-layouts: 9.95 us -> none  [kernel_block(): return jnp.transpose(ordered, (0, 2, 1, 3, 4)).reshape(taps, chans, width)]
    ppermute x3, waiting for transfers between devices: 8.1 us -> 0.01 us  [chip_gather(): firsts.append(lax.ppermute(block, 'ha', shift_pairs(count_a, step)))]
    ppermute x2, waiting for transfers between devices: 0.01 us -> 6.58 us  [with_row_halo(): top = lax.ppermute(cells[:, -1:], axis_name, down)]
    dynamic_update_slice x17 -> x6, local copies, waits for them, and re-layouts: 8.95 us -> 3.94 us  [redistribute(): out = lax.dynamic_update_slice(out, piece, (0, source * in_block, 0))]
    ppermute x12 -> x13, starting transfers between devices: 13.3 us -> 17.9 us  [the longest x6 9.75 us: chip_gather(): bundles.append(lax.ppermute(firsts, 'hb', shift_pairs(count_b, step)))]
    unnamed x0 -> x3, other arithmetic: none -> 3.41 us
  transfers between devices with their start and end apart: 36 -> 37, of which waited for: 17 -> 22; matrix products, arithmetic and copies ran while one was open for 15% -> 19% of each run, Pallas kernels for 8% -> 8%
where the time goes in v8:
time: 220 us
  waiting for transfers between devices  70.4 us (32%)
  starting transfers between devices  48.4 us (22%)
  Pallas kernels  37.1 us (17%)
  other arithmetic  25.1 us (11%)
  local copies, waits for them, and re-layouts  24.8 us (11%)
  between operations  13.8 us (6%)
    pallas_call x2, Pallas kernels, causal_conv(): pl.pallas_call(conv_body, grid=(frames,), in_specs=[pl.BlockSpec(padded.s...  37.1 us
    ppermute x1, waiting for transfers between devices, split_block(): received.append(lax.ppermute(gathered, 'groups', shift_pairs(parts, step)))  26.3 us
    ppermute x12, waiting for transfers between devices, butterfly_stats(): other_sums, other_squares = lax.ppermute((sums, squares), axis, pairs)  15.6 us
    ppermute x12, starting transfers between devices, butterfly_stats(): other_sums, other_squares = lax.ppermute((sums, squares), axis, pairs)  14.1 us
    ppermute x6, starting transfers between devices, chip_gather(): bundles.append(lax.ppermute(firsts, 'hb', shift_pairs(count_b, step)))  9.75 us
    ppermute x6, waiting for transfers between devices, redistribute(): piece = lax.ppermute(piece, HQ, shift_pairs(size, step))  8.4 us
    ppermute x2, starting transfers between devices, with_row_halo(): top = lax.ppermute(cells[:, -1:], axis_name, down)  8.11 us
    ppermute x6, starting transfers between devices, redistribute(): piece = lax.ppermute(piece, HQ, shift_pairs(size, step))  7.03 us
  transfers between devices with their start and end apart: 37, of which 22 were waited for; matrix products, arithmetic and copies ran while one was open for 19% of the time, Pallas kernels for 8%

profile of v8, /device:TPU:1, one launch (start us, length us, event | category | flops | bytes accessed | tf_op | source)
XLA Modules:
  0.0 219.6 jit_solution(16125581945148926405)
XLA Ops:
  8.3 2.7 %collective-permute-start.13 = (bf16[27,32,128]{2,1,0:T(8,128)(2,1)S(1)}, bf16[27,32,128]{2,1,0:T(8,128)(2,1)}, u32[]{:S(2)}, u32[]{:S(2)}) collective-permute-start(bf16[27,32,128]{2,1,0:T(8,128)(2,1)S(1)} %get-tuple-element.22), channel_id=1, source_target_pairs={{0,1},{1,2},{2,3},{3,0},{4,5},{5,6},{6,7},{7,4},{8,9},{9,10},{10,1... | collective-permute-start | bytes 663560 | tf_op jit(solution)/shard_map/ppermute | solution.py:150
  11.5 4.2 %collective-permute-done.13 = bf16[27,32,128]{2,1,0:T(8,128)(2,1)} collective-permute-done((bf16[27,32,128]{2,1,0:T(8,128)(2,1)S(1)}, bf16[27,32,128]{2,1,0:T(8,128)(2,1)}, u32[]{:S(2)}, u32[]{:S(2)}) %collective-permute-start.13) | collective-permute-done | bytes 221216 | tf_op jit(solution)/shard_map/ppermute | solution.py:150
  16.6 3.8 %collective-permute-done.14 = bf16[27,32,128]{2,1,0:T(8,128)(2,1)S(1)} collective-permute-done((bf16[27,32,128]{2,1,0:T(8,128)(2,1)S(1)}, bf16[27,32,128]{2,1,0:T(8,128)(2,1)S(1)}, u32[]{:S(2)}, u32[]{:S(2)}) %collective-permute-start.14) | collective-permute-done | bytes 221216 | tf_op jit(solution)/shard_map/ppermute | solution.py:150
  21.9 2.1 collective-permute-start
  30.6 5.0 %collective-permute-done.9 = f32[32]{0:T(128)S(1)} collective-permute-done((f32[32]{0:T(128)S(1)}, f32[32]{0:T(128)S(1)}, u32[]{:S(2)}, u32[]{:S(2)}) %collective-permute-start.9) | collective-permute-done | bytes 160 | tf_op jit(solution)/shard_map/ppermute | solution.py:25
  47.5 2.8 %collective-permute-start.31 = (bf16[27,32,128]{2,1,0:T(8,128)(2,1)}, bf16[27,32,128]{2,1,0:T(8,128)(2,1)}, u32[]{:S(2)}, u32[]{:S(2)}) collective-permute-start(bf16[27,32,128]{2,1,0:T(8,128)(2,1)} %get-tuple-element.17), channel_id=1, source_target_pairs={{0,3},{1,0},{2,1},{3,2},{4,7},{5,4},{6,5},{7,6},{8,11},{9,8},{10,9... | collective-permute-start | bytes 663560 | tf_op jit(solution)/shard_map/ppermute | solution.py:150
  51.5 3.4 %collective-permute-start.3 = (bf16[3,1,80,512]{3,2,1,0:T(8,128)(2,1)}, bf16[3,1,80,512]{3,2,1,0:T(8,128)(2,1)}, u32[]{:S(2)}, u32[]{:S(2)}) collective-permute-start(bf16[3,1,80,512]{3,2,1,0:T(8,128)(2,1)} %slice.34), channel_id=1, source_target_pairs={{0,4},{4,8},{8,12},{1,5},{5,9},{9,13},{2,6},{6,10},{10,14},{3,7},{... | collective-permute-start | bytes 737288 | tf_op jit(solution)/shard_map/ppermute | solution.py:94
  58.7 6.6 %collective-permute-done.3 = bf16[3,1,80,512]{3,2,1,0:T(8,128)(2,1)} collective-permute-done((bf16[3,1,80,512]{3,2,1,0:T(8,128)(2,1)}, bf16[3,1,80,512]{3,2,1,0:T(8,128)(2,1)}, u32[]{:S(2)}, u32[]{:S(2)}) %collective-permute-start.3) | collective-permute-done | bytes 245792 | tf_op jit(solution)/shard_map/ppermute | solution.py:94
  74.5 4.2 %collective-permute-done.4 = bf16[3,1,80,512]{3,2,1,0:T(8,128)(2,1)} collective-permute-done((bf16[3,1,80,512]{3,2,1,0:T(8,128)(2,1)}, bf16[3,1,80,512]{3,2,1,0:T(8,128)(2,1)}, u32[]{:S(2)}, u32[]{:S(2)}) %collective-permute-start.4) | collective-permute-done | bytes 245792 | tf_op jit(solution)/shard_map/ppermute | solution.py:95
  80.3 3.2 %fusion.6 = bf16[3,10,80,512]{3,2,1,0:T(8,128)(2,1)S(1)} fusion(bf16[3,10,80,512]{3,2,1,0:T(8,128)(2,1)} %constant_dynamic-update-slice_fusion, f32[512]{0:T(512)S(1)} %copy-done.7, f32[512]{0:T(512)S(1)} %copy-done.8, f32[512]{0:T(512)S(1)} %mul.144, f32[512]{0:T(512)S(1)} %sub.56, pred[10]{0:T(512)(128)(4,1)S(1)} %or_and_fusion), kind=kLoop, calls=%fused_computation.13 | loop fusion | flops 13516800 | bytes 4923402 | tf_op jit(solution)/shard_map/jit(_where)/select_n | solution.py:87
  83.5 3.2 %fusion.5.x_ref = bf16[5,10,82,512]{3,2,1,0:T(8,128)(2,1)} fusion(bf16[3,10,80,512]{3,2,1,0:T(8,128)(2,1)S(1)} %fusion.6, bf16[1,10,80,512]{3,2,1,0:T(8,128)(2,1)S(1)} %slice.36), kind=kLoop, calls=%fused_computation.11 | loop fusion | flops 25190400 | bytes 7475200 | tf_op jit(solution)/shard_map/concatenate | solution.py:117
  86.7 26.3 %collective-permute-done.16 = bf16[27,4,64,128]{3,2,1,0:T(8,128)(2,1)S(1)} collective-permute-done((bf16[27,4,64,128]{3,2,1,0:T(8,128)(2,1)}, bf16[27,4,64,128]{3,2,1,0:T(8,128)(2,1)S(1)}, u32[]{:S(2)}, u32[]{:S(2)}) %collective-permute-start.16) | collective-permute-done | bytes 1769504 | tf_op jit(solution)/shard_map/ppermute | solution.py:171
  113.5 2.5 %copy.11 = bf16[27,4,2,64,128]{4,3,2,1,0:T(8,128)(2,1)} copy(bf16[27,4,2,64,128]{4,3,1,0,2:T(8,128)(2,1)S(1)} %pad_maximum_fusion) | data formatting | bytes 7077888 | tf_op jit(solution)/shard_map/stack | solution.py:178
  116.1 18.5 %shard_map.91 = bf16[3,8,80,128]{3,2,1,0:T(8,128)(2,1)} custom-call(bf16[5,10,82,512]{3,2,1,0:T(8,128)(2,1)} %fusion.5.x_ref, bf16[27,512,128]{2,1,0:T(8,128)(2,1)} %bitcast.20, f32[1,128]{1,0:T(1,128)} %dynamic-slice_bitcast_fusion.1.b_ref), custom_call_target="tpu_custom_call" | custom-call | flops 6794772480 | bytes 8720384 | tf_op jit(solution)/shard_map/pallas_call | solution.py:125
  137.0 4.8 %collective-permute-start.17 = (bf16[3,1,80,128]{3,2,1,0:T(8,128)(2,1)S(1)}, bf16[3,1,80,128]{3,2,1,0:T(8,128)(2,1)S(1)}, u32[]{:S(2)}, u32[]{:S(2)}) collective-permute-start(bf16[3,1,80,128]{3,2,1,0:T(8,128)(2,1)S(1)} %get-tuple-element.29), channel_id=1, source_target_pairs={{0,4},{4,8},{8,12},{1,5},{5,9},{9,13},{2,6},{6,10},{10,14},{3,7},{... | collective-permute-start | bytes 184328 | tf_op jit(solution)/shard_map/ppermute | solution.py:94
  143.3 3.0 %collective-permute-start.22 = (f32[8]{0:T(128)S(1)}, f32[8]{0:T(128)S(1)}, u32[]{:S(2)}, u32[]{:S(2)}) collective-permute-start(f32[8]{0:T(128)S(1)} %reduce_sum.72), channel_id=1, source_target_pairs={{0,4},{4,0},{8,12},{12,8},{1,5},{5,1},{9,13},{13,9},{2,6},{6,2},{1... | collective-permute-start | bytes 104 | tf_op jit(solution)/shard_map/ppermute | solution.py:25
  154.7 2.7 %collective-permute-start.23 = (f32[8]{0:T(128)S(1)}, f32[8]{0:T(128)S(1)}, u32[]{:S(2)}, u32[]{:S(2)}) collective-permute-start(f32[8]{0:T(128)S(1)} %get-tuple-element.39), channel_id=1, source_target_pairs={{0,8},{4,12},{8,0},{12,4},{1,9},{5,13},{9,1},{13,5},{2,10},{6,14},... | collective-permute-start | bytes 104 | tf_op jit(solution)/shard_map/ppermute | solution.py:25
  158.3 2.4 %collective-permute-done.25 = f32[8]{0:T(128)S(1)} collective-permute-done((f32[8]{0:T(128)S(1)}, f32[8]{0:T(128)S(1)}, u32[]{:S(2)}, u32[]{:S(2)}) %collective-permute-start.25) | collective-permute-done | bytes 64 | tf_op jit(solution)/shard_map/ppermute | solution.py:25
  161.4 6.1 %collective-permute-start.28 = (f32[2,8]{1,0:T(2,128)S(1)}, f32[2,8]{1,0:T(2,128)S(1)}, u32[]{:S(2)}, u32[]{:S(2)}) collective-permute-start(f32[2,8]{1,0:T(2,128)S(1)} %pad_maximum_fusion.2), channel_id=1, source_target_pairs={{0,1},{1,0},{2,3},{3,2},{4,5},{5,4},{6,7},{7,6},{8,9},{9,8},{10,11... | collective-permute-start | bytes 200 | tf_op jit(solution)/shard_map/ppermute | solution.py:66
  167.5 2.7 %collective-permute-start.27 = (f32[2,8]{1,0:T(2,128)S(1)}, f32[2,8]{1,0:T(2,128)S(1)}, u32[]{:S(2)}, u32[]{:S(2)}) collective-permute-start(f32[2,8]{1,0:T(2,128)S(1)} %collective-permute-done.26), channel_id=1, source_target_pairs={{0,1},{1,0},{2,3},{3,2},{4,5},{5,4},{6,7},{7,6},{8,9},{9,8},{10,11... | collective-permute-start | bytes 200 | tf_op jit(solution)/shard_map/ppermute | solution.py:66
  178.1 3.2 %select_maximum_fusion.x_ref = bf16[5,10,82,512]{3,2,1,0:T(8,128)(2,1)} fusion(bf16[3,10,80,512]{3,2,1,0:T(8,128)(2,1)S(1)} %fusion.7, bf16[1,10,80,512]{3,2,1,0:T(8,128)(2,1)S(1)} %slice.39), kind=kLoop, calls=%fused_computation.5 | loop fusion | flops 25190400 | bytes 7475200 | tf_op jit(solution)/shard_map/concatenate | solution.py:117
  181.2 18.6 %shard_map.92 = f32[3,8,80,128]{3,2,1,0:T(8,128)} custom-call(bf16[5,10,82,512]{3,2,1,0:T(8,128)(2,1)} %select_maximum_fusion.x_ref, bf16[27,512,128]{2,1,0:T(8,128)(2,1)} %all-gather.4.cloned.1.call-done.w_ref, f32[1,128]{1,0:T(1,128)} %dynamic-slice_bitcast_fusion.b_ref), custom_call_target="tpu_custom_call" | custom-call | flops 6794772480 | bytes 8720384 | tf_op jit(solution)/shard_map/pallas_call | solution.py:125
  204.1 4.0 %collective-permute-done.33 = bf16[3,2,80,128]{3,2,1,0:T(8,128)(2,1)S(1)} collective-permute-done((bf16[3,2,80,128]{3,2,1,0:T(8,128)(2,1)S(1)}, bf16[3,2,80,128]{3,2,1,0:T(8,128)(2,1)S(1)}, u32[]{:S(2)}, u32[]{:S(2)}) %collective-permute-start.33) | collective-permute-done | bytes 122912 | tf_op jit(solution)/shard_map/ppermute | solution.py:191
  210.6 2.2 reshape.63
  (158 shorter events, 68.1 us)
Async XLA Ops:
  6.5 66.8 %all-gather.6.cloned.1.call-start = ((), (), s32[]{:S(2)}) async-start(), calls=%async_computation.1 | async-start | bytes 2211840 | tf_op jit(solution)/shard_map/all_gather | solution.py:168
  8.3 7.3 %collective-permute-start.13 = (bf16[27,32,128]{2,1,0:T(8,128)(2,1)S(1)}, bf16[27,32,128]{2,1,0:T(8,128)(2,1)}, u32[]{:S(2)}, u32[]{:S(2)}) collective-permute-start(bf16[27,32,128]{2,1,0:T(8,128)(2,1)S(1)} %get-tuple-element.22), channel_id=1, source_target_pairs={{0,1},{1,2},{2,3},{3,0},{4,5},{5,6},{6,7},{7,4},{8,9},{9,10},{10,1... | collective-permute-start | bytes 663560 | tf_op jit(solution)/shard_map/ppermute | solution.py:150
  11.0 9.4 %collective-permute-start.14 = (bf16[27,32,128]{2,1,0:T(8,128)(2,1)S(1)}, bf16[27,32,128]{2,1,0:T(8,128)(2,1)S(1)}, u32[]{:S(2)}, u32[]{:S(2)}) collective-permute-start(bf16[27,32,128]{2,1,0:T(8,128)(2,1)S(1)} %get-tuple-element.24), channel_id=1, source_target_pairs={{0,2},{1,3},{2,0},{3,1},{4,6},{5,7},{6,4},{7,5},{8,10},{9,11},{10,... | collective-permute-start | bytes 663560 | tf_op jit(solution)/shard_map/ppermute | solution.py:150
  11.0 9.9 %collective-permute-start.15 = (bf16[27,32,128]{2,1,0:T(8,128)(2,1)S(1)}, bf16[27,32,128]{2,1,0:T(8,128)(2,1)S(1)}, u32[]{:S(2)}, u32[]{:S(2)}) collective-permute-start(bf16[27,32,128]{2,1,0:T(8,128)(2,1)S(1)} %get-tuple-element.21), channel_id=1, source_target_pairs={{0,3},{1,0},{2,1},{3,2},{4,7},{5,4},{6,5},{7,6},{8,11},{9,8},{10,9... | collective-permute-start | bytes 663560 | tf_op jit(solution)/shard_map/ppermute | solution.py:150
  21.8 159.4 %all-gather.4.cloned.1.call-start = ((), (), s32[]{:S(2)}) async-start(), calls=%async_computation | async-start | bytes 4423680 | tf_op jit(solution)/shard_map/all_gather | solution.py:157
  21.9 14.8 %collective-permute-start = (bf16[3,2,80,512]{3,2,1,0:T(8,128)(2,1)S(1)}, bf16[3,2,80,512]{3,2,1,0:T(8,128)(2,1)S(1)}, u32[]{:S(2)}, u32[]{:S(2)}) collective-permute-start(bf16[3,2,80,512]{3,2,1,0:T(8,128)(2,1)S(1)} %copy-done.1), channel_id=1, source_target_pairs={{0,2},{2,0},{1,3},{3,1},{4,6},{6,4},{5,7},{7,5},{8,10},{10,8},{9,1... | collective-permute-start | bytes 1474568 | tf_op jit(solution)/shard_map/ppermute | solution.py:62
  23.9 26.7 %collective-permute-start.2 = (bf16[3,2,80,512]{3,2,1,0:T(8,128)(2,1)S(1)}, bf16[3,2,80,512]{3,2,1,0:T(8,128)(2,1)S(1)}, u32[]{:S(2)}, u32[]{:S(2)}) collective-permute-start(bf16[3,2,80,512]{3,2,1,0:T(8,128)(2,1)S(1)} %copy-done.1), channel_id=1, source_target_pairs={{0,1},{1,0},{2,3},{3,2},{4,5},{5,4},{6,7},{7,6},{8,9},{9,8},{10,11... | collective-permute-start | bytes 1474568 | tf_op jit(solution)/shard_map/ppermute | solution.py:66
  24.3 11.3 %collective-permute-start.5 = (f32[32]{0:T(128)S(1)}, f32[32]{0:T(128)S(1)}, u32[]{:S(2)}, u32[]{:S(2)}) collective-permute-start(f32[32]{0:T(128)S(1)} %reduce_sum.51), channel_id=1, source_target_pairs={{0,2},{2,0},{1,3},{3,1},{4,6},{6,4},{5,7},{7,5},{8,10},{10,8},{9,1... | collective-permute-start | bytes 392 | tf_op jit(solution)/shard_map/ppermute | solution.py:25
  25.1 10.4 %collective-permute-start.9 = (f32[32]{0:T(128)S(1)}, f32[32]{0:T(128)S(1)}, u32[]{:S(2)}, u32[]{:S(2)}) collective-permute-start(f32[32]{0:T(128)S(1)} %reduce_sum.54), channel_id=1, source_target_pairs={{0,2},{2,0},{1,3},{3,1},{4,6},{6,4},{5,7},{7,5},{8,10},{10,8},{9,1... | collective-permute-start | bytes 392 | tf_op jit(solution)/shard_map/ppermute | solution.py:25
  27.5 27.3 %collective-permute-start.29 = (bf16[27,32,128]{2,1,0:T(8,128)(2,1)}, bf16[27,32,128]{2,1,0:T(8,128)(2,1)}, u32[]{:S(2)}, u32[]{:S(2)}) collective-permute-start(bf16[27,32,128]{2,1,0:T(8,128)(2,1)} %get-tuple-element.18), channel_id=1, source_target_pairs={{0,1},{1,2},{2,3},{3,0},{4,5},{5,6},{6,7},{7,4},{8,9},{9,10},{10,1... | collective-permute-start | bytes 663560 | tf_op jit(solution)/shard_map/ppermute | solution.py:150
  36.7 13.9 %collective-permute-start.1 = (bf16[3,2,80,512]{3,2,1,0:T(8,128)(2,1)S(1)}, bf16[3,2,80,512]{3,2,1,0:T(8,128)(2,1)S(1)}, u32[]{:S(2)}, u32[]{:S(2)}) collective-permute-start(bf16[3,2,80,512]{3,2,1,0:T(8,128)(2,1)S(1)} %collective-permute-done), channel_id=1, source_target_pairs={{0,1},{1,0},{2,3},{3,2},{4,5},{5,4},{6,7},{7,6},{8,9},{9,8},{10,11... | collective-permute-start | bytes 1474568 | tf_op jit(solution)/shard_map/ppermute | solution.py:66
  45.7 10.1 %collective-permute-start.30 = (bf16[27,32,128]{2,1,0:T(8,128)(2,1)}, bf16[27,32,128]{2,1,0:T(8,128)(2,1)}, u32[]{:S(2)}, u32[]{:S(2)}) collective-permute-start(bf16[27,32,128]{2,1,0:T(8,128)(2,1)} %get-tuple-element.20), channel_id=1, source_target_pairs={{0,2},{1,3},{2,0},{3,1},{4,6},{5,7},{6,4},{7,5},{8,10},{9,11},{10,... | collective-permute-start | bytes 663560 | tf_op jit(solution)/shard_map/ppermute | solution.py:150
  47.5 9.3 %collective-permute-start.31 = (bf16[27,32,128]{2,1,0:T(8,128)(2,1)}, bf16[27,32,128]{2,1,0:T(8,128)(2,1)}, u32[]{:S(2)}, u32[]{:S(2)}) collective-permute-start(bf16[27,32,128]{2,1,0:T(8,128)(2,1)} %get-tuple-element.17), channel_id=1, source_target_pairs={{0,3},{1,0},{2,1},{3,2},{4,7},{5,4},{6,5},{7,6},{8,11},{9,8},{10,9... | collective-permute-start | bytes 663560 | tf_op jit(solution)/shard_map/ppermute | solution.py:150
  51.5 13.8 %collective-permute-start.3 = (bf16[3,1,80,512]{3,2,1,0:T(8,128)(2,1)}, bf16[3,1,80,512]{3,2,1,0:T(8,128)(2,1)}, u32[]{:S(2)}, u32[]{:S(2)}) collective-permute-start(bf16[3,1,80,512]{3,2,1,0:T(8,128)(2,1)} %slice.34), channel_id=1, source_target_pairs={{0,4},{4,8},{8,12},{1,5},{5,9},{9,13},{2,6},{6,10},{10,14},{3,7},{... | collective-permute-start | bytes 737288 | tf_op jit(solution)/shard_map/ppermute | solution.py:94
  68.7 9.9 %collective-permute-start.4 = (bf16[3,1,80,512]{3,2,1,0:T(8,128)(2,1)}, bf16[3,1,80,512]{3,2,1,0:T(8,128)(2,1)}, u32[]{:S(2)}, u32[]{:S(2)}) collective-permute-start(bf16[3,1,80,512]{3,2,1,0:T(8,128)(2,1)} %slice.35), channel_id=1, source_target_pairs={{4,0},{8,4},{12,8},{5,1},{9,5},{13,9},{6,2},{10,6},{14,10},{7,3},{... | collective-permute-start | bytes 737288 | tf_op jit(solution)/shard_map/ppermute | solution.py:95
  73.4 39.6 %collective-permute-start.16 = (bf16[27,4,64,128]{3,2,1,0:T(8,128)(2,1)}, bf16[27,4,64,128]{3,2,1,0:T(8,128)(2,1)S(1)}, u32[]{:S(2)}, u32[]{:S(2)}) collective-permute-start(bf16[27,4,64,128]{3,2,1,0:T(8,128)(2,1)} %bitcast.21), channel_id=1, source_target_pairs={{0,16},{16,0},{1,17},{17,1},{2,18},{18,2},{3,19},{19,3},{4,20},{20... | collective-permute-start | bytes 5308424 | tf_op jit(solution)/shard_map/ppermute | solution.py:171
  137.0 9.4 %collective-permute-start.17 = (bf16[3,1,80,128]{3,2,1,0:T(8,128)(2,1)S(1)}, bf16[3,1,80,128]{3,2,1,0:T(8,128)(2,1)S(1)}, u32[]{:S(2)}, u32[]{:S(2)}) collective-permute-start(bf16[3,1,80,128]{3,2,1,0:T(8,128)(2,1)S(1)} %get-tuple-element.29), channel_id=1, source_target_pairs={{0,4},{4,8},{8,12},{1,5},{5,9},{9,13},{2,6},{6,10},{10,14},{3,7},{... | collective-permute-start | bytes 184328 | tf_op jit(solution)/shard_map/ppermute | solution.py:94
  141.8 5.8 %collective-permute-start.18 = (bf16[3,1,80,128]{3,2,1,0:T(8,128)(2,1)S(1)}, bf16[3,1,80,128]{3,2,1,0:T(8,128)(2,1)S(1)}, u32[]{:S(2)}, u32[]{:S(2)}) collective-permute-start(bf16[3,1,80,128]{3,2,1,0:T(8,128)(2,1)S(1)} %get-tuple-element.30), channel_id=1, source_target_pairs={{4,0},{8,4},{12,8},{5,1},{9,5},{13,9},{6,2},{10,6},{14,10},{7,3},{... | collective-permute-start | bytes 184328 | tf_op jit(solution)/shard_map/ppermute | solution.py:95
  143.3 11.4 %collective-permute-start.22 = (f32[8]{0:T(128)S(1)}, f32[8]{0:T(128)S(1)}, u32[]{:S(2)}, u32[]{:S(2)}) collective-permute-start(f32[8]{0:T(128)S(1)} %reduce_sum.72), channel_id=1, source_target_pairs={{0,4},{4,0},{8,12},{12,8},{1,5},{5,1},{9,13},{13,9},{2,6},{6,2},{1... | collective-permute-start | bytes 104 | tf_op jit(solution)/shard_map/ppermute | solution.py:25
  149.5 20.7 %collective-permute-start.19 = (bf16[3,10,80,128]{3,2,1,0:T(8,128)(2,1)}, bf16[3,10,80,128]{3,2,1,0:T(8,128)(2,1)S(1)}, u32[]{:S(2)}, u32[]{:S(2)}) collective-permute-start(bf16[3,10,80,128]{3,2,1,0:T(8,128)(2,1)} %pad_maximum_fusion.1), channel_id=1, source_target_pairs={{0,2},{2,0},{1,3},{3,1},{4,6},{6,4},{5,7},{7,5},{8,10},{10,8},{9,1... | collective-permute-start | bytes 1843208 | tf_op jit(solution)/shard_map/ppermute | solution.py:62
  160.7 6.8 %collective-permute-start.26 = (f32[2,8]{1,0:T(2,128)S(1)}, f32[2,8]{1,0:T(2,128)S(1)}, u32[]{:S(2)}, u32[]{:S(2)}) collective-permute-start(f32[2,8]{1,0:T(2,128)S(1)} %pad_maximum_fusion.2), channel_id=1, source_target_pairs={{0,2},{2,0},{1,3},{3,1},{4,6},{6,4},{5,7},{7,5},{8,10},{10,8},{9,1... | collective-permute-start | bytes 200 | tf_op jit(solution)/shard_map/ppermute | solution.py:62
  161.4 9.3 %collective-permute-start.28 = (f32[2,8]{1,0:T(2,128)S(1)}, f32[2,8]{1,0:T(2,128)S(1)}, u32[]{:S(2)}, u32[]{:S(2)}) collective-permute-start(f32[2,8]{1,0:T(2,128)S(1)} %pad_maximum_fusion.2), channel_id=1, source_target_pairs={{0,1},{1,0},{2,3},{3,2},{4,5},{5,4},{6,7},{7,6},{8,9},{9,8},{10,11... | collective-permute-start | bytes 200 | tf_op jit(solution)/shard_map/ppermute | solution.py:66
  201.8 6.2 %collective-permute-start.33 = (bf16[3,2,80,128]{3,2,1,0:T(8,128)(2,1)S(1)}, bf16[3,2,80,128]{3,2,1,0:T(8,128)(2,1)S(1)}, u32[]{:S(2)}, u32[]{:S(2)}) collective-permute-start(bf16[3,2,80,128]{3,2,1,0:T(8,128)(2,1)S(1)} %get-tuple-element.26), channel_id=1, source_target_pairs={{0,2},{1,3},{2,0},{3,1},{4,6},{5,7},{6,4},{7,5},{8,10},{9,11},{10,... | collective-permute-start | bytes 368648 | tf_op jit(solution)/shard_map/ppermute | solution.py:191
  202.8 6.2 %collective-permute-start.34 = (bf16[3,2,80,128]{3,2,1,0:T(8,128)(2,1)S(1)}, bf16[3,2,80,128]{3,2,1,0:T(8,128)(2,1)S(1)}, u32[]{:S(2)}, u32[]{:S(2)}) collective-permute-start(bf16[3,2,80,128]{3,2,1,0:T(8,128)(2,1)S(1)} %get-tuple-element.25), channel_id=1, source_target_pairs={{0,3},{1,0},{2,1},{3,2},{4,7},{5,4},{6,5},{7,6},{8,11},{9,8},{10,9... | collective-permute-start | bytes 368648 | tf_op jit(solution)/shard_map/ppermute | solution.py:191
  (24 other events, 268.5 us)
Sparse Core Ops, SparseCore 0:
  21.9 44.0 all-gather.5
  67.6 71.2 all-gather.3

commit v9 on v7

--- a/solution.py
+++ b/solution.py
@@ -96,20 +96,24 @@
 
 
 def conv_body(x_ref, w_ref, b_ref, o_ref, acc_ref):
-    step = pl.program_id(0)
-    rows, cols, outs = o_ref.shape[1:]
+    frames, rows, cols, outs = o_ref.shape
     chans = x_ref.shape[-1]
     acc_ref[...] = jnp.broadcast_to(b_ref[...], acc_ref.shape)
-    for i in range(3):
-        for j in range(3):
-            for k in range(3):
-                patch = x_ref[step + i, pl.ds(j, rows), pl.ds(k, cols), :]
-                acc_ref[...] += jnp.dot(
-                    patch.reshape(rows * cols, chans),
-                    w_ref[9 * i + 3 * j + k],
-                    preferred_element_type=jnp.float32,
-                )
-    o_ref[0] = acc_ref[...].reshape(rows, cols, outs).astype(o_ref.dtype)
+
+    def tap_row(index, carry):
+        i = index // 3
+        j = index % 3
+        for k in range(3):
+            patch = x_ref[pl.ds(i, frames), pl.ds(j, rows), pl.ds(k, cols), :]
+            acc_ref[...] += jnp.dot(
+                patch.reshape(frames * rows * cols, chans),
+                w_ref[3 * index + k],
+                preferred_element_type=jnp.float32,
+            )
+        return carry
+
+    lax.fori_loop(0, 9, tap_row, 0)
+    o_ref[...] = acc_ref[...].reshape(frames, rows, cols, outs).astype(o_ref.dtype)
 
 
 def causal_conv(extended, kernel, bias, out_dtype):
@@ -123,15 +127,15 @@
     moved = padded.size * 2 + kernel.size * 2 + frames * rows * cols * outs * 4
     return pl.pallas_call(
         conv_body,
-        grid=(frames,),
+        grid=(1,),
         in_specs=[
             pl.BlockSpec(padded.shape, lambda t: (0, 0, 0, 0)),
             pl.BlockSpec(kernel.shape, lambda t: (0, 0, 0)),
             pl.BlockSpec((1, outs), lambda t: (0, 0)),
         ],
-        out_specs=pl.BlockSpec((1, rows, cols, outs), lambda t: (t, 0, 0, 0)),
+        out_specs=pl.BlockSpec((frames, rows, cols, outs), lambda t: (0, 0, 0, 0)),
         out_shape=jax.ShapeDtypeStruct((frames, rows, cols, outs), out_dtype),
-        scratch_shapes=[pltpu.VMEM((rows * cols, outs), jnp.float32)],
+        scratch_shapes=[pltpu.VMEM((frames * rows * cols, outs), jnp.float32)],
         cost_estimate=pl.CostEstimate(flops=flops, bytes_accessed=moved, transcendentals=0),
     )(padded, kernel, bias.reshape(1, outs))
 

time: 210 us -> 211 us (level)
  starting transfers between devices: 48 us -> 42.6 us
  waiting for transfers between devices: 64.6 us -> 68.5 us
  Pallas kernels: 37 us -> 40.3 us
    ppermute x6, starting transfers between devices: 12.3 us -> 7.01 us  [chip_gather(): lax.ppermute(firsts, 'hb', shift_pairs(count_b, step))]
    pallas_call x2, Pallas kernels: 37 us -> 40.3 us  [causal_conv(): pl.pallas_call(conv_body, grid=(1,), in_specs=[pl.BlockSpec(padded.shape,...]
    ppermute x3, waiting for transfers between devices: 0.01 us -> 3.28 us  [chip_gather(): firsts.append(lax.ppermute(block, 'ha', shift_pairs(count_a, step)))]
  transfers between devices with their start and end apart: 36 -> 36, of which waited for: 20 -> 22; matrix products, arithmetic and copies ran while one was open for 18% -> 17% of each run, Pallas kernels for 9% -> 10%
where the time goes in v9:
time: 211 us
  waiting for transfers between devices  68.5 us (32%)
  starting transfers between devices  42.6 us (20%)
  Pallas kernels  40.3 us (19%)
  local copies, waits for them, and re-layouts  29.4 us (14%)
  other arithmetic  16.1 us (8%)
  between operations  13.9 us (7%)
    pallas_call x2, Pallas kernels, causal_conv(): pl.pallas_call(conv_body, grid=(1,), in_specs=[pl.BlockSpec(padded.shape,...  40.3 us
    all_gather x2, waiting for transfers between devices, kernel_block(): return lax.all_gather(out, 'hz', axis=1, tiled=True)  20.7 us
    ppermute x12, waiting for transfers between devices, butterfly_stats(): other_sums, other_squares = lax.ppermute((sums, squares), axis, pairs)  14.9 us
    ppermute x2, waiting for transfers between devices, with_row_halo(): bottom = lax.ppermute(cells[:, :1], axis_name, up)  14.7 us
    ppermute x12, starting transfers between devices, butterfly_stats(): other_sums, other_squares = lax.ppermute((sums, squares), axis, pairs)  11.4 us
    dynamic_update_slice x11, local copies, waits for them, and re-layouts, chip_gather(): out = lax.dynamic_update_slice(out, piece, start)  9.92 us
    ppermute x6, waiting for transfers between devices, kernel_block(): piece = lax.ppermute(piece, HQ, shift_pairs(size, step))  8.4 us
    ppermute x2, starting transfers between devices, with_row_halo(): top = lax.ppermute(cells[:, -1:], axis_name, down)  8.17 us
  transfers between devices with their start and end apart: 36, of which 22 were waited for; matrix products, arithmetic and copies ran while one was open for 17% of the time, Pallas kernels for 10%

profile of v9, /device:TPU:1, one launch (start us, length us, event | category | flops | bytes accessed | tf_op | source)
XLA Modules:
  0.0 210.7 jit_solution(16311766503452719781)
XLA Ops:
  8.3 2.7 %collective-permute-start.13 = (bf16[27,32,128]{2,1,0:T(8,128)(2,1)S(1)}, bf16[27,32,128]{2,1,0:T(8,128)(2,1)}, u32[]{:S(2)}, u32[]{:S(2)}) collective-permute-start(bf16[27,32,128]{2,1,0:T(8,128)(2,1)S(1)} %get-tuple-element.12), channel_id=1, source_target_pairs={{0,1},{1,2},{2,3},{3,0},{4,5},{5,6},{6,7},{7,4},{8,9},{9,10},{10,1... | collective-permute-start | bytes 663560 | tf_op jit(solution)/shard_map/ppermute | solution.py:153
  11.5 4.2 %collective-permute-done.13 = bf16[27,32,128]{2,1,0:T(8,128)(2,1)} collective-permute-done((bf16[27,32,128]{2,1,0:T(8,128)(2,1)S(1)}, bf16[27,32,128]{2,1,0:T(8,128)(2,1)}, u32[]{:S(2)}, u32[]{:S(2)}) %collective-permute-start.13) | collective-permute-done | bytes 221216 | tf_op jit(solution)/shard_map/ppermute | solution.py:153
  16.6 3.8 %collective-permute-done.14 = bf16[27,32,128]{2,1,0:T(8,128)(2,1)S(1)} collective-permute-done((bf16[27,32,128]{2,1,0:T(8,128)(2,1)S(1)}, bf16[27,32,128]{2,1,0:T(8,128)(2,1)S(1)}, u32[]{:S(2)}, u32[]{:S(2)}) %collective-permute-start.14) | collective-permute-done | bytes 221216 | tf_op jit(solution)/shard_map/ppermute | solution.py:153
  21.9 2.1 collective-permute-start
  29.5 6.1 %collective-permute-done.5 = f32[32]{0:T(128)S(1)} collective-permute-done((f32[32]{0:T(128)S(1)}, f32[32]{0:T(128)S(1)}, u32[]{:S(2)}, u32[]{:S(2)}) %collective-permute-start.5) | collective-permute-done | bytes 160 | tf_op jit(solution)/shard_map/ppermute | solution.py:25
  46.1 2.3 %collective-permute-done.12 = f32[32]{0:T(128)S(1)} collective-permute-done((f32[32]{0:T(128)S(1)}, f32[32]{0:T(128)S(1)}, u32[]{:S(2)}, u32[]{:S(2)}) %collective-permute-start.12) | collective-permute-done | bytes 160 | tf_op jit(solution)/shard_map/ppermute | solution.py:25
  56.0 4.0 %collective-permute-start.3 = (bf16[3,1,80,512]{3,2,1,0:T(8,128)(2,1)}, bf16[3,1,80,512]{3,2,1,0:T(8,128)(2,1)S(1)}, u32[]{:S(2)}, u32[]{:S(2)}) collective-permute-start(bf16[3,1,80,512]{3,2,1,0:T(8,128)(2,1)} %get-tuple-element.5), channel_id=1, source_target_pairs={{0,4},{4,8},{8,12},{1,5},{5,9},{9,13},{2,6},{6,10},{10,14},{3,7},{... | collective-permute-start | bytes 737288 | tf_op jit(solution)/shard_map/ppermute | solution.py:93
  64.0 12.2 %collective-permute-done.4 = bf16[3,1,80,512]{3,2,1,0:T(8,128)(2,1)S(1)} collective-permute-done((bf16[3,1,80,512]{3,2,1,0:T(8,128)(2,1)}, bf16[3,1,80,512]{3,2,1,0:T(8,128)(2,1)S(1)}, u32[]{:S(2)}, u32[]{:S(2)}) %collective-permute-start.4) | collective-permute-done | bytes 245792 | tf_op jit(solution)/shard_map/ppermute | solution.py:94
  78.2 3.2 %fusion.5.x_ref = bf16[5,10,82,512]{3,2,1,0:T(8,128)(2,1)} fusion(bf16[3,10,80,512]{3,2,1,0:T(8,128)(2,1)S(1)} %fusion.6, bf16[1,10,80,512]{3,2,1,0:T(8,128)(2,1)S(1)} %slice.36), kind=kLoop, calls=%fused_computation.11 | loop fusion | flops 25190400 | bytes 7475200 | tf_op jit(solution)/shard_map/concatenate | solution.py:120
  81.4 17.3 %all-gather.3.cloned.1.call-done.w_ref = bf16[27,512,128]{2,1,0:T(8,128)(2,1)} async-done(((bf16[27,128,128]{2,1,0:T(8,128)(2,1)}), bf16[27,512,128]{2,1,0:T(8,128)(2,1)}) %all-gather.3.cloned.1.call-update) | async-done | bytes 3538960 | tf_op jit(solution)/shard_map/all_gather | solution.py:156
  98.7 20.0 %shard_map.91 = bf16[3,8,80,128]{3,2,1,0:T(8,128)(2,1)} custom-call(bf16[5,10,82,512]{3,2,1,0:T(8,128)(2,1)} %fusion.5.x_ref, bf16[27,512,128]{2,1,0:T(8,128)(2,1)} %all-gather.3.cloned.1.call-done.w_ref, f32[1,128]{1,0:T(1,128)} %dynamic-slice_bitcast_fusion.1.b_ref), custom_call_target="tpu_custom_call" | custom-call | flops 6794772480 | bytes 8720384 | tf_op jit(solution)/shard_map/pallas_call | solution.py:128
  120.9 4.2 %collective-permute-start.16 = (bf16[3,1,80,128]{3,2,1,0:T(8,128)(2,1)S(1)}, bf16[3,1,80,128]{3,2,1,0:T(8,128)(2,1)S(1)}, u32[]{:S(2)}, u32[]{:S(2)}) collective-permute-start(bf16[3,1,80,128]{3,2,1,0:T(8,128)(2,1)S(1)} %get-tuple-element.21), channel_id=1, source_target_pairs={{0,4},{4,8},{8,12},{1,5},{5,9},{9,13},{2,6},{6,10},{10,14},{3,7},{... | collective-permute-start | bytes 184328 | tf_op jit(solution)/shard_map/ppermute | solution.py:93
  126.4 2.5 %collective-permute-done.17 = bf16[3,1,80,128]{3,2,1,0:T(8,128)(2,1)S(1)} collective-permute-done((bf16[3,1,80,128]{3,2,1,0:T(8,128)(2,1)S(1)}, bf16[3,1,80,128]{3,2,1,0:T(8,128)(2,1)S(1)}, u32[]{:S(2)}, u32[]{:S(2)}) %collective-permute-start.17) | collective-permute-done | bytes 61472 | tf_op jit(solution)/shard_map/ppermute | solution.py:94
  130.7 2.0 pad_maximum_fusion
  138.9 3.1 %collective-permute-start.22 = (f32[8]{0:T(128)S(1)}, f32[8]{0:T(128)S(1)}, u32[]{:S(2)}, u32[]{:S(2)}) collective-permute-start(f32[8]{0:T(128)S(1)} %get-tuple-element.28), channel_id=1, source_target_pairs={{0,8},{4,12},{8,0},{12,4},{1,9},{5,13},{9,1},{13,5},{2,10},{6,14},... | collective-permute-start | bytes 104 | tf_op jit(solution)/shard_map/ppermute | solution.py:25
  142.1 3.0 %collective-permute-start.19 = (bf16[3,10,80,128]{3,2,1,0:T(8,128)(2,1)S(1)}, bf16[3,10,80,128]{3,2,1,0:T(8,128)(2,1)}, u32[]{:S(2)}, u32[]{:S(2)}) collective-permute-start(bf16[3,10,80,128]{3,2,1,0:T(8,128)(2,1)S(1)} %get-tuple-element.15), channel_id=1, source_target_pairs={{0,1},{1,0},{2,3},{3,2},{4,5},{5,4},{6,7},{7,6},{8,9},{9,8},{10,11... | collective-permute-start | bytes 1843208 | tf_op jit(solution)/shard_map/ppermute | solution.py:71
  145.1 2.4 %collective-permute-done.18 = bf16[3,10,80,128]{3,2,1,0:T(8,128)(2,1)} collective-permute-done((bf16[3,10,80,128]{3,2,1,0:T(8,128)(2,1)S(1)}, bf16[3,10,80,128]{3,2,1,0:T(8,128)(2,1)}, u32[]{:S(2)}, u32[]{:S(2)}) %collective-permute-start.18) | collective-permute-done | bytes 614432 | tf_op jit(solution)/shard_map/ppermute | solution.py:66
  160.4 3.2 %fusion.7 = bf16[3,10,80,512]{3,2,1,0:T(8,128)(2,1)S(1)} fusion(bf16[3,10,80,512]{3,2,1,0:T(8,128)(2,1)} %constant_dynamic-update-slice_fusion.6, f32[512]{0:T(512)S(1)} %copy-done.8, f32[512]{0:T(512)S(1)} %copy-done.9, f32[512]{0:T(512)S(1)} %mul.221, f32[512]{0:T(512)S(1)} %sub.111, pred[10]{0:T(512)(128)(4,1)S(1)} %or_and_fusion), kind=kLoop, calls=%fused_computation.13 | loop fusion | flops 13516800 | bytes 4923402 | tf_op jit(solution)/shard_map/jit(_where)/select_n | solution.py:86
  163.6 3.2 %select_maximum_fusion.x_ref = bf16[5,10,82,512]{3,2,1,0:T(8,128)(2,1)} fusion(bf16[3,10,80,512]{3,2,1,0:T(8,128)(2,1)S(1)} %fusion.7, bf16[1,10,80,512]{3,2,1,0:T(8,128)(2,1)S(1)} %slice.39), kind=kLoop, calls=%fused_computation.5 | loop fusion | flops 25190400 | bytes 7475200 | tf_op jit(solution)/shard_map/concatenate | solution.py:120
  166.8 3.4 %all-gather.5.cloned.1.call-done.w_ref = bf16[27,512,128]{2,1,0:T(8,128)(2,1)} async-done(((bf16[27,128,128]{2,1,0:T(8,128)(2,1)}), bf16[27,512,128]{2,1,0:T(8,128)(2,1)}) %all-gather.5.cloned.1.call-update) | async-done | bytes 3538960 | tf_op jit(solution)/shard_map/all_gather | solution.py:156
  170.2 20.2 %shard_map.92 = f32[3,8,80,128]{3,2,1,0:T(8,128)} custom-call(bf16[5,10,82,512]{3,2,1,0:T(8,128)(2,1)} %select_maximum_fusion.x_ref, bf16[27,512,128]{2,1,0:T(8,128)(2,1)} %all-gather.5.cloned.1.call-done.w_ref, f32[1,128]{1,0:T(1,128)} %dynamic-slice_bitcast_fusion.b_ref), custom_call_target="tpu_custom_call" | custom-call | flops 6794772480 | bytes 8720384 | tf_op jit(solution)/shard_map/pallas_call | solution.py:128
  194.1 2.1 collective-permute-done.31
  196.2 3.3 %collective-permute-done.32 = bf16[3,2,80,128]{3,2,1,0:T(8,128)(2,1)S(1)} collective-permute-done((bf16[3,2,80,128]{3,2,1,0:T(8,128)(2,1)S(1)}, bf16[3,2,80,128]{3,2,1,0:T(8,128)(2,1)S(1)}, u32[]{:S(2)}, u32[]{:S(2)}) %collective-permute-start.32) | collective-permute-done | bytes 122912 | tf_op jit(solution)/shard_map/ppermute | solution.py:168
  201.7 2.2 %reshape.59 = bf16[3,4,160,512]{3,2,1,0:T(8,128)(2,1)} reshape(bf16[3,4,80,2,512]{4,3,2,1,0:T(2,128)(2,1)S(1)} %broadcast_in_dim.53) | data formatting | bytes 3932160 | tf_op jit(solution)/shard_map/reshape | solution.py:215
  (151 shorter events, 64.4 us)
Async XLA Ops:
  6.5 92.1 %all-gather.3.cloned.1.call-start = ((), (), s32[]{:S(2)}) async-start(), calls=%async_computation | async-start | bytes 4423680 | tf_op jit(solution)/shard_map/all_gather | solution.py:156
  8.3 7.3 %collective-permute-start.13 = (bf16[27,32,128]{2,1,0:T(8,128)(2,1)S(1)}, bf16[27,32,128]{2,1,0:T(8,128)(2,1)}, u32[]{:S(2)}, u32[]{:S(2)}) collective-permute-start(bf16[27,32,128]{2,1,0:T(8,128)(2,1)S(1)} %get-tuple-element.12), channel_id=1, source_target_pairs={{0,1},{1,2},{2,3},{3,0},{4,5},{5,6},{6,7},{7,4},{8,9},{9,10},{10,1... | collective-permute-start | bytes 663560 | tf_op jit(solution)/shard_map/ppermute | solution.py:153
  11.0 9.4 %collective-permute-start.14 = (bf16[27,32,128]{2,1,0:T(8,128)(2,1)S(1)}, bf16[27,32,128]{2,1,0:T(8,128)(2,1)S(1)}, u32[]{:S(2)}, u32[]{:S(2)}) collective-permute-start(bf16[27,32,128]{2,1,0:T(8,128)(2,1)S(1)} %get-tuple-element.14), channel_id=1, source_target_pairs={{0,2},{1,3},{2,0},{3,1},{4,6},{5,7},{6,4},{7,5},{8,10},{9,11},{10,... | collective-permute-start | bytes 663560 | tf_op jit(solution)/shard_map/ppermute | solution.py:153
  11.0 9.9 %collective-permute-start.15 = (bf16[27,32,128]{2,1,0:T(8,128)(2,1)S(1)}, bf16[27,32,128]{2,1,0:T(8,128)(2,1)S(1)}, u32[]{:S(2)}, u32[]{:S(2)}) collective-permute-start(bf16[27,32,128]{2,1,0:T(8,128)(2,1)S(1)} %get-tuple-element.11), channel_id=1, source_target_pairs={{0,3},{1,0},{2,1},{3,2},{4,7},{5,4},{6,5},{7,6},{8,11},{9,8},{10,9... | collective-permute-start | bytes 663560 | tf_op jit(solution)/shard_map/ppermute | solution.py:153
  21.9 148.3 %all-gather.5.cloned.1.call-start = ((), (), s32[]{:S(2)}) async-start(), calls=%async_computation.1 | async-start | bytes 4423680 | tf_op jit(solution)/shard_map/all_gather | solution.py:156
  21.9 17.4 %collective-permute-start = (bf16[3,2,80,512]{3,2,1,0:T(8,128)(2,1)S(1)}, bf16[3,2,80,512]{3,2,1,0:T(8,128)(2,1)}, u32[]{:S(2)}, u32[]{:S(2)}) collective-permute-start(bf16[3,2,80,512]{3,2,1,0:T(8,128)(2,1)S(1)} %copy-done.2), channel_id=1, source_target_pairs={{0,2},{2,0},{1,3},{3,1},{4,6},{6,4},{5,7},{7,5},{8,10},{10,8},{9,1... | collective-permute-start | bytes 1474568 | tf_op jit(solution)/shard_map/ppermute | solution.py:66
  24.0 27.7 %collective-permute-start.1 = (bf16[3,2,80,512]{3,2,1,0:T(8,128)(2,1)S(1)}, bf16[3,2,80,512]{3,2,1,0:T(8,128)(2,1)}, u32[]{:S(2)}, u32[]{:S(2)}) collective-permute-start(bf16[3,2,80,512]{3,2,1,0:T(8,128)(2,1)S(1)} %copy-done.2), channel_id=1, source_target_pairs={{0,1},{1,0},{2,3},{3,2},{4,5},{5,4},{6,7},{7,6},{8,9},{9,8},{10,11... | collective-permute-start | bytes 1474568 | tf_op jit(solution)/shard_map/ppermute | solution.py:71
  24.3 11.3 %collective-permute-start.5 = (f32[32]{0:T(128)S(1)}, f32[32]{0:T(128)S(1)}, u32[]{:S(2)}, u32[]{:S(2)}) collective-permute-start(f32[32]{0:T(128)S(1)} %reduce_sum.51), channel_id=1, source_target_pairs={{0,2},{2,0},{1,3},{3,1},{4,6},{6,4},{5,7},{7,5},{8,10},{10,8},{9,1... | collective-permute-start | bytes 392 | tf_op jit(solution)/shard_map/ppermute | solution.py:25
  25.1 10.4 %collective-permute-start.9 = (f32[32]{0:T(128)S(1)}, f32[32]{0:T(128)S(1)}, u32[]{:S(2)}, u32[]{:S(2)}) collective-permute-start(f32[32]{0:T(128)S(1)} %reduce_sum.54), channel_id=1, source_target_pairs={{0,2},{2,0},{1,3},{3,1},{4,6},{6,4},{5,7},{7,5},{8,10},{10,8},{9,1... | collective-permute-start | bytes 392 | tf_op jit(solution)/shard_map/ppermute | solution.py:25
  27.6 32.4 %collective-permute-start.28 = (bf16[27,32,128]{2,1,0:T(8,128)(2,1)}, bf16[27,32,128]{2,1,0:T(8,128)(2,1)}, u32[]{:S(2)}, u32[]{:S(2)}) collective-permute-start(bf16[27,32,128]{2,1,0:T(8,128)(2,1)} %get-tuple-element.8), channel_id=1, source_target_pairs={{0,1},{1,2},{2,3},{3,0},{4,5},{5,6},{6,7},{7,4},{8,9},{9,10},{10,1... | collective-permute-start | bytes 663560 | tf_op jit(solution)/shard_map/ppermute | solution.py:153
  39.3 13.5 %collective-permute-start.2 = (bf16[3,2,80,512]{3,2,1,0:T(8,128)(2,1)}, bf16[3,2,80,512]{3,2,1,0:T(8,128)(2,1)}, u32[]{:S(2)}, u32[]{:S(2)}) collective-permute-start(bf16[3,2,80,512]{3,2,1,0:T(8,128)(2,1)} %collective-permute-done), channel_id=1, source_target_pairs={{0,1},{1,0},{2,3},{3,2},{4,5},{5,4},{6,7},{7,6},{8,9},{9,8},{10,11... | collective-permute-start | bytes 1474568 | tf_op jit(solution)/shard_map/ppermute | solution.py:71
  45.7 15.3 %collective-permute-start.29 = (bf16[27,32,128]{2,1,0:T(8,128)(2,1)}, bf16[27,32,128]{2,1,0:T(8,128)(2,1)}, u32[]{:S(2)}, u32[]{:S(2)}) collective-permute-start(bf16[27,32,128]{2,1,0:T(8,128)(2,1)} %get-tuple-element.10), channel_id=1, source_target_pairs={{0,2},{1,3},{2,0},{3,1},{4,6},{5,7},{6,4},{7,5},{8,10},{9,11},{10,... | collective-permute-start | bytes 663560 | tf_op jit(solution)/shard_map/ppermute | solution.py:153
  48.5 13.6 %collective-permute-start.30 = (bf16[27,32,128]{2,1,0:T(8,128)(2,1)}, bf16[27,32,128]{2,1,0:T(8,128)(2,1)}, u32[]{:S(2)}, u32[]{:S(2)}) collective-permute-start(bf16[27,32,128]{2,1,0:T(8,128)(2,1)} %get-tuple-element.7), channel_id=1, source_target_pairs={{0,3},{1,0},{2,1},{3,2},{4,7},{5,4},{6,5},{7,6},{8,11},{9,8},{10,9... | collective-permute-start | bytes 663560 | tf_op jit(solution)/shard_map/ppermute | solution.py:153
  54.8 21.5 %collective-permute-start.4 = (bf16[3,1,80,512]{3,2,1,0:T(8,128)(2,1)}, bf16[3,1,80,512]{3,2,1,0:T(8,128)(2,1)S(1)}, u32[]{:S(2)}, u32[]{:S(2)}) collective-permute-start(bf16[3,1,80,512]{3,2,1,0:T(8,128)(2,1)} %get-tuple-element.6), channel_id=1, source_target_pairs={{4,0},{8,4},{12,8},{5,1},{9,5},{13,9},{6,2},{10,6},{14,10},{7,3},{... | collective-permute-start | bytes 737288 | tf_op jit(solution)/shard_map/ppermute | solution.py:94
  56.0 20.2 %collective-permute-start.3 = (bf16[3,1,80,512]{3,2,1,0:T(8,128)(2,1)}, bf16[3,1,80,512]{3,2,1,0:T(8,128)(2,1)S(1)}, u32[]{:S(2)}, u32[]{:S(2)}) collective-permute-start(bf16[3,1,80,512]{3,2,1,0:T(8,128)(2,1)} %get-tuple-element.5), channel_id=1, source_target_pairs={{0,4},{4,8},{8,12},{1,5},{5,9},{9,13},{2,6},{6,10},{10,14},{3,7},{... | collective-permute-start | bytes 737288 | tf_op jit(solution)/shard_map/ppermute | solution.py:93
  119.6 9.3 %collective-permute-start.17 = (bf16[3,1,80,128]{3,2,1,0:T(8,128)(2,1)S(1)}, bf16[3,1,80,128]{3,2,1,0:T(8,128)(2,1)S(1)}, u32[]{:S(2)}, u32[]{:S(2)}) collective-permute-start(bf16[3,1,80,128]{3,2,1,0:T(8,128)(2,1)S(1)} %get-tuple-element.22), channel_id=1, source_target_pairs={{4,0},{8,4},{12,8},{5,1},{9,5},{13,9},{6,2},{10,6},{14,10},{7,3},{... | collective-permute-start | bytes 184328 | tf_op jit(solution)/shard_map/ppermute | solution.py:94
  120.9 8.0 %collective-permute-start.16 = (bf16[3,1,80,128]{3,2,1,0:T(8,128)(2,1)S(1)}, bf16[3,1,80,128]{3,2,1,0:T(8,128)(2,1)S(1)}, u32[]{:S(2)}, u32[]{:S(2)}) collective-permute-start(bf16[3,1,80,128]{3,2,1,0:T(8,128)(2,1)S(1)} %get-tuple-element.21), channel_id=1, source_target_pairs={{0,4},{4,8},{8,12},{1,5},{5,9},{9,13},{2,6},{6,10},{10,14},{3,7},{... | collective-permute-start | bytes 184328 | tf_op jit(solution)/shard_map/ppermute | solution.py:93
  132.7 14.7 %collective-permute-start.18 = (bf16[3,10,80,128]{3,2,1,0:T(8,128)(2,1)S(1)}, bf16[3,10,80,128]{3,2,1,0:T(8,128)(2,1)}, u32[]{:S(2)}, u32[]{:S(2)}) collective-permute-start(bf16[3,10,80,128]{3,2,1,0:T(8,128)(2,1)S(1)} %get-tuple-element.15), channel_id=1, source_target_pairs={{0,2},{2,0},{1,3},{3,1},{4,6},{6,4},{5,7},{7,5},{8,10},{10,8},{9,1... | collective-permute-start | bytes 1843208 | tf_op jit(solution)/shard_map/ppermute | solution.py:66
  138.9 10.2 %collective-permute-start.22 = (f32[8]{0:T(128)S(1)}, f32[8]{0:T(128)S(1)}, u32[]{:S(2)}, u32[]{:S(2)}) collective-permute-start(f32[8]{0:T(128)S(1)} %get-tuple-element.28), channel_id=1, source_target_pairs={{0,8},{4,12},{8,0},{12,4},{1,9},{5,13},{9,1},{13,5},{2,10},{6,14},... | collective-permute-start | bytes 104 | tf_op jit(solution)/shard_map/ppermute | solution.py:25
  142.0 7.1 %collective-permute-start.24 = (f32[8]{0:T(128)S(1)}, f32[8]{0:T(128)S(1)}, u32[]{:S(2)}, u32[]{:S(2)}) collective-permute-start(f32[8]{0:T(128)S(1)} %get-tuple-element.27), channel_id=1, source_target_pairs={{0,8},{4,12},{8,0},{12,4},{1,9},{5,13},{9,1},{13,5},{2,10},{6,14},... | collective-permute-start | bytes 104 | tf_op jit(solution)/shard_map/ppermute | solution.py:25
  142.1 14.4 %collective-permute-start.19 = (bf16[3,10,80,128]{3,2,1,0:T(8,128)(2,1)S(1)}, bf16[3,10,80,128]{3,2,1,0:T(8,128)(2,1)}, u32[]{:S(2)}, u32[]{:S(2)}) collective-permute-start(bf16[3,10,80,128]{3,2,1,0:T(8,128)(2,1)S(1)} %get-tuple-element.15), channel_id=1, source_target_pairs={{0,1},{1,0},{2,3},{3,2},{4,5},{5,4},{6,7},{7,6},{8,9},{9,8},{10,11... | collective-permute-start | bytes 1843208 | tf_op jit(solution)/shard_map/ppermute | solution.py:71
  147.4 11.0 %collective-permute-start.20 = (bf16[3,10,80,128]{3,2,1,0:T(8,128)(2,1)}, bf16[3,10,80,128]{3,2,1,0:T(8,128)(2,1)}, u32[]{:S(2)}, u32[]{:S(2)}) collective-permute-start(bf16[3,10,80,128]{3,2,1,0:T(8,128)(2,1)} %collective-permute-done.18), channel_id=1, source_target_pairs={{0,1},{1,0},{2,3},{3,2},{4,5},{5,4},{6,7},{7,6},{8,9},{9,8},{10,11... | collective-permute-start | bytes 1843208 | tf_op jit(solution)/shard_map/ppermute | solution.py:71
  193.6 5.9 %collective-permute-start.32 = (bf16[3,2,80,128]{3,2,1,0:T(8,128)(2,1)S(1)}, bf16[3,2,80,128]{3,2,1,0:T(8,128)(2,1)S(1)}, u32[]{:S(2)}, u32[]{:S(2)}) collective-permute-start(bf16[3,2,80,128]{3,2,1,0:T(8,128)(2,1)S(1)} %get-tuple-element.18), channel_id=1, source_target_pairs={{0,2},{1,3},{2,0},{3,1},{4,6},{5,7},{6,4},{7,5},{8,10},{9,11},{10,... | collective-permute-start | bytes 368648 | tf_op jit(solution)/shard_map/ppermute | solution.py:168
  193.9 6.2 %collective-permute-start.33 = (bf16[3,2,80,128]{3,2,1,0:T(8,128)(2,1)S(1)}, bf16[3,2,80,128]{3,2,1,0:T(8,128)(2,1)S(1)}, u32[]{:S(2)}, u32[]{:S(2)}) collective-permute-start(bf16[3,2,80,128]{3,2,1,0:T(8,128)(2,1)S(1)} %get-tuple-element.17), channel_id=1, source_target_pairs={{0,3},{1,0},{2,1},{3,2},{4,7},{5,4},{6,5},{7,6},{8,11},{9,8},{10,9... | collective-permute-start | bytes 368648 | tf_op jit(solution)/shard_map/ppermute | solution.py:168
  (22 other events, 273.2 us)
Sparse Core Ops, SparseCore 0:
  22.0 76.6 all-gather.2
  100.2 69.8 all-gather.4

commit v10 on v6

--- a/solution.py
+++ b/solution.py
@@ -57,24 +57,25 @@
     count_b = lax.axis_size("hb")
     me_a = lax.axis_index("ha")
     me_b = lax.axis_index("hb")
-    width = block.shape[dim]
-    shape = list(block.shape)
-    shape[dim] = width * count_a * count_b
     firsts = [block]
-    sources = [me_a]
     for step in range(1, count_a):
         firsts.append(lax.ppermute(block, "ha", shift_pairs(count_a, step)))
-        sources.append((me_a - step) % count_a)
     firsts = tuple(firsts)
-    out = jnp.zeros(shape, block.dtype)
-    for step in range(count_b):
-        bundle = firsts if step == 0 else lax.ppermute(firsts, "hb", shift_pairs(count_b, step))
-        source_b = (me_b - step) % count_b
-        for piece, source_a in zip(bundle, sources):
-            start = [0] * len(shape)
-            start[dim] = (source_a * count_b + source_b) * width
-            out = lax.dynamic_update_slice(out, piece, start)
-    return out
+    bundles = [firsts]
+    for step in range(1, count_b):
+        bundles.append(lax.ppermute(firsts, "hb", shift_pairs(count_b, step)))
+    slots = []
+    for slot_a in range(count_a):
+        for slot_b in range(count_b):
+            piece = bundles[0][0]
+            for sb in range(count_b):
+                for sa in range(count_a):
+                    if sa == 0 and sb == 0:
+                        continue
+                    hit = ((me_a - sa) % count_a == slot_a) & ((me_b - sb) % count_b == slot_b)
+                    piece = jnp.where(hit, bundles[sb][sa], piece)
+            slots.append(piece)
+    return jnp.concatenate(slots, axis=dim)
 
 
 def edge_mask(cells):
@@ -137,12 +138,41 @@
 
 
 def kernel_block(shard, chans):
-    size = lax.axis_size("ha") * lax.axis_size("hb")
+    count_a = lax.axis_size("ha")
+    count_b = lax.axis_size("hb")
+    me_a = lax.axis_index("ha")
+    me_b = lax.axis_index("hb")
     taps, in_block, outs = shard.shape
-    width = outs // size
-    pieces = jnp.transpose(shard.reshape(taps, in_block, size, width), (2, 0, 1, 3))
-    pieces = lax.all_to_all(pieces, HQ, 0, 0, tiled=True)
-    out = jnp.transpose(pieces, (1, 0, 2, 3)).reshape(taps, size * in_block, width)
+    width = outs // (count_a * count_b)
+    row_width = width * count_b
+    firsts = []
+    for step in range(count_a):
+        target = (me_a + step) % count_a
+        piece = lax.dynamic_slice_in_dim(shard, target * row_width, row_width, axis=2)
+        if step:
+            piece = lax.ppermute(piece, "ha", shift_pairs(count_a, step))
+        firsts.append(piece)
+    seconds = []
+    for step in range(count_b):
+        target = (me_b + step) % count_b
+        bundle = tuple(
+            lax.dynamic_slice_in_dim(piece, target * width, width, axis=2) for piece in firsts
+        )
+        if step:
+            bundle = lax.ppermute(bundle, "hb", shift_pairs(count_b, step))
+        seconds.append(bundle)
+    slots = []
+    for slot_a in range(count_a):
+        for slot_b in range(count_b):
+            piece = seconds[0][0]
+            for sb in range(count_b):
+                for sa in range(count_a):
+                    if sa == 0 and sb == 0:
+                        continue
+                    hit = ((me_a - sa) % count_a == slot_a) & ((me_b - sb) % count_b == slot_b)
+                    piece = jnp.where(hit, seconds[sb][sa], piece)
+            slots.append(piece)
+    out = jnp.concatenate(slots, axis=1)
     return lax.all_gather(out, "hz", axis=1, tiled=True)
 
 

time: 212 us -> 212 us (level)
  blocking collectives: 15.9 us -> 0 us
  local copies, waits for them, and re-layouts: 26.3 us -> 14.1 us
  other arithmetic: 16.1 us -> 26.3 us
  waiting for transfers between devices: 64.9 us -> 73.7 us
  starting transfers between devices: 38 us -> 46.6 us
    all_to_all x1 -> x0, blocking collectives: 15.9 us -> none  [kernel_block(): pieces = lax.all_to_all(pieces, HQ, 0, 0, tiled=True)]
    ppermute x2, waiting for transfers between devices: 7.38 us -> 21.9 us  [with_row_halo(): bottom = lax.ppermute(cells[:, :1], axis_name, up)]
    all_gather x2, waiting for transfers between devices: 26.4 us -> 12.6 us  [kernel_block(): return lax.all_gather(out, 'hz', axis=1, tiled=True)]
    ppermute x6 -> x12, waiting for transfers between devices: 0.49 us -> 11 us  [the longest x2 7.73 us: kernel_block(): piece = lax.ppermute(piece, 'ha', shift_pairs(count_a, step))]
    dynamic_update_slice x11 -> x0, local copies, waits for them, and re-layouts: 9.93 us -> none  [chip_gather(): out = lax.dynamic_update_slice(out, piece, start)]
    ppermute x2, waiting for transfers between devices: 0.01 us -> 7.91 us  [with_row_halo(): top = lax.ppermute(cells[:, -1:], axis_name, down)]
    ppermute x6 -> x12, starting transfers between devices: 10.4 us -> 17.5 us  [the longest x6 8.3 us: chip_gather(): bundles.append(lax.ppermute(firsts, 'hb', shift_pairs(count_b, step)))]
    ppermute x3, waiting for transfers between devices: 6.26 us -> 0.01 us  [chip_gather(): firsts.append(lax.ppermute(block, 'ha', shift_pairs(count_a, step)))]
  transfers between devices with their start and end apart: 31 -> 36, of which waited for: 14 -> 21; matrix products, arithmetic and copies ran while one was open for 16% -> 15% of each run, Pallas kernels for 9% -> 9%
where the time goes in v10:
time: 212 us; the launch traced here: 211 us
  waiting for transfers between devices  73.7 us (35%)
  starting transfers between devices  46.6 us (22%)
  Pallas kernels  37 us (17%)
  other arithmetic  26.3 us (12%)
  local copies, waits for them, and re-layouts  14.1 us (7%)
  between operations  13.8 us (7%)
    pallas_call x2, Pallas kernels, causal_conv(): pl.pallas_call(conv_body, grid=(frames,), in_specs=[pl.BlockSpec(padded.s...  37 us
    ppermute x2, waiting for transfers between devices, with_row_halo(): bottom = lax.ppermute(cells[:, :1], axis_name, up)  21.9 us
    ppermute x12, waiting for transfers between devices, butterfly_stats(): other_sums, other_squares = lax.ppermute((sums, squares), axis, pairs)  14.3 us
    ppermute x12, starting transfers between devices, butterfly_stats(): other_sums, other_squares = lax.ppermute((sums, squares), axis, pairs)  13.8 us
    all_gather x2, waiting for transfers between devices, kernel_block(): return lax.all_gather(out, 'hz', axis=1, tiled=True)  12.6 us
    ppermute x6, starting transfers between devices, chip_gather(): bundles.append(lax.ppermute(firsts, 'hb', shift_pairs(count_b, step)))  8.3 us
    ppermute x2, waiting for transfers between devices, with_row_halo(): top = lax.ppermute(cells[:, -1:], axis_name, down)  7.91 us
    ppermute x2, waiting for transfers between devices, kernel_block(): piece = lax.ppermute(piece, 'ha', shift_pairs(count_a, step))  7.73 us
  transfers between devices with their start and end apart: 36, of which 21 were waited for; matrix products, arithmetic and copies ran while one was open for 15% of the time, Pallas kernels for 9%

profile of v10, /device:TPU:1, one launch (start us, length us, event | category | flops | bytes accessed | tf_op | source)
XLA Modules:
  0.0 211.4 jit_solution(6989259130204481606)
XLA Ops:
  7.7 2.1 %collective-permute-start.13 = (bf16[27,32,256]{2,1,0:T(8,128)(2,1)S(1)}, bf16[27,32,256]{2,1,0:T(8,128)(2,1)S(1)}, u32[]{:S(2)}, u32[]{:S(2)}) collective-permute-start(bf16[27,32,256]{2,1,0:T(8,128)(2,1)S(1)} %constant_dynamic-slice_fusion.8), channel_id=1, source_target_pairs={{0,2},{2,0},{1,3},{3,1},{4,6},{6,4},{5,7},{7,5},{8,10},{10,8},{9,1... | collective-permute-start | bytes 1327112 | tf_op jit(solution)/shard_map/ppermute | solution.py:153
  12.0 7.7 %collective-permute-done.13 = bf16[27,32,256]{2,1,0:T(8,128)(2,1)S(1)} collective-permute-done((bf16[27,32,256]{2,1,0:T(8,128)(2,1)S(1)}, bf16[27,32,256]{2,1,0:T(8,128)(2,1)S(1)}, u32[]{:S(2)}, u32[]{:S(2)}) %collective-permute-start.13) | collective-permute-done | bytes 442400 | tf_op jit(solution)/shard_map/ppermute | solution.py:153
  32.2 5.0 %collective-permute-done.5 = f32[32]{0:T(128)S(1)} collective-permute-done((f32[32]{0:T(128)S(1)}, f32[32]{0:T(128)S(1)}, u32[]{:S(2)}, u32[]{:S(2)}) %collective-permute-start.5) | collective-permute-done | bytes 160 | tf_op jit(solution)/shard_map/ppermute | solution.py:25
  37.2 2.1 %collective-permute-start.6 = (f32[32]{0:T(128)S(1)}, f32[32]{0:T(128)S(1)}, u32[]{:S(2)}, u32[]{:S(2)}) collective-permute-start(f32[32]{0:T(128)S(1)} %get-tuple-element.45), channel_id=1, source_target_pairs={{0,1},{1,0},{2,3},{3,2},{4,5},{5,4},{6,7},{7,6},{8,9},{9,8},{10,11... | collective-permute-start | bytes 392 | tf_op jit(solution)/shard_map/ppermute | solution.py:25
  44.8 2.3 %collective-permute-start.8 = (f32[32]{0:T(128)S(1)}, f32[32]{0:T(128)S(1)}, u32[]{:S(2)}, u32[]{:S(2)}) collective-permute-start(f32[32]{0:T(128)S(1)} %get-tuple-element.41), channel_id=1, source_target_pairs={{0,8},{4,12},{8,0},{12,4},{1,9},{5,13},{9,1},{13,5},{2,10},{6,14},... | collective-permute-start | bytes 392 | tf_op jit(solution)/shard_map/ppermute | solution.py:25
  48.5 2.7 %collective-permute-start.30 = (bf16[27,32,128]{2,1,0:T(8,128)(2,1)}, bf16[27,32,128]{2,1,0:T(8,128)(2,1)}, u32[]{:S(2)}, u32[]{:S(2)}) collective-permute-start(bf16[27,32,128]{2,1,0:T(8,128)(2,1)} %constant_dynamic-slice_fusion.3), channel_id=1, source_target_pairs={{0,1},{1,0},{2,3},{3,2},{4,5},{5,4},{6,7},{7,6},{8,9},{9,8},{10,11... | collective-permute-start | bytes 663560 | tf_op jit(solution)/shard_map/ppermute | solution.py:162
  52.4 2.0 collective-permute-start.29
  55.3 3.5 %collective-permute-start.3 = (bf16[3,1,80,512]{3,2,1,0:T(8,128)(2,1)}, bf16[3,1,80,512]{3,2,1,0:T(8,128)(2,1)}, u32[]{:S(2)}, u32[]{:S(2)}) collective-permute-start(bf16[3,1,80,512]{3,2,1,0:T(8,128)(2,1)} %slice.34), channel_id=1, source_target_pairs={{0,4},{4,8},{8,12},{1,5},{5,9},{9,13},{2,6},{6,10},{10,14},{3,7},{... | collective-permute-start | bytes 737288 | tf_op jit(solution)/shard_map/ppermute | solution.py:94
  61.3 7.9 %collective-permute-done.3 = bf16[3,1,80,512]{3,2,1,0:T(8,128)(2,1)} collective-permute-done((bf16[3,1,80,512]{3,2,1,0:T(8,128)(2,1)}, bf16[3,1,80,512]{3,2,1,0:T(8,128)(2,1)}, u32[]{:S(2)}, u32[]{:S(2)}) %collective-permute-start.3) | collective-permute-done | bytes 245792 | tf_op jit(solution)/shard_map/ppermute | solution.py:94
  73.2 21.1 %collective-permute-done.4 = bf16[3,1,80,512]{3,2,1,0:T(8,128)(2,1)S(1)} collective-permute-done((bf16[3,1,80,512]{3,2,1,0:T(8,128)(2,1)S(1)}, bf16[3,1,80,512]{3,2,1,0:T(8,128)(2,1)S(1)}, u32[]{:S(2)}, u32[]{:S(2)}) %collective-permute-start.4) | collective-permute-done | bytes 245792 | tf_op jit(solution)/shard_map/ppermute | solution.py:95
  96.3 3.1 %fusion.5.x_ref = bf16[5,10,82,512]{3,2,1,0:T(8,128)(2,1)} fusion(bf16[3,10,80,512]{3,2,1,0:T(8,128)(2,1)S(1)} %fusion.6, bf16[1,10,80,512]{3,2,1,0:T(8,128)(2,1)S(1)} %slice.36), kind=kLoop, calls=%fused_computation.11 | loop fusion | flops 25190400 | bytes 7475200 | tf_op jit(solution)/shard_map/concatenate | solution.py:117
  101.1 18.4 %shard_map.91 = bf16[3,8,80,128]{3,2,1,0:T(8,128)(2,1)} custom-call(bf16[5,10,82,512]{3,2,1,0:T(8,128)(2,1)} %fusion.5.x_ref, bf16[27,512,128]{2,1,0:T(8,128)(2,1)} %all-gather.3.cloned.1.call-done.w_ref, f32[1,128]{1,0:T(1,128)} %dynamic-slice_bitcast_fusion.1.b_ref), custom_call_target="tpu_custom_call" | custom-call | flops 6794772480 | bytes 8720384 | tf_op jit(solution)/shard_map/pallas_call | solution.py:125
  121.8 4.2 %collective-permute-start.16 = (bf16[3,1,80,128]{3,2,1,0:T(8,128)(2,1)S(1)}, bf16[3,1,80,128]{3,2,1,0:T(8,128)(2,1)S(1)}, u32[]{:S(2)}, u32[]{:S(2)}) collective-permute-start(bf16[3,1,80,128]{3,2,1,0:T(8,128)(2,1)S(1)} %get-tuple-element.27), channel_id=1, source_target_pairs={{0,4},{4,8},{8,12},{1,5},{5,9},{9,13},{2,6},{6,10},{10,14},{3,7},{... | collective-permute-start | bytes 184328 | tf_op jit(solution)/shard_map/ppermute | solution.py:94
  133.1 2.5 %collective-permute-start.23 = (f32[8]{0:T(128)S(1)}, f32[8]{0:T(128)S(1)}, u32[]{:S(2)}, u32[]{:S(2)}) collective-permute-start(f32[8]{0:T(128)S(1)} %reduce_sum.75), channel_id=1, source_target_pairs={{0,4},{4,0},{8,12},{12,8},{1,5},{5,1},{9,13},{13,9},{2,6},{6,2},{1... | collective-permute-start | bytes 104 | tf_op jit(solution)/shard_map/ppermute | solution.py:25
  137.0 3.4 %collective-permute-start.22 = (f32[8]{0:T(128)S(1)}, f32[8]{0:T(128)S(1)}, u32[]{:S(2)}, u32[]{:S(2)}) collective-permute-start(f32[8]{0:T(128)S(1)} %get-tuple-element.37), channel_id=1, source_target_pairs={{0,8},{4,12},{8,0},{12,4},{1,9},{5,13},{9,1},{13,5},{2,10},{6,14},... | collective-permute-start | bytes 104 | tf_op jit(solution)/shard_map/ppermute | solution.py:25
  141.9 2.2 %collective-permute-done.24 = f32[8]{0:T(128)S(1)} collective-permute-done((f32[8]{0:T(128)S(1)}, f32[8]{0:T(128)S(1)}, u32[]{:S(2)}, u32[]{:S(2)}) %collective-permute-start.24) | collective-permute-done | bytes 64 | tf_op jit(solution)/shard_map/ppermute | solution.py:25
  144.2 4.3 %collective-permute-start.27 = (f32[2,8]{1,0:T(2,128)S(1)}, f32[2,8]{1,0:T(2,128)S(1)}, u32[]{:S(2)}, u32[]{:S(2)}) collective-permute-start(f32[2,8]{1,0:T(2,128)S(1)} %pad_maximum_fusion.3), channel_id=1, source_target_pairs={{0,1},{1,0},{2,3},{3,2},{4,5},{5,4},{6,7},{7,6},{8,9},{9,8},{10,11... | collective-permute-start | bytes 200 | tf_op jit(solution)/shard_map/ppermute | solution.py:66
  148.5 2.1 collective-permute-start.26
  158.5 3.1 %select_maximum_fusion.x_ref = bf16[5,10,82,512]{3,2,1,0:T(8,128)(2,1)} fusion(bf16[3,10,80,512]{3,2,1,0:T(8,128)(2,1)S(1)} %fusion.7, bf16[1,10,80,512]{3,2,1,0:T(8,128)(2,1)S(1)} %slice.39), kind=kLoop, calls=%fused_computation.5 | loop fusion | flops 25190400 | bytes 7475200 | tf_op jit(solution)/shard_map/concatenate | solution.py:117
  161.6 10.9 %all-gather.5.cloned.1.call-done.w_ref = bf16[27,512,128]{2,1,0:T(8,128)(2,1)} async-done(((bf16[27,128,128]{2,1,0:T(8,128)(2,1)}), bf16[27,512,128]{2,1,0:T(8,128)(2,1)}) %all-gather.5.cloned.1.call-update) | async-done | bytes 3538960 | tf_op jit(solution)/shard_map/all_gather | solution.py:176
  172.5 18.5 %shard_map.92 = f32[3,8,80,128]{3,2,1,0:T(8,128)} custom-call(bf16[5,10,82,512]{3,2,1,0:T(8,128)(2,1)} %select_maximum_fusion.x_ref, bf16[27,512,128]{2,1,0:T(8,128)(2,1)} %all-gather.5.cloned.1.call-done.w_ref, f32[1,128]{1,0:T(1,128)} %dynamic-slice_bitcast_fusion.b_ref), custom_call_target="tpu_custom_call" | custom-call | flops 6794772480 | bytes 8720384 | tf_op jit(solution)/shard_map/pallas_call | solution.py:125
  194.8 2.1 collective-permute-done.31
  196.9 3.3 %collective-permute-done.32 = bf16[3,2,80,128]{3,2,1,0:T(8,128)(2,1)S(1)} collective-permute-done((bf16[3,2,80,128]{3,2,1,0:T(8,128)(2,1)S(1)}, bf16[3,2,80,128]{3,2,1,0:T(8,128)(2,1)S(1)}, u32[]{:S(2)}, u32[]{:S(2)}) %collective-permute-start.32) | collective-permute-done | bytes 122912 | tf_op jit(solution)/shard_map/ppermute | solution.py:188
  202.4 2.2 %reshape.59 = bf16[3,4,160,512]{3,2,1,0:T(8,128)(2,1)} reshape(bf16[3,4,80,2,512]{4,3,2,1,0:T(2,128)(2,1)S(1)} %broadcast_in_dim.45) | data formatting | bytes 3932160 | tf_op jit(solution)/shard_map/reshape | solution.py:235
  (148 shorter events, 60.8 us)
Async XLA Ops:
  6.5 94.5 %all-gather.3.cloned.1.call-start = ((), (), s32[]{:S(2)}) async-start(), calls=%async_computation | async-start | bytes 4423680 | tf_op jit(solution)/shard_map/all_gather | solution.py:176
  7.7 12.0 %collective-permute-start.13 = (bf16[27,32,256]{2,1,0:T(8,128)(2,1)S(1)}, bf16[27,32,256]{2,1,0:T(8,128)(2,1)S(1)}, u32[]{:S(2)}, u32[]{:S(2)}) collective-permute-start(bf16[27,32,256]{2,1,0:T(8,128)(2,1)S(1)} %constant_dynamic-slice_fusion.8), channel_id=1, source_target_pairs={{0,2},{2,0},{1,3},{3,1},{4,6},{6,4},{5,7},{7,5},{8,10},{10,8},{9,1... | collective-permute-start | bytes 1327112 | tf_op jit(solution)/shard_map/ppermute | solution.py:153
  11.0 10.1 %collective-permute-start.15 = (bf16[27,32,128]{2,1,0:T(8,128)(2,1)S(1)}, bf16[27,32,128]{2,1,0:T(8,128)(2,1)S(1)}, u32[]{:S(2)}, u32[]{:S(2)}) collective-permute-start(bf16[27,32,128]{2,1,0:T(8,128)(2,1)S(1)} %constant_dynamic-slice_fusion.6), channel_id=1, source_target_pairs={{0,1},{1,0},{2,3},{3,2},{4,5},{5,4},{6,7},{7,6},{8,9},{9,8},{10,11... | collective-permute-start | bytes 663560 | tf_op jit(solution)/shard_map/ppermute | solution.py:162
  24.6 147.9 %all-gather.5.cloned.1.call-start = ((), (), s32[]{:S(2)}) async-start(), calls=%async_computation.1 | async-start | bytes 4423680 | tf_op jit(solution)/shard_map/all_gather | solution.py:176
  24.7 17.4 %collective-permute-start = (bf16[3,2,80,512]{3,2,1,0:T(8,128)(2,1)S(1)}, bf16[3,2,80,512]{3,2,1,0:T(8,128)(2,1)S(1)}, u32[]{:S(2)}, u32[]{:S(2)}) collective-permute-start(bf16[3,2,80,512]{3,2,1,0:T(8,128)(2,1)S(1)} %copy-done.1), channel_id=1, source_target_pairs={{0,2},{2,0},{1,3},{3,1},{4,6},{6,4},{5,7},{7,5},{8,10},{10,8},{9,1... | collective-permute-start | bytes 1474568 | tf_op jit(solution)/shard_map/ppermute | solution.py:62
  26.1 28.3 %collective-permute-start.2 = (bf16[3,2,80,512]{3,2,1,0:T(8,128)(2,1)S(1)}, bf16[3,2,80,512]{3,2,1,0:T(8,128)(2,1)S(1)}, u32[]{:S(2)}, u32[]{:S(2)}) collective-permute-start(bf16[3,2,80,512]{3,2,1,0:T(8,128)(2,1)S(1)} %copy-done.1), channel_id=1, source_target_pairs={{0,1},{1,0},{2,3},{3,2},{4,5},{5,4},{6,7},{7,6},{8,9},{9,8},{10,11... | collective-permute-start | bytes 1474568 | tf_op jit(solution)/shard_map/ppermute | solution.py:66
  27.2 10.0 %collective-permute-start.5 = (f32[32]{0:T(128)S(1)}, f32[32]{0:T(128)S(1)}, u32[]{:S(2)}, u32[]{:S(2)}) collective-permute-start(f32[32]{0:T(128)S(1)} %reduce_sum.51), channel_id=1, source_target_pairs={{0,2},{2,0},{1,3},{3,1},{4,6},{6,4},{5,7},{7,5},{8,10},{10,8},{9,1... | collective-permute-start | bytes 392 | tf_op jit(solution)/shard_map/ppermute | solution.py:25
  27.8 9.4 %collective-permute-start.9 = (f32[32]{0:T(128)S(1)}, f32[32]{0:T(128)S(1)}, u32[]{:S(2)}, u32[]{:S(2)}) collective-permute-start(f32[32]{0:T(128)S(1)} %reduce_sum.54), channel_id=1, source_target_pairs={{0,2},{2,0},{1,3},{3,1},{4,6},{6,4},{5,7},{7,5},{8,10},{10,8},{9,1... | collective-permute-start | bytes 392 | tf_op jit(solution)/shard_map/ppermute | solution.py:25
  29.3 22.1 %collective-permute-start.28 = (bf16[27,32,256]{2,1,0:T(8,128)(2,1)S(1)}, bf16[27,32,256]{2,1,0:T(8,128)(2,1)}, u32[]{:S(2)}, u32[]{:S(2)}) collective-permute-start(bf16[27,32,256]{2,1,0:T(8,128)(2,1)S(1)} %constant_dynamic-slice_fusion.5), channel_id=1, source_target_pairs={{0,2},{2,0},{1,3},{3,1},{4,6},{6,4},{5,7},{7,5},{8,10},{10,8},{9,1... | collective-permute-start | bytes 1327112 | tf_op jit(solution)/shard_map/ppermute | solution.py:153
  42.1 12.4 %collective-permute-start.1 = (bf16[3,2,80,512]{3,2,1,0:T(8,128)(2,1)S(1)}, bf16[3,2,80,512]{3,2,1,0:T(8,128)(2,1)S(1)}, u32[]{:S(2)}, u32[]{:S(2)}) collective-permute-start(bf16[3,2,80,512]{3,2,1,0:T(8,128)(2,1)S(1)} %collective-permute-done), channel_id=1, source_target_pairs={{0,1},{1,0},{2,3},{3,2},{4,5},{5,4},{6,7},{7,6},{8,9},{9,8},{10,11... | collective-permute-start | bytes 1474568 | tf_op jit(solution)/shard_map/ppermute | solution.py:66
  48.5 10.3 %collective-permute-start.30 = (bf16[27,32,128]{2,1,0:T(8,128)(2,1)}, bf16[27,32,128]{2,1,0:T(8,128)(2,1)}, u32[]{:S(2)}, u32[]{:S(2)}) collective-permute-start(bf16[27,32,128]{2,1,0:T(8,128)(2,1)} %constant_dynamic-slice_fusion.3), channel_id=1, source_target_pairs={{0,1},{1,0},{2,3},{3,2},{4,5},{5,4},{6,7},{7,6},{8,9},{9,8},{10,11... | collective-permute-start | bytes 663560 | tf_op jit(solution)/shard_map/ppermute | solution.py:162
  52.4 6.3 %collective-permute-start.29 = (bf16[27,32,128]{2,1,0:T(8,128)(2,1)S(1)}, bf16[27,32,128]{2,1,0:T(8,128)(2,1)S(1)}, u32[]{:S(2)}, u32[]{:S(2)}) collective-permute-start(bf16[27,32,128]{2,1,0:T(8,128)(2,1)S(1)} %constant_dynamic-slice_fusion.4), channel_id=1, source_target_pairs={{0,1},{1,0},{2,3},{3,2},{4,5},{5,4},{6,7},{7,6},{8,9},{9,8},{10,11... | collective-permute-start | bytes 663560 | tf_op jit(solution)/shard_map/ppermute | solution.py:162
  55.3 13.9 %collective-permute-start.3 = (bf16[3,1,80,512]{3,2,1,0:T(8,128)(2,1)}, bf16[3,1,80,512]{3,2,1,0:T(8,128)(2,1)}, u32[]{:S(2)}, u32[]{:S(2)}) collective-permute-start(bf16[3,1,80,512]{3,2,1,0:T(8,128)(2,1)} %slice.34), channel_id=1, source_target_pairs={{0,4},{4,8},{8,12},{1,5},{5,9},{9,13},{2,6},{6,10},{10,14},{3,7},{... | collective-permute-start | bytes 737288 | tf_op jit(solution)/shard_map/ppermute | solution.py:94
  70.5 23.8 %collective-permute-start.4 = (bf16[3,1,80,512]{3,2,1,0:T(8,128)(2,1)S(1)}, bf16[3,1,80,512]{3,2,1,0:T(8,128)(2,1)S(1)}, u32[]{:S(2)}, u32[]{:S(2)}) collective-permute-start(bf16[3,1,80,512]{3,2,1,0:T(8,128)(2,1)S(1)} %slice.35), channel_id=1, source_target_pairs={{4,0},{8,4},{12,8},{5,1},{9,5},{13,9},{6,2},{10,6},{14,10},{7,3},{... | collective-permute-start | bytes 737288 | tf_op jit(solution)/shard_map/ppermute | solution.py:95
  120.5 8.0 %collective-permute-start.17 = (bf16[3,1,80,128]{3,2,1,0:T(8,128)(2,1)S(1)}, bf16[3,1,80,128]{3,2,1,0:T(8,128)(2,1)S(1)}, u32[]{:S(2)}, u32[]{:S(2)}) collective-permute-start(bf16[3,1,80,128]{3,2,1,0:T(8,128)(2,1)S(1)} %get-tuple-element.28), channel_id=1, source_target_pairs={{4,0},{8,4},{12,8},{5,1},{9,5},{13,9},{6,2},{10,6},{14,10},{7,3},{... | collective-permute-start | bytes 184328 | tf_op jit(solution)/shard_map/ppermute | solution.py:95
  121.8 6.8 %collective-permute-start.16 = (bf16[3,1,80,128]{3,2,1,0:T(8,128)(2,1)S(1)}, bf16[3,1,80,128]{3,2,1,0:T(8,128)(2,1)S(1)}, u32[]{:S(2)}, u32[]{:S(2)}) collective-permute-start(bf16[3,1,80,128]{3,2,1,0:T(8,128)(2,1)S(1)} %get-tuple-element.27), channel_id=1, source_target_pairs={{0,4},{4,8},{8,12},{1,5},{5,9},{9,13},{2,6},{6,10},{10,14},{3,7},{... | collective-permute-start | bytes 184328 | tf_op jit(solution)/shard_map/ppermute | solution.py:94
  127.4 8.2 %collective-permute-start.21 = (f32[8]{0:T(128)S(1)}, f32[8]{0:T(128)S(1)}, u32[]{:S(2)}, u32[]{:S(2)}) collective-permute-start(f32[8]{0:T(128)S(1)} %reduce_sum.72), channel_id=1, source_target_pairs={{0,4},{4,0},{8,12},{12,8},{1,5},{5,1},{9,13},{13,9},{2,6},{6,2},{1... | collective-permute-start | bytes 104 | tf_op jit(solution)/shard_map/ppermute | solution.py:25
  130.4 20.2 %collective-permute-start.18 = (bf16[3,10,80,128]{3,2,1,0:T(8,128)(2,1)}, bf16[3,10,80,128]{3,2,1,0:T(8,128)(2,1)S(1)}, u32[]{:S(2)}, u32[]{:S(2)}) collective-permute-start(bf16[3,10,80,128]{3,2,1,0:T(8,128)(2,1)} %pad_maximum_fusion.2), channel_id=1, source_target_pairs={{0,2},{2,0},{1,3},{3,1},{4,6},{6,4},{5,7},{7,5},{8,10},{10,8},{9,1... | collective-permute-start | bytes 1843208 | tf_op jit(solution)/shard_map/ppermute | solution.py:62
  137.0 4.9 %collective-permute-start.22 = (f32[8]{0:T(128)S(1)}, f32[8]{0:T(128)S(1)}, u32[]{:S(2)}, u32[]{:S(2)}) collective-permute-start(f32[8]{0:T(128)S(1)} %get-tuple-element.37), channel_id=1, source_target_pairs={{0,8},{4,12},{8,0},{12,4},{1,9},{5,13},{9,1},{13,5},{2,10},{6,14},... | collective-permute-start | bytes 104 | tf_op jit(solution)/shard_map/ppermute | solution.py:25
  144.1 4.5 %collective-permute-start.25 = (f32[2,8]{1,0:T(2,128)S(1)}, f32[2,8]{1,0:T(2,128)S(1)}, u32[]{:S(2)}, u32[]{:S(2)}) collective-permute-start(f32[2,8]{1,0:T(2,128)S(1)} %pad_maximum_fusion.3), channel_id=1, source_target_pairs={{0,2},{2,0},{1,3},{3,1},{4,6},{6,4},{5,7},{7,5},{8,10},{10,8},{9,1... | collective-permute-start | bytes 200 | tf_op jit(solution)/shard_map/ppermute | solution.py:62
  144.2 6.9 %collective-permute-start.27 = (f32[2,8]{1,0:T(2,128)S(1)}, f32[2,8]{1,0:T(2,128)S(1)}, u32[]{:S(2)}, u32[]{:S(2)}) collective-permute-start(f32[2,8]{1,0:T(2,128)S(1)} %pad_maximum_fusion.3), channel_id=1, source_target_pairs={{0,1},{1,0},{2,3},{3,2},{4,5},{5,4},{6,7},{7,6},{8,9},{9,8},{10,11... | collective-permute-start | bytes 200 | tf_op jit(solution)/shard_map/ppermute | solution.py:66
  192.5 4.3 %collective-permute-start.31 = (bf16[3,2,80,128]{3,2,1,0:T(8,128)(2,1)S(1)}, bf16[3,2,80,128]{3,2,1,0:T(8,128)(2,1)S(1)}, u32[]{:S(2)}, u32[]{:S(2)}) collective-permute-start(bf16[3,2,80,128]{3,2,1,0:T(8,128)(2,1)S(1)} %get-tuple-element.25), channel_id=1, source_target_pairs={{0,1},{1,2},{2,3},{3,0},{4,5},{5,6},{6,7},{7,4},{8,9},{9,10},{10,1... | collective-permute-start | bytes 368648 | tf_op jit(solution)/shard_map/ppermute | solution.py:188
  194.3 5.9 %collective-permute-start.32 = (bf16[3,2,80,128]{3,2,1,0:T(8,128)(2,1)S(1)}, bf16[3,2,80,128]{3,2,1,0:T(8,128)(2,1)S(1)}, u32[]{:S(2)}, u32[]{:S(2)}) collective-permute-start(bf16[3,2,80,128]{3,2,1,0:T(8,128)(2,1)S(1)} %get-tuple-element.24), channel_id=1, source_target_pairs={{0,2},{1,3},{2,0},{3,1},{4,6},{5,7},{6,4},{7,5},{8,10},{9,11},{10,... | collective-permute-start | bytes 368648 | tf_op jit(solution)/shard_map/ppermute | solution.py:188
  194.6 6.2 %collective-permute-start.33 = (bf16[3,2,80,128]{3,2,1,0:T(8,128)(2,1)S(1)}, bf16[3,2,80,128]{3,2,1,0:T(8,128)(2,1)S(1)}, u32[]{:S(2)}, u32[]{:S(2)}) collective-permute-start(bf16[3,2,80,128]{3,2,1,0:T(8,128)(2,1)S(1)} %get-tuple-element.23), channel_id=1, source_target_pairs={{0,3},{1,0},{2,1},{3,2},{4,7},{5,4},{6,5},{7,6},{8,11},{9,8},{10,9... | collective-permute-start | bytes 368648 | tf_op jit(solution)/shard_map/ppermute | solution.py:188
  (21 other events, 270.8 us)
Sparse Core Ops, SparseCore 0:
  24.7 76.2 all-gather.2
  102.6 69.8 all-gather.4

commit v11 on v10

--- a/solution.py
+++ b/solution.py
@@ -137,7 +137,7 @@
     )(padded, kernel, bias.reshape(1, outs))
 
 
-def kernel_block(shard, chans):
+def kernel_block(shard, chans, by_permutes=False):
     count_a = lax.axis_size("ha")
     count_b = lax.axis_size("hb")
     me_a = lax.axis_index("ha")
@@ -173,7 +173,23 @@
                     piece = jnp.where(hit, seconds[sb][sa], piece)
             slots.append(piece)
     out = jnp.concatenate(slots, axis=1)
-    return lax.all_gather(out, "hz", axis=1, tiled=True)
+    if not by_permutes:
+        return lax.all_gather(out, "hz", axis=1, tiled=True)
+    size = lax.axis_size("hz")
+    me = lax.axis_index("hz")
+    received = [(out, 0)]
+    for step in range(1, size):
+        down = [(i, i + step) for i in range(size - step)]
+        up = [(i + step, i) for i in range(size - step)]
+        received.append((lax.ppermute(out, "hz", down), -step))
+        received.append((lax.ppermute(out, "hz", up), step))
+    slots = []
+    for slot in range(size):
+        piece = jnp.zeros_like(out)
+        for block, offset in received:
+            piece = jnp.where(me + offset == slot, block, piece)
+        slots.append(piece)
+    return jnp.concatenate(slots, axis=1)
 
 
 def scatter_rows(branch, slab_rows, chans):
@@ -209,7 +225,7 @@
     group_size = chans // GROUPS
 
     weights_first = kernel_block(kernel_first, chans)
-    weights_second = kernel_block(kernel_second, chans)
+    weights_second = kernel_block(kernel_second, chans, by_permutes=True)
 
     values = latent.astype(jnp.float32)
     sums, squares, count = local_stats(values, GROUPS)

time: 212 us -> 310 us (1.46)
  waiting for transfers between devices: 73.7 us -> 137 us
  starting transfers between devices: 46.6 us -> 67.5 us
  other arithmetic: 26.3 us -> 37.3 us
    ppermute x2, waiting for transfers between devices: 7.91 us -> 49.5 us  [with_row_halo(): top = lax.ppermute(cells[:, -1:], axis_name, down)]
    ppermute x2, waiting for transfers between devices: 21.9 us -> 56.1 us  [with_row_halo(): bottom = lax.ppermute(cells[:, :1], axis_name, up)]
    ppermute x0 -> x6, starting transfers between devices: none -> 20.7 us  [the longest x3 16.9 us: kernel_block(): received.append((lax.ppermute(out, 'hz', down), -step))]
    ppermute x0 -> x6, waiting for transfers between devices: none -> 13.5 us  [the longest x3 12.5 us: kernel_block(): received.append((lax.ppermute(out, 'hz', up), step))]
    all_gather x2 -> x1, waiting for transfers between devices: 12.6 us -> 0.01 us  [kernel_block(): return lax.all_gather(out, 'hz', axis=1, tiled=True)]
    ppermute x12, waiting for transfers between devices: 14.3 us -> 7.69 us  [butterfly_stats(): other_sums, other_squares = lax.ppermute((sums, squares), axis, pairs)]
    ppermute x2, waiting for transfers between devices: 7.73 us -> 2.41 us  [kernel_block(): piece = lax.ppermute(piece, 'ha', shift_pairs(count_a, step))]
    select_n x0 -> x4, other arithmetic: none -> 4.13 us  [kernel_block(): piece = jnp.where(me + offset == slot, block, piece)]
  transfers between devices with their start and end apart: 36 -> 41, of which waited for: 21 -> 19; matrix products, arithmetic and copies ran while one was open for 15% -> 12% of each run, Pallas kernels for 9% -> 0%
where the time goes in v11:
time: 310 us; the launch traced here: 309 us
  waiting for transfers between devices  137 us (44%)
  starting transfers between devices  67.5 us (22%)
  other arithmetic  37.3 us (12%)
  Pallas kernels  37.1 us (12%)
  local copies, waits for them, and re-layouts  15.9 us (5%)
  between operations  14.2 us (5%)
    ppermute x2, waiting for transfers between devices, with_row_halo(): bottom = lax.ppermute(cells[:, :1], axis_name, up)  56.1 us
    ppermute x2, waiting for transfers between devices, with_row_halo(): top = lax.ppermute(cells[:, -1:], axis_name, down)  49.5 us
    pallas_call x2, Pallas kernels, causal_conv(): pl.pallas_call(conv_body, grid=(frames,), in_specs=[pl.BlockSpec(padded.s...  37.1 us
    ppermute x3, starting transfers between devices, kernel_block(): received.append((lax.ppermute(out, 'hz', down), -step))  16.9 us
    ppermute x12, starting transfers between devices, butterfly_stats(): other_sums, other_squares = lax.ppermute((sums, squares), axis, pairs)  16 us
    ppermute x3, waiting for transfers between devices, kernel_block(): received.append((lax.ppermute(out, 'hz', up), step))  12.5 us
    ppermute x6, starting transfers between devices, chip_gather(): bundles.append(lax.ppermute(firsts, 'hb', shift_pairs(count_b, step)))  9.45 us
    ppermute x12, waiting for transfers between devices, butterfly_stats(): other_sums, other_squares = lax.ppermute((sums, squares), axis, pairs)  7.69 us
  transfers between devices with their start and end apart: 41, of which 19 were waited for; matrix products, arithmetic and copies ran while one was open for 12% of the time, Pallas kernels for 0%

profile of v11, /device:TPU:1, one launch (start us, length us, event | category | flops | bytes accessed | tf_op | source)
XLA Modules:
  0.0 309.2 jit_solution(15923823134661229611)
XLA Ops:
  6.5 2.1 collective-permute-start
  19.9 2.2 collective-permute-start.6
  27.8 2.3 collective-permute-start.8
  32.6 2.8 collective-permute-start.30
  36.4 2.4 collective-permute-done.13
  45.2 6.0 %collective-permute-start.32 = (bf16[27,128,128]{2,1,0:T(8,128)(2,1)}, bf16[27,128,128]{2,1,0:T(8,128)(2,1)S(1)}, u32[]{:S(2)}, u32[]{:S(2)}) collective-permute-start(bf16[27,128,128]{2,1,0:T(8,128)(2,1)} %pad_maximum_fusion.2), channel_id=1, source_target_pairs={{0,12},{1,13},{2,14},{3,15},{16,28},{17,29},{18,30},{19,31}} | collective-permute-start | bytes 2654216 | tf_op jit(solution)/shard_map/ppermute | solution.py:184
  55.4 5.9 %collective-permute-start.34 = (bf16[27,128,128]{2,1,0:T(8,128)(2,1)}, bf16[27,128,128]{2,1,0:T(8,128)(2,1)}, u32[]{:S(2)}, u32[]{:S(2)}) collective-permute-start(bf16[27,128,128]{2,1,0:T(8,128)(2,1)} %pad_maximum_fusion.2), channel_id=1, source_target_pairs={{0,8},{4,12},{1,9},{5,13},{2,10},{6,14},{3,11},{7,15},{16,24},{20,... | collective-permute-start | bytes 2654216 | tf_op jit(solution)/shard_map/ppermute | solution.py:184
  65.7 49.5 %collective-permute-done.3 = bf16[3,1,80,512]{3,2,1,0:T(8,128)(2,1)} collective-permute-done((bf16[3,1,80,512]{3,2,1,0:T(8,128)(2,1)}, bf16[3,1,80,512]{3,2,1,0:T(8,128)(2,1)}, u32[]{:S(2)}, u32[]{:S(2)}) %collective-permute-start.3) | collective-permute-done | bytes 245792 | tf_op jit(solution)/shard_map/ppermute | solution.py:94
  122.1 56.1 %collective-permute-done.4 = bf16[3,1,80,512]{3,2,1,0:T(8,128)(2,1)S(1)} collective-permute-done((bf16[3,1,80,512]{3,2,1,0:T(8,128)(2,1)S(1)}, bf16[3,1,80,512]{3,2,1,0:T(8,128)(2,1)S(1)}, u32[]{:S(2)}, u32[]{:S(2)}) %collective-permute-start.4) | collective-permute-done | bytes 245792 | tf_op jit(solution)/shard_map/ppermute | solution.py:95
  179.5 5.0 %collective-permute-start.36 = (bf16[27,128,128]{2,1,0:T(8,128)(2,1)}, bf16[27,128,128]{2,1,0:T(8,128)(2,1)S(1)}, u32[]{:S(2)}, u32[]{:S(2)}) collective-permute-start(bf16[27,128,128]{2,1,0:T(8,128)(2,1)} %pad_maximum_fusion.2), channel_id=1, source_target_pairs={{0,4},{4,8},{8,12},{1,5},{5,9},{9,13},{2,6},{6,10},{10,14},{3,7},{... | collective-permute-start | bytes 2654216 | tf_op jit(solution)/shard_map/ppermute | solution.py:184
  186.5 3.1 %fusion.5.x_ref = bf16[5,10,82,512]{3,2,1,0:T(8,128)(2,1)} fusion(bf16[3,10,80,512]{3,2,1,0:T(8,128)(2,1)S(1)} %fusion.6, bf16[1,10,80,512]{3,2,1,0:T(8,128)(2,1)S(1)} %slice.36), kind=kLoop, calls=%fused_computation.11 | loop fusion | flops 25190400 | bytes 7475200 | tf_op jit(solution)/shard_map/concatenate | solution.py:117
  189.7 12.5 %collective-permute-done.35 = bf16[27,128,128]{2,1,0:T(8,128)(2,1)S(1)} collective-permute-done((bf16[27,128,128]{2,1,0:T(8,128)(2,1)}, bf16[27,128,128]{2,1,0:T(8,128)(2,1)S(1)}, u32[]{:S(2)}, u32[]{:S(2)}) %collective-permute-start.35) | collective-permute-done | bytes 884768 | tf_op jit(solution)/shard_map/ppermute | solution.py:185
  207.3 4.0 %pad_maximum_fusion.w_ref = bf16[27,512,128]{2,1,0:T(8,128)(2,1)} fusion(bf16[27,128,128]{2,1,0:T(8,128)(2,1)S(1)} %select_select_fusion, bf16[27,128,128]{2,1,0:T(8,128)(2,1)S(1)} %select_select_fusion.1, bf16[27,128,128]{2,1,0:T(8,128)(2,1)S(1)} %select_select_fusion.2, bf16[27,128,128]{2,1,0:T(8,128)(2,1)S(1)} %select_select_fusion.3), kind=kLoop, calls=%fused_computation.12 | loop fusion | flops 14155776 | bytes 7077888 | tf_op jit(solution)/shard_map/concatenate | solution.py:192
  211.4 18.5 %shard_map.91 = bf16[3,8,80,128]{3,2,1,0:T(8,128)(2,1)} custom-call(bf16[5,10,82,512]{3,2,1,0:T(8,128)(2,1)} %fusion.5.x_ref, bf16[27,512,128]{2,1,0:T(8,128)(2,1)} %all-gather.2.cloned.1.call-done.w_ref, f32[1,128]{1,0:T(1,128)} %dynamic-slice_bitcast_fusion.1.b_ref), custom_call_target="tpu_custom_call" | custom-call | flops 6794772480 | bytes 8720384 | tf_op jit(solution)/shard_map/pallas_call | solution.py:125
  233.4 4.6 %collective-permute-start.16 = (bf16[3,1,80,128]{3,2,1,0:T(8,128)(2,1)S(1)}, bf16[3,1,80,128]{3,2,1,0:T(8,128)(2,1)S(1)}, u32[]{:S(2)}, u32[]{:S(2)}) collective-permute-start(bf16[3,1,80,128]{3,2,1,0:T(8,128)(2,1)S(1)} %get-tuple-element.27), channel_id=1, source_target_pairs={{0,4},{4,8},{8,12},{1,5},{5,9},{9,13},{2,6},{6,10},{10,14},{3,7},{... | collective-permute-start | bytes 184328 | tf_op jit(solution)/shard_map/ppermute | solution.py:94
  238.2 3.0 collective-permute-start.21
  246.5 2.5 collective-permute-start.22
  249.9 2.4 collective-permute-done.24
  253.8 5.5 %collective-permute-start.27 = (f32[2,8]{1,0:T(2,128)S(1)}, f32[2,8]{1,0:T(2,128)S(1)}, u32[]{:S(2)}, u32[]{:S(2)}) collective-permute-start(f32[2,8]{1,0:T(2,128)S(1)} %pad_maximum_fusion.4), channel_id=1, source_target_pairs={{0,1},{1,0},{2,3},{3,2},{4,5},{5,4},{6,7},{7,6},{8,9},{9,8},{10,11... | collective-permute-start | bytes 200 | tf_op jit(solution)/shard_map/ppermute | solution.py:66
  259.3 2.4 collective-permute-start.26
  267.5 3.1 %select_maximum_fusion.x_ref = bf16[5,10,82,512]{3,2,1,0:T(8,128)(2,1)} fusion(bf16[3,10,80,512]{3,2,1,0:T(8,128)(2,1)S(1)} %fusion.7, bf16[1,10,80,512]{3,2,1,0:T(8,128)(2,1)S(1)} %slice.39), kind=kLoop, calls=%fused_computation.5 | loop fusion | flops 25190400 | bytes 7475200 | tf_op jit(solution)/shard_map/concatenate | solution.py:117
  270.7 18.7 %shard_map.92 = f32[3,8,80,128]{3,2,1,0:T(8,128)} custom-call(bf16[5,10,82,512]{3,2,1,0:T(8,128)(2,1)} %select_maximum_fusion.x_ref, bf16[27,512,128]{2,1,0:T(8,128)(2,1)} %pad_maximum_fusion.w_ref, f32[1,128]{1,0:T(1,128)} %dynamic-slice_bitcast_fusion.b_ref), custom_call_target="tpu_custom_call" | custom-call | flops 6794772480 | bytes 8720384 | tf_op jit(solution)/shard_map/pallas_call | solution.py:125
  293.9 3.7 %collective-permute-done.38 = bf16[3,2,80,128]{3,2,1,0:T(8,128)(2,1)S(1)} collective-permute-done((bf16[3,2,80,128]{3,2,1,0:T(8,128)(2,1)S(1)}, bf16[3,2,80,128]{3,2,1,0:T(8,128)(2,1)S(1)}, u32[]{:S(2)}, u32[]{:S(2)}) %collective-permute-start.38) | collective-permute-done | bytes 122912 | tf_op jit(solution)/shard_map/ppermute | solution.py:204
  300.1 2.2 reshape.59
  (196 shorter events, 74.6 us)
Async XLA Ops:
  6.5 204.8 %all-gather.2.cloned.1.call-start = ((), (), s32[]{:S(2)}) async-start(), calls=%async_computation | async-start | bytes 4423680 | tf_op jit(solution)/shard_map/all_gather | solution.py:177
  6.5 33.5 %collective-permute-start = (bf16[3,2,80,512]{3,2,1,0:T(8,128)(2,1)}, bf16[3,2,80,512]{3,2,1,0:T(8,128)(2,1)S(1)}, u32[]{:S(2)}, u32[]{:S(2)}) collective-permute-start(bf16[3,2,80,512]{3,2,1,0:T(8,128)(2,1)} %param.9), channel_id=1, source_target_pairs={{0,2},{2,0},{1,3},{3,1},{4,6},{6,4},{5,7},{7,5},{8,10},{10,8},{9,1... | collective-permute-start | bytes 1474568 | tf_op jit(solution)/shard_map/ppermute | solution.py:62
  8.7 36.5 %collective-permute-start.2 = (bf16[3,2,80,512]{3,2,1,0:T(8,128)(2,1)}, bf16[3,2,80,512]{3,2,1,0:T(8,128)(2,1)}, u32[]{:S(2)}, u32[]{:S(2)}) collective-permute-start(bf16[3,2,80,512]{3,2,1,0:T(8,128)(2,1)} %param.9), channel_id=1, source_target_pairs={{0,1},{1,0},{2,3},{3,2},{4,5},{5,4},{6,7},{7,6},{8,9},{9,8},{10,11... | collective-permute-start | bytes 1474568 | tf_op jit(solution)/shard_map/ppermute | solution.py:66
  11.0 8.9 %collective-permute-start.5 = (f32[32]{0:T(128)S(1)}, f32[32]{0:T(128)S(1)}, u32[]{:S(2)}, u32[]{:S(2)}) collective-permute-start(f32[32]{0:T(128)S(1)} %reduce_sum.51), channel_id=1, source_target_pairs={{0,2},{2,0},{1,3},{3,1},{4,6},{6,4},{5,7},{7,5},{8,10},{10,8},{9,1... | collective-permute-start | bytes 392 | tf_op jit(solution)/shard_map/ppermute | solution.py:25
  12.6 7.2 %collective-permute-start.9 = (f32[32]{0:T(128)S(1)}, f32[32]{0:T(128)S(1)}, u32[]{:S(2)}, u32[]{:S(2)}) collective-permute-start(f32[32]{0:T(128)S(1)} %reduce_sum.54), channel_id=1, source_target_pairs={{0,2},{2,0},{1,3},{3,1},{4,6},{6,4},{5,7},{7,5},{8,10},{10,8},{9,1... | collective-permute-start | bytes 392 | tf_op jit(solution)/shard_map/ppermute | solution.py:25
  15.2 15.0 %collective-permute-start.28 = (bf16[27,32,256]{2,1,0:T(8,128)(2,1)S(1)}, bf16[27,32,256]{2,1,0:T(8,128)(2,1)}, u32[]{:S(2)}, u32[]{:S(2)}) collective-permute-start(bf16[27,32,256]{2,1,0:T(8,128)(2,1)S(1)} %constant_dynamic-slice_fusion.5), channel_id=1, source_target_pairs={{0,2},{2,0},{1,3},{3,1},{4,6},{6,4},{5,7},{7,5},{8,10},{10,8},{9,1... | collective-permute-start | bytes 1327112 | tf_op jit(solution)/shard_map/ppermute | solution.py:153
  26.3 12.5 %collective-permute-start.13 = (bf16[27,32,256]{2,1,0:T(8,128)(2,1)}, bf16[27,32,256]{2,1,0:T(8,128)(2,1)S(1)}, u32[]{:S(2)}, u32[]{:S(2)}) collective-permute-start(bf16[27,32,256]{2,1,0:T(8,128)(2,1)} %constant_dynamic-slice_fusion.8), channel_id=1, source_target_pairs={{0,2},{2,0},{1,3},{3,1},{4,6},{6,4},{5,7},{7,5},{8,10},{10,8},{9,1... | collective-permute-start | bytes 1327112 | tf_op jit(solution)/shard_map/ppermute | solution.py:153
  32.6 7.6 %collective-permute-start.30 = (bf16[27,32,128]{2,1,0:T(8,128)(2,1)S(1)}, bf16[27,32,128]{2,1,0:T(8,128)(2,1)S(1)}, u32[]{:S(2)}, u32[]{:S(2)}) collective-permute-start(bf16[27,32,128]{2,1,0:T(8,128)(2,1)S(1)} %constant_dynamic-slice_fusion.3), channel_id=1, source_target_pairs={{0,1},{1,0},{2,3},{3,2},{4,5},{5,4},{6,7},{7,6},{8,9},{9,8},{10,11... | collective-permute-start | bytes 663560 | tf_op jit(solution)/shard_map/ppermute | solution.py:162
  38.8 16.5 %collective-permute-start.15 = (bf16[27,32,128]{2,1,0:T(8,128)(2,1)}, bf16[27,32,128]{2,1,0:T(8,128)(2,1)S(1)}, u32[]{:S(2)}, u32[]{:S(2)}) collective-permute-start(bf16[27,32,128]{2,1,0:T(8,128)(2,1)} %constant_dynamic-slice_fusion.6), channel_id=1, source_target_pairs={{0,1},{1,0},{2,3},{3,2},{4,5},{5,4},{6,7},{7,6},{8,9},{9,8},{10,11... | collective-permute-start | bytes 663560 | tf_op jit(solution)/shard_map/ppermute | solution.py:162
  40.1 11.2 %collective-permute-start.1 = (bf16[3,2,80,512]{3,2,1,0:T(8,128)(2,1)S(1)}, bf16[3,2,80,512]{3,2,1,0:T(8,128)(2,1)}, u32[]{:S(2)}, u32[]{:S(2)}) collective-permute-start(bf16[3,2,80,512]{3,2,1,0:T(8,128)(2,1)S(1)} %collective-permute-done), channel_id=1, source_target_pairs={{0,1},{1,0},{2,3},{3,2},{4,5},{5,4},{6,7},{7,6},{8,9},{9,8},{10,11... | collective-permute-start | bytes 1474568 | tf_op jit(solution)/shard_map/ppermute | solution.py:66
  40.2 21.0 %collective-permute-start.14 = (bf16[27,32,128]{2,1,0:T(8,128)(2,1)S(1)}, bf16[27,32,128]{2,1,0:T(8,128)(2,1)S(1)}, u32[]{:S(2)}, u32[]{:S(2)}) collective-permute-start(bf16[27,32,128]{2,1,0:T(8,128)(2,1)S(1)} %constant_dynamic-slice_fusion.7), channel_id=1, source_target_pairs={{0,1},{1,0},{2,3},{3,2},{4,5},{5,4},{6,7},{7,6},{8,9},{9,8},{10,11... | collective-permute-start | bytes 663560 | tf_op jit(solution)/shard_map/ppermute | solution.py:162
  43.9 135.6 %collective-permute-start.31 = (bf16[27,128,128]{2,1,0:T(8,128)(2,1)}, bf16[27,128,128]{2,1,0:T(8,128)(2,1)S(1)}, u32[]{:S(2)}, u32[]{:S(2)}) collective-permute-start(bf16[27,128,128]{2,1,0:T(8,128)(2,1)} %pad_maximum_fusion.2), channel_id=1, source_target_pairs={{12,0},{13,1},{14,2},{15,3},{28,16},{29,17},{30,18},{31,19}} | collective-permute-start | bytes 2654216 | tf_op jit(solution)/shard_map/ppermute | solution.py:185
  45.2 144.4 %collective-permute-start.32 = (bf16[27,128,128]{2,1,0:T(8,128)(2,1)}, bf16[27,128,128]{2,1,0:T(8,128)(2,1)S(1)}, u32[]{:S(2)}, u32[]{:S(2)}) collective-permute-start(bf16[27,128,128]{2,1,0:T(8,128)(2,1)} %pad_maximum_fusion.2), channel_id=1, source_target_pairs={{0,12},{1,13},{2,14},{3,15},{16,28},{17,29},{18,30},{19,31}} | collective-permute-start | bytes 2654216 | tf_op jit(solution)/shard_map/ppermute | solution.py:184
  51.3 138.4 %collective-permute-start.33 = (bf16[27,128,128]{2,1,0:T(8,128)(2,1)}, bf16[27,128,128]{2,1,0:T(8,128)(2,1)S(1)}, u32[]{:S(2)}, u32[]{:S(2)}) collective-permute-start(bf16[27,128,128]{2,1,0:T(8,128)(2,1)} %pad_maximum_fusion.2), channel_id=1, source_target_pairs={{8,0},{12,4},{9,1},{13,5},{10,2},{14,6},{11,3},{15,7},{24,16},{28,... | collective-permute-start | bytes 2654216 | tf_op jit(solution)/shard_map/ppermute | solution.py:185
  55.4 134.3 %collective-permute-start.34 = (bf16[27,128,128]{2,1,0:T(8,128)(2,1)}, bf16[27,128,128]{2,1,0:T(8,128)(2,1)}, u32[]{:S(2)}, u32[]{:S(2)}) collective-permute-start(bf16[27,128,128]{2,1,0:T(8,128)(2,1)} %pad_maximum_fusion.2), channel_id=1, source_target_pairs={{0,8},{4,12},{1,9},{5,13},{2,10},{6,14},{3,11},{7,15},{16,24},{20,... | collective-permute-start | bytes 2654216 | tf_op jit(solution)/shard_map/ppermute | solution.py:184
  61.2 53.9 %collective-permute-start.3 = (bf16[3,1,80,512]{3,2,1,0:T(8,128)(2,1)}, bf16[3,1,80,512]{3,2,1,0:T(8,128)(2,1)}, u32[]{:S(2)}, u32[]{:S(2)}) collective-permute-start(bf16[3,1,80,512]{3,2,1,0:T(8,128)(2,1)} %slice.34), channel_id=1, source_target_pairs={{0,4},{4,8},{8,12},{1,5},{5,9},{9,13},{2,6},{6,10},{10,14},{3,7},{... | collective-permute-start | bytes 737288 | tf_op jit(solution)/shard_map/ppermute | solution.py:94
  117.5 60.7 %collective-permute-start.4 = (bf16[3,1,80,512]{3,2,1,0:T(8,128)(2,1)S(1)}, bf16[3,1,80,512]{3,2,1,0:T(8,128)(2,1)S(1)}, u32[]{:S(2)}, u32[]{:S(2)}) collective-permute-start(bf16[3,1,80,512]{3,2,1,0:T(8,128)(2,1)S(1)} %slice.35), channel_id=1, source_target_pairs={{4,0},{8,4},{12,8},{5,1},{9,5},{13,9},{6,2},{10,6},{14,10},{7,3},{... | collective-permute-start | bytes 737288 | tf_op jit(solution)/shard_map/ppermute | solution.py:95
  178.2 24.0 %collective-permute-start.35 = (bf16[27,128,128]{2,1,0:T(8,128)(2,1)}, bf16[27,128,128]{2,1,0:T(8,128)(2,1)S(1)}, u32[]{:S(2)}, u32[]{:S(2)}) collective-permute-start(bf16[27,128,128]{2,1,0:T(8,128)(2,1)} %pad_maximum_fusion.2), channel_id=1, source_target_pairs={{4,0},{8,4},{12,8},{5,1},{9,5},{13,9},{6,2},{10,6},{14,10},{7,3},{... | collective-permute-start | bytes 2654216 | tf_op jit(solution)/shard_map/ppermute | solution.py:185
  179.5 23.7 %collective-permute-start.36 = (bf16[27,128,128]{2,1,0:T(8,128)(2,1)}, bf16[27,128,128]{2,1,0:T(8,128)(2,1)S(1)}, u32[]{:S(2)}, u32[]{:S(2)}) collective-permute-start(bf16[27,128,128]{2,1,0:T(8,128)(2,1)} %pad_maximum_fusion.2), channel_id=1, source_target_pairs={{0,4},{4,8},{8,12},{1,5},{5,9},{9,13},{2,6},{6,10},{10,14},{3,7},{... | collective-permute-start | bytes 2654216 | tf_op jit(solution)/shard_map/ppermute | solution.py:184
  232.1 9.3 %collective-permute-start.17 = (bf16[3,1,80,128]{3,2,1,0:T(8,128)(2,1)S(1)}, bf16[3,1,80,128]{3,2,1,0:T(8,128)(2,1)S(1)}, u32[]{:S(2)}, u32[]{:S(2)}) collective-permute-start(bf16[3,1,80,128]{3,2,1,0:T(8,128)(2,1)S(1)} %get-tuple-element.28), channel_id=1, source_target_pairs={{4,0},{8,4},{12,8},{5,1},{9,5},{13,9},{6,2},{10,6},{14,10},{7,3},{... | collective-permute-start | bytes 184328 | tf_op jit(solution)/shard_map/ppermute | solution.py:95
  233.4 8.0 %collective-permute-start.16 = (bf16[3,1,80,128]{3,2,1,0:T(8,128)(2,1)S(1)}, bf16[3,1,80,128]{3,2,1,0:T(8,128)(2,1)S(1)}, u32[]{:S(2)}, u32[]{:S(2)}) collective-permute-start(bf16[3,1,80,128]{3,2,1,0:T(8,128)(2,1)S(1)} %get-tuple-element.27), channel_id=1, source_target_pairs={{0,4},{4,8},{8,12},{1,5},{5,9},{9,13},{2,6},{6,10},{10,14},{3,7},{... | collective-permute-start | bytes 184328 | tf_op jit(solution)/shard_map/ppermute | solution.py:94
  242.5 19.2 %collective-permute-start.18 = (bf16[3,10,80,128]{3,2,1,0:T(8,128)(2,1)S(1)}, bf16[3,10,80,128]{3,2,1,0:T(8,128)(2,1)S(1)}, u32[]{:S(2)}, u32[]{:S(2)}) collective-permute-start(bf16[3,10,80,128]{3,2,1,0:T(8,128)(2,1)S(1)} %pad_maximum_fusion.3), channel_id=1, source_target_pairs={{0,2},{2,0},{1,3},{3,1},{4,6},{6,4},{5,7},{7,5},{8,10},{10,8},{9,1... | collective-permute-start | bytes 1843208 | tf_op jit(solution)/shard_map/ppermute | solution.py:62
  252.3 7.0 %collective-permute-start.25 = (f32[2,8]{1,0:T(2,128)S(1)}, f32[2,8]{1,0:T(2,128)S(1)}, u32[]{:S(2)}, u32[]{:S(2)}) collective-permute-start(f32[2,8]{1,0:T(2,128)S(1)} %pad_maximum_fusion.4), channel_id=1, source_target_pairs={{0,2},{2,0},{1,3},{3,1},{4,6},{6,4},{5,7},{7,5},{8,10},{10,8},{9,1... | collective-permute-start | bytes 200 | tf_op jit(solution)/shard_map/ppermute | solution.py:62
  253.8 8.4 %collective-permute-start.27 = (f32[2,8]{1,0:T(2,128)S(1)}, f32[2,8]{1,0:T(2,128)S(1)}, u32[]{:S(2)}, u32[]{:S(2)}) collective-permute-start(f32[2,8]{1,0:T(2,128)S(1)} %pad_maximum_fusion.4), channel_id=1, source_target_pairs={{0,1},{1,0},{2,3},{3,2},{4,5},{5,4},{6,7},{7,6},{8,9},{9,8},{10,11... | collective-permute-start | bytes 200 | tf_op jit(solution)/shard_map/ppermute | solution.py:66
  (43 other events, 516.7 us)
Sparse Core Ops, SparseCore 0:
  65.8 98.8 all-gather.1

commit v12 on v8

--- a/solution.py
+++ b/solution.py
@@ -137,7 +137,7 @@
     )(padded, kernel, bias.reshape(1, outs))
 
 
-def redistribute(shard):
+def kernel_block(shard, chans):
     size = lax.axis_size("ha") * lax.axis_size("hb")
     me = lax.axis_index(HQ)
     taps, in_block, outs = shard.shape
@@ -150,48 +150,26 @@
             piece = lax.ppermute(piece, HQ, shift_pairs(size, step))
         source = (me - step) % size
         out = lax.dynamic_update_slice(out, piece, (0, source * in_block, 0))
-    return out
-
-
-def kernel_block(shard, chans):
-    return lax.all_gather(redistribute(shard), "hz", axis=1, tiled=True)
-
-
-def split_block(shard, chans):
-    out = redistribute(shard)
-    taps, rows_in, width = out.shape
-    parts = lax.axis_size("groups")
-    part = lax.axis_index("groups")
-    rows = lax.axis_size("hz")
-    share = rows_in // parts
-    mine = lax.dynamic_slice_in_dim(out, part * share, share, axis=1)
-    gathered = lax.all_gather(mine, "hz", axis=1)
-    received = [gathered]
-    for step in range(1, parts):
-        received.append(lax.ppermute(gathered, "groups", shift_pairs(parts, step)))
-    slots = []
-    for slot in range(parts):
-        piece = received[0]
-        for step in range(1, parts):
-            piece = jnp.where((part - step) % parts == slot, received[step], piece)
-        slots.append(piece)
-    stacked = jnp.stack(slots, axis=2)
-    return stacked.reshape(taps, chans, width)
+    return lax.all_gather(out, "hz", axis=1, tiled=True)
 
 
 def scatter_rows(branch, slab_rows, chans):
     size = lax.axis_size("ha") * lax.axis_size("hb")
     me = lax.axis_index(HQ)
-    frames, rows, cols, width = branch.shape
-    out = jnp.zeros((frames, slab_rows, cols, chans), branch.dtype)
+    received = []
     for step in range(size):
         target = (me + step) % size
         piece = lax.dynamic_slice_in_dim(branch, target * slab_rows, slab_rows, axis=1)
         if step:
             piece = lax.ppermute(piece, HQ, shift_pairs(size, step))
-        source = (me - step) % size
-        out = lax.dynamic_update_slice(out, piece, (0, 0, 0, source * width))
-    return out
+        received.append(piece)
+    slots = []
+    for slot in range(size):
+        piece = received[0]
+        for step in range(1, size):
+            piece = jnp.where((me - step) % size == slot, received[step], piece)
+        slots.append(piece)
+    return jnp.concatenate(slots, axis=3)
 
 
 def per_device(
@@ -211,7 +189,7 @@
     me = lax.axis_index(HQ)
     group_size = chans // GROUPS
 
-    weights_first = split_block(kernel_first, chans)
+    weights_first = kernel_block(kernel_first, chans)
     weights_second = kernel_block(kernel_second, chans)
 
     values = latent.astype(jnp.float32)

time: 220 us -> 210 us (0.955)
  local copies, waits for them, and re-layouts: 24.8 us -> 18.3 us
  starting transfers between devices: 48.4 us -> 42.1 us
  waiting for transfers between devices: 70.4 us -> 75.6 us
  other arithmetic: 25.1 us -> 21.7 us
    ppermute x7 -> x6, waiting for transfers between devices: 34.7 us -> 8.4 us  [kernel_block(): piece = lax.ppermute(piece, HQ, shift_pairs(size, step))]
    ppermute x2, waiting for transfers between devices: 5.27 us -> 24.9 us  [with_row_halo(): bottom = lax.ppermute(cells[:, :1], axis_name, up)]
    all_gather x2, waiting for transfers between devices: 0.01 us -> 14.3 us  [kernel_block(): return lax.all_gather(out, 'hz', axis=1, tiled=True)]
    ppermute x2, starting transfers between devices: 8.11 us -> 5.12 us  [with_row_halo(): top = lax.ppermute(cells[:, -1:], axis_name, down)]
    ppermute x6, starting transfers between devices: 9.75 us -> 7.12 us  [chip_gather(): bundles.append(lax.ppermute(firsts, 'hb', shift_pairs(count_b, step)))]
    another operation x3 -> x2, local copies, waits for them, and re-layouts: 2.92 us -> 0.38 us  [the longest x1 2.54 us: split_block(): stacked = jnp.stack(slots, axis=2)]
    ppermute x7 -> x6, starting transfers between devices: 8.13 us -> 6.48 us  [kernel_block(): piece = lax.ppermute(piece, HQ, shift_pairs(size, step))]
  transfers between devices with their start and end apart: 37 -> 36, of which waited for: 22 -> 23; matrix products, arithmetic and copies ran while one was open for 19% -> 15% of each run, Pallas kernels for 8% -> 9%
where the time goes in v12:
time: 210 us; the launch traced here: 208 us
  waiting for transfers between devices  75.6 us (36%)
  starting transfers between devices  42.1 us (20%)
  Pallas kernels  37 us (18%)
  other arithmetic  21.7 us (10%)
  local copies, waits for them, and re-layouts  18.3 us (9%)
  between operations  13.9 us (7%)
    pallas_call x2, Pallas kernels, causal_conv(): pl.pallas_call(conv_body, grid=(frames,), in_specs=[pl.BlockSpec(padded.s...  37 us
    ppermute x2, waiting for transfers between devices, with_row_halo(): bottom = lax.ppermute(cells[:, :1], axis_name, up)  24.9 us
    ppermute x12, waiting for transfers between devices, butterfly_stats(): other_sums, other_squares = lax.ppermute((sums, squares), axis, pairs)  14.8 us
    all_gather x2, waiting for transfers between devices, kernel_block(): return lax.all_gather(out, 'hz', axis=1, tiled=True)  14.3 us
    ppermute x12, starting transfers between devices, butterfly_stats(): other_sums, other_squares = lax.ppermute((sums, squares), axis, pairs)  13.4 us
    ppermute x6, waiting for transfers between devices, kernel_block(): piece = lax.ppermute(piece, HQ, shift_pairs(size, step))  8.4 us
    ppermute x6, starting transfers between devices, chip_gather(): bundles.append(lax.ppermute(firsts, 'hb', shift_pairs(count_b, step)))  7.12 us
    ppermute x2, waiting for transfers between devices, with_row_halo(): top = lax.ppermute(cells[:, -1:], axis_name, down)  6.54 us
  transfers between devices with their start and end apart: 36, of which 23 were waited for; matrix products, arithmetic and copies ran while one was open for 15% of the time, Pallas kernels for 9%

profile of v12, /device:TPU:1, one launch (start us, length us, event | category | flops | bytes accessed | tf_op | source)
XLA Modules:
  0.0 208.5 jit_solution(13110730415267939961)
XLA Ops:
  8.3 2.7 %collective-permute-start.13 = (bf16[27,32,128]{2,1,0:T(8,128)(2,1)S(1)}, bf16[27,32,128]{2,1,0:T(8,128)(2,1)}, u32[]{:S(2)}, u32[]{:S(2)}) collective-permute-start(bf16[27,32,128]{2,1,0:T(8,128)(2,1)S(1)} %get-tuple-element.20), channel_id=1, source_target_pairs={{0,1},{1,2},{2,3},{3,0},{4,5},{5,6},{6,7},{7,4},{8,9},{9,10},{10,1... | collective-permute-start | bytes 663560 | tf_op jit(solution)/shard_map/ppermute | solution.py:150
  11.5 4.2 %collective-permute-done.13 = bf16[27,32,128]{2,1,0:T(8,128)(2,1)} collective-permute-done((bf16[27,32,128]{2,1,0:T(8,128)(2,1)S(1)}, bf16[27,32,128]{2,1,0:T(8,128)(2,1)}, u32[]{:S(2)}, u32[]{:S(2)}) %collective-permute-start.13) | collective-permute-done | bytes 221216 | tf_op jit(solution)/shard_map/ppermute | solution.py:150
  16.6 3.8 %collective-permute-done.14 = bf16[27,32,128]{2,1,0:T(8,128)(2,1)S(1)} collective-permute-done((bf16[27,32,128]{2,1,0:T(8,128)(2,1)S(1)}, bf16[27,32,128]{2,1,0:T(8,128)(2,1)S(1)}, u32[]{:S(2)}, u32[]{:S(2)}) %collective-permute-start.14) | collective-permute-done | bytes 221216 | tf_op jit(solution)/shard_map/ppermute | solution.py:150
  21.9 2.1 collective-permute-start
  30.6 5.0 %collective-permute-done.9 = f32[32]{0:T(128)S(1)} collective-permute-done((f32[32]{0:T(128)S(1)}, f32[32]{0:T(128)S(1)}, u32[]{:S(2)}, u32[]{:S(2)}) %collective-permute-start.9) | collective-permute-done | bytes 160 | tf_op jit(solution)/shard_map/ppermute | solution.py:25
  46.1 2.3 %collective-permute-done.8 = f32[32]{0:T(128)S(1)} collective-permute-done((f32[32]{0:T(128)S(1)}, f32[32]{0:T(128)S(1)}, u32[]{:S(2)}, u32[]{:S(2)}) %collective-permute-start.8) | collective-permute-done | bytes 160 | tf_op jit(solution)/shard_map/ppermute | solution.py:25
  51.4 3.8 %collective-permute-start.3 = (bf16[3,1,80,512]{3,2,1,0:T(8,128)(2,1)}, bf16[3,1,80,512]{3,2,1,0:T(8,128)(2,1)}, u32[]{:S(2)}, u32[]{:S(2)}) collective-permute-start(bf16[3,1,80,512]{3,2,1,0:T(8,128)(2,1)} %slice.34), channel_id=1, source_target_pairs={{0,4},{4,8},{8,12},{1,5},{5,9},{9,13},{2,6},{6,10},{10,14},{3,7},{... | collective-permute-start | bytes 737288 | tf_op jit(solution)/shard_map/ppermute | solution.py:94
  59.2 6.5 %collective-permute-done.3 = bf16[3,1,80,512]{3,2,1,0:T(8,128)(2,1)} collective-permute-done((bf16[3,1,80,512]{3,2,1,0:T(8,128)(2,1)}, bf16[3,1,80,512]{3,2,1,0:T(8,128)(2,1)}, u32[]{:S(2)}, u32[]{:S(2)}) %collective-permute-start.3) | collective-permute-done | bytes 245792 | tf_op jit(solution)/shard_map/ppermute | solution.py:94
  69.7 20.3 %collective-permute-done.4 = bf16[3,1,80,512]{3,2,1,0:T(8,128)(2,1)S(1)} collective-permute-done((bf16[3,1,80,512]{3,2,1,0:T(8,128)(2,1)S(1)}, bf16[3,1,80,512]{3,2,1,0:T(8,128)(2,1)S(1)}, u32[]{:S(2)}, u32[]{:S(2)}) %collective-permute-start.4) | collective-permute-done | bytes 245792 | tf_op jit(solution)/shard_map/ppermute | solution.py:95
  92.1 3.2 %fusion.5.x_ref = bf16[5,10,82,512]{3,2,1,0:T(8,128)(2,1)} fusion(bf16[3,10,80,512]{3,2,1,0:T(8,128)(2,1)S(1)} %fusion.6, bf16[1,10,80,512]{3,2,1,0:T(8,128)(2,1)S(1)} %slice.36), kind=kLoop, calls=%fused_computation.11 | loop fusion | flops 25190400 | bytes 7475200 | tf_op jit(solution)/shard_map/concatenate | solution.py:117
  95.3 3.4 %all-gather.3.cloned.1.call-done.w_ref = bf16[27,512,128]{2,1,0:T(8,128)(2,1)} async-done(((bf16[27,128,128]{2,1,0:T(8,128)(2,1)}), bf16[27,512,128]{2,1,0:T(8,128)(2,1)}) %all-gather.3.cloned.1.call-update) | async-done | bytes 3538960 | tf_op jit(solution)/shard_map/all_gather | solution.py:153
  98.7 18.5 %shard_map.91 = bf16[3,8,80,128]{3,2,1,0:T(8,128)(2,1)} custom-call(bf16[5,10,82,512]{3,2,1,0:T(8,128)(2,1)} %fusion.5.x_ref, bf16[27,512,128]{2,1,0:T(8,128)(2,1)} %all-gather.3.cloned.1.call-done.w_ref, f32[1,128]{1,0:T(1,128)} %dynamic-slice_bitcast_fusion.1.b_ref), custom_call_target="tpu_custom_call" | custom-call | flops 6794772480 | bytes 8720384 | tf_op jit(solution)/shard_map/pallas_call | solution.py:125
  122.4 2.3 %collective-permute-start.21 = (f32[8]{0:T(128)S(1)}, f32[8]{0:T(128)S(1)}, u32[]{:S(2)}, u32[]{:S(2)}) collective-permute-start(f32[8]{0:T(128)S(1)} %reduce_sum.72), channel_id=1, source_target_pairs={{0,4},{4,0},{8,12},{12,8},{1,5},{5,1},{9,13},{13,9},{2,6},{6,2},{1... | collective-permute-start | bytes 104 | tf_op jit(solution)/shard_map/ppermute | solution.py:25
  124.9 4.6 %collective-permute-done.17 = bf16[3,1,80,128]{3,2,1,0:T(8,128)(2,1)S(1)} collective-permute-done((bf16[3,1,80,128]{3,2,1,0:T(8,128)(2,1)S(1)}, bf16[3,1,80,128]{3,2,1,0:T(8,128)(2,1)S(1)}, u32[]{:S(2)}, u32[]{:S(2)}) %collective-permute-start.17) | collective-permute-done | bytes 61472 | tf_op jit(solution)/shard_map/ppermute | solution.py:95
  134.0 2.1 %collective-permute-start.23 = (f32[8]{0:T(128)S(1)}, f32[8]{0:T(128)S(1)}, u32[]{:S(2)}, u32[]{:S(2)}) collective-permute-start(f32[8]{0:T(128)S(1)} %reduce_sum.75), channel_id=1, source_target_pairs={{0,4},{4,0},{8,12},{12,8},{1,5},{5,1},{9,13},{13,9},{2,6},{6,2},{1... | collective-permute-start | bytes 104 | tf_op jit(solution)/shard_map/ppermute | solution.py:25
  137.6 2.4 %collective-permute-start.24 = (f32[8]{0:T(128)S(1)}, f32[8]{0:T(128)S(1)}, u32[]{:S(2)}, u32[]{:S(2)}) collective-permute-start(f32[8]{0:T(128)S(1)} %get-tuple-element.39), channel_id=1, source_target_pairs={{0,8},{4,12},{8,0},{12,4},{1,9},{5,13},{9,1},{13,5},{2,10},{6,14},... | collective-permute-start | bytes 104 | tf_op jit(solution)/shard_map/ppermute | solution.py:25
  142.1 4.1 %collective-permute-start.27 = (f32[2,8]{1,0:T(2,128)S(1)}, f32[2,8]{1,0:T(2,128)S(1)}, u32[]{:S(2)}, u32[]{:S(2)}) collective-permute-start(f32[2,8]{1,0:T(2,128)S(1)} %pad_maximum_fusion.2), channel_id=1, source_target_pairs={{0,1},{1,0},{2,3},{3,2},{4,5},{5,4},{6,7},{7,6},{8,9},{9,8},{10,11... | collective-permute-start | bytes 200 | tf_op jit(solution)/shard_map/ppermute | solution.py:66
  146.2 2.1 %collective-permute-start.26 = (f32[2,8]{1,0:T(2,128)S(1)}, f32[2,8]{1,0:T(2,128)S(1)}, u32[]{:S(2)}, u32[]{:S(2)}) collective-permute-start(f32[2,8]{1,0:T(2,128)S(1)} %collective-permute-done.25), channel_id=1, source_target_pairs={{0,1},{1,0},{2,3},{3,2},{4,5},{5,4},{6,7},{7,6},{8,9},{9,8},{10,11... | collective-permute-start | bytes 200 | tf_op jit(solution)/shard_map/ppermute | solution.py:66
  154.1 2.0 fusion.7
  156.1 3.2 %select_maximum_fusion.x_ref = bf16[5,10,82,512]{3,2,1,0:T(8,128)(2,1)} fusion(bf16[3,10,80,512]{3,2,1,0:T(8,128)(2,1)S(1)} %fusion.7, bf16[1,10,80,512]{3,2,1,0:T(8,128)(2,1)S(1)} %slice.39), kind=kLoop, calls=%fused_computation.5 | loop fusion | flops 25190400 | bytes 7475200 | tf_op jit(solution)/shard_map/concatenate | solution.py:117
  159.3 10.9 %all-gather.5.cloned.1.call-done.w_ref = bf16[27,512,128]{2,1,0:T(8,128)(2,1)} async-done(((bf16[27,128,128]{2,1,0:T(8,128)(2,1)}), bf16[27,512,128]{2,1,0:T(8,128)(2,1)}) %all-gather.5.cloned.1.call-update) | async-done | bytes 3538960 | tf_op jit(solution)/shard_map/all_gather | solution.py:153
  170.2 18.5 %shard_map.92 = f32[3,8,80,128]{3,2,1,0:T(8,128)} custom-call(bf16[5,10,82,512]{3,2,1,0:T(8,128)(2,1)} %select_maximum_fusion.x_ref, bf16[27,512,128]{2,1,0:T(8,128)(2,1)} %all-gather.5.cloned.1.call-done.w_ref, f32[1,128]{1,0:T(1,128)} %dynamic-slice_bitcast_fusion.b_ref), custom_call_target="tpu_custom_call" | custom-call | flops 6794772480 | bytes 8720384 | tf_op jit(solution)/shard_map/pallas_call | solution.py:125
  193.4 2.3 %collective-permute-done.31 = bf16[3,2,80,128]{3,2,1,0:T(8,128)(2,1)S(1)} collective-permute-done((bf16[3,2,80,128]{3,2,1,0:T(8,128)(2,1)S(1)}, bf16[3,2,80,128]{3,2,1,0:T(8,128)(2,1)S(1)}, u32[]{:S(2)}, u32[]{:S(2)}) %collective-permute-start.31) | collective-permute-done | bytes 122912 | tf_op jit(solution)/shard_map/ppermute | solution.py:164
  199.5 2.2 %reshape.59 = bf16[3,4,160,512]{3,2,1,0:T(8,128)(2,1)} reshape(bf16[3,4,80,2,512]{4,3,2,1,0:T(2,128)(2,1)S(1)} %broadcast_in_dim.41) | data formatting | bytes 3932160 | tf_op jit(solution)/shard_map/reshape | solution.py:216
  (150 shorter events, 62.3 us)
Async XLA Ops:
  6.5 92.2 %all-gather.3.cloned.1.call-start = ((), (), s32[]{:S(2)}) async-start(), calls=%async_computation | async-start | bytes 4423680 | tf_op jit(solution)/shard_map/all_gather | solution.py:153
  8.3 7.3 %collective-permute-start.13 = (bf16[27,32,128]{2,1,0:T(8,128)(2,1)S(1)}, bf16[27,32,128]{2,1,0:T(8,128)(2,1)}, u32[]{:S(2)}, u32[]{:S(2)}) collective-permute-start(bf16[27,32,128]{2,1,0:T(8,128)(2,1)S(1)} %get-tuple-element.20), channel_id=1, source_target_pairs={{0,1},{1,2},{2,3},{3,0},{4,5},{5,6},{6,7},{7,4},{8,9},{9,10},{10,1... | collective-permute-start | bytes 663560 | tf_op jit(solution)/shard_map/ppermute | solution.py:150
  11.0 9.4 %collective-permute-start.14 = (bf16[27,32,128]{2,1,0:T(8,128)(2,1)S(1)}, bf16[27,32,128]{2,1,0:T(8,128)(2,1)S(1)}, u32[]{:S(2)}, u32[]{:S(2)}) collective-permute-start(bf16[27,32,128]{2,1,0:T(8,128)(2,1)S(1)} %get-tuple-element.22), channel_id=1, source_target_pairs={{0,2},{1,3},{2,0},{3,1},{4,6},{5,7},{6,4},{7,5},{8,10},{9,11},{10,... | collective-permute-start | bytes 663560 | tf_op jit(solution)/shard_map/ppermute | solution.py:150
  11.0 9.9 %collective-permute-start.15 = (bf16[27,32,128]{2,1,0:T(8,128)(2,1)S(1)}, bf16[27,32,128]{2,1,0:T(8,128)(2,1)S(1)}, u32[]{:S(2)}, u32[]{:S(2)}) collective-permute-start(bf16[27,32,128]{2,1,0:T(8,128)(2,1)S(1)} %get-tuple-element.19), channel_id=1, source_target_pairs={{0,3},{1,0},{2,1},{3,2},{4,7},{5,4},{6,5},{7,6},{8,11},{9,8},{10,9... | collective-permute-start | bytes 663560 | tf_op jit(solution)/shard_map/ppermute | solution.py:150
  21.9 148.3 %all-gather.5.cloned.1.call-start = ((), (), s32[]{:S(2)}) async-start(), calls=%async_computation.1 | async-start | bytes 4423680 | tf_op jit(solution)/shard_map/all_gather | solution.py:153
  21.9 14.8 %collective-permute-start = (bf16[3,2,80,512]{3,2,1,0:T(8,128)(2,1)S(1)}, bf16[3,2,80,512]{3,2,1,0:T(8,128)(2,1)S(1)}, u32[]{:S(2)}, u32[]{:S(2)}) collective-permute-start(bf16[3,2,80,512]{3,2,1,0:T(8,128)(2,1)S(1)} %copy-done.1), channel_id=1, source_target_pairs={{0,2},{2,0},{1,3},{3,1},{4,6},{6,4},{5,7},{7,5},{8,10},{10,8},{9,1... | collective-permute-start | bytes 1474568 | tf_op jit(solution)/shard_map/ppermute | solution.py:62
  24.0 26.6 %collective-permute-start.2 = (bf16[3,2,80,512]{3,2,1,0:T(8,128)(2,1)S(1)}, bf16[3,2,80,512]{3,2,1,0:T(8,128)(2,1)S(1)}, u32[]{:S(2)}, u32[]{:S(2)}) collective-permute-start(bf16[3,2,80,512]{3,2,1,0:T(8,128)(2,1)S(1)} %copy-done.1), channel_id=1, source_target_pairs={{0,1},{1,0},{2,3},{3,2},{4,5},{5,4},{6,7},{7,6},{8,9},{9,8},{10,11... | collective-permute-start | bytes 1474568 | tf_op jit(solution)/shard_map/ppermute | solution.py:66
  24.3 11.3 %collective-permute-start.5 = (f32[32]{0:T(128)S(1)}, f32[32]{0:T(128)S(1)}, u32[]{:S(2)}, u32[]{:S(2)}) collective-permute-start(f32[32]{0:T(128)S(1)} %reduce_sum.51), channel_id=1, source_target_pairs={{0,2},{2,0},{1,3},{3,1},{4,6},{6,4},{5,7},{7,5},{8,10},{10,8},{9,1... | collective-permute-start | bytes 392 | tf_op jit(solution)/shard_map/ppermute | solution.py:25
  25.1 10.4 %collective-permute-start.9 = (f32[32]{0:T(128)S(1)}, f32[32]{0:T(128)S(1)}, u32[]{:S(2)}, u32[]{:S(2)}) collective-permute-start(f32[32]{0:T(128)S(1)} %reduce_sum.54), channel_id=1, source_target_pairs={{0,2},{2,0},{1,3},{3,1},{4,6},{6,4},{5,7},{7,5},{8,10},{10,8},{9,1... | collective-permute-start | bytes 392 | tf_op jit(solution)/shard_map/ppermute | solution.py:25
  27.6 27.7 %collective-permute-start.28 = (bf16[27,32,128]{2,1,0:T(8,128)(2,1)}, bf16[27,32,128]{2,1,0:T(8,128)(2,1)}, u32[]{:S(2)}, u32[]{:S(2)}) collective-permute-start(bf16[27,32,128]{2,1,0:T(8,128)(2,1)} %get-tuple-element.16), channel_id=1, source_target_pairs={{0,1},{1,2},{2,3},{3,0},{4,5},{5,6},{6,7},{7,4},{8,9},{9,10},{10,1... | collective-permute-start | bytes 663560 | tf_op jit(solution)/shard_map/ppermute | solution.py:150
  36.7 13.9 %collective-permute-start.1 = (bf16[3,2,80,512]{3,2,1,0:T(8,128)(2,1)S(1)}, bf16[3,2,80,512]{3,2,1,0:T(8,128)(2,1)S(1)}, u32[]{:S(2)}, u32[]{:S(2)}) collective-permute-start(bf16[3,2,80,512]{3,2,1,0:T(8,128)(2,1)S(1)} %collective-permute-done), channel_id=1, source_target_pairs={{0,1},{1,0},{2,3},{3,2},{4,5},{5,4},{6,7},{7,6},{8,9},{9,8},{10,11... | collective-permute-start | bytes 1474568 | tf_op jit(solution)/shard_map/ppermute | solution.py:66
  45.7 10.6 %collective-permute-start.29 = (bf16[27,32,128]{2,1,0:T(8,128)(2,1)}, bf16[27,32,128]{2,1,0:T(8,128)(2,1)}, u32[]{:S(2)}, u32[]{:S(2)}) collective-permute-start(bf16[27,32,128]{2,1,0:T(8,128)(2,1)} %get-tuple-element.18), channel_id=1, source_target_pairs={{0,2},{1,3},{2,0},{3,1},{4,6},{5,7},{6,4},{7,5},{8,10},{9,11},{10,... | collective-permute-start | bytes 663560 | tf_op jit(solution)/shard_map/ppermute | solution.py:150
  48.5 8.8 %collective-permute-start.30 = (bf16[27,32,128]{2,1,0:T(8,128)(2,1)}, bf16[27,32,128]{2,1,0:T(8,128)(2,1)}, u32[]{:S(2)}, u32[]{:S(2)}) collective-permute-start(bf16[27,32,128]{2,1,0:T(8,128)(2,1)} %get-tuple-element.15), channel_id=1, source_target_pairs={{0,3},{1,0},{2,1},{3,2},{4,7},{5,4},{6,5},{7,6},{8,11},{9,8},{10,9... | collective-permute-start | bytes 663560 | tf_op jit(solution)/shard_map/ppermute | solution.py:150
  51.4 14.3 %collective-permute-start.3 = (bf16[3,1,80,512]{3,2,1,0:T(8,128)(2,1)}, bf16[3,1,80,512]{3,2,1,0:T(8,128)(2,1)}, u32[]{:S(2)}, u32[]{:S(2)}) collective-permute-start(bf16[3,1,80,512]{3,2,1,0:T(8,128)(2,1)} %slice.34), channel_id=1, source_target_pairs={{0,4},{4,8},{8,12},{1,5},{5,9},{9,13},{2,6},{6,10},{10,14},{3,7},{... | collective-permute-start | bytes 737288 | tf_op jit(solution)/shard_map/ppermute | solution.py:94
  67.0 23.0 %collective-permute-start.4 = (bf16[3,1,80,512]{3,2,1,0:T(8,128)(2,1)S(1)}, bf16[3,1,80,512]{3,2,1,0:T(8,128)(2,1)S(1)}, u32[]{:S(2)}, u32[]{:S(2)}) collective-permute-start(bf16[3,1,80,512]{3,2,1,0:T(8,128)(2,1)S(1)} %slice.35), channel_id=1, source_target_pairs={{4,0},{8,4},{12,8},{5,1},{9,5},{13,9},{6,2},{10,6},{14,10},{7,3},{... | collective-permute-start | bytes 737288 | tf_op jit(solution)/shard_map/ppermute | solution.py:95
  119.6 5.2 %collective-permute-start.16 = (bf16[3,1,80,128]{3,2,1,0:T(8,128)(2,1)S(1)}, bf16[3,1,80,128]{3,2,1,0:T(8,128)(2,1)S(1)}, u32[]{:S(2)}, u32[]{:S(2)}) collective-permute-start(bf16[3,1,80,128]{3,2,1,0:T(8,128)(2,1)S(1)} %get-tuple-element.30), channel_id=1, source_target_pairs={{0,4},{4,8},{8,12},{1,5},{5,9},{9,13},{2,6},{6,10},{10,14},{3,7},{... | collective-permute-start | bytes 184328 | tf_op jit(solution)/shard_map/ppermute | solution.py:94
  120.9 8.6 %collective-permute-start.17 = (bf16[3,1,80,128]{3,2,1,0:T(8,128)(2,1)S(1)}, bf16[3,1,80,128]{3,2,1,0:T(8,128)(2,1)S(1)}, u32[]{:S(2)}, u32[]{:S(2)}) collective-permute-start(bf16[3,1,80,128]{3,2,1,0:T(8,128)(2,1)S(1)} %get-tuple-element.31), channel_id=1, source_target_pairs={{4,0},{8,4},{12,8},{5,1},{9,5},{13,9},{6,2},{10,6},{14,10},{7,3},{... | collective-permute-start | bytes 184328 | tf_op jit(solution)/shard_map/ppermute | solution.py:95
  122.4 15.1 %collective-permute-start.21 = (f32[8]{0:T(128)S(1)}, f32[8]{0:T(128)S(1)}, u32[]{:S(2)}, u32[]{:S(2)}) collective-permute-start(f32[8]{0:T(128)S(1)} %reduce_sum.72), channel_id=1, source_target_pairs={{0,4},{4,0},{8,12},{12,8},{1,5},{5,1},{9,13},{13,9},{2,6},{6,2},{1... | collective-permute-start | bytes 104 | tf_op jit(solution)/shard_map/ppermute | solution.py:25
  131.4 16.9 %collective-permute-start.18 = (bf16[3,10,80,128]{3,2,1,0:T(8,128)(2,1)}, bf16[3,10,80,128]{3,2,1,0:T(8,128)(2,1)S(1)}, u32[]{:S(2)}, u32[]{:S(2)}) collective-permute-start(bf16[3,10,80,128]{3,2,1,0:T(8,128)(2,1)} %pad_maximum_fusion), channel_id=1, source_target_pairs={{0,2},{2,0},{1,3},{3,1},{4,6},{6,4},{5,7},{7,5},{8,10},{10,8},{9,1... | collective-permute-start | bytes 1843208 | tf_op jit(solution)/shard_map/ppermute | solution.py:62
  141.4 4.9 %collective-permute-start.25 = (f32[2,8]{1,0:T(2,128)S(1)}, f32[2,8]{1,0:T(2,128)S(1)}, u32[]{:S(2)}, u32[]{:S(2)}) collective-permute-start(f32[2,8]{1,0:T(2,128)S(1)} %pad_maximum_fusion.2), channel_id=1, source_target_pairs={{0,2},{2,0},{1,3},{3,1},{4,6},{6,4},{5,7},{7,5},{8,10},{10,8},{9,1... | collective-permute-start | bytes 200 | tf_op jit(solution)/shard_map/ppermute | solution.py:62
  142.1 6.7 %collective-permute-start.27 = (f32[2,8]{1,0:T(2,128)S(1)}, f32[2,8]{1,0:T(2,128)S(1)}, u32[]{:S(2)}, u32[]{:S(2)}) collective-permute-start(f32[2,8]{1,0:T(2,128)S(1)} %pad_maximum_fusion.2), channel_id=1, source_target_pairs={{0,1},{1,0},{2,3},{3,2},{4,5},{5,4},{6,7},{7,6},{8,9},{9,8},{10,11... | collective-permute-start | bytes 200 | tf_op jit(solution)/shard_map/ppermute | solution.py:66
  190.1 5.6 %collective-permute-start.31 = (bf16[3,2,80,128]{3,2,1,0:T(8,128)(2,1)S(1)}, bf16[3,2,80,128]{3,2,1,0:T(8,128)(2,1)S(1)}, u32[]{:S(2)}, u32[]{:S(2)}) collective-permute-start(bf16[3,2,80,128]{3,2,1,0:T(8,128)(2,1)S(1)} %get-tuple-element.29), channel_id=1, source_target_pairs={{0,3},{1,0},{2,1},{3,2},{4,7},{5,4},{6,5},{7,6},{8,11},{9,8},{10,9... | collective-permute-start | bytes 368648 | tf_op jit(solution)/shard_map/ppermute | solution.py:164
  190.8 5.3 %collective-permute-start.32 = (bf16[3,2,80,128]{3,2,1,0:T(8,128)(2,1)S(1)}, bf16[3,2,80,128]{3,2,1,0:T(8,128)(2,1)S(1)}, u32[]{:S(2)}, u32[]{:S(2)}) collective-permute-start(bf16[3,2,80,128]{3,2,1,0:T(8,128)(2,1)S(1)} %get-tuple-element.28), channel_id=1, source_target_pairs={{0,2},{1,3},{2,0},{3,1},{4,6},{5,7},{6,4},{7,5},{8,10},{9,11},{10,... | collective-permute-start | bytes 368648 | tf_op jit(solution)/shard_map/ppermute | solution.py:164
  192.0 5.8 %collective-permute-start.33 = (bf16[3,2,80,128]{3,2,1,0:T(8,128)(2,1)S(1)}, bf16[3,2,80,128]{3,2,1,0:T(8,128)(2,1)S(1)}, u32[]{:S(2)}, u32[]{:S(2)}) collective-permute-start(bf16[3,2,80,128]{3,2,1,0:T(8,128)(2,1)S(1)} %get-tuple-element.27), channel_id=1, source_target_pairs={{0,1},{1,2},{2,3},{3,0},{4,5},{5,6},{6,7},{7,4},{8,9},{9,10},{10,1... | collective-permute-start | bytes 368648 | tf_op jit(solution)/shard_map/ppermute | solution.py:164
  (23 other events, 266.7 us)
Sparse Core Ops, SparseCore 0:
  22.0 76.6 all-gather.2
  100.3 69.8 all-gather.4

commit v13 on v12

--- a/solution.py
+++ b/solution.py
@@ -104,7 +104,7 @@
     for i in range(3):
         for j in range(3):
             for k in range(3):
-                patch = x_ref[step + i, pl.ds(j, rows), pl.ds(k, cols), :]
+                patch = x_ref[k, step + i, pl.ds(j, rows)]
                 acc_ref[...] += jnp.dot(
                     patch.reshape(rows * cols, chans),
                     w_ref[9 * i + 3 * j + k],
@@ -119,14 +119,15 @@
     frames = extended.shape[0]
     rows = extended.shape[1] - 2
     cols = extended.shape[2]
+    shifted = jnp.stack([padded[:, :, k : k + cols] for k in range(3)])
     taps, chans, outs = kernel.shape
     flops = 2 * frames * rows * cols * chans * outs * taps
-    moved = padded.size * 2 + kernel.size * 2 + frames * rows * cols * outs * 4
+    moved = shifted.size * 2 + kernel.size * 2 + frames * rows * cols * outs * 4
     return pl.pallas_call(
         conv_body,
         grid=(frames,),
         in_specs=[
-            pl.BlockSpec(padded.shape, lambda t: (0, 0, 0, 0)),
+            pl.BlockSpec(shifted.shape, lambda t: (0, 0, 0, 0, 0)),
             pl.BlockSpec(kernel.shape, lambda t: (0, 0, 0)),
             pl.BlockSpec((1, outs), lambda t: (0, 0)),
         ],
@@ -134,7 +135,7 @@
         out_shape=jax.ShapeDtypeStruct((frames, rows, cols, outs), out_dtype),
         scratch_shapes=[pltpu.VMEM((rows * cols, outs), jnp.float32)],
         cost_estimate=pl.CostEstimate(flops=flops, bytes_accessed=moved, transcendentals=0),
-    )(padded, kernel, bias.reshape(1, outs))
+    )(shifted, kernel, bias.reshape(1, outs))
 
 
 def kernel_block(shard, chans):

time: 210 us -> 227 us (1.081)
  other arithmetic: 21.7 us -> 33.7 us
  waiting for transfers between devices: 75.6 us -> 63.7 us
  local copies, waits for them, and re-layouts: 18.3 us -> 28.5 us
  Pallas kernels: 37 us -> 41.7 us
    another operation x0 -> x4, other arithmetic: none -> 18.3 us  [causal_conv(): shifted = jnp.stack([padded[:, :, k:k + cols] for k in range(3)])]
    all_gather x2, waiting for transfers between devices: 14.3 us -> 0.01 us  [kernel_block(): return lax.all_gather(out, 'hz', axis=1, tiled=True)]
    another operation x2 -> x4, local copies, waits for them, and re-layouts: 0.38 us -> 10.6 us  [the longest x2 10.2 us: causal_conv(): shifted = jnp.stack([padded[:, :, k:k + cols] for k in range(3)])]
    concatenate x2 -> x0, other arithmetic: 6.35 us -> none  [causal_conv(): leading = jnp.concatenate([extended[:1], extended[:1], extended], axis=0)]
    pallas_call x2, Pallas kernels: 37 us -> 41.7 us  [causal_conv(): pl.pallas_call(conv_body, grid=(frames,), in_specs=[pl.BlockSpec(shifted....]
    ppermute x2, starting transfers between devices: 5.12 us -> 8.09 us  [with_row_halo(): top = lax.ppermute(cells[:, -1:], axis_name, down)]
  transfers between devices with their start and end apart: 36 -> 36, of which waited for: 23 -> 20; matrix products, arithmetic and copies ran while one was open for 15% -> 24% of each run, Pallas kernels for 9% -> 9%
where the time goes in v13:
time: 227 us; the launch traced here: 223 us
  waiting for transfers between devices  63.7 us (28%)
  starting transfers between devices  41.9 us (18%)
  Pallas kernels  41.7 us (18%)
  other arithmetic  33.7 us (15%)
  local copies, waits for them, and re-layouts  28.5 us (13%)
  between operations  13.9 us (6%)
    pallas_call x2, Pallas kernels, causal_conv(): pl.pallas_call(conv_body, grid=(frames,), in_specs=[pl.BlockSpec(shifted....  41.7 us
    ppermute x2, waiting for transfers between devices, with_row_halo(): bottom = lax.ppermute(cells[:, :1], axis_name, up)  25.4 us
    another operation x4, other arithmetic, causal_conv(): shifted = jnp.stack([padded[:, :, k:k + cols] for k in range(3)])  18.3 us
    ppermute x12, waiting for transfers between devices, butterfly_stats(): other_sums, other_squares = lax.ppermute((sums, squares), axis, pairs)  16.9 us
    ppermute x12, starting transfers between devices, butterfly_stats(): other_sums, other_squares = lax.ppermute((sums, squares), axis, pairs)  11.2 us
    another operation x2, local copies, waits for them, and re-layouts, causal_conv(): shifted = jnp.stack([padded[:, :, k:k + cols] for k in range(3)])  10.2 us
    ppermute x6, waiting for transfers between devices, kernel_block(): piece = lax.ppermute(piece, HQ, shift_pairs(size, step))  8.4 us
    ppermute x2, starting transfers between devices, with_row_halo(): top = lax.ppermute(cells[:, -1:], axis_name, down)  8.09 us
  transfers between devices with their start and end apart: 36, of which 20 were waited for; matrix products, arithmetic and copies ran while one was open for 24% of the time, Pallas kernels for 9%

profile of v13, /device:TPU:1, one launch (start us, length us, event | category | flops | bytes accessed | tf_op | source)
XLA Modules:
  0.0 223.4 jit_solution(4511389282611780963)
XLA Ops:
  8.3 2.7 %collective-permute-start.13 = (bf16[27,32,128]{2,1,0:T(8,128)(2,1)S(1)}, bf16[27,32,128]{2,1,0:T(8,128)(2,1)}, u32[]{:S(2)}, u32[]{:S(2)}) collective-permute-start(bf16[27,32,128]{2,1,0:T(8,128)(2,1)S(1)} %get-tuple-element.28), channel_id=1, source_target_pairs={{0,1},{1,2},{2,3},{3,0},{4,5},{5,6},{6,7},{7,4},{8,9},{9,10},{10,1... | collective-permute-start | bytes 663560 | tf_op jit(solution)/shard_map/ppermute | solution.py:151
  11.5 4.2 %collective-permute-done.13 = bf16[27,32,128]{2,1,0:T(8,128)(2,1)} collective-permute-done((bf16[27,32,128]{2,1,0:T(8,128)(2,1)S(1)}, bf16[27,32,128]{2,1,0:T(8,128)(2,1)}, u32[]{:S(2)}, u32[]{:S(2)}) %collective-permute-start.13) | collective-permute-done | bytes 221216 | tf_op jit(solution)/shard_map/ppermute | solution.py:151
  16.6 3.8 %collective-permute-done.14 = bf16[27,32,128]{2,1,0:T(8,128)(2,1)S(1)} collective-permute-done((bf16[27,32,128]{2,1,0:T(8,128)(2,1)S(1)}, bf16[27,32,128]{2,1,0:T(8,128)(2,1)S(1)}, u32[]{:S(2)}, u32[]{:S(2)}) %collective-permute-start.14) | collective-permute-done | bytes 221216 | tf_op jit(solution)/shard_map/ppermute | solution.py:151
  21.9 2.1 collective-permute-start
  30.6 5.0 %collective-permute-done.9 = f32[32]{0:T(128)S(1)} collective-permute-done((f32[32]{0:T(128)S(1)}, f32[32]{0:T(128)S(1)}, u32[]{:S(2)}, u32[]{:S(2)}) %collective-permute-start.9) | collective-permute-done | bytes 160 | tf_op jit(solution)/shard_map/ppermute | solution.py:25
  46.1 2.3 %collective-permute-done.8 = f32[32]{0:T(128)S(1)} collective-permute-done((f32[32]{0:T(128)S(1)}, f32[32]{0:T(128)S(1)}, u32[]{:S(2)}, u32[]{:S(2)}) %collective-permute-start.8) | collective-permute-done | bytes 160 | tf_op jit(solution)/shard_map/ppermute | solution.py:25
  51.5 3.8 %collective-permute-start.3 = (bf16[3,1,80,512]{3,2,1,0:T(8,128)(2,1)}, bf16[3,1,80,512]{3,2,1,0:T(8,128)(2,1)}, u32[]{:S(2)}, u32[]{:S(2)}) collective-permute-start(bf16[3,1,80,512]{3,2,1,0:T(8,128)(2,1)} %slice.52), channel_id=1, source_target_pairs={{0,4},{4,8},{8,12},{1,5},{5,9},{9,13},{2,6},{6,10},{10,14},{3,7},{... | collective-permute-start | bytes 737288 | tf_op jit(solution)/shard_map/ppermute | solution.py:94
  59.2 6.5 %collective-permute-done.3 = bf16[3,1,80,512]{3,2,1,0:T(8,128)(2,1)} collective-permute-done((bf16[3,1,80,512]{3,2,1,0:T(8,128)(2,1)}, bf16[3,1,80,512]{3,2,1,0:T(8,128)(2,1)}, u32[]{:S(2)}, u32[]{:S(2)}) %collective-permute-start.3) | collective-permute-done | bytes 245792 | tf_op jit(solution)/shard_map/ppermute | solution.py:94
  69.7 20.3 %collective-permute-done.4 = bf16[3,1,80,512]{3,2,1,0:T(8,128)(2,1)S(1)} collective-permute-done((bf16[3,1,80,512]{3,2,1,0:T(8,128)(2,1)S(1)}, bf16[3,1,80,512]{3,2,1,0:T(8,128)(2,1)S(1)}, u32[]{:S(2)}, u32[]{:S(2)}) %collective-permute-start.4) | collective-permute-done | bytes 245792 | tf_op jit(solution)/shard_map/ppermute | solution.py:95
  92.7 5.1 %fusion = (bf16[1,5,10,80,512]{4,3,2,1,0:T(8,128)(2,1)S(1)}, bf16[1,5,10,80,512]{4,3,2,1,0:T(8,128)(2,1)S(1)}) fusion(bf16[5,10,80,512]{3,2,1,0:T(8,128)(2,1)S(1)} %get-tuple-element.18), kind=kLoop, calls=%fused_computation.8 | loop fusion | bytes 12288000 | tf_op jit(solution)/shard_map/stack | solution.py:122
  97.8 8.6 %pad_maximum_fusion.x_ref = bf16[3,5,10,80,512]{4,3,2,1,0:T(8,128)(2,1)} fusion(bf16[1,5,10,80,512]{4,3,2,1,0:T(8,128)(2,1)S(1)} %get-tuple-element.14, bf16[1,5,10,80,512]{4,3,2,1,0:T(8,128)(2,1)S(1)} %get-tuple-element.17, bf16[1,5,10,80,512]{4,3,2,1,0:T(8,128)(2,1)S(1)} %get-tuple-element.13), kind=kLoop, calls=%fused_computation | loop fusion | flops 12288000 | bytes 24576000 | tf_op jit(solution)/shard_map/stack | solution.py:122
  106.4 21.1 %shard_map.91 = bf16[3,8,80,128]{3,2,1,0:T(8,128)(2,1)} custom-call(bf16[3,5,10,80,512]{4,3,2,1,0:T(8,128)(2,1)} %pad_maximum_fusion.x_ref, bf16[27,512,128]{2,1,0:T(8,128)(2,1)} %all-gather.3.cloned.1.call-done.w_ref, f32[1,128]{1,0:T(1,128)} %dynamic-slice_bitcast_fusion.1.b_ref), custom_call_target="tpu_custom_call" | custom-call | flops 6794772480 | bytes 16809984 | tf_op jit(solution)/shard_map/pallas_call | solution.py:126
  129.9 4.3 %collective-permute-start.16 = (bf16[3,1,80,128]{3,2,1,0:T(8,128)(2,1)S(1)}, bf16[3,1,80,128]{3,2,1,0:T(8,128)(2,1)S(1)}, u32[]{:S(2)}, u32[]{:S(2)}) collective-permute-start(bf16[3,1,80,128]{3,2,1,0:T(8,128)(2,1)S(1)} %get-tuple-element.38), channel_id=1, source_target_pairs={{0,4},{4,8},{8,12},{1,5},{5,9},{9,13},{2,6},{6,10},{10,14},{3,7},{... | collective-permute-start | bytes 184328 | tf_op jit(solution)/shard_map/ppermute | solution.py:94
  135.7 2.1 collective-permute-start.21
  138.0 5.1 %collective-permute-done.17 = bf16[3,1,80,128]{3,2,1,0:T(8,128)(2,1)S(1)} collective-permute-done((bf16[3,1,80,128]{3,2,1,0:T(8,128)(2,1)S(1)}, bf16[3,1,80,128]{3,2,1,0:T(8,128)(2,1)S(1)}, u32[]{:S(2)}, u32[]{:S(2)}) %collective-permute-start.17) | collective-permute-done | bytes 61472 | tf_op jit(solution)/shard_map/ppermute | solution.py:95
  147.8 3.5 %collective-permute-done.23 = f32[8]{0:T(128)S(1)} collective-permute-done((f32[8]{0:T(128)S(1)}, f32[8]{0:T(128)S(1)}, u32[]{:S(2)}, u32[]{:S(2)}) %collective-permute-start.23) | collective-permute-done | bytes 64 | tf_op jit(solution)/shard_map/ppermute | solution.py:25
  151.4 2.4 %collective-permute-start.24 = (f32[8]{0:T(128)S(1)}, f32[8]{0:T(128)S(1)}, u32[]{:S(2)}, u32[]{:S(2)}) collective-permute-start(f32[8]{0:T(128)S(1)} %get-tuple-element.47), channel_id=1, source_target_pairs={{0,8},{4,12},{8,0},{12,4},{1,9},{5,13},{9,1},{13,5},{2,10},{6,14},... | collective-permute-start | bytes 104 | tf_op jit(solution)/shard_map/ppermute | solution.py:25
  156.5 2.7 %collective-permute-start.27 = (f32[2,8]{1,0:T(2,128)S(1)}, f32[2,8]{1,0:T(2,128)S(1)}, u32[]{:S(2)}, u32[]{:S(2)}) collective-permute-start(f32[2,8]{1,0:T(2,128)S(1)} %pad_maximum_fusion.6), channel_id=1, source_target_pairs={{0,1},{1,0},{2,3},{3,2},{4,5},{5,4},{6,7},{7,6},{8,9},{9,8},{10,11... | collective-permute-start | bytes 200 | tf_op jit(solution)/shard_map/ppermute | solution.py:66
  159.7 2.9 %collective-permute-start.26 = (f32[2,8]{1,0:T(2,128)S(1)}, f32[2,8]{1,0:T(2,128)S(1)}, u32[]{:S(2)}, u32[]{:S(2)}) collective-permute-start(f32[2,8]{1,0:T(2,128)S(1)} %collective-permute-done.25), channel_id=1, source_target_pairs={{0,1},{1,0},{2,3},{3,2},{4,5},{5,4},{6,7},{7,6},{8,9},{9,8},{10,11... | collective-permute-start | bytes 200 | tf_op jit(solution)/shard_map/ppermute | solution.py:66
  171.1 5.1 %fusion.2 = (bf16[1,5,10,80,512]{4,3,2,1,0:T(8,128)(2,1)S(1)}, bf16[1,5,10,80,512]{4,3,2,1,0:T(8,128)(2,1)S(1)}) fusion(bf16[5,10,80,512]{3,2,1,0:T(8,128)(2,1)S(1)} %get-tuple-element.16), kind=kLoop, calls=%fused_computation.10 | loop fusion | bytes 12288000 | tf_op jit(solution)/shard_map/stack | solution.py:122
  176.2 8.6 %pad_maximum_fusion.1.x_ref = bf16[3,5,10,80,512]{4,3,2,1,0:T(8,128)(2,1)} fusion(bf16[1,5,10,80,512]{4,3,2,1,0:T(8,128)(2,1)S(1)} %get-tuple-element.12, bf16[1,5,10,80,512]{4,3,2,1,0:T(8,128)(2,1)S(1)} %get-tuple-element.15, bf16[1,5,10,80,512]{4,3,2,1,0:T(8,128)(2,1)S(1)} %get-tuple-element.11), kind=kLoop, calls=%fused_computation.1 | loop fusion | flops 12288000 | bytes 24576000 | tf_op jit(solution)/shard_map/stack | solution.py:122
  184.8 20.6 %shard_map.92 = f32[3,8,80,128]{3,2,1,0:T(8,128)} custom-call(bf16[3,5,10,80,512]{4,3,2,1,0:T(8,128)(2,1)} %pad_maximum_fusion.1.x_ref, bf16[27,512,128]{2,1,0:T(8,128)(2,1)} %all-gather.5.cloned.1.call-done.w_ref, f32[1,128]{1,0:T(1,128)} %dynamic-slice_bitcast_fusion.b_ref), custom_call_target="tpu_custom_call" | custom-call | flops 6794772480 | bytes 16809984 | tf_op jit(solution)/shard_map/pallas_call | solution.py:126
  209.0 3.7 %collective-permute-done.31 = bf16[3,2,80,128]{3,2,1,0:T(8,128)(2,1)S(1)} collective-permute-done((bf16[3,2,80,128]{3,2,1,0:T(8,128)(2,1)S(1)}, bf16[3,2,80,128]{3,2,1,0:T(8,128)(2,1)S(1)}, u32[]{:S(2)}, u32[]{:S(2)}) %collective-permute-start.31) | collective-permute-done | bytes 122912 | tf_op jit(solution)/shard_map/ppermute | solution.py:165
  214.4 2.2 reshape.59
  (156 shorter events, 60.9 us)
Async XLA Ops:
  6.5 99.8 %all-gather.3.cloned.1.call-start = ((), (), s32[]{:S(2)}) async-start(), calls=%async_computation | async-start | bytes 4423680 | tf_op jit(solution)/shard_map/all_gather | solution.py:154
  8.3 7.3 %collective-permute-start.13 = (bf16[27,32,128]{2,1,0:T(8,128)(2,1)S(1)}, bf16[27,32,128]{2,1,0:T(8,128)(2,1)}, u32[]{:S(2)}, u32[]{:S(2)}) collective-permute-start(bf16[27,32,128]{2,1,0:T(8,128)(2,1)S(1)} %get-tuple-element.28), channel_id=1, source_target_pairs={{0,1},{1,2},{2,3},{3,0},{4,5},{5,6},{6,7},{7,4},{8,9},{9,10},{10,1... | collective-permute-start | bytes 663560 | tf_op jit(solution)/shard_map/ppermute | solution.py:151
  11.0 9.4 %collective-permute-start.14 = (bf16[27,32,128]{2,1,0:T(8,128)(2,1)S(1)}, bf16[27,32,128]{2,1,0:T(8,128)(2,1)S(1)}, u32[]{:S(2)}, u32[]{:S(2)}) collective-permute-start(bf16[27,32,128]{2,1,0:T(8,128)(2,1)S(1)} %get-tuple-element.30), channel_id=1, source_target_pairs={{0,2},{1,3},{2,0},{3,1},{4,6},{5,7},{6,4},{7,5},{8,10},{9,11},{10,... | collective-permute-start | bytes 663560 | tf_op jit(solution)/shard_map/ppermute | solution.py:151
  11.0 9.9 %collective-permute-start.15 = (bf16[27,32,128]{2,1,0:T(8,128)(2,1)S(1)}, bf16[27,32,128]{2,1,0:T(8,128)(2,1)S(1)}, u32[]{:S(2)}, u32[]{:S(2)}) collective-permute-start(bf16[27,32,128]{2,1,0:T(8,128)(2,1)S(1)} %get-tuple-element.27), channel_id=1, source_target_pairs={{0,3},{1,0},{2,1},{3,2},{4,7},{5,4},{6,5},{7,6},{8,11},{9,8},{10,9... | collective-permute-start | bytes 663560 | tf_op jit(solution)/shard_map/ppermute | solution.py:151
  21.9 162.9 %all-gather.5.cloned.1.call-start = ((), (), s32[]{:S(2)}) async-start(), calls=%async_computation.1 | async-start | bytes 4423680 | tf_op jit(solution)/shard_map/all_gather | solution.py:154
  21.9 14.8 %collective-permute-start = (bf16[3,2,80,512]{3,2,1,0:T(8,128)(2,1)S(1)}, bf16[3,2,80,512]{3,2,1,0:T(8,128)(2,1)S(1)}, u32[]{:S(2)}, u32[]{:S(2)}) collective-permute-start(bf16[3,2,80,512]{3,2,1,0:T(8,128)(2,1)S(1)} %copy-done.2), channel_id=1, source_target_pairs={{0,2},{2,0},{1,3},{3,1},{4,6},{6,4},{5,7},{7,5},{8,10},{10,8},{9,1... | collective-permute-start | bytes 1474568 | tf_op jit(solution)/shard_map/ppermute | solution.py:62
  24.0 26.6 %collective-permute-start.2 = (bf16[3,2,80,512]{3,2,1,0:T(8,128)(2,1)S(1)}, bf16[3,2,80,512]{3,2,1,0:T(8,128)(2,1)S(1)}, u32[]{:S(2)}, u32[]{:S(2)}) collective-permute-start(bf16[3,2,80,512]{3,2,1,0:T(8,128)(2,1)S(1)} %copy-done.2), channel_id=1, source_target_pairs={{0,1},{1,0},{2,3},{3,2},{4,5},{5,4},{6,7},{7,6},{8,9},{9,8},{10,11... | collective-permute-start | bytes 1474568 | tf_op jit(solution)/shard_map/ppermute | solution.py:66
  24.3 11.3 %collective-permute-start.5 = (f32[32]{0:T(128)S(1)}, f32[32]{0:T(128)S(1)}, u32[]{:S(2)}, u32[]{:S(2)}) collective-permute-start(f32[32]{0:T(128)S(1)} %reduce_sum.51), channel_id=1, source_target_pairs={{0,2},{2,0},{1,3},{3,1},{4,6},{6,4},{5,7},{7,5},{8,10},{10,8},{9,1... | collective-permute-start | bytes 392 | tf_op jit(solution)/shard_map/ppermute | solution.py:25
  25.1 10.4 %collective-permute-start.9 = (f32[32]{0:T(128)S(1)}, f32[32]{0:T(128)S(1)}, u32[]{:S(2)}, u32[]{:S(2)}) collective-permute-start(f32[32]{0:T(128)S(1)} %reduce_sum.54), channel_id=1, source_target_pairs={{0,2},{2,0},{1,3},{3,1},{4,6},{6,4},{5,7},{7,5},{8,10},{10,8},{9,1... | collective-permute-start | bytes 392 | tf_op jit(solution)/shard_map/ppermute | solution.py:25
  27.6 27.7 %collective-permute-start.28 = (bf16[27,32,128]{2,1,0:T(8,128)(2,1)}, bf16[27,32,128]{2,1,0:T(8,128)(2,1)}, u32[]{:S(2)}, u32[]{:S(2)}) collective-permute-start(bf16[27,32,128]{2,1,0:T(8,128)(2,1)} %get-tuple-element.24), channel_id=1, source_target_pairs={{0,1},{1,2},{2,3},{3,0},{4,5},{5,6},{6,7},{7,4},{8,9},{9,10},{10,1... | collective-permute-start | bytes 663560 | tf_op jit(solution)/shard_map/ppermute | solution.py:151
  36.7 13.9 %collective-permute-start.1 = (bf16[3,2,80,512]{3,2,1,0:T(8,128)(2,1)S(1)}, bf16[3,2,80,512]{3,2,1,0:T(8,128)(2,1)S(1)}, u32[]{:S(2)}, u32[]{:S(2)}) collective-permute-start(bf16[3,2,80,512]{3,2,1,0:T(8,128)(2,1)S(1)} %collective-permute-done), channel_id=1, source_target_pairs={{0,1},{1,0},{2,3},{3,2},{4,5},{5,4},{6,7},{7,6},{8,9},{9,8},{10,11... | collective-permute-start | bytes 1474568 | tf_op jit(solution)/shard_map/ppermute | solution.py:66
  43.9 4.6 %collective-permute-start.8 = (f32[32]{0:T(128)S(1)}, f32[32]{0:T(128)S(1)}, u32[]{:S(2)}, u32[]{:S(2)}) collective-permute-start(f32[32]{0:T(128)S(1)} %get-tuple-element.52), channel_id=1, source_target_pairs={{0,8},{4,12},{8,0},{12,4},{1,9},{5,13},{9,1},{13,5},{2,10},{6,14},... | collective-permute-start | bytes 392 | tf_op jit(solution)/shard_map/ppermute | solution.py:25
  45.7 10.6 %collective-permute-start.29 = (bf16[27,32,128]{2,1,0:T(8,128)(2,1)}, bf16[27,32,128]{2,1,0:T(8,128)(2,1)}, u32[]{:S(2)}, u32[]{:S(2)}) collective-permute-start(bf16[27,32,128]{2,1,0:T(8,128)(2,1)} %get-tuple-element.26), channel_id=1, source_target_pairs={{0,2},{1,3},{2,0},{3,1},{4,6},{5,7},{6,4},{7,5},{8,10},{9,11},{10,... | collective-permute-start | bytes 663560 | tf_op jit(solution)/shard_map/ppermute | solution.py:151
  48.5 8.8 %collective-permute-start.30 = (bf16[27,32,128]{2,1,0:T(8,128)(2,1)}, bf16[27,32,128]{2,1,0:T(8,128)(2,1)}, u32[]{:S(2)}, u32[]{:S(2)}) collective-permute-start(bf16[27,32,128]{2,1,0:T(8,128)(2,1)} %get-tuple-element.23), channel_id=1, source_target_pairs={{0,3},{1,0},{2,1},{3,2},{4,7},{5,4},{6,5},{7,6},{8,11},{9,8},{10,9... | collective-permute-start | bytes 663560 | tf_op jit(solution)/shard_map/ppermute | solution.py:151
  51.5 14.3 %collective-permute-start.3 = (bf16[3,1,80,512]{3,2,1,0:T(8,128)(2,1)}, bf16[3,1,80,512]{3,2,1,0:T(8,128)(2,1)}, u32[]{:S(2)}, u32[]{:S(2)}) collective-permute-start(bf16[3,1,80,512]{3,2,1,0:T(8,128)(2,1)} %slice.52), channel_id=1, source_target_pairs={{0,4},{4,8},{8,12},{1,5},{5,9},{9,13},{2,6},{6,10},{10,14},{3,7},{... | collective-permute-start | bytes 737288 | tf_op jit(solution)/shard_map/ppermute | solution.py:94
  67.1 23.0 %collective-permute-start.4 = (bf16[3,1,80,512]{3,2,1,0:T(8,128)(2,1)S(1)}, bf16[3,1,80,512]{3,2,1,0:T(8,128)(2,1)S(1)}, u32[]{:S(2)}, u32[]{:S(2)}) collective-permute-start(bf16[3,1,80,512]{3,2,1,0:T(8,128)(2,1)S(1)} %slice.53), channel_id=1, source_target_pairs={{4,0},{8,4},{12,8},{5,1},{9,5},{13,9},{6,2},{10,6},{14,10},{7,3},{... | collective-permute-start | bytes 737288 | tf_op jit(solution)/shard_map/ppermute | solution.py:95
  129.9 8.1 %collective-permute-start.16 = (bf16[3,1,80,128]{3,2,1,0:T(8,128)(2,1)S(1)}, bf16[3,1,80,128]{3,2,1,0:T(8,128)(2,1)S(1)}, u32[]{:S(2)}, u32[]{:S(2)}) collective-permute-start(bf16[3,1,80,128]{3,2,1,0:T(8,128)(2,1)S(1)} %get-tuple-element.38), channel_id=1, source_target_pairs={{0,4},{4,8},{8,12},{1,5},{5,9},{9,13},{2,6},{6,10},{10,14},{3,7},{... | collective-permute-start | bytes 184328 | tf_op jit(solution)/shard_map/ppermute | solution.py:94
  134.2 8.9 %collective-permute-start.17 = (bf16[3,1,80,128]{3,2,1,0:T(8,128)(2,1)S(1)}, bf16[3,1,80,128]{3,2,1,0:T(8,128)(2,1)S(1)}, u32[]{:S(2)}, u32[]{:S(2)}) collective-permute-start(bf16[3,1,80,128]{3,2,1,0:T(8,128)(2,1)S(1)} %get-tuple-element.39), channel_id=1, source_target_pairs={{4,0},{8,4},{12,8},{5,1},{9,5},{13,9},{6,2},{10,6},{14,10},{7,3},{... | collective-permute-start | bytes 184328 | tf_op jit(solution)/shard_map/ppermute | solution.py:95
  135.7 15.7 %collective-permute-start.21 = (f32[8]{0:T(128)S(1)}, f32[8]{0:T(128)S(1)}, u32[]{:S(2)}, u32[]{:S(2)}) collective-permute-start(f32[8]{0:T(128)S(1)} %reduce_sum.72), channel_id=1, source_target_pairs={{0,4},{4,0},{8,12},{12,8},{1,5},{5,1},{9,13},{13,9},{2,6},{6,2},{1... | collective-permute-start | bytes 104 | tf_op jit(solution)/shard_map/ppermute | solution.py:25
  145.0 17.7 %collective-permute-start.18 = (bf16[3,10,80,128]{3,2,1,0:T(8,128)(2,1)}, bf16[3,10,80,128]{3,2,1,0:T(8,128)(2,1)S(1)}, u32[]{:S(2)}, u32[]{:S(2)}) collective-permute-start(bf16[3,10,80,128]{3,2,1,0:T(8,128)(2,1)} %pad_maximum_fusion.4), channel_id=1, source_target_pairs={{0,2},{2,0},{1,3},{3,1},{4,6},{6,4},{5,7},{7,5},{8,10},{10,8},{9,1... | collective-permute-start | bytes 1843208 | tf_op jit(solution)/shard_map/ppermute | solution.py:62
  156.5 6.7 %collective-permute-start.27 = (f32[2,8]{1,0:T(2,128)S(1)}, f32[2,8]{1,0:T(2,128)S(1)}, u32[]{:S(2)}, u32[]{:S(2)}) collective-permute-start(f32[2,8]{1,0:T(2,128)S(1)} %pad_maximum_fusion.6), channel_id=1, source_target_pairs={{0,1},{1,0},{2,3},{3,2},{4,5},{5,4},{6,7},{7,6},{8,9},{9,8},{10,11... | collective-permute-start | bytes 200 | tf_op jit(solution)/shard_map/ppermute | solution.py:66
  206.8 5.9 %collective-permute-start.31 = (bf16[3,2,80,128]{3,2,1,0:T(8,128)(2,1)S(1)}, bf16[3,2,80,128]{3,2,1,0:T(8,128)(2,1)S(1)}, u32[]{:S(2)}, u32[]{:S(2)}) collective-permute-start(bf16[3,2,80,128]{3,2,1,0:T(8,128)(2,1)S(1)} %get-tuple-element.37), channel_id=1, source_target_pairs={{0,3},{1,0},{2,1},{3,2},{4,7},{5,4},{6,5},{7,6},{8,11},{9,8},{10,9... | collective-permute-start | bytes 368648 | tf_op jit(solution)/shard_map/ppermute | solution.py:165
  207.0 5.7 %collective-permute-start.32 = (bf16[3,2,80,128]{3,2,1,0:T(8,128)(2,1)S(1)}, bf16[3,2,80,128]{3,2,1,0:T(8,128)(2,1)S(1)}, u32[]{:S(2)}, u32[]{:S(2)}) collective-permute-start(bf16[3,2,80,128]{3,2,1,0:T(8,128)(2,1)S(1)} %get-tuple-element.36), channel_id=1, source_target_pairs={{0,2},{1,3},{2,0},{3,1},{4,6},{5,7},{6,4},{7,5},{8,10},{9,11},{10,... | collective-permute-start | bytes 368648 | tf_op jit(solution)/shard_map/ppermute | solution.py:165
  207.1 5.6 %collective-permute-start.33 = (bf16[3,2,80,128]{3,2,1,0:T(8,128)(2,1)S(1)}, bf16[3,2,80,128]{3,2,1,0:T(8,128)(2,1)S(1)}, u32[]{:S(2)}, u32[]{:S(2)}) collective-permute-start(bf16[3,2,80,128]{3,2,1,0:T(8,128)(2,1)S(1)} %get-tuple-element.35), channel_id=1, source_target_pairs={{0,1},{1,2},{2,3},{3,0},{4,5},{5,6},{6,7},{7,4},{8,9},{9,10},{10,1... | collective-permute-start | bytes 368648 | tf_op jit(solution)/shard_map/ppermute | solution.py:165
  (24 other events, 255.1 us)
Sparse Core Ops, SparseCore 0:
  22.0 76.6 all-gather.2
  100.3 69.8 all-gather.4

commit v14 on v7

--- a/solution.py
+++ b/solution.py
@@ -136,6 +136,32 @@
     )(padded, kernel, bias.reshape(1, outs))
 
 
+def upsample_body(x_ref, d_ref, o_ref):
+    frames, rows = x_ref.shape[:2]
+    for t in range(frames):
+        for h in range(rows):
+            wide = jnp.dot(d_ref[...], x_ref[t, h], preferred_element_type=jnp.float32)
+            wide = wide.astype(o_ref.dtype)
+            o_ref[t, 2 * h] = wide
+            o_ref[t, 2 * h + 1] = wide
+
+
+def upsample(cells):
+    frames, rows, cols, chans = cells.shape
+    wide_col = lax.broadcasted_iota(jnp.int32, (2 * cols, cols), 0) // 2
+    narrow_col = lax.broadcasted_iota(jnp.int32, (2 * cols, cols), 1)
+    dup = (wide_col == narrow_col).astype(cells.dtype)
+    return pl.pallas_call(
+        upsample_body,
+        out_shape=jax.ShapeDtypeStruct((frames, 2 * rows, 2 * cols, chans), cells.dtype),
+        in_specs=[
+            pl.BlockSpec(memory_space=pltpu.VMEM),
+            pl.BlockSpec(memory_space=pltpu.VMEM),
+        ],
+        out_specs=pl.BlockSpec(memory_space=pltpu.VMEM),
+    )(cells, dup)
+
+
 def kernel_block(shard, chans):
     size = lax.axis_size("ha") * lax.axis_size("hb")
     me = lax.axis_index(HQ)
@@ -208,7 +234,7 @@
     own_latent = lax.dynamic_slice_in_dim(raw_rows[:, 1:-1], me * width, width, axis=3)
     summed = (own_latent.astype(jnp.float32) + branch).astype(jnp.bfloat16)
     summed_rows = scatter_rows(summed, slab_rows, chans)
-    return jnp.repeat(jnp.repeat(summed_rows, 2, axis=1), 2, axis=2)
+    return upsample(summed_rows)
 
 
 def solution(mesh):

time: 210 us -> 210 us (level)
  local copies, waits for them, and re-layouts: 29.4 us -> 26.6 us
  Pallas kernels: 37 us -> 39.7 us
    pallas_call x0 -> x1, Pallas kernels: none -> 2.69 us  [upsample(): pl.pallas_call(upsample_body, out_shape=jax.ShapeDtypeStruct((frames, 2 *...]
    reshape x1 -> x0, local copies, waits for them, and re-layouts: 2.19 us -> none  [per_device(): return jnp.repeat(jnp.repeat(summed_rows, 2, axis=1), 2, axis=2)]
where the time goes in v14:
time: 210 us; the launch traced here: 209 us
  waiting for transfers between devices  63.8 us (30%)
  starting transfers between devices  48 us (23%)
  Pallas kernels  39.7 us (19%)
  local copies, waits for them, and re-layouts  26.6 us (13%)
  other arithmetic  16.8 us (8%)
  between operations  13.9 us (7%)
    pallas_call x2, Pallas kernels, causal_conv(): pl.pallas_call(conv_body, grid=(frames,), in_specs=[pl.BlockSpec(padded.s...  37 us
    all_gather x2, waiting for transfers between devices, kernel_block(): return lax.all_gather(out, 'hz', axis=1, tiled=True)  20.9 us
    ppermute x12, waiting for transfers between devices, butterfly_stats(): other_sums, other_squares = lax.ppermute((sums, squares), axis, pairs)  15.4 us
    ppermute x2, waiting for transfers between devices, with_row_halo(): bottom = lax.ppermute(cells[:, :1], axis_name, up)  13.4 us
    ppermute x6, starting transfers between devices, chip_gather(): lax.ppermute(firsts, 'hb', shift_pairs(count_b, step))  12.3 us
    ppermute x12, starting transfers between devices, butterfly_stats(): other_sums, other_squares = lax.ppermute((sums, squares), axis, pairs)  11.7 us
    dynamic_update_slice x11, local copies, waits for them, and re-layouts, chip_gather(): out = lax.dynamic_update_slice(out, piece, start)  9.94 us
    ppermute x6, waiting for transfers between devices, kernel_block(): piece = lax.ppermute(piece, HQ, shift_pairs(size, step))  8.4 us
  transfers between devices with their start and end apart: 36, of which 20 were waited for; matrix products, arithmetic and copies ran while one was open for 18% of the time, Pallas kernels for 9%

profile of v14, /device:TPU:1, one launch (start us, length us, event | category | flops | bytes accessed | tf_op | source)
XLA Modules:
  0.0 208.8 jit_solution(13359773410839402426)
XLA Ops:
  8.3 2.7 %collective-permute-start.13 = (bf16[27,32,128]{2,1,0:T(8,128)(2,1)S(1)}, bf16[27,32,128]{2,1,0:T(8,128)(2,1)}, u32[]{:S(2)}, u32[]{:S(2)}) collective-permute-start(bf16[27,32,128]{2,1,0:T(8,128)(2,1)S(1)} %get-tuple-element.12), channel_id=1, source_target_pairs={{0,1},{1,2},{2,3},{3,0},{4,5},{5,6},{6,7},{7,4},{8,9},{9,10},{10,1... | collective-permute-start | bytes 663560 | tf_op jit(solution)/shard_map/ppermute | solution.py:175
  11.5 4.2 %collective-permute-done.13 = bf16[27,32,128]{2,1,0:T(8,128)(2,1)} collective-permute-done((bf16[27,32,128]{2,1,0:T(8,128)(2,1)S(1)}, bf16[27,32,128]{2,1,0:T(8,128)(2,1)}, u32[]{:S(2)}, u32[]{:S(2)}) %collective-permute-start.13) | collective-permute-done | bytes 221216 | tf_op jit(solution)/shard_map/ppermute | solution.py:175
  16.6 3.8 %collective-permute-done.14 = bf16[27,32,128]{2,1,0:T(8,128)(2,1)S(1)} collective-permute-done((bf16[27,32,128]{2,1,0:T(8,128)(2,1)S(1)}, bf16[27,32,128]{2,1,0:T(8,128)(2,1)S(1)}, u32[]{:S(2)}, u32[]{:S(2)}) %collective-permute-start.14) | collective-permute-done | bytes 221216 | tf_op jit(solution)/shard_map/ppermute | solution.py:175
  21.9 2.1 collective-permute-start
  29.6 6.0 %collective-permute-done.5 = f32[32]{0:T(128)S(1)} collective-permute-done((f32[32]{0:T(128)S(1)}, f32[32]{0:T(128)S(1)}, u32[]{:S(2)}, u32[]{:S(2)}) %collective-permute-start.5) | collective-permute-done | bytes 160 | tf_op jit(solution)/shard_map/ppermute | solution.py:25
  46.1 2.3 %collective-permute-done.12 = f32[32]{0:T(128)S(1)} collective-permute-done((f32[32]{0:T(128)S(1)}, f32[32]{0:T(128)S(1)}, u32[]{:S(2)}, u32[]{:S(2)}) %collective-permute-start.12) | collective-permute-done | bytes 160 | tf_op jit(solution)/shard_map/ppermute | solution.py:25
  56.0 4.0 %collective-permute-start.3 = (bf16[3,1,80,512]{3,2,1,0:T(8,128)(2,1)}, bf16[3,1,80,512]{3,2,1,0:T(8,128)(2,1)S(1)}, u32[]{:S(2)}, u32[]{:S(2)}) collective-permute-start(bf16[3,1,80,512]{3,2,1,0:T(8,128)(2,1)} %get-tuple-element.5), channel_id=1, source_target_pairs={{0,4},{4,8},{8,12},{1,5},{5,9},{9,13},{2,6},{6,10},{10,14},{3,7},{... | collective-permute-start | bytes 737288 | tf_op jit(solution)/shard_map/ppermute | solution.py:93
  64.0 12.2 %collective-permute-done.4 = bf16[3,1,80,512]{3,2,1,0:T(8,128)(2,1)S(1)} collective-permute-done((bf16[3,1,80,512]{3,2,1,0:T(8,128)(2,1)}, bf16[3,1,80,512]{3,2,1,0:T(8,128)(2,1)S(1)}, u32[]{:S(2)}, u32[]{:S(2)}) %collective-permute-start.4) | collective-permute-done | bytes 245792 | tf_op jit(solution)/shard_map/ppermute | solution.py:94
  78.2 3.1 %fusion.5.x_ref = bf16[5,10,82,512]{3,2,1,0:T(8,128)(2,1)} fusion(bf16[3,10,80,512]{3,2,1,0:T(8,128)(2,1)S(1)} %fusion.6, bf16[1,10,80,512]{3,2,1,0:T(8,128)(2,1)S(1)} %slice.36), kind=kLoop, calls=%fused_computation.11 | loop fusion | flops 25190400 | bytes 7475200 | tf_op jit(solution)/shard_map/concatenate | solution.py:116
  81.3 17.3 %all-gather.3.cloned.1.call-done.w_ref = bf16[27,512,128]{2,1,0:T(8,128)(2,1)} async-done(((bf16[27,128,128]{2,1,0:T(8,128)(2,1)}), bf16[27,512,128]{2,1,0:T(8,128)(2,1)}) %all-gather.3.cloned.1.call-update) | async-done | bytes 3538960 | tf_op jit(solution)/shard_map/all_gather | solution.py:178
  98.7 18.5 %shard_map.91 = bf16[3,8,80,128]{3,2,1,0:T(8,128)(2,1)} custom-call(bf16[5,10,82,512]{3,2,1,0:T(8,128)(2,1)} %fusion.5.x_ref, bf16[27,512,128]{2,1,0:T(8,128)(2,1)} %all-gather.3.cloned.1.call-done.w_ref, f32[1,128]{1,0:T(1,128)} %dynamic-slice_bitcast_fusion.1.b_ref), custom_call_target="tpu_custom_call" | custom-call | flops 6794772480 | bytes 8720384 | tf_op jit(solution)/shard_map/pallas_call | solution.py:124
  119.4 4.2 %collective-permute-start.16 = (bf16[3,1,80,128]{3,2,1,0:T(8,128)(2,1)S(1)}, bf16[3,1,80,128]{3,2,1,0:T(8,128)(2,1)S(1)}, u32[]{:S(2)}, u32[]{:S(2)}) collective-permute-start(bf16[3,1,80,128]{3,2,1,0:T(8,128)(2,1)S(1)} %get-tuple-element.21), channel_id=1, source_target_pairs={{0,4},{4,8},{8,12},{1,5},{5,9},{9,13},{2,6},{6,10},{10,14},{3,7},{... | collective-permute-start | bytes 184328 | tf_op jit(solution)/shard_map/ppermute | solution.py:93
  127.8 2.0 pad_maximum_fusion
  131.4 2.7 %collective-permute-start.21 = (f32[8]{0:T(128)S(1)}, f32[8]{0:T(128)S(1)}, u32[]{:S(2)}, u32[]{:S(2)}) collective-permute-start(f32[8]{0:T(128)S(1)} %reduce_sum.72), channel_id=1, source_target_pairs={{0,4},{4,0},{8,12},{12,8},{1,5},{5,1},{9,13},{13,9},{2,6},{6,2},{1... | collective-permute-start | bytes 104 | tf_op jit(solution)/shard_map/ppermute | solution.py:25
  134.8 2.2 %collective-permute-done.21 = f32[8]{0:T(128)S(1)} collective-permute-done((f32[8]{0:T(128)S(1)}, f32[8]{0:T(128)S(1)}, u32[]{:S(2)}, u32[]{:S(2)}) %collective-permute-start.21) | collective-permute-done | bytes 64 | tf_op jit(solution)/shard_map/ppermute | solution.py:25
  140.0 3.3 %collective-permute-start.19 = (bf16[3,10,80,128]{3,2,1,0:T(8,128)(2,1)S(1)}, bf16[3,10,80,128]{3,2,1,0:T(8,128)(2,1)}, u32[]{:S(2)}, u32[]{:S(2)}) collective-permute-start(bf16[3,10,80,128]{3,2,1,0:T(8,128)(2,1)S(1)} %get-tuple-element.15), channel_id=1, source_target_pairs={{0,1},{1,0},{2,3},{3,2},{4,5},{5,4},{6,7},{7,6},{8,9},{9,8},{10,11... | collective-permute-start | bytes 1843208 | tf_op jit(solution)/shard_map/ppermute | solution.py:71
  143.2 3.0 %collective-permute-start.20 = (bf16[3,10,80,128]{3,2,1,0:T(8,128)(2,1)}, bf16[3,10,80,128]{3,2,1,0:T(8,128)(2,1)}, u32[]{:S(2)}, u32[]{:S(2)}) collective-permute-start(bf16[3,10,80,128]{3,2,1,0:T(8,128)(2,1)} %collective-permute-done.18), channel_id=1, source_target_pairs={{0,1},{1,0},{2,3},{3,2},{4,5},{5,4},{6,7},{7,6},{8,9},{9,8},{10,11... | collective-permute-start | bytes 1843208 | tf_op jit(solution)/shard_map/ppermute | solution.py:71
  147.4 3.4 %collective-permute-start.26 = (f32[2,8]{1,0:T(2,128)S(1)}, f32[2,8]{1,0:T(2,128)S(1)}, u32[]{:S(2)}, u32[]{:S(2)}) collective-permute-start(f32[2,8]{1,0:T(2,128)S(1)} %pad_maximum_fusion.1), channel_id=1, source_target_pairs={{0,1},{1,0},{2,3},{3,2},{4,5},{5,4},{6,7},{7,6},{8,9},{9,8},{10,11... | collective-permute-start | bytes 200 | tf_op jit(solution)/shard_map/ppermute | solution.py:71
  160.2 3.2 %fusion.7 = bf16[3,10,80,512]{3,2,1,0:T(8,128)(2,1)S(1)} fusion(bf16[3,10,80,512]{3,2,1,0:T(8,128)(2,1)} %constant_dynamic-update-slice_fusion.5, f32[512]{0:T(512)S(1)} %copy-done.9, f32[512]{0:T(512)S(1)} %copy-done.10, f32[512]{0:T(512)S(1)} %mul.221, f32[512]{0:T(512)S(1)} %sub.118, pred[10]{0:T(512)(128)(4,1)S(1)} %or_and_fusion), kind=kLoop, calls=%fused_computation.13 | loop fusion | flops 13516800 | bytes 4923402 | tf_op jit(solution)/shard_map/jit(_where)/select_n | solution.py:86
  163.5 3.1 %select_maximum_fusion.x_ref = bf16[5,10,82,512]{3,2,1,0:T(8,128)(2,1)} fusion(bf16[3,10,80,512]{3,2,1,0:T(8,128)(2,1)S(1)} %fusion.7, bf16[1,10,80,512]{3,2,1,0:T(8,128)(2,1)S(1)} %slice.39), kind=kLoop, calls=%fused_computation.5 | loop fusion | flops 25190400 | bytes 7475200 | tf_op jit(solution)/shard_map/concatenate | solution.py:116
  166.6 3.6 %all-gather.5.cloned.1.call-done.w_ref = bf16[27,512,128]{2,1,0:T(8,128)(2,1)} async-done(((bf16[27,128,128]{2,1,0:T(8,128)(2,1)}), bf16[27,512,128]{2,1,0:T(8,128)(2,1)}) %all-gather.5.cloned.1.call-update) | async-done | bytes 3538960 | tf_op jit(solution)/shard_map/all_gather | solution.py:178
  170.2 18.5 %shard_map.92 = f32[3,8,80,128]{3,2,1,0:T(8,128)} custom-call(bf16[5,10,82,512]{3,2,1,0:T(8,128)(2,1)} %select_maximum_fusion.x_ref, bf16[27,512,128]{2,1,0:T(8,128)(2,1)} %all-gather.5.cloned.1.call-done.w_ref, f32[1,128]{1,0:T(1,128)} %dynamic-slice_bitcast_fusion.b_ref), custom_call_target="tpu_custom_call" | custom-call | flops 6794772480 | bytes 8720384 | tf_op jit(solution)/shard_map/pallas_call | solution.py:124
  194.5 3.3 %collective-permute-done.32 = bf16[3,2,80,128]{3,2,1,0:T(8,128)(2,1)S(1)} collective-permute-done((bf16[3,2,80,128]{3,2,1,0:T(8,128)(2,1)S(1)}, bf16[3,2,80,128]{3,2,1,0:T(8,128)(2,1)S(1)}, u32[]{:S(2)}, u32[]{:S(2)}) %collective-permute-start.32) | collective-permute-done | bytes 122912 | tf_op jit(solution)/shard_map/ppermute | solution.py:190
  199.2 2.7 %shard_map.93 = bf16[3,4,160,512]{3,2,1,0:T(8,128)(2,1)} custom-call(bf16[3,2,80,512]{3,2,1,0:T(8,128)(2,1)} %copy-done.5, bf16[160,80]{1,0:T(8,128)(2,1)} %fusion.12.d_ref), custom_call_target="tpu_custom_call" | custom-call | tf_op jit(solution)/shard_map/pallas_call | solution.py:154
  (154 shorter events, 63.7 us)
Async XLA Ops:
  6.5 92.1 %all-gather.3.cloned.1.call-start = ((), (), s32[]{:S(2)}) async-start(), calls=%async_computation | async-start | bytes 4423680 | tf_op jit(solution)/shard_map/all_gather | solution.py:178
  8.3 7.3 %collective-permute-start.13 = (bf16[27,32,128]{2,1,0:T(8,128)(2,1)S(1)}, bf16[27,32,128]{2,1,0:T(8,128)(2,1)}, u32[]{:S(2)}, u32[]{:S(2)}) collective-permute-start(bf16[27,32,128]{2,1,0:T(8,128)(2,1)S(1)} %get-tuple-element.12), channel_id=1, source_target_pairs={{0,1},{1,2},{2,3},{3,0},{4,5},{5,6},{6,7},{7,4},{8,9},{9,10},{10,1... | collective-permute-start | bytes 663560 | tf_op jit(solution)/shard_map/ppermute | solution.py:175
  11.0 9.4 %collective-permute-start.14 = (bf16[27,32,128]{2,1,0:T(8,128)(2,1)S(1)}, bf16[27,32,128]{2,1,0:T(8,128)(2,1)S(1)}, u32[]{:S(2)}, u32[]{:S(2)}) collective-permute-start(bf16[27,32,128]{2,1,0:T(8,128)(2,1)S(1)} %get-tuple-element.14), channel_id=1, source_target_pairs={{0,2},{1,3},{2,0},{3,1},{4,6},{5,7},{6,4},{7,5},{8,10},{9,11},{10,... | collective-permute-start | bytes 663560 | tf_op jit(solution)/shard_map/ppermute | solution.py:175
  11.0 9.9 %collective-permute-start.15 = (bf16[27,32,128]{2,1,0:T(8,128)(2,1)S(1)}, bf16[27,32,128]{2,1,0:T(8,128)(2,1)S(1)}, u32[]{:S(2)}, u32[]{:S(2)}) collective-permute-start(bf16[27,32,128]{2,1,0:T(8,128)(2,1)S(1)} %get-tuple-element.11), channel_id=1, source_target_pairs={{0,3},{1,0},{2,1},{3,2},{4,7},{5,4},{6,5},{7,6},{8,11},{9,8},{10,9... | collective-permute-start | bytes 663560 | tf_op jit(solution)/shard_map/ppermute | solution.py:175
  21.9 148.3 %all-gather.5.cloned.1.call-start = ((), (), s32[]{:S(2)}) async-start(), calls=%async_computation.1 | async-start | bytes 4423680 | tf_op jit(solution)/shard_map/all_gather | solution.py:178
  21.9 17.4 %collective-permute-start = (bf16[3,2,80,512]{3,2,1,0:T(8,128)(2,1)S(1)}, bf16[3,2,80,512]{3,2,1,0:T(8,128)(2,1)}, u32[]{:S(2)}, u32[]{:S(2)}) collective-permute-start(bf16[3,2,80,512]{3,2,1,0:T(8,128)(2,1)S(1)} %copy-done.2), channel_id=1, source_target_pairs={{0,2},{2,0},{1,3},{3,1},{4,6},{6,4},{5,7},{7,5},{8,10},{10,8},{9,1... | collective-permute-start | bytes 1474568 | tf_op jit(solution)/shard_map/ppermute | solution.py:66
  24.0 27.7 %collective-permute-start.1 = (bf16[3,2,80,512]{3,2,1,0:T(8,128)(2,1)S(1)}, bf16[3,2,80,512]{3,2,1,0:T(8,128)(2,1)}, u32[]{:S(2)}, u32[]{:S(2)}) collective-permute-start(bf16[3,2,80,512]{3,2,1,0:T(8,128)(2,1)S(1)} %copy-done.2), channel_id=1, source_target_pairs={{0,1},{1,0},{2,3},{3,2},{4,5},{5,4},{6,7},{7,6},{8,9},{9,8},{10,11... | collective-permute-start | bytes 1474568 | tf_op jit(solution)/shard_map/ppermute | solution.py:71
  24.3 11.3 %collective-permute-start.5 = (f32[32]{0:T(128)S(1)}, f32[32]{0:T(128)S(1)}, u32[]{:S(2)}, u32[]{:S(2)}) collective-permute-start(f32[32]{0:T(128)S(1)} %reduce_sum.51), channel_id=1, source_target_pairs={{0,2},{2,0},{1,3},{3,1},{4,6},{6,4},{5,7},{7,5},{8,10},{10,8},{9,1... | collective-permute-start | bytes 392 | tf_op jit(solution)/shard_map/ppermute | solution.py:25
  25.1 10.4 %collective-permute-start.9 = (f32[32]{0:T(128)S(1)}, f32[32]{0:T(128)S(1)}, u32[]{:S(2)}, u32[]{:S(2)}) collective-permute-start(f32[32]{0:T(128)S(1)} %reduce_sum.54), channel_id=1, source_target_pairs={{0,2},{2,0},{1,3},{3,1},{4,6},{6,4},{5,7},{7,5},{8,10},{10,8},{9,1... | collective-permute-start | bytes 392 | tf_op jit(solution)/shard_map/ppermute | solution.py:25
  27.6 32.4 %collective-permute-start.28 = (bf16[27,32,128]{2,1,0:T(8,128)(2,1)}, bf16[27,32,128]{2,1,0:T(8,128)(2,1)}, u32[]{:S(2)}, u32[]{:S(2)}) collective-permute-start(bf16[27,32,128]{2,1,0:T(8,128)(2,1)} %get-tuple-element.8), channel_id=1, source_target_pairs={{0,1},{1,2},{2,3},{3,0},{4,5},{5,6},{6,7},{7,4},{8,9},{9,10},{10,1... | collective-permute-start | bytes 663560 | tf_op jit(solution)/shard_map/ppermute | solution.py:175
  39.3 13.5 %collective-permute-start.2 = (bf16[3,2,80,512]{3,2,1,0:T(8,128)(2,1)}, bf16[3,2,80,512]{3,2,1,0:T(8,128)(2,1)}, u32[]{:S(2)}, u32[]{:S(2)}) collective-permute-start(bf16[3,2,80,512]{3,2,1,0:T(8,128)(2,1)} %collective-permute-done), channel_id=1, source_target_pairs={{0,1},{1,0},{2,3},{3,2},{4,5},{5,4},{6,7},{7,6},{8,9},{9,8},{10,11... | collective-permute-start | bytes 1474568 | tf_op jit(solution)/shard_map/ppermute | solution.py:71
  45.7 15.3 %collective-permute-start.29 = (bf16[27,32,128]{2,1,0:T(8,128)(2,1)}, bf16[27,32,128]{2,1,0:T(8,128)(2,1)}, u32[]{:S(2)}, u32[]{:S(2)}) collective-permute-start(bf16[27,32,128]{2,1,0:T(8,128)(2,1)} %get-tuple-element.10), channel_id=1, source_target_pairs={{0,2},{1,3},{2,0},{3,1},{4,6},{5,7},{6,4},{7,5},{8,10},{9,11},{10,... | collective-permute-start | bytes 663560 | tf_op jit(solution)/shard_map/ppermute | solution.py:175
  48.5 13.6 %collective-permute-start.30 = (bf16[27,32,128]{2,1,0:T(8,128)(2,1)}, bf16[27,32,128]{2,1,0:T(8,128)(2,1)}, u32[]{:S(2)}, u32[]{:S(2)}) collective-permute-start(bf16[27,32,128]{2,1,0:T(8,128)(2,1)} %get-tuple-element.7), channel_id=1, source_target_pairs={{0,3},{1,0},{2,1},{3,2},{4,7},{5,4},{6,5},{7,6},{8,11},{9,8},{10,9... | collective-permute-start | bytes 663560 | tf_op jit(solution)/shard_map/ppermute | solution.py:175
  54.7 21.5 %collective-permute-start.4 = (bf16[3,1,80,512]{3,2,1,0:T(8,128)(2,1)}, bf16[3,1,80,512]{3,2,1,0:T(8,128)(2,1)S(1)}, u32[]{:S(2)}, u32[]{:S(2)}) collective-permute-start(bf16[3,1,80,512]{3,2,1,0:T(8,128)(2,1)} %get-tuple-element.6), channel_id=1, source_target_pairs={{4,0},{8,4},{12,8},{5,1},{9,5},{13,9},{6,2},{10,6},{14,10},{7,3},{... | collective-permute-start | bytes 737288 | tf_op jit(solution)/shard_map/ppermute | solution.py:94
  56.0 20.2 %collective-permute-start.3 = (bf16[3,1,80,512]{3,2,1,0:T(8,128)(2,1)}, bf16[3,1,80,512]{3,2,1,0:T(8,128)(2,1)S(1)}, u32[]{:S(2)}, u32[]{:S(2)}) collective-permute-start(bf16[3,1,80,512]{3,2,1,0:T(8,128)(2,1)} %get-tuple-element.5), channel_id=1, source_target_pairs={{0,4},{4,8},{8,12},{1,5},{5,9},{9,13},{2,6},{6,10},{10,14},{3,7},{... | collective-permute-start | bytes 737288 | tf_op jit(solution)/shard_map/ppermute | solution.py:93
  118.1 8.0 %collective-permute-start.17 = (bf16[3,1,80,128]{3,2,1,0:T(8,128)(2,1)S(1)}, bf16[3,1,80,128]{3,2,1,0:T(8,128)(2,1)S(1)}, u32[]{:S(2)}, u32[]{:S(2)}) collective-permute-start(bf16[3,1,80,128]{3,2,1,0:T(8,128)(2,1)S(1)} %get-tuple-element.22), channel_id=1, source_target_pairs={{4,0},{8,4},{12,8},{5,1},{9,5},{13,9},{6,2},{10,6},{14,10},{7,3},{... | collective-permute-start | bytes 184328 | tf_op jit(solution)/shard_map/ppermute | solution.py:94
  119.4 6.7 %collective-permute-start.16 = (bf16[3,1,80,128]{3,2,1,0:T(8,128)(2,1)S(1)}, bf16[3,1,80,128]{3,2,1,0:T(8,128)(2,1)S(1)}, u32[]{:S(2)}, u32[]{:S(2)}) collective-permute-start(bf16[3,1,80,128]{3,2,1,0:T(8,128)(2,1)S(1)} %get-tuple-element.21), channel_id=1, source_target_pairs={{0,4},{4,8},{8,12},{1,5},{5,9},{9,13},{2,6},{6,10},{10,14},{3,7},{... | collective-permute-start | bytes 184328 | tf_op jit(solution)/shard_map/ppermute | solution.py:93
  129.8 13.4 %collective-permute-start.18 = (bf16[3,10,80,128]{3,2,1,0:T(8,128)(2,1)S(1)}, bf16[3,10,80,128]{3,2,1,0:T(8,128)(2,1)}, u32[]{:S(2)}, u32[]{:S(2)}) collective-permute-start(bf16[3,10,80,128]{3,2,1,0:T(8,128)(2,1)S(1)} %get-tuple-element.15), channel_id=1, source_target_pairs={{0,2},{2,0},{1,3},{3,1},{4,6},{6,4},{5,7},{7,5},{8,10},{10,8},{9,1... | collective-permute-start | bytes 1843208 | tf_op jit(solution)/shard_map/ppermute | solution.py:66
  137.6 8.6 %collective-permute-start.22 = (f32[8]{0:T(128)S(1)}, f32[8]{0:T(128)S(1)}, u32[]{:S(2)}, u32[]{:S(2)}) collective-permute-start(f32[8]{0:T(128)S(1)} %get-tuple-element.28), channel_id=1, source_target_pairs={{0,8},{4,12},{8,0},{12,4},{1,9},{5,13},{9,1},{13,5},{2,10},{6,14},... | collective-permute-start | bytes 104 | tf_op jit(solution)/shard_map/ppermute | solution.py:25
  139.5 6.7 %collective-permute-start.24 = (f32[8]{0:T(128)S(1)}, f32[8]{0:T(128)S(1)}, u32[]{:S(2)}, u32[]{:S(2)}) collective-permute-start(f32[8]{0:T(128)S(1)} %get-tuple-element.27), channel_id=1, source_target_pairs={{0,8},{4,12},{8,0},{12,4},{1,9},{5,13},{9,1},{13,5},{2,10},{6,14},... | collective-permute-start | bytes 104 | tf_op jit(solution)/shard_map/ppermute | solution.py:25
  140.0 16.3 %collective-permute-start.19 = (bf16[3,10,80,128]{3,2,1,0:T(8,128)(2,1)S(1)}, bf16[3,10,80,128]{3,2,1,0:T(8,128)(2,1)}, u32[]{:S(2)}, u32[]{:S(2)}) collective-permute-start(bf16[3,10,80,128]{3,2,1,0:T(8,128)(2,1)S(1)} %get-tuple-element.15), channel_id=1, source_target_pairs={{0,1},{1,0},{2,3},{3,2},{4,5},{5,4},{6,7},{7,6},{8,9},{9,8},{10,11... | collective-permute-start | bytes 1843208 | tf_op jit(solution)/shard_map/ppermute | solution.py:71
  143.2 15.0 %collective-permute-start.20 = (bf16[3,10,80,128]{3,2,1,0:T(8,128)(2,1)}, bf16[3,10,80,128]{3,2,1,0:T(8,128)(2,1)}, u32[]{:S(2)}, u32[]{:S(2)}) collective-permute-start(bf16[3,10,80,128]{3,2,1,0:T(8,128)(2,1)} %collective-permute-done.18), channel_id=1, source_target_pairs={{0,1},{1,0},{2,3},{3,2},{4,5},{5,4},{6,7},{7,6},{8,9},{9,8},{10,11... | collective-permute-start | bytes 1843208 | tf_op jit(solution)/shard_map/ppermute | solution.py:71
  147.4 5.7 %collective-permute-start.26 = (f32[2,8]{1,0:T(2,128)S(1)}, f32[2,8]{1,0:T(2,128)S(1)}, u32[]{:S(2)}, u32[]{:S(2)}) collective-permute-start(f32[2,8]{1,0:T(2,128)S(1)} %pad_maximum_fusion.1), channel_id=1, source_target_pairs={{0,1},{1,0},{2,3},{3,2},{4,5},{5,4},{6,7},{7,6},{8,9},{9,8},{10,11... | collective-permute-start | bytes 200 | tf_op jit(solution)/shard_map/ppermute | solution.py:71
  191.9 5.9 %collective-permute-start.32 = (bf16[3,2,80,128]{3,2,1,0:T(8,128)(2,1)S(1)}, bf16[3,2,80,128]{3,2,1,0:T(8,128)(2,1)S(1)}, u32[]{:S(2)}, u32[]{:S(2)}) collective-permute-start(bf16[3,2,80,128]{3,2,1,0:T(8,128)(2,1)S(1)} %get-tuple-element.18), channel_id=1, source_target_pairs={{0,2},{1,3},{2,0},{3,1},{4,6},{5,7},{6,4},{7,5},{8,10},{9,11},{10,... | collective-permute-start | bytes 368648 | tf_op jit(solution)/shard_map/ppermute | solution.py:190
  (23 other events, 283.3 us)
Sparse Core Ops, SparseCore 0:
  22.0 76.6 all-gather.2
  100.2 69.8 all-gather.4

commit v15 on v9

--- a/solution.py
+++ b/solution.py
@@ -96,24 +96,27 @@
 
 
 def conv_body(x_ref, w_ref, b_ref, o_ref, acc_ref):
+    tap_row = pl.program_id(0)
+    frame = pl.program_id(1)
     frames, rows, cols, outs = o_ref.shape
     chans = x_ref.shape[-1]
-    acc_ref[...] = jnp.broadcast_to(b_ref[...], acc_ref.shape)
-
-    def tap_row(index, carry):
-        i = index // 3
-        j = index % 3
+
+    @pl.when(tap_row == 0)
+    def _():
+        acc_ref[frame] = jnp.broadcast_to(b_ref[...], acc_ref.shape[1:])
+
+    for j in range(3):
         for k in range(3):
-            patch = x_ref[pl.ds(i, frames), pl.ds(j, rows), pl.ds(k, cols), :]
-            acc_ref[...] += jnp.dot(
-                patch.reshape(frames * rows * cols, chans),
-                w_ref[3 * index + k],
+            patch = x_ref[0, pl.ds(j, rows), pl.ds(k, cols), :]
+            acc_ref[frame] += jnp.dot(
+                patch.reshape(rows * cols, chans),
+                w_ref[3 * j + k],
                 preferred_element_type=jnp.float32,
             )
-        return carry
-
-    lax.fori_loop(0, 9, tap_row, 0)
-    o_ref[...] = acc_ref[...].reshape(frames, rows, cols, outs).astype(o_ref.dtype)
+
+    @pl.when(tap_row == 2)
+    def _():
+        o_ref[frame] = acc_ref[frame].reshape(rows, cols, outs).astype(o_ref.dtype)
 
 
 def causal_conv(extended, kernel, bias, out_dtype):
@@ -124,18 +127,18 @@
     cols = extended.shape[2]
     taps, chans, outs = kernel.shape
     flops = 2 * frames * rows * cols * chans * outs * taps
-    moved = padded.size * 2 + kernel.size * 2 + frames * rows * cols * outs * 4
+    moved = padded.size * 2 * 3 // 5 * 3 + kernel.size * 2 + frames * rows * cols * outs * 4
     return pl.pallas_call(
         conv_body,
-        grid=(1,),
+        grid=(3, frames),
         in_specs=[
-            pl.BlockSpec(padded.shape, lambda t: (0, 0, 0, 0)),
-            pl.BlockSpec(kernel.shape, lambda t: (0, 0, 0)),
-            pl.BlockSpec((1, outs), lambda t: (0, 0)),
+            pl.BlockSpec((1,) + padded.shape[1:], lambda i, t: (t + i, 0, 0, 0)),
+            pl.BlockSpec((9, chans, outs), lambda i, t: (i, 0, 0)),
+            pl.BlockSpec((1, outs), lambda i, t: (0, 0)),
         ],
-        out_specs=pl.BlockSpec((frames, rows, cols, outs), lambda t: (0, 0, 0, 0)),
+        out_specs=pl.BlockSpec((frames, rows, cols, outs), lambda i, t: (0, 0, 0, 0)),
         out_shape=jax.ShapeDtypeStruct((frames, rows, cols, outs), out_dtype),
-        scratch_shapes=[pltpu.VMEM((frames * rows * cols, outs), jnp.float32)],
+        scratch_shapes=[pltpu.VMEM((frames, rows * cols, outs), jnp.float32)],
         cost_estimate=pl.CostEstimate(flops=flops, bytes_accessed=moved, transcendentals=0),
     )(padded, kernel, bias.reshape(1, outs))
 

time: 211 us -> 209 us (level)
  Pallas kernels: 40.3 us -> 36 us
    pallas_call x2, Pallas kernels: 40.3 us -> 36 us  [causal_conv(): pl.pallas_call(conv_body, grid=(3, frames), in_specs=[pl.BlockSpec((1,) +...]
    all_gather x2, waiting for transfers between devices: 20.7 us -> 23.8 us  [kernel_block(): return lax.all_gather(out, 'hz', axis=1, tiled=True)]
  transfers between devices with their start and end apart: 36 -> 36, of which waited for: 22 -> 22; matrix products, arithmetic and copies ran while one was open for 17% -> 18% of each run, Pallas kernels for 10% -> 9%
where the time goes in v15:
time: 209 us
  waiting for transfers between devices  69 us (33%)
  starting transfers between devices  44.1 us (21%)
  Pallas kernels  36 us (17%)
  local copies, waits for them, and re-layouts  29.4 us (14%)
  other arithmetic  16.1 us (8%)
  between operations  13.9 us (7%)
    pallas_call x2, Pallas kernels, causal_conv(): pl.pallas_call(conv_body, grid=(3, frames), in_specs=[pl.BlockSpec((1,) +...  36 us
    all_gather x2, waiting for transfers between devices, kernel_block(): return lax.all_gather(out, 'hz', axis=1, tiled=True)  23.8 us
    ppermute x12, waiting for transfers between devices, butterfly_stats(): other_sums, other_squares = lax.ppermute((sums, squares), axis, pairs)  15.8 us
    ppermute x2, waiting for transfers between devices, with_row_halo(): bottom = lax.ppermute(cells[:, :1], axis_name, up)  12.9 us
    ppermute x12, starting transfers between devices, butterfly_stats(): other_sums, other_squares = lax.ppermute((sums, squares), axis, pairs)  11.3 us
    dynamic_update_slice x11, local copies, waits for them, and re-layouts, chip_gather(): out = lax.dynamic_update_slice(out, piece, start)  9.92 us
    ppermute x6, starting transfers between devices, chip_gather(): lax.ppermute(firsts, 'hb', shift_pairs(count_b, step))  8.76 us
    ppermute x6, waiting for transfers between devices, kernel_block(): piece = lax.ppermute(piece, HQ, shift_pairs(size, step))  8.4 us
  transfers between devices with their start and end apart: 36, of which 22 were waited for; matrix products, arithmetic and copies ran while one was open for 18% of the time, Pallas kernels for 9%

profile of v15, /device:TPU:1, one launch (start us, length us, event | category | flops | bytes accessed | tf_op | source)
XLA Modules:
  0.0 208.6 jit_solution(6098270425065561275)
XLA Ops:
  8.3 2.7 %collective-permute-start.13 = (bf16[27,32,128]{2,1,0:T(8,128)(2,1)S(1)}, bf16[27,32,128]{2,1,0:T(8,128)(2,1)}, u32[]{:S(2)}, u32[]{:S(2)}) collective-permute-start(bf16[27,32,128]{2,1,0:T(8,128)(2,1)S(1)} %get-tuple-element.12), channel_id=1, source_target_pairs={{0,1},{1,2},{2,3},{3,0},{4,5},{5,6},{6,7},{7,4},{8,9},{9,10},{10,1... | collective-permute-start | bytes 663560 | tf_op jit(solution)/shard_map/ppermute | solution.py:156
  11.5 4.2 %collective-permute-done.13 = bf16[27,32,128]{2,1,0:T(8,128)(2,1)} collective-permute-done((bf16[27,32,128]{2,1,0:T(8,128)(2,1)S(1)}, bf16[27,32,128]{2,1,0:T(8,128)(2,1)}, u32[]{:S(2)}, u32[]{:S(2)}) %collective-permute-start.13) | collective-permute-done | bytes 221216 | tf_op jit(solution)/shard_map/ppermute | solution.py:156
  16.6 3.8 %collective-permute-done.14 = bf16[27,32,128]{2,1,0:T(8,128)(2,1)S(1)} collective-permute-done((bf16[27,32,128]{2,1,0:T(8,128)(2,1)S(1)}, bf16[27,32,128]{2,1,0:T(8,128)(2,1)S(1)}, u32[]{:S(2)}, u32[]{:S(2)}) %collective-permute-start.14) | collective-permute-done | bytes 221216 | tf_op jit(solution)/shard_map/ppermute | solution.py:156
  21.9 2.1 collective-permute-start
  29.5 6.1 %collective-permute-done.5 = f32[32]{0:T(128)S(1)} collective-permute-done((f32[32]{0:T(128)S(1)}, f32[32]{0:T(128)S(1)}, u32[]{:S(2)}, u32[]{:S(2)}) %collective-permute-start.5) | collective-permute-done | bytes 160 | tf_op jit(solution)/shard_map/ppermute | solution.py:25
  46.1 2.3 %collective-permute-done.12 = f32[32]{0:T(128)S(1)} collective-permute-done((f32[32]{0:T(128)S(1)}, f32[32]{0:T(128)S(1)}, u32[]{:S(2)}, u32[]{:S(2)}) %collective-permute-start.12) | collective-permute-done | bytes 160 | tf_op jit(solution)/shard_map/ppermute | solution.py:25
  56.0 4.0 %collective-permute-start.3 = (bf16[3,1,80,512]{3,2,1,0:T(8,128)(2,1)}, bf16[3,1,80,512]{3,2,1,0:T(8,128)(2,1)S(1)}, u32[]{:S(2)}, u32[]{:S(2)}) collective-permute-start(bf16[3,1,80,512]{3,2,1,0:T(8,128)(2,1)} %get-tuple-element.5), channel_id=1, source_target_pairs={{0,4},{4,8},{8,12},{1,5},{5,9},{9,13},{2,6},{6,10},{10,14},{3,7},{... | collective-permute-start | bytes 737288 | tf_op jit(solution)/shard_map/ppermute | solution.py:93
  64.0 12.2 %collective-permute-done.4 = bf16[3,1,80,512]{3,2,1,0:T(8,128)(2,1)S(1)} collective-permute-done((bf16[3,1,80,512]{3,2,1,0:T(8,128)(2,1)}, bf16[3,1,80,512]{3,2,1,0:T(8,128)(2,1)S(1)}, u32[]{:S(2)}, u32[]{:S(2)}) %collective-permute-start.4) | collective-permute-done | bytes 245792 | tf_op jit(solution)/shard_map/ppermute | solution.py:94
  78.2 3.2 %fusion.5.x_ref = bf16[5,10,82,512]{3,2,1,0:T(8,128)(2,1)} fusion(bf16[3,10,80,512]{3,2,1,0:T(8,128)(2,1)S(1)} %fusion.6, bf16[1,10,80,512]{3,2,1,0:T(8,128)(2,1)S(1)} %slice.36), kind=kLoop, calls=%fused_computation.11 | loop fusion | flops 25190400 | bytes 7475200 | tf_op jit(solution)/shard_map/concatenate | solution.py:123
  81.4 17.3 %all-gather.3.cloned.1.call-done.w_ref = bf16[27,512,128]{2,1,0:T(8,128)(2,1)} async-done(((bf16[27,128,128]{2,1,0:T(8,128)(2,1)}), bf16[27,512,128]{2,1,0:T(8,128)(2,1)}) %all-gather.3.cloned.1.call-update) | async-done | bytes 3538960 | tf_op jit(solution)/shard_map/all_gather | solution.py:159
  98.7 17.9 %shard_map.91 = bf16[3,8,80,128]{3,2,1,0:T(8,128)(2,1)} custom-call(bf16[5,10,82,512]{3,2,1,0:T(8,128)(2,1)} %fusion.5.x_ref, bf16[27,512,128]{2,1,0:T(8,128)(2,1)} %all-gather.3.cloned.1.call-done.w_ref, f32[1,128]{1,0:T(1,128)} %dynamic-slice_bitcast_fusion.1.b_ref), custom_call_target="tpu_custom_call" | custom-call | flops 6794772480 | bytes 12079104 | tf_op jit(solution)/shard_map/pallas_call | solution.py:131
  118.8 4.2 %collective-permute-start.16 = (bf16[3,1,80,128]{3,2,1,0:T(8,128)(2,1)S(1)}, bf16[3,1,80,128]{3,2,1,0:T(8,128)(2,1)S(1)}, u32[]{:S(2)}, u32[]{:S(2)}) collective-permute-start(bf16[3,1,80,128]{3,2,1,0:T(8,128)(2,1)S(1)} %get-tuple-element.21), channel_id=1, source_target_pairs={{0,4},{4,8},{8,12},{1,5},{5,9},{9,13},{2,6},{6,10},{10,14},{3,7},{... | collective-permute-start | bytes 184328 | tf_op jit(solution)/shard_map/ppermute | solution.py:93
  130.9 2.3 %collective-permute-start.21 = (f32[8]{0:T(128)S(1)}, f32[8]{0:T(128)S(1)}, u32[]{:S(2)}, u32[]{:S(2)}) collective-permute-start(f32[8]{0:T(128)S(1)} %reduce_sum.72), channel_id=1, source_target_pairs={{0,4},{4,0},{8,12},{12,8},{1,5},{5,1},{9,13},{13,9},{2,6},{6,2},{1... | collective-permute-start | bytes 104 | tf_op jit(solution)/shard_map/ppermute | solution.py:25
  134.5 2.5 %collective-permute-done.23 = f32[8]{0:T(128)S(1)} collective-permute-done((f32[8]{0:T(128)S(1)}, f32[8]{0:T(128)S(1)}, u32[]{:S(2)}, u32[]{:S(2)}) %collective-permute-start.23) | collective-permute-done | bytes 64 | tf_op jit(solution)/shard_map/ppermute | solution.py:25
  137.0 2.1 %collective-permute-start.22 = (f32[8]{0:T(128)S(1)}, f32[8]{0:T(128)S(1)}, u32[]{:S(2)}, u32[]{:S(2)}) collective-permute-start(f32[8]{0:T(128)S(1)} %get-tuple-element.28), channel_id=1, source_target_pairs={{0,8},{4,12},{8,0},{12,4},{1,9},{5,13},{9,1},{13,5},{2,10},{6,14},... | collective-permute-start | bytes 104 | tf_op jit(solution)/shard_map/ppermute | solution.py:25
  139.4 3.3 %collective-permute-start.19 = (bf16[3,10,80,128]{3,2,1,0:T(8,128)(2,1)S(1)}, bf16[3,10,80,128]{3,2,1,0:T(8,128)(2,1)}, u32[]{:S(2)}, u32[]{:S(2)}) collective-permute-start(bf16[3,10,80,128]{3,2,1,0:T(8,128)(2,1)S(1)} %get-tuple-element.15), channel_id=1, source_target_pairs={{0,1},{1,0},{2,3},{3,2},{4,5},{5,4},{6,7},{7,6},{8,9},{9,8},{10,11... | collective-permute-start | bytes 1843208 | tf_op jit(solution)/shard_map/ppermute | solution.py:71
  142.7 2.9 %collective-permute-start.20 = (bf16[3,10,80,128]{3,2,1,0:T(8,128)(2,1)}, bf16[3,10,80,128]{3,2,1,0:T(8,128)(2,1)}, u32[]{:S(2)}, u32[]{:S(2)}) collective-permute-start(bf16[3,10,80,128]{3,2,1,0:T(8,128)(2,1)} %collective-permute-done.18), channel_id=1, source_target_pairs={{0,1},{1,0},{2,3},{3,2},{4,5},{5,4},{6,7},{7,6},{8,9},{9,8},{10,11... | collective-permute-start | bytes 1843208 | tf_op jit(solution)/shard_map/ppermute | solution.py:71
  157.3 3.2 %fusion.7 = bf16[3,10,80,512]{3,2,1,0:T(8,128)(2,1)S(1)} fusion(bf16[3,10,80,512]{3,2,1,0:T(8,128)(2,1)} %constant_dynamic-update-slice_fusion.6, f32[512]{0:T(512)S(1)} %copy-done.8, f32[512]{0:T(512)S(1)} %copy-done.9, f32[512]{0:T(512)S(1)} %mul.221, f32[512]{0:T(512)S(1)} %sub.111, pred[10]{0:T(512)(128)(4,1)S(1)} %or_and_fusion), kind=kLoop, calls=%fused_computation.13 | loop fusion | flops 13516800 | bytes 4923402 | tf_op jit(solution)/shard_map/jit(_where)/select_n | solution.py:86
  160.5 3.2 %select_maximum_fusion.x_ref = bf16[5,10,82,512]{3,2,1,0:T(8,128)(2,1)} fusion(bf16[3,10,80,512]{3,2,1,0:T(8,128)(2,1)S(1)} %fusion.7, bf16[1,10,80,512]{3,2,1,0:T(8,128)(2,1)S(1)} %slice.39), kind=kLoop, calls=%fused_computation.5 | loop fusion | flops 25190400 | bytes 7475200 | tf_op jit(solution)/shard_map/concatenate | solution.py:123
  163.7 6.5 %all-gather.5.cloned.1.call-done.w_ref = bf16[27,512,128]{2,1,0:T(8,128)(2,1)} async-done(((bf16[27,128,128]{2,1,0:T(8,128)(2,1)}), bf16[27,512,128]{2,1,0:T(8,128)(2,1)}) %all-gather.5.cloned.1.call-update) | async-done | bytes 3538960 | tf_op jit(solution)/shard_map/all_gather | solution.py:159
  170.2 18.1 %shard_map.92 = f32[3,8,80,128]{3,2,1,0:T(8,128)} custom-call(bf16[5,10,82,512]{3,2,1,0:T(8,128)(2,1)} %select_maximum_fusion.x_ref, bf16[27,512,128]{2,1,0:T(8,128)(2,1)} %all-gather.5.cloned.1.call-done.w_ref, f32[1,128]{1,0:T(1,128)} %dynamic-slice_bitcast_fusion.b_ref), custom_call_target="tpu_custom_call" | custom-call | flops 6794772480 | bytes 12079104 | tf_op jit(solution)/shard_map/pallas_call | solution.py:131
  192.0 2.1 collective-permute-done.31
  194.1 3.3 %collective-permute-done.32 = bf16[3,2,80,128]{3,2,1,0:T(8,128)(2,1)S(1)} collective-permute-done((bf16[3,2,80,128]{3,2,1,0:T(8,128)(2,1)S(1)}, bf16[3,2,80,128]{3,2,1,0:T(8,128)(2,1)S(1)}, u32[]{:S(2)}, u32[]{:S(2)}) %collective-permute-start.32) | collective-permute-done | bytes 122912 | tf_op jit(solution)/shard_map/ppermute | solution.py:171
  199.6 2.2 %reshape.59 = bf16[3,4,160,512]{3,2,1,0:T(8,128)(2,1)} reshape(bf16[3,4,80,2,512]{4,3,2,1,0:T(2,128)(2,1)S(1)} %broadcast_in_dim.53) | data formatting | bytes 3932160 | tf_op jit(solution)/shard_map/reshape | solution.py:218
  (151 shorter events, 63.3 us)
Async XLA Ops:
  6.5 92.1 %all-gather.3.cloned.1.call-start = ((), (), s32[]{:S(2)}) async-start(), calls=%async_computation | async-start | bytes 4423680 | tf_op jit(solution)/shard_map/all_gather | solution.py:159
  8.3 7.3 %collective-permute-start.13 = (bf16[27,32,128]{2,1,0:T(8,128)(2,1)S(1)}, bf16[27,32,128]{2,1,0:T(8,128)(2,1)}, u32[]{:S(2)}, u32[]{:S(2)}) collective-permute-start(bf16[27,32,128]{2,1,0:T(8,128)(2,1)S(1)} %get-tuple-element.12), channel_id=1, source_target_pairs={{0,1},{1,2},{2,3},{3,0},{4,5},{5,6},{6,7},{7,4},{8,9},{9,10},{10,1... | collective-permute-start | bytes 663560 | tf_op jit(solution)/shard_map/ppermute | solution.py:156
  11.0 9.4 %collective-permute-start.14 = (bf16[27,32,128]{2,1,0:T(8,128)(2,1)S(1)}, bf16[27,32,128]{2,1,0:T(8,128)(2,1)S(1)}, u32[]{:S(2)}, u32[]{:S(2)}) collective-permute-start(bf16[27,32,128]{2,1,0:T(8,128)(2,1)S(1)} %get-tuple-element.14), channel_id=1, source_target_pairs={{0,2},{1,3},{2,0},{3,1},{4,6},{5,7},{6,4},{7,5},{8,10},{9,11},{10,... | collective-permute-start | bytes 663560 | tf_op jit(solution)/shard_map/ppermute | solution.py:156
  11.0 9.9 %collective-permute-start.15 = (bf16[27,32,128]{2,1,0:T(8,128)(2,1)S(1)}, bf16[27,32,128]{2,1,0:T(8,128)(2,1)S(1)}, u32[]{:S(2)}, u32[]{:S(2)}) collective-permute-start(bf16[27,32,128]{2,1,0:T(8,128)(2,1)S(1)} %get-tuple-element.11), channel_id=1, source_target_pairs={{0,3},{1,0},{2,1},{3,2},{4,7},{5,4},{6,5},{7,6},{8,11},{9,8},{10,9... | collective-permute-start | bytes 663560 | tf_op jit(solution)/shard_map/ppermute | solution.py:156
  21.9 148.3 %all-gather.5.cloned.1.call-start = ((), (), s32[]{:S(2)}) async-start(), calls=%async_computation.1 | async-start | bytes 4423680 | tf_op jit(solution)/shard_map/all_gather | solution.py:159
  21.9 17.4 %collective-permute-start = (bf16[3,2,80,512]{3,2,1,0:T(8,128)(2,1)S(1)}, bf16[3,2,80,512]{3,2,1,0:T(8,128)(2,1)}, u32[]{:S(2)}, u32[]{:S(2)}) collective-permute-start(bf16[3,2,80,512]{3,2,1,0:T(8,128)(2,1)S(1)} %copy-done.2), channel_id=1, source_target_pairs={{0,2},{2,0},{1,3},{3,1},{4,6},{6,4},{5,7},{7,5},{8,10},{10,8},{9,1... | collective-permute-start | bytes 1474568 | tf_op jit(solution)/shard_map/ppermute | solution.py:66
  24.0 27.7 %collective-permute-start.1 = (bf16[3,2,80,512]{3,2,1,0:T(8,128)(2,1)S(1)}, bf16[3,2,80,512]{3,2,1,0:T(8,128)(2,1)}, u32[]{:S(2)}, u32[]{:S(2)}) collective-permute-start(bf16[3,2,80,512]{3,2,1,0:T(8,128)(2,1)S(1)} %copy-done.2), channel_id=1, source_target_pairs={{0,1},{1,0},{2,3},{3,2},{4,5},{5,4},{6,7},{7,6},{8,9},{9,8},{10,11... | collective-permute-start | bytes 1474568 | tf_op jit(solution)/shard_map/ppermute | solution.py:71
  24.3 11.3 %collective-permute-start.5 = (f32[32]{0:T(128)S(1)}, f32[32]{0:T(128)S(1)}, u32[]{:S(2)}, u32[]{:S(2)}) collective-permute-start(f32[32]{0:T(128)S(1)} %reduce_sum.51), channel_id=1, source_target_pairs={{0,2},{2,0},{1,3},{3,1},{4,6},{6,4},{5,7},{7,5},{8,10},{10,8},{9,1... | collective-permute-start | bytes 392 | tf_op jit(solution)/shard_map/ppermute | solution.py:25
  25.1 10.4 %collective-permute-start.9 = (f32[32]{0:T(128)S(1)}, f32[32]{0:T(128)S(1)}, u32[]{:S(2)}, u32[]{:S(2)}) collective-permute-start(f32[32]{0:T(128)S(1)} %reduce_sum.54), channel_id=1, source_target_pairs={{0,2},{2,0},{1,3},{3,1},{4,6},{6,4},{5,7},{7,5},{8,10},{10,8},{9,1... | collective-permute-start | bytes 392 | tf_op jit(solution)/shard_map/ppermute | solution.py:25
  27.6 32.4 %collective-permute-start.28 = (bf16[27,32,128]{2,1,0:T(8,128)(2,1)}, bf16[27,32,128]{2,1,0:T(8,128)(2,1)}, u32[]{:S(2)}, u32[]{:S(2)}) collective-permute-start(bf16[27,32,128]{2,1,0:T(8,128)(2,1)} %get-tuple-element.8), channel_id=1, source_target_pairs={{0,1},{1,2},{2,3},{3,0},{4,5},{5,6},{6,7},{7,4},{8,9},{9,10},{10,1... | collective-permute-start | bytes 663560 | tf_op jit(solution)/shard_map/ppermute | solution.py:156
  39.3 13.5 %collective-permute-start.2 = (bf16[3,2,80,512]{3,2,1,0:T(8,128)(2,1)}, bf16[3,2,80,512]{3,2,1,0:T(8,128)(2,1)}, u32[]{:S(2)}, u32[]{:S(2)}) collective-permute-start(bf16[3,2,80,512]{3,2,1,0:T(8,128)(2,1)} %collective-permute-done), channel_id=1, source_target_pairs={{0,1},{1,0},{2,3},{3,2},{4,5},{5,4},{6,7},{7,6},{8,9},{9,8},{10,11... | collective-permute-start | bytes 1474568 | tf_op jit(solution)/shard_map/ppermute | solution.py:71
  45.7 15.3 %collective-permute-start.29 = (bf16[27,32,128]{2,1,0:T(8,128)(2,1)}, bf16[27,32,128]{2,1,0:T(8,128)(2,1)}, u32[]{:S(2)}, u32[]{:S(2)}) collective-permute-start(bf16[27,32,128]{2,1,0:T(8,128)(2,1)} %get-tuple-element.10), channel_id=1, source_target_pairs={{0,2},{1,3},{2,0},{3,1},{4,6},{5,7},{6,4},{7,5},{8,10},{9,11},{10,... | collective-permute-start | bytes 663560 | tf_op jit(solution)/shard_map/ppermute | solution.py:156
  48.5 13.6 %collective-permute-start.30 = (bf16[27,32,128]{2,1,0:T(8,128)(2,1)}, bf16[27,32,128]{2,1,0:T(8,128)(2,1)}, u32[]{:S(2)}, u32[]{:S(2)}) collective-permute-start(bf16[27,32,128]{2,1,0:T(8,128)(2,1)} %get-tuple-element.7), channel_id=1, source_target_pairs={{0,3},{1,0},{2,1},{3,2},{4,7},{5,4},{6,5},{7,6},{8,11},{9,8},{10,9... | collective-permute-start | bytes 663560 | tf_op jit(solution)/shard_map/ppermute | solution.py:156
  54.8 21.5 %collective-permute-start.4 = (bf16[3,1,80,512]{3,2,1,0:T(8,128)(2,1)}, bf16[3,1,80,512]{3,2,1,0:T(8,128)(2,1)S(1)}, u32[]{:S(2)}, u32[]{:S(2)}) collective-permute-start(bf16[3,1,80,512]{3,2,1,0:T(8,128)(2,1)} %get-tuple-element.6), channel_id=1, source_target_pairs={{4,0},{8,4},{12,8},{5,1},{9,5},{13,9},{6,2},{10,6},{14,10},{7,3},{... | collective-permute-start | bytes 737288 | tf_op jit(solution)/shard_map/ppermute | solution.py:94
  56.0 20.2 %collective-permute-start.3 = (bf16[3,1,80,512]{3,2,1,0:T(8,128)(2,1)}, bf16[3,1,80,512]{3,2,1,0:T(8,128)(2,1)S(1)}, u32[]{:S(2)}, u32[]{:S(2)}) collective-permute-start(bf16[3,1,80,512]{3,2,1,0:T(8,128)(2,1)} %get-tuple-element.5), channel_id=1, source_target_pairs={{0,4},{4,8},{8,12},{1,5},{5,9},{9,13},{2,6},{6,10},{10,14},{3,7},{... | collective-permute-start | bytes 737288 | tf_op jit(solution)/shard_map/ppermute | solution.py:93
  117.5 7.5 %collective-permute-start.17 = (bf16[3,1,80,128]{3,2,1,0:T(8,128)(2,1)S(1)}, bf16[3,1,80,128]{3,2,1,0:T(8,128)(2,1)S(1)}, u32[]{:S(2)}, u32[]{:S(2)}) collective-permute-start(bf16[3,1,80,128]{3,2,1,0:T(8,128)(2,1)S(1)} %get-tuple-element.22), channel_id=1, source_target_pairs={{4,0},{8,4},{12,8},{5,1},{9,5},{13,9},{6,2},{10,6},{14,10},{7,3},{... | collective-permute-start | bytes 184328 | tf_op jit(solution)/shard_map/ppermute | solution.py:94
  118.8 6.6 %collective-permute-start.16 = (bf16[3,1,80,128]{3,2,1,0:T(8,128)(2,1)S(1)}, bf16[3,1,80,128]{3,2,1,0:T(8,128)(2,1)S(1)}, u32[]{:S(2)}, u32[]{:S(2)}) collective-permute-start(bf16[3,1,80,128]{3,2,1,0:T(8,128)(2,1)S(1)} %get-tuple-element.21), channel_id=1, source_target_pairs={{0,4},{4,8},{8,12},{1,5},{5,9},{9,13},{2,6},{6,10},{10,14},{3,7},{... | collective-permute-start | bytes 184328 | tf_op jit(solution)/shard_map/ppermute | solution.py:93
  129.3 13.4 %collective-permute-start.18 = (bf16[3,10,80,128]{3,2,1,0:T(8,128)(2,1)S(1)}, bf16[3,10,80,128]{3,2,1,0:T(8,128)(2,1)}, u32[]{:S(2)}, u32[]{:S(2)}) collective-permute-start(bf16[3,10,80,128]{3,2,1,0:T(8,128)(2,1)S(1)} %get-tuple-element.15), channel_id=1, source_target_pairs={{0,2},{2,0},{1,3},{3,1},{4,6},{6,4},{5,7},{7,5},{8,10},{10,8},{9,1... | collective-permute-start | bytes 1843208 | tf_op jit(solution)/shard_map/ppermute | solution.py:66
  137.0 8.6 %collective-permute-start.22 = (f32[8]{0:T(128)S(1)}, f32[8]{0:T(128)S(1)}, u32[]{:S(2)}, u32[]{:S(2)}) collective-permute-start(f32[8]{0:T(128)S(1)} %get-tuple-element.28), channel_id=1, source_target_pairs={{0,8},{4,12},{8,0},{12,4},{1,9},{5,13},{9,1},{13,5},{2,10},{6,14},... | collective-permute-start | bytes 104 | tf_op jit(solution)/shard_map/ppermute | solution.py:25
  139.1 6.5 %collective-permute-start.24 = (f32[8]{0:T(128)S(1)}, f32[8]{0:T(128)S(1)}, u32[]{:S(2)}, u32[]{:S(2)}) collective-permute-start(f32[8]{0:T(128)S(1)} %get-tuple-element.27), channel_id=1, source_target_pairs={{0,8},{4,12},{8,0},{12,4},{1,9},{5,13},{9,1},{13,5},{2,10},{6,14},... | collective-permute-start | bytes 104 | tf_op jit(solution)/shard_map/ppermute | solution.py:25
  139.4 13.9 %collective-permute-start.19 = (bf16[3,10,80,128]{3,2,1,0:T(8,128)(2,1)S(1)}, bf16[3,10,80,128]{3,2,1,0:T(8,128)(2,1)}, u32[]{:S(2)}, u32[]{:S(2)}) collective-permute-start(bf16[3,10,80,128]{3,2,1,0:T(8,128)(2,1)S(1)} %get-tuple-element.15), channel_id=1, source_target_pairs={{0,1},{1,0},{2,3},{3,2},{4,5},{5,4},{6,7},{7,6},{8,9},{9,8},{10,11... | collective-permute-start | bytes 1843208 | tf_op jit(solution)/shard_map/ppermute | solution.py:71
  142.7 12.6 %collective-permute-start.20 = (bf16[3,10,80,128]{3,2,1,0:T(8,128)(2,1)}, bf16[3,10,80,128]{3,2,1,0:T(8,128)(2,1)}, u32[]{:S(2)}, u32[]{:S(2)}) collective-permute-start(bf16[3,10,80,128]{3,2,1,0:T(8,128)(2,1)} %collective-permute-done.18), channel_id=1, source_target_pairs={{0,1},{1,0},{2,3},{3,2},{4,5},{5,4},{6,7},{7,6},{8,9},{9,8},{10,11... | collective-permute-start | bytes 1843208 | tf_op jit(solution)/shard_map/ppermute | solution.py:71
  191.5 5.9 %collective-permute-start.32 = (bf16[3,2,80,128]{3,2,1,0:T(8,128)(2,1)S(1)}, bf16[3,2,80,128]{3,2,1,0:T(8,128)(2,1)S(1)}, u32[]{:S(2)}, u32[]{:S(2)}) collective-permute-start(bf16[3,2,80,128]{3,2,1,0:T(8,128)(2,1)S(1)} %get-tuple-element.18), channel_id=1, source_target_pairs={{0,2},{1,3},{2,0},{3,1},{4,6},{5,7},{6,4},{7,5},{8,10},{9,11},{10,... | collective-permute-start | bytes 368648 | tf_op jit(solution)/shard_map/ppermute | solution.py:171
  191.8 6.2 %collective-permute-start.33 = (bf16[3,2,80,128]{3,2,1,0:T(8,128)(2,1)S(1)}, bf16[3,2,80,128]{3,2,1,0:T(8,128)(2,1)S(1)}, u32[]{:S(2)}, u32[]{:S(2)}) collective-permute-start(bf16[3,2,80,128]{3,2,1,0:T(8,128)(2,1)S(1)} %get-tuple-element.17), channel_id=1, source_target_pairs={{0,3},{1,0},{2,1},{3,2},{4,7},{5,4},{6,5},{7,6},{8,11},{9,8},{10,9... | collective-permute-start | bytes 368648 | tf_op jit(solution)/shard_map/ppermute | solution.py:171
  (22 other events, 271.7 us)
Sparse Core Ops, SparseCore 0:
  22.0 76.6 all-gather.2
  100.2 69.8 all-gather.4

commit v16 on v7

--- a/solution.py
+++ b/solution.py
@@ -99,17 +99,20 @@
     step = pl.program_id(0)
     rows, cols, outs = o_ref.shape[1:]
     chans = x_ref.shape[-1]
-    acc_ref[...] = jnp.broadcast_to(b_ref[...], acc_ref.shape)
-    for i in range(3):
-        for j in range(3):
-            for k in range(3):
-                patch = x_ref[step + i, pl.ds(j, rows), pl.ds(k, cols), :]
-                acc_ref[...] += jnp.dot(
-                    patch.reshape(rows * cols, chans),
-                    w_ref[9 * i + 3 * j + k],
-                    preferred_element_type=jnp.float32,
-                )
-    o_ref[0] = acc_ref[...].reshape(rows, cols, outs).astype(o_ref.dtype)
+    part = rows // 2
+    for half in range(2):
+        first = half * part
+        total = jnp.broadcast_to(b_ref[...], (part * cols, outs))
+        for i in range(3):
+            for j in range(3):
+                for k in range(3):
+                    patch = x_ref[step + i, pl.ds(first + j, part), pl.ds(k, cols), :]
+                    total = total + jnp.dot(
+                        patch.reshape(part * cols, chans),
+                        w_ref[9 * i + 3 * j + k],
+                        preferred_element_type=jnp.float32,
+                    )
+        o_ref[0, pl.ds(first, part)] = total.reshape(part, cols, outs).astype(o_ref.dtype)
 
 
 def causal_conv(extended, kernel, bias, out_dtype):

time: 210 us -> 210 us (level)
  waiting for transfers between devices: 64.6 us -> 66.9 us
  starting transfers between devices: 48 us -> 45.8 us
    ppermute x6, starting transfers between devices: 12.3 us -> 10 us  [chip_gather(): lax.ppermute(firsts, 'hb', shift_pairs(count_b, step))]
    all_gather x2, waiting for transfers between devices: 20.9 us -> 23.2 us  [kernel_block(): return lax.all_gather(out, 'hz', axis=1, tiled=True)]
  transfers between devices with their start and end apart: 36 -> 36, of which waited for: 20 -> 21; matrix products, arithmetic and copies ran while one was open for 18% -> 18% of each run, Pallas kernels for 9% -> 9%
where the time goes in v16:
time: 210 us; the launch traced here: 209 us
  waiting for transfers between devices  66.9 us (32%)
  starting transfers between devices  45.8 us (22%)
  Pallas kernels  36.8 us (18%)
  local copies, waits for them, and re-layouts  29.4 us (14%)
  other arithmetic  16.1 us (8%)
  between operations  13.9 us (7%)
    pallas_call x2, Pallas kernels, causal_conv(): pl.pallas_call(conv_body, grid=(frames,), in_specs=[pl.BlockSpec(padded.s...  36.8 us
    all_gather x2, waiting for transfers between devices, kernel_block(): return lax.all_gather(out, 'hz', axis=1, tiled=True)  23.2 us
    ppermute x12, waiting for transfers between devices, butterfly_stats(): other_sums, other_squares = lax.ppermute((sums, squares), axis, pairs)  15.5 us
    ppermute x2, waiting for transfers between devices, with_row_halo(): bottom = lax.ppermute(cells[:, :1], axis_name, up)  13.3 us
    ppermute x12, starting transfers between devices, butterfly_stats(): other_sums, other_squares = lax.ppermute((sums, squares), axis, pairs)  11.7 us
    ppermute x6, starting transfers between devices, chip_gather(): lax.ppermute(firsts, 'hb', shift_pairs(count_b, step))  10 us
    dynamic_update_slice x11, local copies, waits for them, and re-layouts, chip_gather(): out = lax.dynamic_update_slice(out, piece, start)  9.92 us
    ppermute x6, waiting for transfers between devices, kernel_block(): piece = lax.ppermute(piece, HQ, shift_pairs(size, step))  8.4 us
  transfers between devices with their start and end apart: 36, of which 21 were waited for; matrix products, arithmetic and copies ran while one was open for 18% of the time, Pallas kernels for 9%

profile of v16, /device:TPU:1, one launch (start us, length us, event | category | flops | bytes accessed | tf_op | source)
XLA Modules:
  0.0 208.9 jit_solution(4957397715235380260)
XLA Ops:
  8.3 2.7 %collective-permute-start.13 = (bf16[27,32,128]{2,1,0:T(8,128)(2,1)S(1)}, bf16[27,32,128]{2,1,0:T(8,128)(2,1)}, u32[]{:S(2)}, u32[]{:S(2)}) collective-permute-start(bf16[27,32,128]{2,1,0:T(8,128)(2,1)S(1)} %get-tuple-element.12), channel_id=1, source_target_pairs={{0,1},{1,2},{2,3},{3,0},{4,5},{5,6},{6,7},{7,4},{8,9},{9,10},{10,1... | collective-permute-start | bytes 663560 | tf_op jit(solution)/shard_map/ppermute | solution.py:152
  11.5 4.2 %collective-permute-done.13 = bf16[27,32,128]{2,1,0:T(8,128)(2,1)} collective-permute-done((bf16[27,32,128]{2,1,0:T(8,128)(2,1)S(1)}, bf16[27,32,128]{2,1,0:T(8,128)(2,1)}, u32[]{:S(2)}, u32[]{:S(2)}) %collective-permute-start.13) | collective-permute-done | bytes 221216 | tf_op jit(solution)/shard_map/ppermute | solution.py:152
  16.6 3.8 %collective-permute-done.14 = bf16[27,32,128]{2,1,0:T(8,128)(2,1)S(1)} collective-permute-done((bf16[27,32,128]{2,1,0:T(8,128)(2,1)S(1)}, bf16[27,32,128]{2,1,0:T(8,128)(2,1)S(1)}, u32[]{:S(2)}, u32[]{:S(2)}) %collective-permute-start.14) | collective-permute-done | bytes 221216 | tf_op jit(solution)/shard_map/ppermute | solution.py:152
  21.9 2.1 collective-permute-start
  29.5 6.1 %collective-permute-done.5 = f32[32]{0:T(128)S(1)} collective-permute-done((f32[32]{0:T(128)S(1)}, f32[32]{0:T(128)S(1)}, u32[]{:S(2)}, u32[]{:S(2)}) %collective-permute-start.5) | collective-permute-done | bytes 160 | tf_op jit(solution)/shard_map/ppermute | solution.py:25
  46.1 2.3 %collective-permute-done.12 = f32[32]{0:T(128)S(1)} collective-permute-done((f32[32]{0:T(128)S(1)}, f32[32]{0:T(128)S(1)}, u32[]{:S(2)}, u32[]{:S(2)}) %collective-permute-start.12) | collective-permute-done | bytes 160 | tf_op jit(solution)/shard_map/ppermute | solution.py:25
  56.0 4.0 %collective-permute-start.3 = (bf16[3,1,80,512]{3,2,1,0:T(8,128)(2,1)}, bf16[3,1,80,512]{3,2,1,0:T(8,128)(2,1)S(1)}, u32[]{:S(2)}, u32[]{:S(2)}) collective-permute-start(bf16[3,1,80,512]{3,2,1,0:T(8,128)(2,1)} %get-tuple-element.5), channel_id=1, source_target_pairs={{0,4},{4,8},{8,12},{1,5},{5,9},{9,13},{2,6},{6,10},{10,14},{3,7},{... | collective-permute-start | bytes 737288 | tf_op jit(solution)/shard_map/ppermute | solution.py:93
  64.0 12.2 %collective-permute-done.4 = bf16[3,1,80,512]{3,2,1,0:T(8,128)(2,1)S(1)} collective-permute-done((bf16[3,1,80,512]{3,2,1,0:T(8,128)(2,1)}, bf16[3,1,80,512]{3,2,1,0:T(8,128)(2,1)S(1)}, u32[]{:S(2)}, u32[]{:S(2)}) %collective-permute-start.4) | collective-permute-done | bytes 245792 | tf_op jit(solution)/shard_map/ppermute | solution.py:94
  78.2 3.2 %fusion.5.x_ref = bf16[5,10,82,512]{3,2,1,0:T(8,128)(2,1)} fusion(bf16[3,10,80,512]{3,2,1,0:T(8,128)(2,1)S(1)} %fusion.6, bf16[1,10,80,512]{3,2,1,0:T(8,128)(2,1)S(1)} %slice.36), kind=kLoop, calls=%fused_computation.11 | loop fusion | flops 25190400 | bytes 7475200 | tf_op jit(solution)/shard_map/concatenate | solution.py:119
  81.4 17.3 %all-gather.3.cloned.1.call-done.w_ref = bf16[27,512,128]{2,1,0:T(8,128)(2,1)} async-done(((bf16[27,128,128]{2,1,0:T(8,128)(2,1)}), bf16[27,512,128]{2,1,0:T(8,128)(2,1)}) %all-gather.3.cloned.1.call-update) | async-done | bytes 3538960 | tf_op jit(solution)/shard_map/all_gather | solution.py:155
  98.7 18.4 %shard_map.91 = bf16[3,8,80,128]{3,2,1,0:T(8,128)(2,1)} custom-call(bf16[5,10,82,512]{3,2,1,0:T(8,128)(2,1)} %fusion.5.x_ref, bf16[27,512,128]{2,1,0:T(8,128)(2,1)} %all-gather.3.cloned.1.call-done.w_ref, f32[1,128]{1,0:T(1,128)} %dynamic-slice_bitcast_fusion.1.b_ref), custom_call_target="tpu_custom_call" | custom-call | flops 6794772480 | bytes 8720384 | tf_op jit(solution)/shard_map/pallas_call | solution.py:127
  119.3 4.2 %collective-permute-start.16 = (bf16[3,1,80,128]{3,2,1,0:T(8,128)(2,1)S(1)}, bf16[3,1,80,128]{3,2,1,0:T(8,128)(2,1)S(1)}, u32[]{:S(2)}, u32[]{:S(2)}) collective-permute-start(bf16[3,1,80,128]{3,2,1,0:T(8,128)(2,1)S(1)} %get-tuple-element.21), channel_id=1, source_target_pairs={{0,4},{4,8},{8,12},{1,5},{5,9},{9,13},{2,6},{6,10},{10,14},{3,7},{... | collective-permute-start | bytes 184328 | tf_op jit(solution)/shard_map/ppermute | solution.py:93
  127.6 2.0 pad_maximum_fusion
  131.3 2.7 %collective-permute-start.21 = (f32[8]{0:T(128)S(1)}, f32[8]{0:T(128)S(1)}, u32[]{:S(2)}, u32[]{:S(2)}) collective-permute-start(f32[8]{0:T(128)S(1)} %reduce_sum.72), channel_id=1, source_target_pairs={{0,4},{4,0},{8,12},{12,8},{1,5},{5,1},{9,13},{13,9},{2,6},{6,2},{1... | collective-permute-start | bytes 104 | tf_op jit(solution)/shard_map/ppermute | solution.py:25
  134.7 2.3 %collective-permute-done.21 = f32[8]{0:T(128)S(1)} collective-permute-done((f32[8]{0:T(128)S(1)}, f32[8]{0:T(128)S(1)}, u32[]{:S(2)}, u32[]{:S(2)}) %collective-permute-start.21) | collective-permute-done | bytes 64 | tf_op jit(solution)/shard_map/ppermute | solution.py:25
  139.9 3.3 %collective-permute-start.19 = (bf16[3,10,80,128]{3,2,1,0:T(8,128)(2,1)S(1)}, bf16[3,10,80,128]{3,2,1,0:T(8,128)(2,1)}, u32[]{:S(2)}, u32[]{:S(2)}) collective-permute-start(bf16[3,10,80,128]{3,2,1,0:T(8,128)(2,1)S(1)} %get-tuple-element.15), channel_id=1, source_target_pairs={{0,1},{1,0},{2,3},{3,2},{4,5},{5,4},{6,7},{7,6},{8,9},{9,8},{10,11... | collective-permute-start | bytes 1843208 | tf_op jit(solution)/shard_map/ppermute | solution.py:71
  143.2 2.9 %collective-permute-start.20 = (bf16[3,10,80,128]{3,2,1,0:T(8,128)(2,1)}, bf16[3,10,80,128]{3,2,1,0:T(8,128)(2,1)}, u32[]{:S(2)}, u32[]{:S(2)}) collective-permute-start(bf16[3,10,80,128]{3,2,1,0:T(8,128)(2,1)} %collective-permute-done.18), channel_id=1, source_target_pairs={{0,1},{1,0},{2,3},{3,2},{4,5},{5,4},{6,7},{7,6},{8,9},{9,8},{10,11... | collective-permute-start | bytes 1843208 | tf_op jit(solution)/shard_map/ppermute | solution.py:71
  157.9 3.2 %fusion.7 = bf16[3,10,80,512]{3,2,1,0:T(8,128)(2,1)S(1)} fusion(bf16[3,10,80,512]{3,2,1,0:T(8,128)(2,1)} %constant_dynamic-update-slice_fusion.6, f32[512]{0:T(512)S(1)} %copy-done.8, f32[512]{0:T(512)S(1)} %copy-done.9, f32[512]{0:T(512)S(1)} %mul.221, f32[512]{0:T(512)S(1)} %sub.111, pred[10]{0:T(512)(128)(4,1)S(1)} %or_and_fusion), kind=kLoop, calls=%fused_computation.13 | loop fusion | flops 13516800 | bytes 4923402 | tf_op jit(solution)/shard_map/jit(_where)/select_n | solution.py:86
  161.2 3.2 %select_maximum_fusion.x_ref = bf16[5,10,82,512]{3,2,1,0:T(8,128)(2,1)} fusion(bf16[3,10,80,512]{3,2,1,0:T(8,128)(2,1)S(1)} %fusion.7, bf16[1,10,80,512]{3,2,1,0:T(8,128)(2,1)S(1)} %slice.39), kind=kLoop, calls=%fused_computation.5 | loop fusion | flops 25190400 | bytes 7475200 | tf_op jit(solution)/shard_map/concatenate | solution.py:119
  164.3 5.8 %all-gather.5.cloned.1.call-done.w_ref = bf16[27,512,128]{2,1,0:T(8,128)(2,1)} async-done(((bf16[27,128,128]{2,1,0:T(8,128)(2,1)}), bf16[27,512,128]{2,1,0:T(8,128)(2,1)}) %all-gather.5.cloned.1.call-update) | async-done | bytes 3538960 | tf_op jit(solution)/shard_map/all_gather | solution.py:155
  170.2 18.4 %shard_map.92 = f32[3,8,80,128]{3,2,1,0:T(8,128)} custom-call(bf16[5,10,82,512]{3,2,1,0:T(8,128)(2,1)} %select_maximum_fusion.x_ref, bf16[27,512,128]{2,1,0:T(8,128)(2,1)} %all-gather.5.cloned.1.call-done.w_ref, f32[1,128]{1,0:T(1,128)} %dynamic-slice_bitcast_fusion.b_ref), custom_call_target="tpu_custom_call" | custom-call | flops 6794772480 | bytes 8720384 | tf_op jit(solution)/shard_map/pallas_call | solution.py:127
  192.3 2.1 collective-permute-done.31
  194.4 3.3 %collective-permute-done.32 = bf16[3,2,80,128]{3,2,1,0:T(8,128)(2,1)S(1)} collective-permute-done((bf16[3,2,80,128]{3,2,1,0:T(8,128)(2,1)S(1)}, bf16[3,2,80,128]{3,2,1,0:T(8,128)(2,1)S(1)}, u32[]{:S(2)}, u32[]{:S(2)}) %collective-permute-start.32) | collective-permute-done | bytes 122912 | tf_op jit(solution)/shard_map/ppermute | solution.py:167
  199.9 2.2 %reshape.59 = bf16[3,4,160,512]{3,2,1,0:T(8,128)(2,1)} reshape(bf16[3,4,80,2,512]{4,3,2,1,0:T(2,128)(2,1)S(1)} %broadcast_in_dim.53) | data formatting | bytes 3932160 | tf_op jit(solution)/shard_map/reshape | solution.py:214
  (151 shorter events, 63.4 us)
Async XLA Ops:
  6.5 92.1 %all-gather.3.cloned.1.call-start = ((), (), s32[]{:S(2)}) async-start(), calls=%async_computation | async-start | bytes 4423680 | tf_op jit(solution)/shard_map/all_gather | solution.py:155
  8.3 7.3 %collective-permute-start.13 = (bf16[27,32,128]{2,1,0:T(8,128)(2,1)S(1)}, bf16[27,32,128]{2,1,0:T(8,128)(2,1)}, u32[]{:S(2)}, u32[]{:S(2)}) collective-permute-start(bf16[27,32,128]{2,1,0:T(8,128)(2,1)S(1)} %get-tuple-element.12), channel_id=1, source_target_pairs={{0,1},{1,2},{2,3},{3,0},{4,5},{5,6},{6,7},{7,4},{8,9},{9,10},{10,1... | collective-permute-start | bytes 663560 | tf_op jit(solution)/shard_map/ppermute | solution.py:152
  11.0 9.4 %collective-permute-start.14 = (bf16[27,32,128]{2,1,0:T(8,128)(2,1)S(1)}, bf16[27,32,128]{2,1,0:T(8,128)(2,1)S(1)}, u32[]{:S(2)}, u32[]{:S(2)}) collective-permute-start(bf16[27,32,128]{2,1,0:T(8,128)(2,1)S(1)} %get-tuple-element.14), channel_id=1, source_target_pairs={{0,2},{1,3},{2,0},{3,1},{4,6},{5,7},{6,4},{7,5},{8,10},{9,11},{10,... | collective-permute-start | bytes 663560 | tf_op jit(solution)/shard_map/ppermute | solution.py:152
  11.0 9.9 %collective-permute-start.15 = (bf16[27,32,128]{2,1,0:T(8,128)(2,1)S(1)}, bf16[27,32,128]{2,1,0:T(8,128)(2,1)S(1)}, u32[]{:S(2)}, u32[]{:S(2)}) collective-permute-start(bf16[27,32,128]{2,1,0:T(8,128)(2,1)S(1)} %get-tuple-element.11), channel_id=1, source_target_pairs={{0,3},{1,0},{2,1},{3,2},{4,7},{5,4},{6,5},{7,6},{8,11},{9,8},{10,9... | collective-permute-start | bytes 663560 | tf_op jit(solution)/shard_map/ppermute | solution.py:152
  21.9 148.3 %all-gather.5.cloned.1.call-start = ((), (), s32[]{:S(2)}) async-start(), calls=%async_computation.1 | async-start | bytes 4423680 | tf_op jit(solution)/shard_map/all_gather | solution.py:155
  21.9 17.4 %collective-permute-start = (bf16[3,2,80,512]{3,2,1,0:T(8,128)(2,1)S(1)}, bf16[3,2,80,512]{3,2,1,0:T(8,128)(2,1)}, u32[]{:S(2)}, u32[]{:S(2)}) collective-permute-start(bf16[3,2,80,512]{3,2,1,0:T(8,128)(2,1)S(1)} %copy-done.2), channel_id=1, source_target_pairs={{0,2},{2,0},{1,3},{3,1},{4,6},{6,4},{5,7},{7,5},{8,10},{10,8},{9,1... | collective-permute-start | bytes 1474568 | tf_op jit(solution)/shard_map/ppermute | solution.py:66
  24.0 27.7 %collective-permute-start.1 = (bf16[3,2,80,512]{3,2,1,0:T(8,128)(2,1)S(1)}, bf16[3,2,80,512]{3,2,1,0:T(8,128)(2,1)}, u32[]{:S(2)}, u32[]{:S(2)}) collective-permute-start(bf16[3,2,80,512]{3,2,1,0:T(8,128)(2,1)S(1)} %copy-done.2), channel_id=1, source_target_pairs={{0,1},{1,0},{2,3},{3,2},{4,5},{5,4},{6,7},{7,6},{8,9},{9,8},{10,11... | collective-permute-start | bytes 1474568 | tf_op jit(solution)/shard_map/ppermute | solution.py:71
  24.3 11.3 %collective-permute-start.5 = (f32[32]{0:T(128)S(1)}, f32[32]{0:T(128)S(1)}, u32[]{:S(2)}, u32[]{:S(2)}) collective-permute-start(f32[32]{0:T(128)S(1)} %reduce_sum.51), channel_id=1, source_target_pairs={{0,2},{2,0},{1,3},{3,1},{4,6},{6,4},{5,7},{7,5},{8,10},{10,8},{9,1... | collective-permute-start | bytes 392 | tf_op jit(solution)/shard_map/ppermute | solution.py:25
  25.1 10.4 %collective-permute-start.9 = (f32[32]{0:T(128)S(1)}, f32[32]{0:T(128)S(1)}, u32[]{:S(2)}, u32[]{:S(2)}) collective-permute-start(f32[32]{0:T(128)S(1)} %reduce_sum.54), channel_id=1, source_target_pairs={{0,2},{2,0},{1,3},{3,1},{4,6},{6,4},{5,7},{7,5},{8,10},{10,8},{9,1... | collective-permute-start | bytes 392 | tf_op jit(solution)/shard_map/ppermute | solution.py:25
  27.6 32.4 %collective-permute-start.28 = (bf16[27,32,128]{2,1,0:T(8,128)(2,1)}, bf16[27,32,128]{2,1,0:T(8,128)(2,1)}, u32[]{:S(2)}, u32[]{:S(2)}) collective-permute-start(bf16[27,32,128]{2,1,0:T(8,128)(2,1)} %get-tuple-element.8), channel_id=1, source_target_pairs={{0,1},{1,2},{2,3},{3,0},{4,5},{5,6},{6,7},{7,4},{8,9},{9,10},{10,1... | collective-permute-start | bytes 663560 | tf_op jit(solution)/shard_map/ppermute | solution.py:152
  39.3 13.5 %collective-permute-start.2 = (bf16[3,2,80,512]{3,2,1,0:T(8,128)(2,1)}, bf16[3,2,80,512]{3,2,1,0:T(8,128)(2,1)}, u32[]{:S(2)}, u32[]{:S(2)}) collective-permute-start(bf16[3,2,80,512]{3,2,1,0:T(8,128)(2,1)} %collective-permute-done), channel_id=1, source_target_pairs={{0,1},{1,0},{2,3},{3,2},{4,5},{5,4},{6,7},{7,6},{8,9},{9,8},{10,11... | collective-permute-start | bytes 1474568 | tf_op jit(solution)/shard_map/ppermute | solution.py:71
  45.7 15.3 %collective-permute-start.29 = (bf16[27,32,128]{2,1,0:T(8,128)(2,1)}, bf16[27,32,128]{2,1,0:T(8,128)(2,1)}, u32[]{:S(2)}, u32[]{:S(2)}) collective-permute-start(bf16[27,32,128]{2,1,0:T(8,128)(2,1)} %get-tuple-element.10), channel_id=1, source_target_pairs={{0,2},{1,3},{2,0},{3,1},{4,6},{5,7},{6,4},{7,5},{8,10},{9,11},{10,... | collective-permute-start | bytes 663560 | tf_op jit(solution)/shard_map/ppermute | solution.py:152
  48.5 13.6 %collective-permute-start.30 = (bf16[27,32,128]{2,1,0:T(8,128)(2,1)}, bf16[27,32,128]{2,1,0:T(8,128)(2,1)}, u32[]{:S(2)}, u32[]{:S(2)}) collective-permute-start(bf16[27,32,128]{2,1,0:T(8,128)(2,1)} %get-tuple-element.7), channel_id=1, source_target_pairs={{0,3},{1,0},{2,1},{3,2},{4,7},{5,4},{6,5},{7,6},{8,11},{9,8},{10,9... | collective-permute-start | bytes 663560 | tf_op jit(solution)/shard_map/ppermute | solution.py:152
  54.8 21.5 %collective-permute-start.4 = (bf16[3,1,80,512]{3,2,1,0:T(8,128)(2,1)}, bf16[3,1,80,512]{3,2,1,0:T(8,128)(2,1)S(1)}, u32[]{:S(2)}, u32[]{:S(2)}) collective-permute-start(bf16[3,1,80,512]{3,2,1,0:T(8,128)(2,1)} %get-tuple-element.6), channel_id=1, source_target_pairs={{4,0},{8,4},{12,8},{5,1},{9,5},{13,9},{6,2},{10,6},{14,10},{7,3},{... | collective-permute-start | bytes 737288 | tf_op jit(solution)/shard_map/ppermute | solution.py:94
  56.0 20.2 %collective-permute-start.3 = (bf16[3,1,80,512]{3,2,1,0:T(8,128)(2,1)}, bf16[3,1,80,512]{3,2,1,0:T(8,128)(2,1)S(1)}, u32[]{:S(2)}, u32[]{:S(2)}) collective-permute-start(bf16[3,1,80,512]{3,2,1,0:T(8,128)(2,1)} %get-tuple-element.5), channel_id=1, source_target_pairs={{0,4},{4,8},{8,12},{1,5},{5,9},{9,13},{2,6},{6,10},{10,14},{3,7},{... | collective-permute-start | bytes 737288 | tf_op jit(solution)/shard_map/ppermute | solution.py:93
  118.0 7.9 %collective-permute-start.17 = (bf16[3,1,80,128]{3,2,1,0:T(8,128)(2,1)S(1)}, bf16[3,1,80,128]{3,2,1,0:T(8,128)(2,1)S(1)}, u32[]{:S(2)}, u32[]{:S(2)}) collective-permute-start(bf16[3,1,80,128]{3,2,1,0:T(8,128)(2,1)S(1)} %get-tuple-element.22), channel_id=1, source_target_pairs={{4,0},{8,4},{12,8},{5,1},{9,5},{13,9},{6,2},{10,6},{14,10},{7,3},{... | collective-permute-start | bytes 184328 | tf_op jit(solution)/shard_map/ppermute | solution.py:94
  119.3 6.6 %collective-permute-start.16 = (bf16[3,1,80,128]{3,2,1,0:T(8,128)(2,1)S(1)}, bf16[3,1,80,128]{3,2,1,0:T(8,128)(2,1)S(1)}, u32[]{:S(2)}, u32[]{:S(2)}) collective-permute-start(bf16[3,1,80,128]{3,2,1,0:T(8,128)(2,1)S(1)} %get-tuple-element.21), channel_id=1, source_target_pairs={{0,4},{4,8},{8,12},{1,5},{5,9},{9,13},{2,6},{6,10},{10,14},{3,7},{... | collective-permute-start | bytes 184328 | tf_op jit(solution)/shard_map/ppermute | solution.py:93
  129.7 13.5 %collective-permute-start.18 = (bf16[3,10,80,128]{3,2,1,0:T(8,128)(2,1)S(1)}, bf16[3,10,80,128]{3,2,1,0:T(8,128)(2,1)}, u32[]{:S(2)}, u32[]{:S(2)}) collective-permute-start(bf16[3,10,80,128]{3,2,1,0:T(8,128)(2,1)S(1)} %get-tuple-element.15), channel_id=1, source_target_pairs={{0,2},{2,0},{1,3},{3,1},{4,6},{6,4},{5,7},{7,5},{8,10},{10,8},{9,1... | collective-permute-start | bytes 1843208 | tf_op jit(solution)/shard_map/ppermute | solution.py:66
  137.5 8.5 %collective-permute-start.22 = (f32[8]{0:T(128)S(1)}, f32[8]{0:T(128)S(1)}, u32[]{:S(2)}, u32[]{:S(2)}) collective-permute-start(f32[8]{0:T(128)S(1)} %get-tuple-element.28), channel_id=1, source_target_pairs={{0,8},{4,12},{8,0},{12,4},{1,9},{5,13},{9,1},{13,5},{2,10},{6,14},... | collective-permute-start | bytes 104 | tf_op jit(solution)/shard_map/ppermute | solution.py:25
  139.4 6.6 %collective-permute-start.24 = (f32[8]{0:T(128)S(1)}, f32[8]{0:T(128)S(1)}, u32[]{:S(2)}, u32[]{:S(2)}) collective-permute-start(f32[8]{0:T(128)S(1)} %get-tuple-element.27), channel_id=1, source_target_pairs={{0,8},{4,12},{8,0},{12,4},{1,9},{5,13},{9,1},{13,5},{2,10},{6,14},... | collective-permute-start | bytes 104 | tf_op jit(solution)/shard_map/ppermute | solution.py:25
  139.9 14.1 %collective-permute-start.19 = (bf16[3,10,80,128]{3,2,1,0:T(8,128)(2,1)S(1)}, bf16[3,10,80,128]{3,2,1,0:T(8,128)(2,1)}, u32[]{:S(2)}, u32[]{:S(2)}) collective-permute-start(bf16[3,10,80,128]{3,2,1,0:T(8,128)(2,1)S(1)} %get-tuple-element.15), channel_id=1, source_target_pairs={{0,1},{1,0},{2,3},{3,2},{4,5},{5,4},{6,7},{7,6},{8,9},{9,8},{10,11... | collective-permute-start | bytes 1843208 | tf_op jit(solution)/shard_map/ppermute | solution.py:71
  143.2 12.8 %collective-permute-start.20 = (bf16[3,10,80,128]{3,2,1,0:T(8,128)(2,1)}, bf16[3,10,80,128]{3,2,1,0:T(8,128)(2,1)}, u32[]{:S(2)}, u32[]{:S(2)}) collective-permute-start(bf16[3,10,80,128]{3,2,1,0:T(8,128)(2,1)} %collective-permute-done.18), channel_id=1, source_target_pairs={{0,1},{1,0},{2,3},{3,2},{4,5},{5,4},{6,7},{7,6},{8,9},{9,8},{10,11... | collective-permute-start | bytes 1843208 | tf_op jit(solution)/shard_map/ppermute | solution.py:71
  191.8 5.9 %collective-permute-start.32 = (bf16[3,2,80,128]{3,2,1,0:T(8,128)(2,1)S(1)}, bf16[3,2,80,128]{3,2,1,0:T(8,128)(2,1)S(1)}, u32[]{:S(2)}, u32[]{:S(2)}) collective-permute-start(bf16[3,2,80,128]{3,2,1,0:T(8,128)(2,1)S(1)} %get-tuple-element.18), channel_id=1, source_target_pairs={{0,2},{1,3},{2,0},{3,1},{4,6},{5,7},{6,4},{7,5},{8,10},{9,11},{10,... | collective-permute-start | bytes 368648 | tf_op jit(solution)/shard_map/ppermute | solution.py:167
  192.1 6.2 %collective-permute-start.33 = (bf16[3,2,80,128]{3,2,1,0:T(8,128)(2,1)S(1)}, bf16[3,2,80,128]{3,2,1,0:T(8,128)(2,1)S(1)}, u32[]{:S(2)}, u32[]{:S(2)}) collective-permute-start(bf16[3,2,80,128]{3,2,1,0:T(8,128)(2,1)S(1)} %get-tuple-element.17), channel_id=1, source_target_pairs={{0,3},{1,0},{2,1},{3,2},{4,7},{5,4},{6,5},{7,6},{8,11},{9,8},{10,9... | collective-permute-start | bytes 368648 | tf_op jit(solution)/shard_map/ppermute | solution.py:167
  (22 other events, 274.3 us)
Sparse Core Ops, SparseCore 0:
  22.0 76.6 all-gather.2
  100.2 69.8 all-gather.4

commit v17 on v7

--- a/solution.py
+++ b/solution.py
@@ -95,8 +95,9 @@
     return jnp.concatenate([top, cells, bottom], axis=1)
 
 
-def conv_body(x_ref, w_ref, b_ref, o_ref, acc_ref):
+def conv_body(x_ref, w_ref, b_ref, *rest):
     step = pl.program_id(0)
+    o_ref, acc_ref = rest[-2:]
     rows, cols, outs = o_ref.shape[1:]
     chans = x_ref.shape[-1]
     acc_ref[...] = jnp.broadcast_to(b_ref[...], acc_ref.shape)
@@ -109,10 +110,13 @@
                     w_ref[9 * i + 3 * j + k],
                     preferred_element_type=jnp.float32,
                 )
-    o_ref[0] = acc_ref[...].reshape(rows, cols, outs).astype(o_ref.dtype)
-
-
-def causal_conv(extended, kernel, bias, out_dtype):
+    total = acc_ref[...].reshape(rows, cols, outs)
+    if len(rest) == 3:
+        total = rest[0][0].astype(jnp.float32) + total
+    o_ref[0] = total.astype(o_ref.dtype)
+
+
+def causal_conv(extended, kernel, bias, out_dtype, residual=None):
     leading = jnp.concatenate([extended[:1], extended[:1], extended], axis=0)
     padded = jnp.pad(leading, ((0, 0), (0, 0), (1, 1), (0, 0)))
     frames = extended.shape[0]
@@ -121,19 +125,24 @@
     taps, chans, outs = kernel.shape
     flops = 2 * frames * rows * cols * chans * outs * taps
     moved = padded.size * 2 + kernel.size * 2 + frames * rows * cols * outs * 4
+    in_specs = [
+        pl.BlockSpec(padded.shape, lambda t: (0, 0, 0, 0)),
+        pl.BlockSpec(kernel.shape, lambda t: (0, 0, 0)),
+        pl.BlockSpec((1, outs), lambda t: (0, 0)),
+    ]
+    operands = [padded, kernel, bias.reshape(1, outs)]
+    if residual is not None:
+        in_specs.append(pl.BlockSpec((1, rows, cols, outs), lambda t: (t, 0, 0, 0)))
+        operands.append(residual)
     return pl.pallas_call(
         conv_body,
         grid=(frames,),
-        in_specs=[
-            pl.BlockSpec(padded.shape, lambda t: (0, 0, 0, 0)),
-            pl.BlockSpec(kernel.shape, lambda t: (0, 0, 0)),
-            pl.BlockSpec((1, outs), lambda t: (0, 0)),
-        ],
+        in_specs=in_specs,
         out_specs=pl.BlockSpec((1, rows, cols, outs), lambda t: (t, 0, 0, 0)),
         out_shape=jax.ShapeDtypeStruct((frames, rows, cols, outs), out_dtype),
         scratch_shapes=[pltpu.VMEM((rows * cols, outs), jnp.float32)],
         cost_estimate=pl.CostEstimate(flops=flops, bytes_accessed=moved, transcendentals=0),
-    )(padded, kernel, bias.reshape(1, outs))
+    )(*operands)
 
 
 def kernel_block(shard, chans):
@@ -203,10 +212,11 @@
     mean_chan, scale_chan = group_scale(packed[0], packed[1], count, group_size)
     act_second = activate(raw_next.astype(jnp.float32), mean_chan, scale_chan, gain_second, shift_second)
     own_bias_next = lax.dynamic_slice_in_dim(bias_second, me * width, width)
-    branch = causal_conv(edge_mask(act_second), weights_second, own_bias_next, jnp.float32)
 
     own_latent = lax.dynamic_slice_in_dim(raw_rows[:, 1:-1], me * width, width, axis=3)
-    summed = (own_latent.astype(jnp.float32) + branch).astype(jnp.bfloat16)
+    summed = causal_conv(
+        edge_mask(act_second), weights_second, own_bias_next, jnp.bfloat16, own_latent
+    )
     summed_rows = scatter_rows(summed, slab_rows, chans)
     return jnp.repeat(jnp.repeat(summed_rows, 2, axis=1), 2, axis=2)
 

time: 210 us -> 210 us (level)
  waiting for transfers between devices: 64.6 us -> 72.6 us
  starting transfers between devices: 48 us -> 44.6 us
  other arithmetic: 16.1 us -> 13.5 us
    all_gather x2, waiting for transfers between devices: 20.9 us -> 29 us  [kernel_block(): return lax.all_gather(out, 'hz', axis=1, tiled=True)]
    dynamic_update_slice x11, local copies, waits for them, and re-layouts: 9.92 us -> 6.61 us  [chip_gather(): out = lax.dynamic_update_slice(out, piece, start)]
    ppermute x6, starting transfers between devices: 12.3 us -> 9.05 us  [chip_gather(): lax.ppermute(firsts, 'hb', shift_pairs(count_b, step))]
  transfers between devices with their start and end apart: 36 -> 36, of which waited for: 20 -> 19; matrix products, arithmetic and copies ran while one was open for 18% -> 15% of each run, Pallas kernels for 9% -> 9%
where the time goes in v17:
time: 210 us
  waiting for transfers between devices  72.6 us (35%)
  starting transfers between devices  44.6 us (21%)
  Pallas kernels  37.4 us (18%)
  local copies, waits for them, and re-layouts  27.5 us (13%)
  between operations  14 us (7%)
  other arithmetic  13.5 us (6%)
    pallas_call x2, Pallas kernels, causal_conv(): pl.pallas_call(conv_body, grid=(frames,), in_specs=in_specs, out_specs=pl...  37.4 us
    all_gather x2, waiting for transfers between devices, kernel_block(): return lax.all_gather(out, 'hz', axis=1, tiled=True)  29 us
    ppermute x12, waiting for transfers between devices, butterfly_stats(): other_sums, other_squares = lax.ppermute((sums, squares), axis, pairs)  15 us
    ppermute x2, waiting for transfers between devices, with_row_halo(): bottom = lax.ppermute(cells[:, :1], axis_name, up)  14.1 us
    ppermute x12, starting transfers between devices, butterfly_stats(): other_sums, other_squares = lax.ppermute((sums, squares), axis, pairs)  11.1 us
    ppermute x6, starting transfers between devices, chip_gather(): lax.ppermute(firsts, 'hb', shift_pairs(count_b, step))  9.05 us
    ppermute x2, starting transfers between devices, with_row_halo(): top = lax.ppermute(cells[:, -1:], axis_name, down)  8.4 us
    ppermute x6, waiting for transfers between devices, kernel_block(): piece = lax.ppermute(piece, HQ, shift_pairs(size, step))  7.95 us
  transfers between devices with their start and end apart: 36, of which 19 were waited for; matrix products, arithmetic and copies ran while one was open for 15% of the time, Pallas kernels for 9%

profile of v17, /device:TPU:1, one launch (start us, length us, event | category | flops | bytes accessed | tf_op | source)
XLA Modules:
  0.0 209.7 jit_solution(9896695808960756482)
XLA Ops:
  8.3 2.7 %collective-permute-start.13 = (bf16[27,32,128]{2,1,0:T(8,128)(2,1)S(1)}, bf16[27,32,128]{2,1,0:T(8,128)(2,1)}, u32[]{:S(2)}, u32[]{:S(2)}) collective-permute-start(bf16[27,32,128]{2,1,0:T(8,128)(2,1)S(1)} %get-tuple-element.12), channel_id=1, source_target_pairs={{0,1},{1,2},{2,3},{3,0},{4,5},{5,6},{6,7},{7,4},{8,9},{9,10},{10,1... | collective-permute-start | bytes 663560 | tf_op jit(solution)/shard_map/ppermute | solution.py:158
  11.5 4.2 %collective-permute-done.13 = bf16[27,32,128]{2,1,0:T(8,128)(2,1)} collective-permute-done((bf16[27,32,128]{2,1,0:T(8,128)(2,1)S(1)}, bf16[27,32,128]{2,1,0:T(8,128)(2,1)}, u32[]{:S(2)}, u32[]{:S(2)}) %collective-permute-start.13) | collective-permute-done | bytes 221216 | tf_op jit(solution)/shard_map/ppermute | solution.py:158
  16.6 3.8 %collective-permute-done.14 = bf16[27,32,128]{2,1,0:T(8,128)(2,1)} collective-permute-done((bf16[27,32,128]{2,1,0:T(8,128)(2,1)S(1)}, bf16[27,32,128]{2,1,0:T(8,128)(2,1)}, u32[]{:S(2)}, u32[]{:S(2)}) %collective-permute-start.14) | collective-permute-done | bytes 221216 | tf_op jit(solution)/shard_map/ppermute | solution.py:158
  22.4 2.1 collective-permute-start
  31.4 4.9 %collective-permute-done.5 = f32[32]{0:T(128)S(1)} collective-permute-done((f32[32]{0:T(128)S(1)}, f32[32]{0:T(128)S(1)}, u32[]{:S(2)}, u32[]{:S(2)}) %collective-permute-start.5) | collective-permute-done | bytes 160 | tf_op jit(solution)/shard_map/ppermute | solution.py:25
  41.7 2.0 collective-permute-start.8
  46.6 2.4 %collective-permute-done.12 = f32[32]{0:T(128)S(1)} collective-permute-done((f32[32]{0:T(128)S(1)}, f32[32]{0:T(128)S(1)}, u32[]{:S(2)}, u32[]{:S(2)}) %collective-permute-start.12) | collective-permute-done | bytes 160 | tf_op jit(solution)/shard_map/ppermute | solution.py:25
  56.0 4.2 %collective-permute-start.3 = (bf16[3,1,80,512]{3,2,1,0:T(8,128)(2,1)}, bf16[3,1,80,512]{3,2,1,0:T(8,128)(2,1)S(1)}, u32[]{:S(2)}, u32[]{:S(2)}) collective-permute-start(bf16[3,1,80,512]{3,2,1,0:T(8,128)(2,1)} %get-tuple-element.5), channel_id=1, source_target_pairs={{0,4},{4,8},{8,12},{1,5},{5,9},{9,13},{2,6},{6,10},{10,14},{3,7},{... | collective-permute-start | bytes 737288 | tf_op jit(solution)/shard_map/ppermute | solution.py:93
  64.2 12.5 %collective-permute-done.4 = bf16[3,1,80,512]{3,2,1,0:T(8,128)(2,1)S(1)} collective-permute-done((bf16[3,1,80,512]{3,2,1,0:T(8,128)(2,1)}, bf16[3,1,80,512]{3,2,1,0:T(8,128)(2,1)S(1)}, u32[]{:S(2)}, u32[]{:S(2)}) %collective-permute-start.4) | collective-permute-done | bytes 245792 | tf_op jit(solution)/shard_map/ppermute | solution.py:94
  78.7 3.2 %fusion.5.x_ref = bf16[5,10,82,512]{3,2,1,0:T(8,128)(2,1)} fusion(bf16[3,10,80,512]{3,2,1,0:T(8,128)(2,1)S(1)} %fusion.6, bf16[1,10,80,512]{3,2,1,0:T(8,128)(2,1)S(1)} %slice.36), kind=kLoop, calls=%fused_computation.11 | loop fusion | flops 25190400 | bytes 7475200 | tf_op jit(solution)/shard_map/concatenate | solution.py:120
  81.8 17.3 %all-gather.3.cloned.1.call-done.w_ref = bf16[27,512,128]{2,1,0:T(8,128)(2,1)} async-done(((bf16[27,128,128]{2,1,0:T(8,128)(2,1)}), bf16[27,512,128]{2,1,0:T(8,128)(2,1)}) %all-gather.3.cloned.1.call-update) | async-done | bytes 3538960 | tf_op jit(solution)/shard_map/all_gather | solution.py:161
  99.2 18.5 %shard_map.91 = bf16[3,8,80,128]{3,2,1,0:T(8,128)(2,1)} custom-call(bf16[5,10,82,512]{3,2,1,0:T(8,128)(2,1)} %fusion.5.x_ref, bf16[27,512,128]{2,1,0:T(8,128)(2,1)} %all-gather.3.cloned.1.call-done.w_ref, f32[1,128]{1,0:T(1,128)} %dynamic-slice_bitcast_fusion.1.b_ref), custom_call_target="tpu_custom_call" | custom-call | flops 6794772480 | bytes 8720384 | tf_op jit(solution)/shard_map/pallas_call | solution.py:137
  119.8 4.2 %collective-permute-start.16 = (bf16[3,1,80,128]{3,2,1,0:T(8,128)(2,1)S(1)}, bf16[3,1,80,128]{3,2,1,0:T(8,128)(2,1)S(1)}, u32[]{:S(2)}, u32[]{:S(2)}) collective-permute-start(bf16[3,1,80,128]{3,2,1,0:T(8,128)(2,1)S(1)} %get-tuple-element.21), channel_id=1, source_target_pairs={{0,4},{4,8},{8,12},{1,5},{5,9},{9,13},{2,6},{6,10},{10,14},{3,7},{... | collective-permute-start | bytes 184328 | tf_op jit(solution)/shard_map/ppermute | solution.py:93
  126.8 2.0 pad_maximum_fusion
  130.5 2.6 %collective-permute-start.21 = (f32[8]{0:T(128)S(1)}, f32[8]{0:T(128)S(1)}, u32[]{:S(2)}, u32[]{:S(2)}) collective-permute-start(f32[8]{0:T(128)S(1)} %reduce_sum.72), channel_id=1, source_target_pairs={{0,4},{4,0},{8,12},{12,8},{1,5},{5,1},{9,13},{13,9},{2,6},{6,2},{1... | collective-permute-start | bytes 104 | tf_op jit(solution)/shard_map/ppermute | solution.py:25
  134.4 3.1 %collective-permute-done.23 = f32[8]{0:T(128)S(1)} collective-permute-done((f32[8]{0:T(128)S(1)}, f32[8]{0:T(128)S(1)}, u32[]{:S(2)}, u32[]{:S(2)}) %collective-permute-start.23) | collective-permute-done | bytes 64 | tf_op jit(solution)/shard_map/ppermute | solution.py:25
  139.9 2.3 %collective-permute-start.19 = (bf16[3,10,80,128]{3,2,1,0:T(8,128)(2,1)}, bf16[3,10,80,128]{3,2,1,0:T(8,128)(2,1)}, u32[]{:S(2)}, u32[]{:S(2)}) collective-permute-start(bf16[3,10,80,128]{3,2,1,0:T(8,128)(2,1)} %get-tuple-element.15), channel_id=1, source_target_pairs={{0,1},{1,0},{2,3},{3,2},{4,5},{5,4},{6,7},{7,6},{8,9},{9,8},{10,11... | collective-permute-start | bytes 1843208 | tf_op jit(solution)/shard_map/ppermute | solution.py:71
  142.2 3.1 %collective-permute-start.20 = (bf16[3,10,80,128]{3,2,1,0:T(8,128)(2,1)}, bf16[3,10,80,128]{3,2,1,0:T(8,128)(2,1)S(1)}, u32[]{:S(2)}, u32[]{:S(2)}) collective-permute-start(bf16[3,10,80,128]{3,2,1,0:T(8,128)(2,1)} %collective-permute-done.18), channel_id=1, source_target_pairs={{0,1},{1,0},{2,3},{3,2},{4,5},{5,4},{6,7},{7,6},{8,9},{9,8},{10,11... | collective-permute-start | bytes 1843208 | tf_op jit(solution)/shard_map/ppermute | solution.py:71
  155.8 3.2 %select_maximum_fusion.x_ref = bf16[5,10,82,512]{3,2,1,0:T(8,128)(2,1)} fusion(bf16[3,10,80,512]{3,2,1,0:T(8,128)(2,1)S(1)} %fusion.7, bf16[1,10,80,512]{3,2,1,0:T(8,128)(2,1)S(1)} %slice.39), kind=kLoop, calls=%fused_computation.5 | loop fusion | flops 25190400 | bytes 7475200 | tf_op jit(solution)/shard_map/concatenate | solution.py:120
  159.0 11.7 %all-gather.5.cloned.1.call-done.w_ref = bf16[27,512,128]{2,1,0:T(8,128)(2,1)} async-done(((bf16[27,128,128]{2,1,0:T(8,128)(2,1)}), bf16[27,512,128]{2,1,0:T(8,128)(2,1)}) %all-gather.5.cloned.1.call-update) | async-done | bytes 3538960 | tf_op jit(solution)/shard_map/all_gather | solution.py:161
  170.7 19.0 %shard_map.92 = bf16[3,8,80,128]{3,2,1,0:T(8,128)(2,1)} custom-call(bf16[5,10,82,512]{3,2,1,0:T(8,128)(2,1)} %select_maximum_fusion.x_ref, bf16[27,512,128]{2,1,0:T(8,128)(2,1)} %all-gather.5.cloned.1.call-done.w_ref, f32[1,128]{1,0:T(1,128)} %dynamic-slice_bitcast_fusion.b_ref, bf16[3,8,80,128]{3,2,1,0:T(8,128)(2,1)} %constant_dynamic-slice_fusion.3.rest_0_), custom_call_target="tpu_custom_call" | custom-call | flops 6794772480 | bytes 8720384 | tf_op jit(solution)/shard_map/pallas_call | solution.py:137
  193.1 2.1 collective-permute-done.31
  195.2 3.3 %collective-permute-done.32 = bf16[3,2,80,128]{3,2,1,0:T(8,128)(2,1)S(1)} collective-permute-done((bf16[3,2,80,128]{3,2,1,0:T(8,128)(2,1)S(1)}, bf16[3,2,80,128]{3,2,1,0:T(8,128)(2,1)S(1)}, u32[]{:S(2)}, u32[]{:S(2)}) %collective-permute-start.32) | collective-permute-done | bytes 122912 | tf_op jit(solution)/shard_map/ppermute | solution.py:173
  200.7 2.2 %reshape.59 = bf16[3,4,160,512]{3,2,1,0:T(8,128)(2,1)} reshape(bf16[3,4,80,2,512]{4,3,2,1,0:T(2,128)(2,1)S(1)} %broadcast_in_dim.53) | data formatting | bytes 3932160 | tf_op jit(solution)/shard_map/reshape | solution.py:221
  (151 shorter events, 59.2 us)
Async XLA Ops:
  6.5 92.6 %all-gather.3.cloned.1.call-start = ((), (), s32[]{:S(2)}) async-start(), calls=%async_computation | async-start | bytes 4423680 | tf_op jit(solution)/shard_map/all_gather | solution.py:161
  8.3 7.3 %collective-permute-start.13 = (bf16[27,32,128]{2,1,0:T(8,128)(2,1)S(1)}, bf16[27,32,128]{2,1,0:T(8,128)(2,1)}, u32[]{:S(2)}, u32[]{:S(2)}) collective-permute-start(bf16[27,32,128]{2,1,0:T(8,128)(2,1)S(1)} %get-tuple-element.12), channel_id=1, source_target_pairs={{0,1},{1,2},{2,3},{3,0},{4,5},{5,6},{6,7},{7,4},{8,9},{9,10},{10,1... | collective-permute-start | bytes 663560 | tf_op jit(solution)/shard_map/ppermute | solution.py:158
  11.0 9.4 %collective-permute-start.14 = (bf16[27,32,128]{2,1,0:T(8,128)(2,1)S(1)}, bf16[27,32,128]{2,1,0:T(8,128)(2,1)}, u32[]{:S(2)}, u32[]{:S(2)}) collective-permute-start(bf16[27,32,128]{2,1,0:T(8,128)(2,1)S(1)} %get-tuple-element.14), channel_id=1, source_target_pairs={{0,2},{1,3},{2,0},{3,1},{4,6},{5,7},{6,4},{7,5},{8,10},{9,11},{10,... | collective-permute-start | bytes 663560 | tf_op jit(solution)/shard_map/ppermute | solution.py:158
  11.0 10.3 %collective-permute-start.15 = (bf16[27,32,128]{2,1,0:T(8,128)(2,1)S(1)}, bf16[27,32,128]{2,1,0:T(8,128)(2,1)S(1)}, u32[]{:S(2)}, u32[]{:S(2)}) collective-permute-start(bf16[27,32,128]{2,1,0:T(8,128)(2,1)S(1)} %get-tuple-element.11), channel_id=1, source_target_pairs={{0,3},{1,0},{2,1},{3,2},{4,7},{5,4},{6,5},{7,6},{8,11},{9,8},{10,9... | collective-permute-start | bytes 663560 | tf_op jit(solution)/shard_map/ppermute | solution.py:158
  22.4 148.3 %all-gather.5.cloned.1.call-start = ((), (), s32[]{:S(2)}) async-start(), calls=%async_computation.1 | async-start | bytes 4423680 | tf_op jit(solution)/shard_map/all_gather | solution.py:161
  22.4 16.9 %collective-permute-start = (bf16[3,2,80,512]{3,2,1,0:T(8,128)(2,1)S(1)}, bf16[3,2,80,512]{3,2,1,0:T(8,128)(2,1)}, u32[]{:S(2)}, u32[]{:S(2)}) collective-permute-start(bf16[3,2,80,512]{3,2,1,0:T(8,128)(2,1)S(1)} %copy-done.2), channel_id=1, source_target_pairs={{0,2},{2,0},{1,3},{3,1},{4,6},{6,4},{5,7},{7,5},{8,10},{10,8},{9,1... | collective-permute-start | bytes 1474568 | tf_op jit(solution)/shard_map/ppermute | solution.py:66
  24.5 27.2 %collective-permute-start.1 = (bf16[3,2,80,512]{3,2,1,0:T(8,128)(2,1)S(1)}, bf16[3,2,80,512]{3,2,1,0:T(8,128)(2,1)}, u32[]{:S(2)}, u32[]{:S(2)}) collective-permute-start(bf16[3,2,80,512]{3,2,1,0:T(8,128)(2,1)S(1)} %copy-done.2), channel_id=1, source_target_pairs={{0,1},{1,0},{2,3},{3,2},{4,5},{5,4},{6,7},{7,6},{8,9},{9,8},{10,11... | collective-permute-start | bytes 1474568 | tf_op jit(solution)/shard_map/ppermute | solution.py:71
  24.8 11.5 %collective-permute-start.5 = (f32[32]{0:T(128)S(1)}, f32[32]{0:T(128)S(1)}, u32[]{:S(2)}, u32[]{:S(2)}) collective-permute-start(f32[32]{0:T(128)S(1)} %reduce_sum.51), channel_id=1, source_target_pairs={{0,2},{2,0},{1,3},{3,1},{4,6},{6,4},{5,7},{7,5},{8,10},{10,8},{9,1... | collective-permute-start | bytes 392 | tf_op jit(solution)/shard_map/ppermute | solution.py:25
  25.5 10.8 %collective-permute-start.9 = (f32[32]{0:T(128)S(1)}, f32[32]{0:T(128)S(1)}, u32[]{:S(2)}, u32[]{:S(2)}) collective-permute-start(f32[32]{0:T(128)S(1)} %reduce_sum.54), channel_id=1, source_target_pairs={{0,2},{2,0},{1,3},{3,1},{4,6},{6,4},{5,7},{7,5},{8,10},{10,8},{9,1... | collective-permute-start | bytes 392 | tf_op jit(solution)/shard_map/ppermute | solution.py:25
  28.1 32.2 %collective-permute-start.28 = (bf16[27,32,128]{2,1,0:T(8,128)(2,1)}, bf16[27,32,128]{2,1,0:T(8,128)(2,1)}, u32[]{:S(2)}, u32[]{:S(2)}) collective-permute-start(bf16[27,32,128]{2,1,0:T(8,128)(2,1)} %get-tuple-element.8), channel_id=1, source_target_pairs={{0,1},{1,2},{2,3},{3,0},{4,5},{5,6},{6,7},{7,4},{8,9},{9,10},{10,1... | collective-permute-start | bytes 663560 | tf_op jit(solution)/shard_map/ppermute | solution.py:158
  39.3 13.5 %collective-permute-start.2 = (bf16[3,2,80,512]{3,2,1,0:T(8,128)(2,1)}, bf16[3,2,80,512]{3,2,1,0:T(8,128)(2,1)}, u32[]{:S(2)}, u32[]{:S(2)}) collective-permute-start(bf16[3,2,80,512]{3,2,1,0:T(8,128)(2,1)} %collective-permute-done), channel_id=1, source_target_pairs={{0,1},{1,0},{2,3},{3,2},{4,5},{5,4},{6,7},{7,6},{8,9},{9,8},{10,11... | collective-permute-start | bytes 1474568 | tf_op jit(solution)/shard_map/ppermute | solution.py:71
  45.5 15.8 %collective-permute-start.29 = (bf16[27,32,128]{2,1,0:T(8,128)(2,1)}, bf16[27,32,128]{2,1,0:T(8,128)(2,1)}, u32[]{:S(2)}, u32[]{:S(2)}) collective-permute-start(bf16[27,32,128]{2,1,0:T(8,128)(2,1)} %get-tuple-element.10), channel_id=1, source_target_pairs={{0,2},{1,3},{2,0},{3,1},{4,6},{5,7},{6,4},{7,5},{8,10},{9,11},{10,... | collective-permute-start | bytes 663560 | tf_op jit(solution)/shard_map/ppermute | solution.py:158
  49.0 13.3 %collective-permute-start.30 = (bf16[27,32,128]{2,1,0:T(8,128)(2,1)}, bf16[27,32,128]{2,1,0:T(8,128)(2,1)}, u32[]{:S(2)}, u32[]{:S(2)}) collective-permute-start(bf16[27,32,128]{2,1,0:T(8,128)(2,1)} %get-tuple-element.7), channel_id=1, source_target_pairs={{0,3},{1,0},{2,1},{3,2},{4,7},{5,4},{6,5},{7,6},{8,11},{9,8},{10,9... | collective-permute-start | bytes 663560 | tf_op jit(solution)/shard_map/ppermute | solution.py:158
  54.7 22.0 %collective-permute-start.4 = (bf16[3,1,80,512]{3,2,1,0:T(8,128)(2,1)}, bf16[3,1,80,512]{3,2,1,0:T(8,128)(2,1)S(1)}, u32[]{:S(2)}, u32[]{:S(2)}) collective-permute-start(bf16[3,1,80,512]{3,2,1,0:T(8,128)(2,1)} %get-tuple-element.6), channel_id=1, source_target_pairs={{4,0},{8,4},{12,8},{5,1},{9,5},{13,9},{6,2},{10,6},{14,10},{7,3},{... | collective-permute-start | bytes 737288 | tf_op jit(solution)/shard_map/ppermute | solution.py:94
  56.0 20.7 %collective-permute-start.3 = (bf16[3,1,80,512]{3,2,1,0:T(8,128)(2,1)}, bf16[3,1,80,512]{3,2,1,0:T(8,128)(2,1)S(1)}, u32[]{:S(2)}, u32[]{:S(2)}) collective-permute-start(bf16[3,1,80,512]{3,2,1,0:T(8,128)(2,1)} %get-tuple-element.5), channel_id=1, source_target_pairs={{0,4},{4,8},{8,12},{1,5},{5,9},{9,13},{2,6},{6,10},{10,14},{3,7},{... | collective-permute-start | bytes 737288 | tf_op jit(solution)/shard_map/ppermute | solution.py:93
  118.5 7.9 %collective-permute-start.17 = (bf16[3,1,80,128]{3,2,1,0:T(8,128)(2,1)S(1)}, bf16[3,1,80,128]{3,2,1,0:T(8,128)(2,1)S(1)}, u32[]{:S(2)}, u32[]{:S(2)}) collective-permute-start(bf16[3,1,80,128]{3,2,1,0:T(8,128)(2,1)S(1)} %get-tuple-element.22), channel_id=1, source_target_pairs={{4,0},{8,4},{12,8},{5,1},{9,5},{13,9},{6,2},{10,6},{14,10},{7,3},{... | collective-permute-start | bytes 184328 | tf_op jit(solution)/shard_map/ppermute | solution.py:94
  119.8 6.6 %collective-permute-start.16 = (bf16[3,1,80,128]{3,2,1,0:T(8,128)(2,1)S(1)}, bf16[3,1,80,128]{3,2,1,0:T(8,128)(2,1)S(1)}, u32[]{:S(2)}, u32[]{:S(2)}) collective-permute-start(bf16[3,1,80,128]{3,2,1,0:T(8,128)(2,1)S(1)} %get-tuple-element.21), channel_id=1, source_target_pairs={{0,4},{4,8},{8,12},{1,5},{5,9},{9,13},{2,6},{6,10},{10,14},{3,7},{... | collective-permute-start | bytes 184328 | tf_op jit(solution)/shard_map/ppermute | solution.py:93
  128.8 13.4 %collective-permute-start.18 = (bf16[3,10,80,128]{3,2,1,0:T(8,128)(2,1)}, bf16[3,10,80,128]{3,2,1,0:T(8,128)(2,1)}, u32[]{:S(2)}, u32[]{:S(2)}) collective-permute-start(bf16[3,10,80,128]{3,2,1,0:T(8,128)(2,1)} %get-tuple-element.15), channel_id=1, source_target_pairs={{0,2},{2,0},{1,3},{3,1},{4,6},{6,4},{5,7},{7,5},{8,10},{10,8},{9,1... | collective-permute-start | bytes 1843208 | tf_op jit(solution)/shard_map/ppermute | solution.py:66
  137.6 7.8 %collective-permute-start.22 = (f32[8]{0:T(128)S(1)}, f32[8]{0:T(128)S(1)}, u32[]{:S(2)}, u32[]{:S(2)}) collective-permute-start(f32[8]{0:T(128)S(1)} %get-tuple-element.28), channel_id=1, source_target_pairs={{0,8},{4,12},{8,0},{12,4},{1,9},{5,13},{9,1},{13,5},{2,10},{6,14},... | collective-permute-start | bytes 104 | tf_op jit(solution)/shard_map/ppermute | solution.py:25
  138.5 6.8 %collective-permute-start.24 = (f32[8]{0:T(128)S(1)}, f32[8]{0:T(128)S(1)}, u32[]{:S(2)}, u32[]{:S(2)}) collective-permute-start(f32[8]{0:T(128)S(1)} %get-tuple-element.27), channel_id=1, source_target_pairs={{0,8},{4,12},{8,0},{12,4},{1,9},{5,13},{9,1},{13,5},{2,10},{6,14},... | collective-permute-start | bytes 104 | tf_op jit(solution)/shard_map/ppermute | solution.py:25
  139.9 12.5 %collective-permute-start.19 = (bf16[3,10,80,128]{3,2,1,0:T(8,128)(2,1)}, bf16[3,10,80,128]{3,2,1,0:T(8,128)(2,1)}, u32[]{:S(2)}, u32[]{:S(2)}) collective-permute-start(bf16[3,10,80,128]{3,2,1,0:T(8,128)(2,1)} %get-tuple-element.15), channel_id=1, source_target_pairs={{0,1},{1,0},{2,3},{3,2},{4,5},{5,4},{6,7},{7,6},{8,9},{9,8},{10,11... | collective-permute-start | bytes 1843208 | tf_op jit(solution)/shard_map/ppermute | solution.py:71
  142.2 11.4 %collective-permute-start.20 = (bf16[3,10,80,128]{3,2,1,0:T(8,128)(2,1)}, bf16[3,10,80,128]{3,2,1,0:T(8,128)(2,1)S(1)}, u32[]{:S(2)}, u32[]{:S(2)}) collective-permute-start(bf16[3,10,80,128]{3,2,1,0:T(8,128)(2,1)} %collective-permute-done.18), channel_id=1, source_target_pairs={{0,1},{1,0},{2,3},{3,2},{4,5},{5,4},{6,7},{7,6},{8,9},{9,8},{10,11... | collective-permute-start | bytes 1843208 | tf_op jit(solution)/shard_map/ppermute | solution.py:71
  192.7 5.9 %collective-permute-start.32 = (bf16[3,2,80,128]{3,2,1,0:T(8,128)(2,1)S(1)}, bf16[3,2,80,128]{3,2,1,0:T(8,128)(2,1)S(1)}, u32[]{:S(2)}, u32[]{:S(2)}) collective-permute-start(bf16[3,2,80,128]{3,2,1,0:T(8,128)(2,1)S(1)} %get-tuple-element.18), channel_id=1, source_target_pairs={{0,2},{1,3},{2,0},{3,1},{4,6},{5,7},{6,4},{7,5},{8,10},{9,11},{10,... | collective-permute-start | bytes 368648 | tf_op jit(solution)/shard_map/ppermute | solution.py:173
  192.9 6.2 %collective-permute-start.33 = (bf16[3,2,80,128]{3,2,1,0:T(8,128)(2,1)S(1)}, bf16[3,2,80,128]{3,2,1,0:T(8,128)(2,1)S(1)}, u32[]{:S(2)}, u32[]{:S(2)}) collective-permute-start(bf16[3,2,80,128]{3,2,1,0:T(8,128)(2,1)S(1)} %get-tuple-element.17), channel_id=1, source_target_pairs={{0,3},{1,0},{2,1},{3,2},{4,7},{5,4},{6,5},{7,6},{8,11},{9,8},{10,9... | collective-permute-start | bytes 368648 | tf_op jit(solution)/shard_map/ppermute | solution.py:173
  (22 other events, 261.3 us)
Sparse Core Ops, SparseCore 0:
  22.5 76.6 all-gather.2
  100.7 69.9 all-gather.4
